TPU v7x, 32 devices: a whole 2x2x4 slice. The times are simulated.
32 devices in a mesh: grp: 4 (over x, core), ep: 8 (over z, y).
Axes of the slice: x: 2, y: 2, z: 4, core: 2. Of those that a mesh axis runs over, the one named last changes fastest.
Arguments:
- tokens: bfloat16 [2048, 5120], P('ep', 'grp'), may hold values from -6 to 6
- cotangent: bfloat16 [2048, 5120], P('ep', 'grp'), may hold values from -0.59765625 to 0.59765625
- gate_weights: bfloat16 [2048, 6], P('ep'), may hold values from 0.099609375 to 1
- expert_ids: int32 [2048, 6], P('ep'), may hold values from 0 to 159, all different within a row; in each aligned block of 256 rows (0 to 255, 256 to 511, ...) at most 16 rows name the same one
- hot_ids: int32 [2], replicated, may hold values from 8 to 159, as said below
- gate_cold: bfloat16 [8, 5120, 768], P('ep', 'grp'), may hold values from -0.078125 to 0.078125
- up_cold: bfloat16 [8, 5120, 768], P('ep', 'grp'), may hold values from -0.078125 to 0.078125
- down_cold: bfloat16 [8, 768, 5120], P('ep', None, 'grp'), may hold values from -0.21875 to 0.21875
- gate_hot: bfloat16 [2, 5120, 768], P(None, 'grp', 'ep'), may hold values from -0.078125 to 0.078125
- up_hot: bfloat16 [2, 5120, 768], P(None, 'grp', 'ep'), may hold values from -0.078125 to 0.078125
- down_hot: bfloat16 [2, 768, 5120], P(None, 'ep', 'grp'), may hold values from -0.21875 to 0.21875
Outputs:
- grad_gate_cold: bfloat16 [8, 5120, 768], P('ep', 'grp')
- grad_up_cold: bfloat16 [8, 5120, 768], P('ep', 'grp')
- grad_down_cold: bfloat16 [8, 768, 5120], P('ep', None, 'grp')
- grad_gate_hot: float32 [2, 5120, 768], P(None, 'grp', 'ep')
- grad_up_hot: float32 [2, 5120, 768], P(None, 'grp', 'ep')
- grad_down_hot: float32 [2, 768, 5120], P(None, 'ep', 'grp')
- gate_weight_grad: float32 [2048, 6], P('ep')
Inputs may be any that keep to these rules, and one draw needn't show every extreme that they name: `expert_ids`: each row names 6 different experts. Among the routes of the 256 tokens of one index of ep (aligned blocks of rows) no expert is named more than 16 times, a bound that some block reaches. `hot_ids`: distinct expert numbers, none below 8; expert 160 - 1 is always among them.
All inputs are finite; a program needn't handle non-finite values.
Results may differ from a plain program's by a relative error of at most 0.02.
Values may be sent and summed in bfloat16 or wider, within the bound.
No kernel may reach another device: no remote copies, remote signals or barrier semaphores. Data moves between devices by JAX's collectives and lax.ppermute only.
A program may use at most 128 MiB of HBM per device.

v0:
```python
import jax
import jax.numpy as jnp
from jax import lax
from jax.sharding import PartitionSpec as P


def route_table(flat_ids, targets, capacity):
    matches = (flat_ids[:, None] == targets[None, :]).astype(jnp.int32)
    rank_of = jnp.cumsum(matches, axis=0) - 1
    slot_of = jnp.sum(matches * rank_of, axis=1)
    owner_of = jnp.sum(matches * jnp.arange(targets.shape[0], dtype=jnp.int32)[None, :], axis=1)
    usable = jnp.sum(matches, axis=1) > 0
    row_of = owner_of * capacity + slot_of
    rows_total = targets.shape[0] * capacity
    route_map = (row_of[None, :] == jnp.arange(rows_total, dtype=jnp.int32)[:, None]) & usable[
        None, :
    ]
    return route_map.astype(jnp.float32)


def gather_rows(route_map, tokens, cotangent, flat_weights, tok_rows, top_count):
    per_token = jnp.sum(route_map.reshape(route_map.shape[0], tok_rows, top_count), axis=2)
    token_map = per_token.astype(jnp.bfloat16)
    feat_rows = jnp.dot(token_map, tokens, preferred_element_type=jnp.float32).astype(jnp.bfloat16)
    cotan_rows = jnp.dot(token_map, cotangent, preferred_element_type=jnp.float32).astype(
        jnp.bfloat16
    )
    scale_rows = jnp.dot(
        route_map, flat_weights.astype(jnp.float32), precision=lax.Precision.HIGHEST
    )
    return (feat_rows, cotan_rows, scale_rows.astype(jnp.bfloat16))


def swiglu_back(pre_gate, pre_up, grad_hidden):
    sigmoid_gate = jax.nn.sigmoid(pre_gate)
    activated = pre_gate * sigmoid_gate
    hidden = (activated * pre_up).astype(jnp.bfloat16)
    back_gate = (
        grad_hidden * pre_up * sigmoid_gate * (1.0 + pre_gate * (1.0 - sigmoid_gate))
    ).astype(jnp.bfloat16)
    back_up = (grad_hidden * activated).astype(jnp.bfloat16)
    return (hidden, back_gate, back_up)


def body(
    tokens,
    cotangent,
    gate_weights,
    expert_ids,
    hot_ids,
    gate_cold,
    up_cold,
    down_cold,
    gate_hot,
    up_hot,
    down_hot,
):
    tok_rows, slice_width = tokens.shape
    top_count = expert_ids.shape[1]
    cold_count = lax.axis_size("ep")
    hot_count = hot_ids.shape[0]
    capacity = tok_rows // 16
    flat_ids = expert_ids.reshape(-1)
    flat_weights = gate_weights.reshape(-1)
    cold_map = route_table(flat_ids, jnp.arange(cold_count, dtype=jnp.int32), capacity)
    hot_map = route_table(flat_ids, hot_ids, capacity)
    cold_feats, cold_cotan, cold_scale = gather_rows(
        cold_map, tokens, cotangent, flat_weights, tok_rows, top_count
    )
    hot_feats, hot_cotan, hot_scale = gather_rows(
        hot_map, tokens, cotangent, flat_weights, tok_rows, top_count
    )
    outgoing = (
        cold_feats.reshape(cold_count, capacity, slice_width),
        cold_cotan.reshape(cold_count, capacity, slice_width),
        cold_scale.reshape(cold_count, capacity),
    )
    recv_feats, recv_cotan, recv_scale = (
        lax.all_to_all(outgoing[0], "ep", split_axis=0, concat_axis=0, tiled=True),
        lax.all_to_all(outgoing[1], "ep", split_axis=0, concat_axis=0, tiled=True),
        lax.all_to_all(outgoing[2], "ep", split_axis=0, concat_axis=0, tiled=True),
    )
    recv_feats = recv_feats.reshape(-1, slice_width)
    recv_cotan = recv_cotan.reshape(-1, slice_width)
    weighted = (
        recv_scale.reshape(-1).astype(jnp.float32)[:, None] * recv_cotan.astype(jnp.float32)
    ).astype(jnp.bfloat16)
    w_gate = gate_cold[0]
    w_up = up_cold[0]
    w_down = down_cold[0]
    part_gate = jnp.dot(recv_feats, w_gate, preferred_element_type=jnp.float32)
    part_up = jnp.dot(recv_feats, w_up, preferred_element_type=jnp.float32)
    part_hidden = lax.dot_general(
        weighted, w_down, (((1,), (1,)), ((), ())), preferred_element_type=jnp.float32
    )
    pre_gate, pre_up, grad_hidden = (
        lax.psum(part_gate.astype(jnp.bfloat16), "grp").astype(jnp.float32),
        lax.psum(part_up.astype(jnp.bfloat16), "grp").astype(jnp.float32),
        lax.psum(part_hidden.astype(jnp.bfloat16), "grp").astype(jnp.float32),
    )
    hidden, back_gate, back_up = swiglu_back(pre_gate, pre_up, grad_hidden)
    output_slice = jnp.dot(hidden, w_down, preferred_element_type=jnp.float32)
    cold_route = jnp.sum(output_slice * recv_cotan.astype(jnp.float32), axis=1)
    contract_rows = (((0,), (0,)), ((), ()))
    grad_gate_cold = lax.dot_general(
        recv_feats, back_gate, contract_rows, preferred_element_type=jnp.float32
    )
    grad_up_cold = lax.dot_general(
        recv_feats, back_up, contract_rows, preferred_element_type=jnp.float32
    )
    grad_down_cold = lax.dot_general(
        hidden, weighted, contract_rows, preferred_element_type=jnp.float32
    )
    hot_feats = hot_feats.reshape(hot_count, capacity, slice_width)
    hot_cotan = hot_cotan.reshape(hot_count, capacity, slice_width)
    hot_scale = hot_scale.reshape(hot_count, capacity)
    full_gate, full_up = (
        lax.all_gather(gate_hot, "ep", axis=2, tiled=True),
        lax.all_gather(up_hot, "ep", axis=2, tiled=True),
    )
    full_down = lax.all_gather(down_hot, "ep", axis=1, tiled=True)
    hot_weighted = (
        hot_scale.astype(jnp.float32)[:, :, None] * hot_cotan.astype(jnp.float32)
    ).astype(jnp.bfloat16)
    part_gate_hot = jnp.einsum(
        "jcd,jdh->jch", hot_feats, full_gate, preferred_element_type=jnp.float32
    )
    part_up_hot = jnp.einsum("jcd,jdh->jch", hot_feats, full_up, preferred_element_type=jnp.float32)
    part_hidden_hot = jnp.einsum(
        "jcd,jhd->jch", hot_weighted, full_down, preferred_element_type=jnp.float32
    )
    pre_gate_hot, pre_up_hot, grad_hidden_hot = (
        lax.psum(part_gate_hot.astype(jnp.bfloat16), "grp").astype(jnp.float32),
        lax.psum(part_up_hot.astype(jnp.bfloat16), "grp").astype(jnp.float32),
        lax.psum(part_hidden_hot.astype(jnp.bfloat16), "grp").astype(jnp.float32),
    )
    hidden_hot, back_gate_hot, back_up_hot = swiglu_back(pre_gate_hot, pre_up_hot, grad_hidden_hot)
    output_hot = jnp.einsum(
        "jch,jhd->jcd", hidden_hot, full_down, preferred_element_type=jnp.float32
    )
    hot_route_part = jnp.sum(output_hot * hot_cotan.astype(jnp.float32), axis=2)
    shadow_gate = jnp.einsum(
        "jcd,jch->jdh", hot_feats, back_gate_hot, preferred_element_type=jnp.float32
    )
    shadow_up = jnp.einsum(
        "jcd,jch->jdh", hot_feats, back_up_hot, preferred_element_type=jnp.float32
    )
    shadow_down = jnp.einsum(
        "jch,jcd->jdh", hidden_hot, hot_weighted, preferred_element_type=jnp.float32
    )
    grad_gate_hot, grad_up_hot, down_turned = (
        lax.psum_scatter(
            shadow_gate.astype(jnp.bfloat16), "ep", scatter_dimension=2, tiled=True
        ).astype(jnp.float32),
        lax.psum_scatter(
            shadow_up.astype(jnp.bfloat16), "ep", scatter_dimension=2, tiled=True
        ).astype(jnp.float32),
        lax.psum_scatter(
            shadow_down.astype(jnp.bfloat16), "ep", scatter_dimension=2, tiled=True
        ).astype(jnp.float32),
    )
    grad_down_hot = jnp.transpose(down_turned, (0, 2, 1))
    cold_route, hot_route = lax.psum((cold_route, hot_route_part), "grp")
    cold_back = lax.all_to_all(
        cold_route.reshape(cold_count, capacity), "ep", split_axis=0, concat_axis=0, tiled=True
    )
    route_flat = jnp.dot(cold_back.reshape(-1), cold_map, precision=lax.Precision.HIGHEST)
    route_flat = route_flat + jnp.dot(
        hot_route.reshape(-1), hot_map, precision=lax.Precision.HIGHEST
    )
    gate_weight_grad = route_flat.reshape(tok_rows, top_count)
    return (
        grad_gate_cold[None].astype(jnp.bfloat16),
        grad_up_cold[None].astype(jnp.bfloat16),
        grad_down_cold[None].astype(jnp.bfloat16),
        grad_gate_hot,
        grad_up_hot,
        grad_down_hot,
        gate_weight_grad,
    )


def solution(mesh):
    in_specs = (
        P("ep", "grp"),
        P("ep", "grp"),
        P("ep", None),
        P("ep", None),
        P(),
        P("ep", "grp", None),
        P("ep", "grp", None),
        P("ep", None, "grp"),
        P(None, "grp", "ep"),
        P(None, "grp", "ep"),
        P(None, "ep", "grp"),
    )
    out_specs = (
        P("ep", "grp", None),
        P("ep", "grp", None),
        P("ep", None, "grp"),
        P(None, "grp", "ep"),
        P(None, "grp", "ep"),
        P(None, "ep", "grp"),
        P("ep", None),
    )
    return jax.shard_map(body, mesh=mesh, in_specs=in_specs, out_specs=out_specs, check_vma=False)
```

profile of v0, /device:TPU:0, one launch (start us, length us, event | category | flops | bytes accessed | tf_op | source)
XLA Modules:
  0.0 574.7 jit_solution(6589414462695450256)
XLA Ops:
  14.0 2.3 reduce-window.14
  17.9 7.3 %all-to-all-start.1 = ((bf16[8,1,16]{2,1,0:T(2,128)(2,1)}), bf16[8,1,16]{2,1,0:T(2,128)(2,1)S(1)}, u32[]{:S(2)}, u32[]{:S(2)}) async-start(bf16[8,1,16]{2,1,0:T(2,128)(2,1)} %all_to_all.24), calls=%async_computation.1 | async-start | bytes 8192 | tf_op jit(solution)/shard_map/all_to_all | solution.py:81
  33.5 6.0 %all-to-all-start = ((bf16[8,16,1280]{2,1,0:T(8,128)(2,1)}), bf16[8,16,1280]{2,1,0:T(8,128)(2,1)S(1)}, u32[]{:S(2)}, u32[]{:S(2)}) async-start(bf16[8,16,1280]{2,1,0:T(8,128)(2,1)} %bitcast.121), calls=%async_computation | async-start | bytes 655360 | tf_op jit(solution)/shard_map/all_to_all | solution.py:79
  40.7 11.0 %all-to-all-done = bf16[8,16,1280]{2,1,0:T(8,128)(2,1)S(1)} async-done(((bf16[8,16,1280]{2,1,0:T(8,128)(2,1)}), bf16[8,16,1280]{2,1,0:T(8,128)(2,1)S(1)}, u32[]{:S(2)}, u32[]{:S(2)}) %all-to-all-start) | async-done | bytes 327712 | tf_op jit(solution)/shard_map/all_to_all | solution.py:79
  51.8 5.0 all-to-all-start.2
  56.8 2.7 fusion.16
  59.4 2.7 fusion.19
  62.1 13.3 %all-to-all-done.2 = bf16[8,16,1280]{2,1,0:T(8,128)(2,1)S(1)} async-done(((bf16[8,16,1280]{2,1,0:T(8,128)(2,1)}), bf16[8,16,1280]{2,1,0:T(8,128)(2,1)S(1)}, u32[]{:S(2)}, u32[]{:S(2)}) %all-to-all-start.2) | async-done | bytes 327712 | tf_op jit(solution)/shard_map/all_to_all | solution.py:80
  75.5 12.9 %all-gather.8.cloned.1.call-done = bf16[2,1280,768]{1,2,0:T(8,128)(2,1)} async-done(((bf16[2,1280,96]{1,2,0:T(8,128)(2,1)}), bf16[2,1280,768]{1,2,0:T(8,128)(2,1)}) %all-gather.8.cloned.1.call-update) | async-done | bytes 3932176 | tf_op jit(solution)/shard_map/all_gather | solution.py:118
  88.4 3.9 convolution_convert_fusion.10
  92.3 67.5 %all-gather.6.cloned.1.call-done = bf16[2,1280,768]{1,2,0:T(8,128)(2,1)} async-done(((bf16[2,1280,96]{1,2,0:T(8,128)(2,1)}), bf16[2,1280,768]{1,2,0:T(8,128)(2,1)}) %all-gather.6.cloned.1.call-update) | async-done | bytes 3932176 | tf_op jit(solution)/shard_map/all_gather | solution.py:119
  159.7 3.9 convolution_convert_fusion.11
  163.6 66.8 %all-gather.4.cloned.1.call-done = bf16[2,768,1280]{2,1,0:T(8,128)(2,1)} async-done(((bf16[2,96,1280]{2,1,0:T(8,128)(2,1)}), bf16[2,768,1280]{2,1,0:T(8,128)(2,1)}) %all-gather.4.cloned.1.call-update) | async-done | bytes 3932176 | tf_op jit(solution)/shard_map/all_gather | solution.py:121
  230.4 3.9 convolution_convert_fusion.12
  235.9 27.8 %all-reduce.6.cloned.1.call-done = (bf16[2,16,768]{2,1,0:T(8,128)(2,1)}, bf16[2,16,768]{2,1,0:T(8,128)(2,1)}, bf16[2,16,768]{2,1,0:T(8,128)(2,1)}) async-done(((bf16[2,16,768]{2,1,0:T(8,128)(2,1)}, bf16[2,16,768]{2,1,0:T(8,128)(2,1)}, bf16[2,16,768]{2,1,0:T(8,128)(2,1)}), (bf16[2,16,768]{2,1,0:T(8,128)(2,1)}, bf16[2,16,768]{2,1,0:T(8,128)(2,1)}, bf16[2,16,768]{2,1,0:T(8,128)(2,1)})) %all-reduce.6.cloned.1.call-update) | async-done | bytes 147472 | tf_op jit(solution)/shard_map/psum | solution.py:134
  263.8 4.0 convolution_convert_fusion.1
  267.9 3.2 convolution_convert_fusion
  271.4 3.2 convolution_convert_fusion.2
  274.8 26.7 %all-reduce.8.cloned.1.call-done = (bf16[128,768]{1,0:T(8,128)(2,1)}, bf16[128,768]{1,0:T(8,128)(2,1)}, bf16[128,768]{1,0:T(8,128)(2,1)}) async-done(((bf16[128,768]{1,0:T(8,128)(2,1)}, bf16[128,768]{1,0:T(8,128)(2,1)}, bf16[128,768]{1,0:T(8,128)(2,1)}), (bf16[128,768]{1,0:T(8,128)(2,1)}, bf16[128,768]{1,0:T(8,128)(2,1)}, bf16[128,768]{1,0:T(8,128)(2,1)})) %all-reduce.8.cloned.1.call-update) | async-done | bytes 589840 | tf_op jit(solution)/shard_map/psum | solution.py:98
  301.5 1.6 fusion.10
  303.3 2.0 fusion.2
  305.3 2.9 fusion.1
  308.2 2.0 fusion
  311.0 6.4 %all-reduce = (f32[8,1,16]{2,0,1:T(8,128)}, f32[32]{0:T(128)S(1)}) all-reduce(f32[8,1,16]{2,0,1:T(8,128)S(1)} %all_to_all.22, f32[32]{0:T(128)S(1)} %reshape.191), channel_id=1, replica_groups=mesh['grp'=4,'ep'=8] {'grp'}, use_global_device_ids=true, to_apply=%region_22.23 | all-reduce | flops 160 | bytes 1280 | tf_op jit(solution)/shard_map/psum | solution.py:163
  317.4 5.8 %all-to-all-start.3 = ((f32[8,1,16]{2,1,0:T(1,128)}), f32[8,1,16]{2,1,0:T(1,128)S(1)}, u32[]{:S(2)}, u32[]{:S(2)}) async-start(f32[8,1,16]{2,1,0:T(1,128)} %bitcast.19), calls=%async_computation.6 | async-start | bytes 8192 | tf_op jit(solution)/shard_map/all_to_all | solution.py:164
  323.5 6.4 %all-to-all-done.3 = f32[8,1,16]{2,1,0:T(1,128)S(1)} async-done(((f32[8,1,16]{2,1,0:T(1,128)}), f32[8,1,16]{2,1,0:T(1,128)S(1)}, u32[]{:S(2)}, u32[]{:S(2)}) %all-to-all-start.3) | async-done | bytes 544 | tf_op jit(solution)/shard_map/all_to_all | solution.py:164
  332.4 57.6 %reduce-scatter.6.cloned.1.call-done = bf16[2,1280,96]{1,2,0:T(8,128)(2,1)} async-done(((bf16[2,1280,768]{1,2,0:T(8,128)(2,1)}), bf16[2,1280,96]{1,2,0:T(8,128)(2,1)}) %reduce-scatter.6.cloned.1.call-update) | async-done | bytes 491536 | tf_op jit(solution)/shard_map/reduce_scatter | solution.py:155
  390.0 2.0 convert_element_type.245
  392.0 85.7 %reduce-scatter.8.cloned.1.call-done = bf16[2,1280,96]{1,2,0:T(8,128)(2,1)} async-done(((bf16[2,1280,768]{1,2,0:T(8,128)(2,1)}), bf16[2,1280,96]{1,2,0:T(8,128)(2,1)}) %reduce-scatter.8.cloned.1.call-update) | async-done | bytes 491536 | tf_op jit(solution)/shard_map/reduce_scatter | solution.py:158
  477.7 2.0 convert_bitcast_fusion
  479.7 86.1 %reduce-scatter.4.cloned.1.call-done = bf16[2,1280,96]{1,2,0:T(8,128)(2,1)} async-done(((bf16[2,1280,768]{1,2,0:T(8,128)(2,1)}), bf16[2,1280,96]{1,2,0:T(8,128)(2,1)}) %reduce-scatter.4.cloned.1.call-update) | async-done | bytes 491536 | tf_op jit(solution)/shard_map/reduce_scatter | solution.py:152
  565.9 2.0 convert_element_type.242
  (91 shorter events, 23.6 us)
Async XLA Ops:
  7.2 227.2 %copy-start = (bf16[1,768,1280]{2,1,0:T(8,128)(2,1)S(1)}, bf16[1,768,1280]{2,1,0:T(8,128)(2,1)}, u32[]{:S(2)}) copy-start(bf16[1,768,1280]{2,1,0:T(8,128)(2,1)} %param.18) | copy-start | bytes 5898244
  7.2 24.8 %copy-start.2 = (bf16[256,1280]{1,0:T(8,128)(2,1)S(1)}, bf16[256,1280]{1,0:T(8,128)(2,1)}, u32[]{:S(2)}) copy-start(bf16[256,1280]{1,0:T(8,128)(2,1)} %param.11) | copy-start | bytes 1966084
  7.2 26.1 %copy-start.3 = (bf16[256,1280]{1,0:T(8,128)(2,1)S(1)}, bf16[256,1280]{1,0:T(8,128)(2,1)}, u32[]{:S(2)}) copy-start(bf16[256,1280]{1,0:T(8,128)(2,1)} %param.12) | copy-start | bytes 1966084
  7.2 81.2 %all-gather.8.cloned.1.call-start = ((), (), s32[]{:S(2)}) async-start(), calls=%async_computation.9 | async-start | bytes 4423680 | tf_op jit(solution)/shard_map/all_gather | solution.py:118
  7.9 151.8 %all-gather.6.cloned.1.call-start = ((), (), s32[]{:S(2)}) async-start(), calls=%async_computation.8 | async-start | bytes 4423680 | tf_op jit(solution)/shard_map/all_gather | solution.py:119
  8.7 221.7 %all-gather.4.cloned.1.call-start = ((), (), s32[]{:S(2)}) async-start(), calls=%async_computation.7 | async-start | bytes 4423680 | tf_op jit(solution)/shard_map/all_gather | solution.py:121
  17.9 15.6 %all-to-all-start.1 = ((bf16[8,1,16]{2,1,0:T(2,128)(2,1)}), bf16[8,1,16]{2,1,0:T(2,128)(2,1)S(1)}, u32[]{:S(2)}, u32[]{:S(2)}) async-start(bf16[8,1,16]{2,1,0:T(2,128)(2,1)} %all_to_all.24), calls=%async_computation.1 | async-start | bytes 8192 | tf_op jit(solution)/shard_map/all_to_all | solution.py:81
  33.5 18.3 %all-to-all-start = ((bf16[8,16,1280]{2,1,0:T(8,128)(2,1)}), bf16[8,16,1280]{2,1,0:T(8,128)(2,1)S(1)}, u32[]{:S(2)}, u32[]{:S(2)}) async-start(bf16[8,16,1280]{2,1,0:T(8,128)(2,1)} %bitcast.121), calls=%async_computation | async-start | bytes 655360 | tf_op jit(solution)/shard_map/all_to_all | solution.py:79
  51.8 23.6 %all-to-all-start.2 = ((bf16[8,16,1280]{2,1,0:T(8,128)(2,1)}), bf16[8,16,1280]{2,1,0:T(8,128)(2,1)S(1)}, u32[]{:S(2)}, u32[]{:S(2)}) async-start(bf16[8,16,1280]{2,1,0:T(8,128)(2,1)} %bitcast.122), calls=%async_computation.2 | async-start | bytes 655360 | tf_op jit(solution)/shard_map/all_to_all | solution.py:80
  56.7 207.0 %all-reduce.6.cloned.1.call-start = ((), (), s32[]{:S(2)}) async-start(), calls=%async_computation.13 | async-start | bytes 294912 | tf_op jit(solution)/shard_map/psum | solution.py:134
  234.3 67.2 %all-reduce.8.cloned.1.call-start = ((), (), s32[]{:S(2)}) async-start(), calls=%async_computation.14 | async-start | bytes 1179648 | tf_op jit(solution)/shard_map/psum | solution.py:98
  235.9 154.1 %reduce-scatter.6.cloned.1.call-start = ((), (), s32[]{:S(2)}) async-start(), calls=%async_computation.11 | async-start | bytes 4423680 | tf_op jit(solution)/shard_map/reduce_scatter | solution.py:155
  263.7 4.1 copy-start.5
  263.7 4.1 copy-start.6
  267.8 209.9 %reduce-scatter.8.cloned.1.call-start = ((), (), s32[]{:S(2)}) async-start(), calls=%async_computation.12 | async-start | bytes 4423680 | tf_op jit(solution)/shard_map/reduce_scatter | solution.py:158
  267.9 3.5 copy-start.9
  271.1 294.7 %reduce-scatter.4.cloned.1.call-start = ((), (), s32[]{:S(2)}) async-start(), calls=%async_computation.10 | async-start | bytes 4423680 | tf_op jit(solution)/shard_map/reduce_scatter | solution.py:152
  301.5 1.7 copy-start.4
  301.5 1.7 copy-start.7
  303.2 5.0 copy-start.8
  303.3 7.0 %copy-start.1 = (bf16[2,768,1280]{2,1,0:T(8,128)(2,1)S(1)}, bf16[2,768,1280]{2,1,0:T(8,128)(2,1)}, u32[]{:S(2)}) copy-start(bf16[2,768,1280]{2,1,0:T(8,128)(2,1)} %all-gather.4.cloned.1.call-done) | copy-start | bytes 11796484
  317.4 12.4 %all-to-all-start.3 = ((f32[8,1,16]{2,1,0:T(1,128)}), f32[8,1,16]{2,1,0:T(1,128)S(1)}, u32[]{:S(2)}, u32[]{:S(2)}) async-start(f32[8,1,16]{2,1,0:T(1,128)} %bitcast.19), calls=%async_computation.6 | async-start | bytes 8192 | tf_op jit(solution)/shard_map/all_to_all | solution.py:164
Sparse Core Ops, SparseCore 0:
  10.2 78.1 all-gather.7
  90.6 69.1 all-gather.5
  161.9 68.4 all-gather.3
  234.4 29.2 all-reduce.5
  266.9 34.6 all-reduce.7
  305.5 84.4 reduce-scatter.5
  393.7 83.9 reduce-scatter.7
  481.8 83.9 reduce-scatter.3
where the time goes:
time: 576 us; the launch traced here: 575 us
  waiting for transfers between devices  464 us (81%)
  matrix products  41.6 us (7%)
  starting transfers between devices  24.6 us (4%)
  between operations  14.4 us (2%)
  other arithmetic  12.2 us (2%)
  local copies, waits for them, and re-layouts  11.6 us (2%)
  blocking collectives  6.41 us (1%)
    reduce_scatter x1, waiting for transfers between devices, body(): lax.psum_scatter(shadow_gate.astype(jnp.bfloat16), 'ep', scatter_dimensio...  86.1 us
    reduce_scatter x1, waiting for transfers between devices, body(): lax.psum_scatter(shadow_down.astype(jnp.bfloat16), 'ep', scatter_dimensio...  85.7 us
    all_gather x1, waiting for transfers between devices, body(): lax.all_gather(up_hot, 'ep', axis=2, tiled=True)  67.5 us
    all_gather x1, waiting for transfers between devices, body(): full_down = lax.all_gather(down_hot, 'ep', axis=1, tiled=True)  66.8 us
    reduce_scatter x1, waiting for transfers between devices, body(): lax.psum_scatter(shadow_up.astype(jnp.bfloat16), 'ep', scatter_dimension=...  57.6 us
    psum x1, waiting for transfers between devices, body(): lax.psum(part_up_hot.astype(jnp.bfloat16), 'grp').astype(jnp.float32)  27.8 us
    psum x1, waiting for transfers between devices, body(): lax.psum(part_up.astype(jnp.bfloat16), 'grp').astype(jnp.float32)  26.7 us
    all_to_all x1, waiting for transfers between devices, body(): lax.all_to_all(outgoing[1], 'ep', split_axis=0, concat_axis=0, tiled=True)  13.3 us
  transfers between devices with their start and end apart: 12, of which 11 were waited for; matrix products, arithmetic and copies ran while one was open for 10% of the time, Pallas kernels for 0%

commit v1 on v0

--- a/solution.py
+++ b/solution.py
@@ -111,56 +111,48 @@
     grad_down_cold = lax.dot_general(
         hidden, weighted, contract_rows, preferred_element_type=jnp.float32
     )
-    hot_feats = hot_feats.reshape(hot_count, capacity, slice_width)
-    hot_cotan = hot_cotan.reshape(hot_count, capacity, slice_width)
-    hot_scale = hot_scale.reshape(hot_count, capacity)
-    full_gate, full_up = (
-        lax.all_gather(gate_hot, "ep", axis=2, tiled=True),
-        lax.all_gather(up_hot, "ep", axis=2, tiled=True),
+    hot_weighted_local = (
+        hot_scale.astype(jnp.float32)[:, None] * hot_cotan.astype(jnp.float32)
+    ).astype(jnp.bfloat16)
+    blocks = lax.axis_size("ep")
+    stacked = jnp.stack([hot_feats, hot_cotan, hot_weighted_local])
+    all_rows = lax.all_gather(stacked, "ep", axis=1, tiled=False)
+    all_rows = all_rows.reshape(3, blocks, hot_count, capacity, slice_width)
+    all_rows = jnp.transpose(all_rows, (0, 2, 1, 3, 4)).reshape(
+        3, hot_count, blocks * capacity, slice_width
     )
-    full_down = lax.all_gather(down_hot, "ep", axis=1, tiled=True)
-    hot_weighted = (
-        hot_scale.astype(jnp.float32)[:, :, None] * hot_cotan.astype(jnp.float32)
-    ).astype(jnp.bfloat16)
+    rows_feat, rows_cot, rows_wt = all_rows[0], all_rows[1], all_rows[2]
     part_gate_hot = jnp.einsum(
-        "jcd,jdh->jch", hot_feats, full_gate, preferred_element_type=jnp.float32
+        "jrd,jdh->jrh", rows_feat, gate_hot, preferred_element_type=jnp.float32
     )
-    part_up_hot = jnp.einsum("jcd,jdh->jch", hot_feats, full_up, preferred_element_type=jnp.float32)
+    part_up_hot = jnp.einsum("jrd,jdh->jrh", rows_feat, up_hot, preferred_element_type=jnp.float32)
     part_hidden_hot = jnp.einsum(
-        "jcd,jhd->jch", hot_weighted, full_down, preferred_element_type=jnp.float32
+        "jrd,jhd->jrh", rows_wt, down_hot, preferred_element_type=jnp.float32
     )
-    pre_gate_hot, pre_up_hot, grad_hidden_hot = (
-        lax.psum(part_gate_hot.astype(jnp.bfloat16), "grp").astype(jnp.float32),
-        lax.psum(part_up_hot.astype(jnp.bfloat16), "grp").astype(jnp.float32),
-        lax.psum(part_hidden_hot.astype(jnp.bfloat16), "grp").astype(jnp.float32),
+    cot_down = jnp.einsum("jrd,jhd->jrh", rows_cot, down_hot, preferred_element_type=jnp.float32)
+    hot_parts = lax.psum(
+        jnp.stack([part_gate_hot, part_up_hot, part_hidden_hot]).astype(jnp.bfloat16), "grp"
+    ).astype(jnp.float32)
+    hidden_hot, back_gate_hot, back_up_hot = swiglu_back(hot_parts[0], hot_parts[1], hot_parts[2])
+    hot_route_part = jnp.sum(hidden_hot.astype(jnp.float32) * cot_down, axis=2)
+    hidden_blk = hidden_hot.shape[2]
+    feat_b = rows_feat.reshape(hot_count, blocks, capacity, slice_width)
+    wt_b = rows_wt.reshape(hot_count, blocks, capacity, slice_width)
+    bg_b = back_gate_hot.reshape(hot_count, blocks, capacity, hidden_blk)
+    bu_b = back_up_hot.reshape(hot_count, blocks, capacity, hidden_blk)
+    hid_b = hidden_hot.reshape(hot_count, blocks, capacity, hidden_blk)
+    blk_gate = jnp.einsum("jbcd,jbch->jbdh", feat_b, bg_b, preferred_element_type=jnp.float32)
+    blk_up = jnp.einsum("jbcd,jbch->jbdh", feat_b, bu_b, preferred_element_type=jnp.float32)
+    blk_down = jnp.einsum("jbch,jbcd->jbhd", hid_b, wt_b, preferred_element_type=jnp.float32)
+    grad_gate_hot = jnp.sum(blk_gate.astype(jnp.bfloat16).astype(jnp.float32), axis=1)
+    grad_up_hot = jnp.sum(blk_up.astype(jnp.bfloat16).astype(jnp.float32), axis=1)
+    grad_down_hot = jnp.sum(blk_down.astype(jnp.bfloat16).astype(jnp.float32), axis=1)
+    hot_route_all = lax.psum(hot_route_part, ("grp", "ep"))
+    me = lax.axis_index("ep")
+    hot_route = lax.dynamic_index_in_dim(
+        hot_route_all.reshape(hot_count, blocks, capacity), me, axis=1, keepdims=False
     )
-    hidden_hot, back_gate_hot, back_up_hot = swiglu_back(pre_gate_hot, pre_up_hot, grad_hidden_hot)
-    output_hot = jnp.einsum(
-        "jch,jhd->jcd", hidden_hot, full_down, preferred_element_type=jnp.float32
-    )
-    hot_route_part = jnp.sum(output_hot * hot_cotan.astype(jnp.float32), axis=2)
-    shadow_gate = jnp.einsum(
-        "jcd,jch->jdh", hot_feats, back_gate_hot, preferred_element_type=jnp.float32
-    )
-    shadow_up = jnp.einsum(
-        "jcd,jch->jdh", hot_feats, back_up_hot, preferred_element_type=jnp.float32
-    )
-    shadow_down = jnp.einsum(
-        "jch,jcd->jdh", hidden_hot, hot_weighted, preferred_element_type=jnp.float32
-    )
-    grad_gate_hot, grad_up_hot, down_turned = (
-        lax.psum_scatter(
-            shadow_gate.astype(jnp.bfloat16), "ep", scatter_dimension=2, tiled=True
-        ).astype(jnp.float32),
-        lax.psum_scatter(
-            shadow_up.astype(jnp.bfloat16), "ep", scatter_dimension=2, tiled=True
-        ).astype(jnp.float32),
-        lax.psum_scatter(
-            shadow_down.astype(jnp.bfloat16), "ep", scatter_dimension=2, tiled=True
-        ).astype(jnp.float32),
-    )
-    grad_down_hot = jnp.transpose(down_turned, (0, 2, 1))
-    cold_route, hot_route = lax.psum((cold_route, hot_route_part), "grp")
+    cold_route = lax.psum(cold_route, "grp")
     cold_back = lax.all_to_all(
         cold_route.reshape(cold_count, capacity), "ep", split_axis=0, concat_axis=0, tiled=True
     )

time: 576 us -> 195 us (0.34)
  waiting for transfers between devices: 464 us -> 64.2 us
  blocking collectives: 6.41 us -> 46.4 us
  matrix products: 41.6 us -> 29.2 us
    reduce_scatter x3 -> x0, waiting for transfers between devices: 229 us -> none  [the longest x1 86.1 us: body(): lax.psum_scatter(shadow_gate.astype(jnp.bfloat16), 'ep', scatter_dimensio...]
    all_gather x3 -> x1, waiting for transfers between devices: 147 us -> 2.09 us  [body(): all_rows = lax.all_gather(stacked, 'ep', axis=1, tiled=False)]
    psum x1 -> x2, blocking collectives: 6.41 us -> 46.4 us  [the longest x1 40.2 us: body(): hot_route_all = lax.psum(hot_route_part, ('grp', 'ep'))]
    psum x1 -> x0, waiting for transfers between devices: 27.8 us -> none  [body(): lax.psum(part_up_hot.astype(jnp.bfloat16), 'grp').astype(jnp.float32)]
    dot_general x7, matrix products: 22.8 us -> 12.7 us  [the longest x1 3.41 us: body(): jnp.einsum('jbcd,jbch->jbdh', feat_b, bu_b, preferred_element_type=jnp.fl...]
    psum x1, waiting for transfers between devices: 26.7 us -> 33.6 us  [body(): lax.psum(part_up.astype(jnp.bfloat16), 'grp').astype(jnp.float32)]
    all_to_all x1, waiting for transfers between devices: 6.42 us -> 0.01 us  [body(): lax.all_to_all(cold_route.reshape(cold_count, capacity), 'ep', split_axis...]
  transfers between devices with their start and end apart: 12 -> 6, of which waited for: 11 -> 5; matrix products, arithmetic and copies ran while one was open for 10% -> 8% of each run, Pallas kernels for 0% -> 0%
where the time goes in v1:
time: 195 us
  waiting for transfers between devices  64.2 us (33%)
  blocking collectives  46.4 us (24%)
  matrix products  29.2 us (15%)
  starting transfers between devices  20.2 us (10%)
  between operations  14.4 us (7%)
  local copies, waits for them, and re-layouts  10.9 us (6%)
  other arithmetic  9.22 us (5%)
    psum x1, blocking collectives, body(): hot_route_all = lax.psum(hot_route_part, ('grp', 'ep'))  40.2 us
    psum x1, waiting for transfers between devices, body(): lax.psum(part_up.astype(jnp.bfloat16), 'grp').astype(jnp.float32)  33.6 us
    all_to_all x1, waiting for transfers between devices, body(): lax.all_to_all(outgoing[1], 'ep', split_axis=0, concat_axis=0, tiled=True)  14.6 us
    all_to_all x1, waiting for transfers between devices, body(): lax.all_to_all(outgoing[0], 'ep', split_axis=0, concat_axis=0, tiled=True)  9.11 us
    all_to_all x1, starting transfers between devices, body(): lax.all_to_all(outgoing[2], 'ep', split_axis=0, concat_axis=0, tiled=True)  7.28 us
    psum x1, blocking collectives, body(): cold_route = lax.psum(cold_route, 'grp')  6.24 us
    all_to_all x1, starting transfers between devices, body(): lax.all_to_all(cold_route.reshape(cold_count, capacity), 'ep', split_axis...  5.52 us
    all_to_all x1, waiting for transfers between devices, body(): lax.all_to_all(outgoing[2], 'ep', split_axis=0, concat_axis=0, tiled=True)  4.77 us
  transfers between devices with their start and end apart: 6, of which 5 were waited for; matrix products, arithmetic and copies ran while one was open for 8% of the time, Pallas kernels for 0%

profile of v1, /device:TPU:0, one launch (start us, length us, event | category | flops | bytes accessed | tf_op | source)
XLA Modules:
  0.0 194.5 jit_solution(9976301442183095189)
XLA Ops:
  7.2 1.0 copy.45
  8.5 0.8 copy.49
  11.2 0.8 fusion.78
  12.8 1.3 convolution_convert_fusion.8
  15.2 2.3 %reduce-window.14 = s32[8,12,128]{2,1,0:T(8,128)S(1)} reduce-window(s32[8,12,128]{2,1,0:T(8,128)S(1)} %fusion.69, s32[]{:T(128)} %constant.15.clone.1), window={size=1x1x128 pad=0_0x0_0x127_0}, to_apply=%region_1.2 | reduce-window | flops 1560576 | bytes 98308 | tf_op jit(solution)/shard_map/reduce-window
  19.1 7.3 %all-to-all-start.1 = ((bf16[8,1,16]{2,1,0:T(2,128)(2,1)}), bf16[8,1,16]{2,1,0:T(2,128)(2,1)S(1)}, u32[]{:S(2)}, u32[]{:S(2)}) async-start(bf16[8,1,16]{2,1,0:T(2,128)(2,1)} %all_to_all.24), calls=%async_computation.1 | async-start | bytes 8192 | tf_op jit(solution)/shard_map/all_to_all | solution.py:81
  27.0 1.0 convolution_convert_fusion.7
  28.0 4.8 %all-to-all-done.1 = bf16[8,1,16]{2,1,0:T(2,128)(2,1)S(1)} async-done(((bf16[8,1,16]{2,1,0:T(2,128)(2,1)}), bf16[8,1,16]{2,1,0:T(2,128)(2,1)S(1)}, u32[]{:S(2)}, u32[]{:S(2)}) %all-to-all-start.1) | async-done | bytes 288 | tf_op jit(solution)/shard_map/all_to_all | solution.py:81
  32.8 3.4 %all-to-all-start = ((bf16[8,16,1280]{2,1,0:T(8,128)(2,1)}), bf16[8,16,1280]{2,1,0:T(8,128)(2,1)S(1)}, u32[]{:S(2)}, u32[]{:S(2)}) async-start(bf16[8,16,1280]{2,1,0:T(8,128)(2,1)} %bitcast.165), calls=%async_computation | async-start | bytes 655360 | tf_op jit(solution)/shard_map/all_to_all | solution.py:79
  36.2 1.0 convolution_convert_fusion.6
  37.3 9.1 %all-to-all-done = bf16[8,16,1280]{2,1,0:T(8,128)(2,1)S(1)} async-done(((bf16[8,16,1280]{2,1,0:T(8,128)(2,1)}), bf16[8,16,1280]{2,1,0:T(8,128)(2,1)S(1)}, u32[]{:S(2)}, u32[]{:S(2)}) %all-to-all-start) | async-done | bytes 327712 | tf_op jit(solution)/shard_map/all_to_all | solution.py:79
  46.4 3.9 %all-to-all-start.2 = ((bf16[8,16,1280]{2,1,0:T(8,128)(2,1)}), bf16[8,16,1280]{2,1,0:T(8,128)(2,1)S(1)}, u32[]{:S(2)}, u32[]{:S(2)}) async-start(bf16[8,16,1280]{2,1,0:T(8,128)(2,1)} %bitcast.166), calls=%async_computation.2 | async-start | bytes 655360 | tf_op jit(solution)/shard_map/all_to_all | solution.py:80
  50.3 2.8 %fusion.20 = bf16[128,768]{1,0:T(8,128)(2,1)} fusion(bf16[128,1280]{1,0:T(8,128)(2,1)S(1)} %bitcast.155, bf16[1,1280,768]{2,1,0:T(8,128)(2,1)} %param.16), kind=kOutput, calls=%fused_computation.29 | convolution fusion | flops 251756544 | bytes 2490368 | tf_op jit(solution)/shard_map/dot_general | solution.py:91
  53.1 1.1 fusion.17
  54.3 14.6 %all-to-all-done.2 = bf16[8,16,1280]{2,1,0:T(8,128)(2,1)S(1)} async-done(((bf16[8,16,1280]{2,1,0:T(8,128)(2,1)}), bf16[8,16,1280]{2,1,0:T(8,128)(2,1)S(1)}, u32[]{:S(2)}, u32[]{:S(2)}) %all-to-all-start.2) | async-done | bytes 327712 | tf_op jit(solution)/shard_map/all_to_all | solution.py:80
  69.0 1.5 fusion.14
  70.5 2.1 %all-gather.3.cloned.1.call-done = bf16[3,256,1280]{2,1,0:T(8,128)(2,1)} async-done(((bf16[3,32,1280]{2,1,0:T(8,128)(2,1)}), bf16[3,256,1280]{2,1,0:T(8,128)(2,1)}) %all-gather.3.cloned.1.call-update) | async-done | bytes 1966096 | tf_op jit(solution)/shard_map/all_gather | solution.py:119
  72.6 1.7 copy.68
  74.4 1.0 fusion.92
  78.1 33.6 %all-reduce.3.cloned.1.call-done = (bf16[128,768]{1,0:T(8,128)(2,1)}, bf16[128,768]{1,0:T(8,128)(2,1)}, bf16[128,768]{1,0:T(8,128)(2,1)}, bf16[3,2,128,96]{2,3,1,0:T(8,128)(2,1)}) async-done(((bf16[128,768]{1,0:T(8,128)(2,1)}, bf16[128,768]{1,0:T(8,128)(2,1)}, bf16[128,768]{1,0:T(8,128)(2,1)}, bf16[3,2,128,96]{2,3,1,0:T(8,128)(2,1)}), (bf16[128,768]{1,0:T(8,128)(2,1)}, bf16[128,768]{1,0:T(8,128)(2,1)}, ...) | async-done | bytes 737296 | tf_op jit(solution)/shard_map/psum | solution.py:98
  111.7 1.6 convert_element_type.217
  113.3 0.9 fusion.93
  114.5 3.3 %convert_reduce_fusion = f32[2,96,1280]{2,1,0:T(8,128)} fusion(f32[2,8,16,96]{3,2,1,0:T(8,128)S(1)} %bitcast.169, f32[2,8,16,96]{3,2,1,0:T(8,128)S(1)} %bitcast.171, bf16[3,2,8,16,1280]{4,3,2,1,0:T(8,128)(2,1)} %bitcast.152), kind=kOutput, calls=%fused_computation | convolution fusion | flops 68714496 | bytes 1835008 | tf_op jit(solution)/shard_map/jbch,jbcd->jbhd/dot_general | solution.py:146
  117.8 3.3 %convert_reduce_fusion.2 = f32[2,1280,96]{1,2,0:T(8,128)} fusion(f32[2,8,16,96]{3,2,1,0:T(8,128)S(1)} %bitcast.172, f32[2,8,16,96]{3,2,1,0:T(8,128)S(1)} %bitcast.174, f32[2,8,16,96]{3,2,1,0:T(8,128)S(1)} %bitcast.170, bf16[3,2,8,16,1280]{4,3,2,1,0:T(8,128)(2,1)} %bitcast.153), kind=kOutput, calls=%fused_computation.2 | convolution fusion | flops 68812800 | bytes 1933312 | tf_op jit(solution)/shard_map/jbcd,jbch->jbdh/dot_general | solution.py:144
  121.1 3.4 %convert_reduce_fusion.1 = f32[2,1280,96]{1,2,0:T(8,128)} fusion(f32[2,8,16,96]{3,2,1,0:T(8,128)S(1)} %bitcast.175, f32[2,8,16,96]{3,2,1,0:T(8,128)S(1)} %bitcast.173, bf16[3,2,8,16,1280]{4,3,2,1,0:T(8,128)(2,1)} %bitcast.154), kind=kOutput, calls=%fused_computation.1 | convolution fusion | flops 68714496 | bytes 1835008 | tf_op jit(solution)/shard_map/jbcd,jbch->jbdh/dot_general | solution.py:145
  124.6 2.0 %fusion.1 = bf16[1,1280,768]{2,1,0:T(8,128)(2,1)} fusion(bf16[128,1280]{1,0:T(8,128)(2,1)S(1)} %bitcast.157, bf16[128,768]{1,0:T(8,128)(2,1)S(1)} %copy-done.7, bf16[128,768]{1,0:T(8,128)(2,1)S(1)} %copy-done.5), kind=kOutput, calls=%fused_computation.10 | convolution fusion | flops 253427712 | bytes 2686976 | tf_op jit(solution)/shard_map/dot_general | solution.py:108
  126.5 2.0 %fusion = bf16[1,1280,768]{2,1,0:T(8,128)(2,1)} fusion(bf16[128,1280]{1,0:T(8,128)(2,1)S(1)} %bitcast.158, bf16[128,768]{1,0:T(8,128)(2,1)S(1)} %copy-done.6, bf16[128,768]{1,0:T(8,128)(2,1)S(1)} %copy-done.7, bf16[128,768]{1,0:T(8,128)(2,1)S(1)} %copy-done.5), kind=kOutput, calls=%fused_computation.9 | convolution fusion | flops 253919232 | bytes 2883584 | tf_op jit(solution)/shard_map/dot_general | solution.py:105
  129.2 6.2 %psum.46 = f32[8,1,16]{2,0,1:T(8,128)} all-reduce(f32[8,1,16]{2,0,1:T(8,128)S(1)} %all_to_all.22), channel_id=1, replica_groups=mesh['grp'=4,'ep'=8] {'grp'}, use_global_device_ids=true, to_apply=%region_20.21 | all-reduce | flops 128 | bytes 1024 | tf_op jit(solution)/shard_map/psum | solution.py:155
  135.4 5.5 %all-to-all-start.3 = ((f32[8,1,16]{2,1,0:T(1,128)}), f32[8,1,16]{2,1,0:T(1,128)S(1)}, u32[]{:S(2)}, u32[]{:S(2)}) async-start(f32[8,1,16]{2,1,0:T(1,128)} %bitcast.31), calls=%async_computation.3 | async-start | bytes 8192 | tf_op jit(solution)/shard_map/all_to_all | solution.py:156
  140.9 1.6 fusion.23
  142.6 40.2 %psum.47 = f32[2,8,16]{2,1,0:T(8,128)S(1)} all-reduce(f32[2,8,16]{2,1,0:T(8,128)S(1)} %reshape.204), channel_id=1, replica_groups=mesh['grp'=4,'ep'=8] {'grp','ep'}, use_global_device_ids=true, to_apply=%region_22.23 | all-reduce | flops 256 | bytes 2048 | tf_op jit(solution)/shard_map/psum | solution.py:150
  183.0 2.0 %fusion.2 = bf16[1,768,1280]{2,1,0:T(8,128)(2,1)} fusion(bf16[128,1280]{1,0:T(8,128)(2,1)S(1)} %fusion.37, bf16[128,768]{1,0:T(8,128)(2,1)S(1)} %copy-done.6, bf16[128,768]{1,0:T(8,128)(2,1)S(1)} %copy-done.5), kind=kOutput, calls=%fused_computation.11 | convolution fusion | flops 253427712 | bytes 2686976 | tf_op jit(solution)/shard_map/dot_general | solution.py:111
  (84 shorter events, 12.9 us)
Async XLA Ops:
  7.2 61.9 %copy-start = (bf16[1,768,1280]{2,1,0:T(8,128)(2,1)S(1)}, bf16[1,768,1280]{2,1,0:T(8,128)(2,1)}, u32[]{:S(2)}) copy-start(bf16[1,768,1280]{2,1,0:T(8,128)(2,1)} %param.18) | copy-start | bytes 5898244
  7.2 6.9 %copy-start.2 = (bf16[256,1280]{1,0:T(8,128)(2,1)S(1)}, bf16[256,1280]{1,0:T(8,128)(2,1)}, u32[]{:S(2)}) copy-start(bf16[256,1280]{1,0:T(8,128)(2,1)} %param.11) | copy-start | bytes 1966084
  7.2 65.4 %all-gather.3.cloned.1.call-start = ((), (), s32[]{:S(2)}) async-start(), calls=%async_computation.4 | async-start | bytes 2211840 | tf_op jit(solution)/shard_map/all_gather | solution.py:119
  14.4 21.8 %copy-start.3 = (bf16[256,1280]{1,0:T(8,128)(2,1)S(1)}, bf16[256,1280]{1,0:T(8,128)(2,1)}, u32[]{:S(2)}) copy-start(bf16[256,1280]{1,0:T(8,128)(2,1)} %param.12) | copy-start | bytes 1966084
  19.1 13.7 %all-to-all-start.1 = ((bf16[8,1,16]{2,1,0:T(2,128)(2,1)}), bf16[8,1,16]{2,1,0:T(2,128)(2,1)S(1)}, u32[]{:S(2)}, u32[]{:S(2)}) async-start(bf16[8,1,16]{2,1,0:T(2,128)(2,1)} %all_to_all.24), calls=%async_computation.1 | async-start | bytes 8192 | tf_op jit(solution)/shard_map/all_to_all | solution.py:81
  32.8 13.6 %all-to-all-start = ((bf16[8,16,1280]{2,1,0:T(8,128)(2,1)}), bf16[8,16,1280]{2,1,0:T(8,128)(2,1)S(1)}, u32[]{:S(2)}, u32[]{:S(2)}) async-start(bf16[8,16,1280]{2,1,0:T(8,128)(2,1)} %bitcast.165), calls=%async_computation | async-start | bytes 655360 | tf_op jit(solution)/shard_map/all_to_all | solution.py:79
  46.4 22.5 %all-to-all-start.2 = ((bf16[8,16,1280]{2,1,0:T(8,128)(2,1)}), bf16[8,16,1280]{2,1,0:T(8,128)(2,1)S(1)}, u32[]{:S(2)}, u32[]{:S(2)}) async-start(bf16[8,16,1280]{2,1,0:T(8,128)(2,1)} %bitcast.166), calls=%async_computation.2 | async-start | bytes 655360 | tf_op jit(solution)/shard_map/all_to_all | solution.py:80
  50.3 61.4 %all-reduce.3.cloned.1.call-start = ((), (), s32[]{:S(2)}) async-start(), calls=%async_computation.5 | async-start | bytes 1474560 | tf_op jit(solution)/shard_map/psum | solution.py:98
  50.3 2.8 %copy-start.4 = (bf16[1,1280,768]{2,1,0:T(8,128)(2,1)S(1)}, bf16[1,1280,768]{2,1,0:T(8,128)(2,1)}, u32[]{:S(2)}) copy-start(bf16[1,1280,768]{2,1,0:T(8,128)(2,1)} %param.17) | copy-start | bytes 5898244
  74.3 1.5 copy-start.1
  74.3 1.5 copy-start.8
  74.4 1.9 copy-start.9
  75.8 1.1 copy-start.10
  121.1 3.4 %copy-start.5 = (bf16[128,768]{1,0:T(8,128)(2,1)S(1)}, bf16[128,768]{1,0:T(8,128)(2,1)}, u32[]{:S(2)}) copy-start(bf16[128,768]{1,0:T(8,128)(2,1)} %get-tuple-element.36) | copy-start | bytes 589828
  121.1 3.4 %copy-start.7 = (bf16[128,768]{1,0:T(8,128)(2,1)S(1)}, bf16[128,768]{1,0:T(8,128)(2,1)}, u32[]{:S(2)}) copy-start(bf16[128,768]{1,0:T(8,128)(2,1)} %get-tuple-element.35) | copy-start | bytes 589828
  124.5 2.0 %copy-start.6 = (bf16[128,768]{1,0:T(8,128)(2,1)S(1)}, bf16[128,768]{1,0:T(8,128)(2,1)}, u32[]{:S(2)}) copy-start(bf16[128,768]{1,0:T(8,128)(2,1)} %get-tuple-element.34) | copy-start | bytes 589828
  135.4 49.7 %all-to-all-start.3 = ((f32[8,1,16]{2,1,0:T(1,128)}), f32[8,1,16]{2,1,0:T(1,128)S(1)}, u32[]{:S(2)}, u32[]{:S(2)}) async-start(f32[8,1,16]{2,1,0:T(1,128)} %bitcast.31), calls=%async_computation.3 | async-start | bytes 8192 | tf_op jit(solution)/shard_map/all_to_all | solution.py:156
Sparse Core Ops, SparseCore 0:
  15.3 57.2 all-gather.2
  78.1 33.5 all-reduce.2

commit v2 on v1

--- a/solution.py
+++ b/solution.py
@@ -70,21 +70,21 @@
     hot_feats, hot_cotan, hot_scale = gather_rows(
         hot_map, tokens, cotangent, flat_weights, tok_rows, top_count
     )
-    outgoing = (
-        cold_feats.reshape(cold_count, capacity, slice_width),
-        cold_cotan.reshape(cold_count, capacity, slice_width),
-        cold_scale.reshape(cold_count, capacity),
-    )
-    recv_feats, recv_cotan, recv_scale = (
-        lax.all_to_all(outgoing[0], "ep", split_axis=0, concat_axis=0, tiled=True),
-        lax.all_to_all(outgoing[1], "ep", split_axis=0, concat_axis=0, tiled=True),
-        lax.all_to_all(outgoing[2], "ep", split_axis=0, concat_axis=0, tiled=True),
-    )
-    recv_feats = recv_feats.reshape(-1, slice_width)
-    recv_cotan = recv_cotan.reshape(-1, slice_width)
-    weighted = (
-        recv_scale.reshape(-1).astype(jnp.float32)[:, None] * recv_cotan.astype(jnp.float32)
+    cold_weighted = (
+        cold_scale.astype(jnp.float32)[:, None] * cold_cotan.astype(jnp.float32)
     ).astype(jnp.bfloat16)
+    outgoing = jnp.stack(
+        [
+            cold_feats.reshape(cold_count, capacity, slice_width),
+            cold_cotan.reshape(cold_count, capacity, slice_width),
+            cold_weighted.reshape(cold_count, capacity, slice_width),
+        ],
+        axis=1,
+    )
+    received = lax.all_to_all(outgoing, "ep", split_axis=0, concat_axis=0, tiled=True)
+    recv_feats = received[:, 0].reshape(-1, slice_width)
+    recv_cotan = received[:, 1].reshape(-1, slice_width)
+    weighted = received[:, 2].reshape(-1, slice_width)
     w_gate = gate_cold[0]
     w_up = up_cold[0]
     w_down = down_cold[0]
@@ -111,17 +111,19 @@
     grad_down_cold = lax.dot_general(
         hidden, weighted, contract_rows, preferred_element_type=jnp.float32
     )
-    hot_weighted_local = (
-        hot_scale.astype(jnp.float32)[:, None] * hot_cotan.astype(jnp.float32)
+    blocks = lax.axis_size("ep")
+    all_rows = lax.all_gather(jnp.stack([hot_feats, hot_cotan]), "ep", axis=1, tiled=False)
+    all_rows = all_rows.reshape(2, blocks, hot_count, capacity, slice_width)
+    all_rows = jnp.transpose(all_rows, (0, 2, 1, 3, 4)).reshape(
+        2, hot_count, blocks * capacity, slice_width
+    )
+    all_scale = lax.all_gather(hot_scale, "ep", axis=0, tiled=False)
+    all_scale = jnp.transpose(all_scale.reshape(blocks, hot_count, capacity), (1, 0, 2))
+    rows_feat, rows_cot = all_rows[0], all_rows[1]
+    rows_wt = (
+        all_scale.reshape(hot_count, blocks * capacity, 1).astype(jnp.float32)
+        * rows_cot.astype(jnp.float32)
     ).astype(jnp.bfloat16)
-    blocks = lax.axis_size("ep")
-    stacked = jnp.stack([hot_feats, hot_cotan, hot_weighted_local])
-    all_rows = lax.all_gather(stacked, "ep", axis=1, tiled=False)
-    all_rows = all_rows.reshape(3, blocks, hot_count, capacity, slice_width)
-    all_rows = jnp.transpose(all_rows, (0, 2, 1, 3, 4)).reshape(
-        3, hot_count, blocks * capacity, slice_width
-    )
-    rows_feat, rows_cot, rows_wt = all_rows[0], all_rows[1], all_rows[2]
     part_gate_hot = jnp.einsum(
         "jrd,jdh->jrh", rows_feat, gate_hot, preferred_element_type=jnp.float32
     )
@@ -147,15 +149,17 @@
     grad_gate_hot = jnp.sum(blk_gate.astype(jnp.bfloat16).astype(jnp.float32), axis=1)
     grad_up_hot = jnp.sum(blk_up.astype(jnp.bfloat16).astype(jnp.float32), axis=1)
     grad_down_hot = jnp.sum(blk_down.astype(jnp.bfloat16).astype(jnp.float32), axis=1)
-    hot_route_all = lax.psum(hot_route_part, ("grp", "ep"))
-    me = lax.axis_index("ep")
-    hot_route = lax.dynamic_index_in_dim(
-        hot_route_all.reshape(hot_count, blocks, capacity), me, axis=1, keepdims=False
-    )
-    cold_route = lax.psum(cold_route, "grp")
-    cold_back = lax.all_to_all(
-        cold_route.reshape(cold_count, capacity), "ep", split_axis=0, concat_axis=0, tiled=True
-    )
+    route_parts = jnp.concatenate(
+        [
+            cold_route.reshape(cold_count, 1, capacity),
+            jnp.transpose(hot_route_part.reshape(hot_count, blocks, capacity), (1, 0, 2)),
+        ],
+        axis=1,
+    )
+    route_parts = lax.psum(route_parts, "grp")
+    route_back = lax.all_to_all(route_parts, "ep", split_axis=0, concat_axis=0, tiled=True)
+    cold_back = route_back[:, 0, :]
+    hot_route = jnp.sum(route_back[:, 1:, :], axis=0)
     route_flat = jnp.dot(cold_back.reshape(-1), cold_map, precision=lax.Precision.HIGHEST)
     route_flat = route_flat + jnp.dot(
         hot_route.reshape(-1), hot_map, precision=lax.Precision.HIGHEST

time: 195 us -> 163 us (0.84)
  waiting for transfers between devices: 64.2 us -> 47.3 us
  blocking collectives: 46.4 us -> 35.7 us
  starting transfers between devices: 20.2 us -> 12.9 us
  local copies, waits for them, and re-layouts: 10.9 us -> 15.5 us
  matrix products: 29.2 us -> 27.2 us
    psum x2 -> x1, blocking collectives: 46.4 us -> 10.3 us  [body(): route_parts = lax.psum(route_parts, 'grp')]
    all_to_all x4 -> x2, waiting for transfers between devices: 28.5 us -> 0.01 us  [the longest x1 0.01 us: body(): lax.all_to_all(outgoing, 'ep', split_axis=0, concat_axis=0, tiled=True)]
    unnamed x0 -> x1, blocking collectives: none -> 25.4 us
    all_gather x1, waiting for transfers between devices: 2.09 us -> 13.8 us  [body(): lax.all_gather(jnp.stack([hot_feats, hot_cotan]), 'ep', axis=1, tiled=False)]
    all_to_all x4 -> x2, starting transfers between devices: 20.1 us -> 12.8 us  [the longest x1 7.41 us: body(): lax.all_to_all(outgoing, 'ep', split_axis=0, concat_axis=0, tiled=True)]
    unnamed x25 -> x50, local copies, waits for them, and re-layouts: 3.43 us -> 5.14 us
  transfers between devices with their start and end apart: 6 -> 4, of which waited for: 5 -> 2; matrix products, arithmetic and copies ran while one was open for 8% -> 13% of each run, Pallas kernels for 0% -> 0%
where the time goes in v2:
time: 163 us; the launch traced here: 162 us
  waiting for transfers between devices  47.3 us (29%)
  blocking collectives  35.7 us (22%)
  matrix products  27.2 us (17%)
  local copies, waits for them, and re-layouts  15.5 us (10%)
  between operations  15.1 us (9%)
  starting transfers between devices  12.9 us (8%)
  other arithmetic  8.7 us (5%)
    psum x1, waiting for transfers between devices, body(): lax.psum(part_up.astype(jnp.bfloat16), 'grp').astype(jnp.float32)  33.4 us
    unnamed x1, blocking collectives  25.4 us
    all_gather x1, waiting for transfers between devices, body(): lax.all_gather(jnp.stack([hot_feats, hot_cotan]), 'ep', axis=1, tiled=False)  13.8 us
    psum x1, blocking collectives, body(): route_parts = lax.psum(route_parts, 'grp')  10.3 us
    all_to_all x1, starting transfers between devices, body(): lax.all_to_all(outgoing, 'ep', split_axis=0, concat_axis=0, tiled=True)  7.41 us
    all_to_all x1, starting transfers between devices, body(): lax.all_to_all(route_parts, 'ep', split_axis=0, concat_axis=0, tiled=True)  5.38 us
    unnamed x50, local copies, waits for them, and re-layouts  5.14 us
  transfers between devices with their start and end apart: 4, of which 2 were waited for; matrix products, arithmetic and copies ran while one was open for 13% of the time, Pallas kernels for 0%

profile of v2, /device:TPU:0, one launch (start us, length us, event | category | flops | bytes accessed | tf_op | source)
XLA Modules:
  0.0 162.3 jit_solution(10509885931166549547)
XLA Ops:
  7.2 1.0 copy.73
  8.5 0.8 copy.77
  9.5 2.3 %reduce-window.14 = s32[8,12,128]{2,1,0:T(8,128)S(1)} reduce-window(s32[8,12,128]{2,1,0:T(8,128)S(1)} %fusion.72, s32[]{:T(128)} %constant.20.clone.1), window={size=1x1x128 pad=0_0x0_0x127_0}, to_apply=%region_1.2 | reduce-window | flops 1560576 | bytes 98308 | tf_op jit(solution)/shard_map/reduce-window
  13.9 1.0 pad_maximum_fusion
  14.9 7.4 %all-to-all-start = ((bf16[8,3,16,1280]{3,2,1,0:T(8,128)(2,1)}), bf16[8,3,16,1280]{3,2,1,0:T(8,128)(2,1)S(1)}, u32[]{:S(2)}, u32[]{:S(2)}) async-start(bf16[8,3,16,1280]{3,2,1,0:T(8,128)(2,1)} %pad_maximum_fusion), calls=%async_computation | async-start | bytes 1966080 | tf_op jit(solution)/shard_map/all_to_all | solution.py:84
  24.2 1.3 fusion.4
  25.5 1.3 fusion.3
  29.2 25.4 %all-reduce = bf16[256]{0:T(256)(128)(2,1)S(1)} all-reduce(bf16[256]{0:T(256)(128)(2,1)S(1)} %dynamic-update-slice), channel_id=3, replica_groups=mesh['grp'=4,'ep'=8] {'ep'}, use_global_device_ids=true, to_apply=%add | all-reduce | flops 256 | bytes 1024
  54.8 0.8 fusion.95
  55.6 0.8 copy-done.6
  56.5 1.1 fusion.22
  57.6 1.1 fusion.19
  58.7 1.5 fusion.16
  60.2 13.8 %all-gather.4.cloned.1.call-done = bf16[2,256,1280]{2,1,0:T(8,128)(2,1)} async-done(((bf16[2,32,1280]{2,1,0:T(8,128)(2,1)}), bf16[2,256,1280]{2,1,0:T(8,128)(2,1)}) %all-gather.4.cloned.1.call-update) | async-done | bytes 1310736 | tf_op jit(solution)/shard_map/all_gather | solution.py:115
  74.0 1.4 copy.96
  75.6 0.9 copy-done.12
  78.3 33.4 %all-reduce.4.cloned.1.call-done = (bf16[128,768]{1,0:T(8,128)(2,1)}, bf16[128,768]{1,0:T(8,128)(2,1)}, bf16[128,768]{1,0:T(8,128)(2,1)}, bf16[3,2,128,96]{2,3,1,0:T(8,128)(2,1)}) async-done(((bf16[128,768]{1,0:T(8,128)(2,1)}, bf16[128,768]{1,0:T(8,128)(2,1)}, bf16[128,768]{1,0:T(8,128)(2,1)}, bf16[3,2,128,96]{2,3,1,0:T(8,128)(2,1)}), (bf16[128,768]{1,0:T(8,128)(2,1)}, bf16[128,768]{1,0:T(8,128)(2,1)}, ...) | async-done | bytes 737296 | tf_op jit(solution)/shard_map/psum | solution.py:98
  111.7 1.7 %convert_element_type.222 = f32[3,2,128,96]{2,3,1,0:T(8,128)} convert(bf16[3,2,128,96]{2,3,1,0:T(8,128)(2,1)} %get-tuple-element.51) | non-fusion elementwise | flops 73728 | bytes 442368 | tf_op jit(solution)/shard_map/convert_element_type | solution.py:137
  113.4 1.5 fusion.96
  115.0 3.2 %fusion.2 = bf16[1,768,1280]{2,1,0:T(8,128)(2,1)} fusion(bf16[128,1280]{1,0:T(8,128)(2,1)} %bitcast.164, bf16[128,768]{1,0:T(8,128)(2,1)} %get-tuple-element.48, bf16[128,768]{1,0:T(8,128)(2,1)} %get-tuple-element.50), kind=kOutput, calls=%fused_computation.11 | convolution fusion | flops 253427712 | bytes 2686976 | tf_op jit(solution)/shard_map/dot_general | solution.py:111
  118.2 2.0 %fusion = bf16[1,1280,768]{2,1,0:T(8,128)(2,1)} fusion(bf16[128,1280]{1,0:T(8,128)(2,1)S(1)} %bitcast.159, bf16[128,768]{1,0:T(8,128)(2,1)S(1)} %copy-done.9, bf16[128,768]{1,0:T(8,128)(2,1)S(1)} %copy-done.10, bf16[128,768]{1,0:T(8,128)(2,1)S(1)} %copy-done.8), kind=kOutput, calls=%fused_computation.9 | convolution fusion | flops 253919232 | bytes 2883584 | tf_op jit(solution)/shard_map/dot_general | solution.py:105
  120.2 2.0 %fusion.1 = bf16[1,1280,768]{2,1,0:T(8,128)(2,1)} fusion(bf16[128,1280]{1,0:T(8,128)(2,1)S(1)} %bitcast.160, bf16[128,768]{1,0:T(8,128)(2,1)S(1)} %copy-done.10, bf16[128,768]{1,0:T(8,128)(2,1)S(1)} %copy-done.8), kind=kOutput, calls=%fused_computation.10 | convolution fusion | flops 253427712 | bytes 2686976 | tf_op jit(solution)/shard_map/dot_general | solution.py:108
  122.8 1.6 %fusion.25 = f32[2,128]{1,0:T(2,128)S(1)} fusion(bf16[2,128,1280]{2,1,0:T(8,128)(2,1)} %bitcast.170, bf16[2,96,1280]{2,1,0:T(8,128)(2,1)} %param.21, f32[3,2,128,96]{2,3,1,0:T(8,128)} %convert_element_type.222), kind=kOutput, calls=%fused_computation.38 | convolution fusion | flops 63135488 | bytes 1344512 | tf_op jit(solution)/shard_map/jrd,jhd->jrh/dot_general | solution.py:134
  124.6 10.3 %psum.39 = f32[8,3,16]{2,0,1:T(8,128)S(1)} all-reduce(f32[8,3,16]{2,0,1:T(8,128)S(1)} %pad_maximum_fusion.3), channel_id=1, replica_groups=mesh['grp'=4,'ep'=8] {'grp'}, use_global_device_ids=true, to_apply=%region_21.22 | all-reduce | flops 384 | bytes 3072 | tf_op jit(solution)/shard_map/psum | solution.py:159
  135.4 5.4 %all-to-all-start.1 = ((f32[8,3,16]{2,1,0:T(4,128)}), f32[8,3,16]{2,1,0:T(4,128)}, u32[]{:S(2)}, u32[]{:S(2)}) async-start(f32[8,3,16]{2,1,0:T(4,128)} %copy.89), calls=%async_computation.1 | async-start | bytes 32768 | tf_op jit(solution)/shard_map/all_to_all | solution.py:160
  140.8 1.0 copy.86
  142.6 1.0 copy.87
  143.6 3.1 %convert_reduce_fusion.1 = f32[2,1280,96]{1,2,0:T(8,128)} fusion(f32[2,8,16,96]{3,2,1,0:T(8,128)} %bitcast.177, f32[2,8,16,96]{3,2,1,0:T(8,128)S(1)} %bitcast.173, bf16[2,2,8,16,1280]{4,3,2,1,0:T(8,128)(2,1)S(1)} %bitcast.154), kind=kOutput, calls=%fused_computation.1 | convolution fusion | flops 68714496 | bytes 1867776 | tf_op jit(solution)/shard_map/jbcd,jbch->jbdh/dot_general | solution.py:147
  146.7 2.2 %convert_reduce_fusion.2 = f32[2,1280,96]{1,2,0:T(8,128)} fusion(f32[2,8,16,96]{3,2,1,0:T(8,128)S(1)} %bitcast.174, f32[2,8,16,96]{3,2,1,0:T(8,128)S(1)} %bitcast.178, f32[2,8,16,96]{3,2,1,0:T(8,128)S(1)} %bitcast.171, bf16[2,2,8,16,1280]{4,3,2,1,0:T(8,128)(2,1)S(1)} %bitcast.155), kind=kOutput, calls=%fused_computation.2 | convolution fusion | flops 68812800 | bytes 2031616 | tf_op jit(solution)/shard_map/jbcd,jbch->jbdh/dot_general | solution.py:146
  148.9 2.2 %convert_reduce_fusion = f32[2,96,1280]{2,1,0:T(8,128)} fusion(f32[2,8,16]{2,1,0:T(8,128)S(1)} %copy.84, f32[2,8,16,96]{3,2,1,0:T(8,128)S(1)} %bitcast.172, f32[2,8,16,96]{3,2,1,0:T(8,128)S(1)} %bitcast.175, bf16[2,2,8,16,1280]{4,3,2,1,0:T(8,128)(2,1)S(1)} %bitcast.156), kind=kOutput, calls=%fused_computation | convolution fusion | flops 69697536 | bytes 1908736 | tf_op jit(solution)/shard_map/jbch,jbcd->jbhd/dot_general | solution.py:148
  151.9 1.1 convolution_reduce_fusion.1
  153.8 0.9 convolution_reduce_fusion
  (105 shorter events, 12.6 us)
Async XLA Ops:
  7.2 51.5 %copy-start = (bf16[1,768,1280]{2,1,0:T(8,128)(2,1)S(1)}, bf16[1,768,1280]{2,1,0:T(8,128)(2,1)}, u32[]{:S(2)}) copy-start(bf16[1,768,1280]{2,1,0:T(8,128)(2,1)} %param.18) | copy-start | bytes 5898244
  7.2 6.1 %copy-start.5 = (bf16[256,1280]{1,0:T(8,128)(2,1)S(1)}, bf16[256,1280]{1,0:T(8,128)(2,1)}, u32[]{:S(2)}) copy-start(bf16[256,1280]{1,0:T(8,128)(2,1)} %param.11) | copy-start | bytes 1966084
  7.2 6.4 %copy-start.4 = (bf16[256,1280]{1,0:T(8,128)(2,1)S(1)}, bf16[256,1280]{1,0:T(8,128)(2,1)}, u32[]{:S(2)}) copy-start(bf16[256,1280]{1,0:T(8,128)(2,1)} %param.12) | copy-start | bytes 1966084
  12.4 2.6 %copy-start.17 = (pred[1536]{0:T(1024)(128)(4,1)}, pred[1536]{0:T(1024)(128)(4,1)S(1)}, u32[]{:S(2)}) copy-start(pred[1536]{0:T(1024)(128)(4,1)S(1)} %broadcast_compare_fusion.1) | copy-start | bytes 4612
  13.9 8.5 %copy-start.19 = (s32[2]{0:T(128)S(1)}, s32[2]{0:T(128)}, u32[]{:S(2)}) copy-start(s32[2]{0:T(128)} %param.15) | copy-start | bytes 28
  14.9 12.7 %copy-start.21 = (u32[32]{0:T(128)S(1)}, u32[32]{0:T(128)}, u32[]{:S(2)}) copy-start(u32[32]{0:T(128)} %constant.30) | copy-start | bytes 388
  14.9 39.9 %all-to-all-start = ((bf16[8,3,16,1280]{3,2,1,0:T(8,128)(2,1)}), bf16[8,3,16,1280]{3,2,1,0:T(8,128)(2,1)S(1)}, u32[]{:S(2)}, u32[]{:S(2)}) async-start(bf16[8,3,16,1280]{3,2,1,0:T(8,128)(2,1)} %pad_maximum_fusion), calls=%async_computation | async-start | bytes 1966080 | tf_op jit(solution)/shard_map/all_to_all | solution.py:84
  22.3 51.7 %all-gather.4.cloned.1.call-start = ((), (), s32[]{:S(2)}) async-start(), calls=%async_computation.2 | async-start | bytes 1474560 | tf_op jit(solution)/shard_map/all_gather | solution.py:115
  23.6 32.0 %copy-start.18 = (pred[1536]{0:T(1024)(128)(4,1)}, pred[1536]{0:T(1024)(128)(4,1)S(1)}, u32[]{:S(2)}) copy-start(pred[1536]{0:T(1024)(128)(4,1)S(1)} %broadcast_compare_fusion) | copy-start | bytes 4612
  23.9 31.7 %copy-start.16 = (s32[1536]{0:T(1024)}, s32[1536]{0:T(1024)S(1)}, u32[]{:S(2)}) copy-start(s32[1536]{0:T(1024)S(1)} %multiply_add_fusion) | copy-start | bytes 18436
  27.6 84.2 %all-reduce.4.cloned.1.call-start = ((), (), s32[]{:S(2)}) async-start(), calls=%async_computation.3 | async-start | bytes 1474560 | tf_op jit(solution)/shard_map/psum | solution.py:98
  54.8 1.7 %copy-start.6 = (bf16[1,1280,768]{2,1,0:T(8,128)(2,1)S(1)}, bf16[1,1280,768]{2,1,0:T(8,128)(2,1)}, u32[]{:S(2)}) copy-start(bf16[1,1280,768]{2,1,0:T(8,128)(2,1)} %param.16) | copy-start | bytes 5898244
  54.8 2.8 %copy-start.7 = (bf16[1,1280,768]{2,1,0:T(8,128)(2,1)S(1)}, bf16[1,1280,768]{2,1,0:T(8,128)(2,1)}, u32[]{:S(2)}) copy-start(bf16[1,1280,768]{2,1,0:T(8,128)(2,1)} %param.17) | copy-start | bytes 5898244
  55.6 3.1 %copy-start.1 = (bf16[8,1,16,1280]{3,2,1,0:T(8,128)(2,1)}, bf16[8,1,16,1280]{3,2,1,0:T(8,128)(2,1)S(1)}, u32[]{:S(2)}) copy-start(bf16[8,1,16,1280]{3,2,1,0:T(8,128)(2,1)S(1)} %get-tuple-element.56) | copy-start | bytes 983044
  55.6 3.1 %copy-start.3 = (bf16[8,1,16,1280]{3,2,1,0:T(8,128)(2,1)}, bf16[8,1,16,1280]{3,2,1,0:T(8,128)(2,1)S(1)}, u32[]{:S(2)}) copy-start(bf16[8,1,16,1280]{3,2,1,0:T(8,128)(2,1)S(1)} %get-tuple-element.55) | copy-start | bytes 983044
  75.5 1.0 copy-start.12
  75.5 1.4 copy-start.13
  75.5 1.7 %copy-start.20 = (bf16[2,96,1280]{2,1,0:T(8,128)(2,1)S(1)}, bf16[2,96,1280]{2,1,0:T(8,128)(2,1)}, u32[]{:S(2)}) copy-start(bf16[2,96,1280]{2,1,0:T(8,128)(2,1)} %param.21) | copy-start | bytes 1474564
  75.6 1.6 %copy-start.11 = (bf16[1,2,8,16,1280]{4,3,2,1,0:T(8,128)(2,1)}, bf16[1,2,8,16,1280]{4,3,2,1,0:T(8,128)(2,1)S(1)}, u32[]{:S(2)}) copy-start(bf16[1,2,8,16,1280]{4,3,2,1,0:T(8,128)(2,1)S(1)} %get-tuple-element.53) | copy-start | bytes 1966084
  111.7 6.5 %copy-start.2 = (bf16[8,1,16,1280]{3,2,1,0:T(8,128)(2,1)S(1)}, bf16[8,1,16,1280]{3,2,1,0:T(8,128)(2,1)}, u32[]{:S(2)}) copy-start(bf16[8,1,16,1280]{3,2,1,0:T(8,128)(2,1)} %copy-done.1) | copy-start | bytes 983044
  111.7 6.5 %copy-start.8 = (bf16[128,768]{1,0:T(8,128)(2,1)S(1)}, bf16[128,768]{1,0:T(8,128)(2,1)}, u32[]{:S(2)}) copy-start(bf16[128,768]{1,0:T(8,128)(2,1)} %get-tuple-element.50) | copy-start | bytes 589828
  111.7 6.5 %copy-start.9 = (bf16[128,768]{1,0:T(8,128)(2,1)S(1)}, bf16[128,768]{1,0:T(8,128)(2,1)}, u32[]{:S(2)}) copy-start(bf16[128,768]{1,0:T(8,128)(2,1)} %get-tuple-element.48) | copy-start | bytes 589828
  111.7 6.5 %copy-start.10 = (bf16[128,768]{1,0:T(8,128)(2,1)S(1)}, bf16[128,768]{1,0:T(8,128)(2,1)}, u32[]{:S(2)}) copy-start(bf16[128,768]{1,0:T(8,128)(2,1)} %get-tuple-element.49) | copy-start | bytes 589828
  120.2 2.0 %copy-start.14 = (bf16[8,1,16,1280]{3,2,1,0:T(8,128)(2,1)S(1)}, bf16[8,1,16,1280]{3,2,1,0:T(8,128)(2,1)}, u32[]{:S(2)}) copy-start(bf16[8,1,16,1280]{3,2,1,0:T(8,128)(2,1)} %get-tuple-element.54) | copy-start | bytes 983044
  135.4 15.6 %all-to-all-start.1 = ((f32[8,3,16]{2,1,0:T(4,128)}), f32[8,3,16]{2,1,0:T(4,128)}, u32[]{:S(2)}, u32[]{:S(2)}) async-start(f32[8,3,16]{2,1,0:T(4,128)} %copy.89), calls=%async_computation.1 | async-start | bytes 32768 | tf_op jit(solution)/shard_map/all_to_all | solution.py:160
  143.6 3.2 %copy-start.15 = (f32[1,2,128,96]{3,2,1,0:T(8,128)S(1)}, f32[1,2,128,96]{3,2,1,0:T(8,128)}, u32[]{:S(2)}) copy-start(f32[1,2,128,96]{3,2,1,0:T(8,128)} %copy.85) | copy-start | bytes 294916
Sparse Core Ops, SparseCore 0:
  27.7 46.3 all-gather.3
  78.5 33.2 all-reduce.3

commit v3 on v2

--- a/solution.py
+++ b/solution.py
@@ -40,6 +40,18 @@
     ).astype(jnp.bfloat16)
     back_up = (grad_hidden * activated).astype(jnp.bfloat16)
     return (hidden, back_gate, back_up)
+
+
+def grp_sum_f32(x, axis_name):
+    size = lax.axis_size(axis_name)
+    if size & (size - 1):
+        return lax.psum(x, axis_name)
+    bit = 1
+    while bit < size:
+        partner = [(i, i ^ bit) for i in range(size)]
+        x = x + lax.ppermute(x, axis_name, partner)
+        bit *= 2
+    return x
 
 
 def body(
@@ -64,11 +76,21 @@
     flat_weights = gate_weights.reshape(-1)
     cold_map = route_table(flat_ids, jnp.arange(cold_count, dtype=jnp.int32), capacity)
     hot_map = route_table(flat_ids, hot_ids, capacity)
+    hot_feats, hot_cotan, hot_scale = gather_rows(
+        hot_map, tokens, cotangent, flat_weights, tok_rows, top_count
+    )
+    hot_rows = hot_count * capacity
+    scale_lines = -(-hot_rows // slice_width)
+    scale_lines = -(-scale_lines // 8) * 8
+    scale_block = jnp.pad(hot_scale, (0, scale_lines * slice_width - hot_rows)).reshape(
+        scale_lines, slice_width
+    )
+    blocks = lax.axis_size("ep")
+    gathered = lax.all_gather(
+        jnp.concatenate([hot_feats, hot_cotan, scale_block], axis=0), "ep", axis=0, tiled=False
+    )
     cold_feats, cold_cotan, cold_scale = gather_rows(
         cold_map, tokens, cotangent, flat_weights, tok_rows, top_count
-    )
-    hot_feats, hot_cotan, hot_scale = gather_rows(
-        hot_map, tokens, cotangent, flat_weights, tok_rows, top_count
     )
     cold_weighted = (
         cold_scale.astype(jnp.float32)[:, None] * cold_cotan.astype(jnp.float32)
@@ -111,13 +133,11 @@
     grad_down_cold = lax.dot_general(
         hidden, weighted, contract_rows, preferred_element_type=jnp.float32
     )
-    blocks = lax.axis_size("ep")
-    all_rows = lax.all_gather(jnp.stack([hot_feats, hot_cotan]), "ep", axis=1, tiled=False)
-    all_rows = all_rows.reshape(2, blocks, hot_count, capacity, slice_width)
-    all_rows = jnp.transpose(all_rows, (0, 2, 1, 3, 4)).reshape(
+    all_rows = gathered[:, : 2 * hot_rows].reshape(blocks, 2, hot_count, capacity, slice_width)
+    all_rows = jnp.transpose(all_rows, (1, 2, 0, 3, 4)).reshape(
         2, hot_count, blocks * capacity, slice_width
     )
-    all_scale = lax.all_gather(hot_scale, "ep", axis=0, tiled=False)
+    all_scale = gathered[:, 2 * hot_rows :].reshape(blocks, -1)[:, :hot_rows]
     all_scale = jnp.transpose(all_scale.reshape(blocks, hot_count, capacity), (1, 0, 2))
     rows_feat, rows_cot = all_rows[0], all_rows[1]
     rows_wt = (
@@ -156,7 +176,7 @@
         ],
         axis=1,
     )
-    route_parts = lax.psum(route_parts, "grp")
+    route_parts = grp_sum_f32(route_parts, "grp")
     route_back = lax.all_to_all(route_parts, "ep", split_axis=0, concat_axis=0, tiled=True)
     cold_back = route_back[:, 0, :]
     hot_route = jnp.sum(route_back[:, 1:, :], axis=0)

time: 163 us -> 162 us (level)
  blocking collectives: 35.7 us -> 0 us
  waiting for transfers between devices: 47.3 us -> 80.6 us
    unnamed x1 -> x0, blocking collectives: 25.4 us -> none
    all_to_all x1, waiting for transfers between devices: 0.01 us -> 24.3 us  [body(): lax.all_to_all(outgoing, 'ep', split_axis=0, concat_axis=0, tiled=True)]
    psum x1 -> x0, blocking collectives: 10.3 us -> none  [body(): route_parts = lax.psum(route_parts, 'grp')]
    all_to_all x1, waiting for transfers between devices: 0.01 us -> 4.51 us  [body(): lax.all_to_all(route_parts, 'ep', split_axis=0, concat_axis=0, tiled=True)]
    all_gather x1, waiting for transfers between devices: 13.8 us -> 17.7 us  [body(): lax.all_gather(jnp.concatenate([hot_feats, hot_cotan, scale_block], axis=...]
    another operation x5 -> x4, other arithmetic: 3.87 us -> 3.2 us
    unnamed x50 -> x55, local copies, waits for them, and re-layouts: 5.14 us -> 5.36 us
  transfers between devices with their start and end apart: 4 -> 6, of which waited for: 2 -> 5; matrix products, arithmetic and copies ran while one was open for 13% -> 16% of each run, Pallas kernels for 0% -> 0%
where the time goes in v3:
time: 162 us
  waiting for transfers between devices  80.6 us (50%)
  matrix products  27.2 us (17%)
  local copies, waits for them, and re-layouts  15.9 us (10%)
  between operations  14.5 us (9%)
  starting transfers between devices  13.5 us (8%)
  other arithmetic  9.97 us (6%)
    psum x1, waiting for transfers between devices, body(): lax.psum(part_up.astype(jnp.bfloat16), 'grp').astype(jnp.float32)  33 us
    all_to_all x1, waiting for transfers between devices, body(): lax.all_to_all(outgoing, 'ep', split_axis=0, concat_axis=0, tiled=True)  24.3 us
    all_gather x1, waiting for transfers between devices, body(): lax.all_gather(jnp.concatenate([hot_feats, hot_cotan, scale_block], axis=...  17.7 us
    all_to_all x1, starting transfers between devices, body(): lax.all_to_all(outgoing, 'ep', split_axis=0, concat_axis=0, tiled=True)  7.28 us
    all_to_all x1, starting transfers between devices, body(): lax.all_to_all(route_parts, 'ep', split_axis=0, concat_axis=0, tiled=True)  5.51 us
    unnamed x55, local copies, waits for them, and re-layouts  5.36 us
    all_to_all x1, waiting for transfers between devices, body(): lax.all_to_all(route_parts, 'ep', split_axis=0, concat_axis=0, tiled=True)  4.51 us
  transfers between devices with their start and end apart: 6, of which 5 were waited for; matrix products, arithmetic and copies ran while one was open for 16% of the time, Pallas kernels for 0%

profile of v3, /device:TPU:0, one launch (start us, length us, event | category | flops | bytes accessed | tf_op | source)
XLA Modules:
  0.0 161.6 jit_solution(11020221444124210087)
XLA Ops:
  7.2 1.0 copy.72
  9.5 2.3 %reduce-window.14 = s32[8,12,128]{2,1,0:T(8,128)S(1)} reduce-window(s32[8,12,128]{2,1,0:T(8,128)S(1)} %fusion.70, s32[]{:T(128)} %constant.21.clone.1), window={size=1x1x128 pad=0_0x0_0x127_0}, to_apply=%region_1.2 | reduce-window | flops 1560576 | bytes 98308 | tf_op jit(solution)/shard_map/reduce-window
  13.9 1.0 pad_maximum_fusion
  14.9 7.3 %all-to-all-start = ((bf16[8,3,16,1280]{3,2,1,0:T(8,128)(2,1)}), bf16[8,3,16,1280]{3,2,1,0:T(8,128)(2,1)S(1)}, u32[]{:S(2)}, u32[]{:S(2)}) async-start(bf16[8,3,16,1280]{3,2,1,0:T(8,128)(2,1)} %pad_maximum_fusion), calls=%async_computation | async-start | bytes 1966080 | tf_op jit(solution)/shard_map/all_to_all | solution.py:106
  24.1 1.3 convolution_convert_fusion.8
  25.7 1.3 convolution_convert_fusion.9
  27.7 24.3 %all-to-all-done = bf16[8,3,16,1280]{3,2,1,0:T(8,128)(2,1)S(1)} async-done(((bf16[8,3,16,1280]{3,2,1,0:T(8,128)(2,1)}), bf16[8,3,16,1280]{3,2,1,0:T(8,128)(2,1)S(1)}, u32[]{:S(2)}, u32[]{:S(2)}) %all-to-all-start) | async-done | bytes 983072 | tf_op jit(solution)/shard_map/all_to_all | solution.py:106
  53.7 1.1 fusion.20
  54.8 1.1 fusion.17
  56.0 1.5 fusion.14
  57.4 17.7 %all-gather.3.cloned.1.call-done = bf16[576,1280]{1,0:T(8,128)(2,1)} async-done(((bf16[72,1280]{1,0:T(8,128)(2,1)}), bf16[576,1280]{1,0:T(8,128)(2,1)}) %all-gather.3.cloned.1.call-update) | async-done | bytes 1474576 | tf_op jit(solution)/shard_map/all_gather | solution.py:89
  75.1 0.9 slice_bitcast_fusion
  76.0 1.4 slice.74
  77.9 0.9 copy-done.13
  80.7 33.0 %all-reduce.4.cloned.1.call-done = (bf16[128,768]{1,0:T(8,128)(2,1)}, bf16[128,768]{1,0:T(8,128)(2,1)}, bf16[128,768]{1,0:T(8,128)(2,1)}, bf16[3,2,128,96]{2,3,1,0:T(8,128)(2,1)}) async-done(((bf16[128,768]{1,0:T(8,128)(2,1)}, bf16[128,768]{1,0:T(8,128)(2,1)}, bf16[128,768]{1,0:T(8,128)(2,1)}, bf16[3,2,128,96]{2,3,1,0:T(8,128)(2,1)}), (bf16[128,768]{1,0:T(8,128)(2,1)}, bf16[128,768]{1,0:T(8,128)(2,1)}, ...) | async-done | bytes 737296 | tf_op jit(solution)/shard_map/psum | solution.py:120
  113.7 1.6 %convert_element_type.224 = f32[3,2,128,96]{2,3,1,0:T(8,128)} convert(bf16[3,2,128,96]{2,3,1,0:T(8,128)(2,1)} %get-tuple-element.51) | non-fusion elementwise | flops 73728 | bytes 442368 | tf_op jit(solution)/shard_map/convert_element_type | solution.py:157
  115.3 1.5 fusion.95
  116.9 1.7 %fusion.11 = f32[128]{0:T(128)S(1)} fusion(bf16[1,768,1280]{2,1,0:T(8,128)(2,1)S(1)} %copy-done, bf16[128,1280]{1,0:T(8,128)(2,1)} %bitcast.177, bf16[128,768]{1,0:T(8,128)(2,1)} %get-tuple-element.48, bf16[128,768]{1,0:T(8,128)(2,1)} %get-tuple-element.50), kind=kOutput, calls=%fused_computation.28 | convolution fusion | flops 252936064 | bytes 2687488 | tf_op jit(solution)/shard_map/dot_general | solution.py:124
  118.7 1.6 %fusion.23 = f32[2,128]{1,0:T(2,128)S(1)} fusion(bf16[2,128,1280]{2,1,0:T(8,128)(2,1)} %bitcast.171, bf16[2,96,1280]{2,1,0:T(8,128)(2,1)} %param.21, f32[3,2,128,96]{2,3,1,0:T(8,128)} %convert_element_type.224), kind=kOutput, calls=%fused_computation.36 | convolution fusion | flops 63135488 | bytes 1344512 | tf_op jit(solution)/shard_map/jrd,jhd->jrh/dot_general | solution.py:154
  121.0 1.0 copy.85
  122.8 1.0 copy.86
  123.8 3.1 %convert_reduce_fusion.1 = f32[2,1280,96]{1,2,0:T(8,128)} fusion(f32[2,8,16,96]{3,2,1,0:T(8,128)} %bitcast.179, f32[2,8,16,96]{3,2,1,0:T(8,128)S(1)} %bitcast.174, bf16[2,2,8,16,1280]{4,3,2,1,0:T(8,128)(2,1)S(1)} %bitcast.153), kind=kOutput, calls=%fused_computation.1 | convolution fusion | flops 68714496 | bytes 1867776 | tf_op jit(solution)/shard_map/jbcd,jbch->jbdh/dot_general | solution.py:167
  126.9 2.2 %convert_reduce_fusion.2 = f32[2,1280,96]{1,2,0:T(8,128)} fusion(f32[2,8,16,96]{3,2,1,0:T(8,128)S(1)} %bitcast.175, f32[2,8,16,96]{3,2,1,0:T(8,128)S(1)} %bitcast.180, f32[2,8,16,96]{3,2,1,0:T(8,128)S(1)} %bitcast.172, bf16[2,2,8,16,1280]{4,3,2,1,0:T(8,128)(2,1)S(1)} %bitcast.154), kind=kOutput, calls=%fused_computation.2 | convolution fusion | flops 68812800 | bytes 2031616 | tf_op jit(solution)/shard_map/jbcd,jbch->jbdh/dot_general | solution.py:166
  129.1 2.0 %fusion = bf16[1,1280,768]{2,1,0:T(8,128)(2,1)} fusion(bf16[128,1280]{1,0:T(8,128)(2,1)S(1)} %bitcast.158, bf16[128,768]{1,0:T(8,128)(2,1)S(1)} %copy-done.10, bf16[128,768]{1,0:T(8,128)(2,1)S(1)} %copy-done.11, bf16[128,768]{1,0:T(8,128)(2,1)S(1)} %copy-done.9), kind=kOutput, calls=%fused_computation.9 | convolution fusion | flops 253919232 | bytes 2883584 | tf_op jit(solution)/shard_map/dot_general | solution.py:127
  131.1 2.0 %fusion.1 = bf16[1,1280,768]{2,1,0:T(8,128)(2,1)} fusion(bf16[128,1280]{1,0:T(8,128)(2,1)S(1)} %bitcast.159, bf16[128,768]{1,0:T(8,128)(2,1)S(1)} %copy-done.11, bf16[128,768]{1,0:T(8,128)(2,1)S(1)} %copy-done.9), kind=kOutput, calls=%fused_computation.10 | convolution fusion | flops 253427712 | bytes 2686976 | tf_op jit(solution)/shard_map/dot_general | solution.py:130
  134.5 2.0 %fusion.2 = bf16[1,768,1280]{2,1,0:T(8,128)(2,1)} fusion(bf16[128,1280]{1,0:T(8,128)(2,1)S(1)} %bitcast.164, bf16[128,768]{1,0:T(8,128)(2,1)S(1)} %copy-done.10, bf16[128,768]{1,0:T(8,128)(2,1)S(1)} %copy-done.9), kind=kOutput, calls=%fused_computation.11 | convolution fusion | flops 253427712 | bytes 2686976 | tf_op jit(solution)/shard_map/dot_general | solution.py:133
  136.5 1.1 collective-permute-done.1
  138.2 5.5 %all-to-all-start.1 = ((f32[8,3,16]{2,1,0:T(4,128)}), f32[8,3,16]{2,1,0:T(4,128)}, u32[]{:S(2)}, u32[]{:S(2)}) async-start(f32[8,3,16]{2,1,0:T(4,128)} %copy.88), calls=%async_computation.1 | async-start | bytes 32768 | tf_op jit(solution)/shard_map/all_to_all | solution.py:180
  143.7 2.2 %convert_reduce_fusion = f32[2,96,1280]{2,1,0:T(8,128)} fusion(f32[2,8,16]{2,1,0:T(8,128)S(1)} %copy.83, f32[2,8,16,96]{3,2,1,0:T(8,128)S(1)} %bitcast.173, f32[2,8,16,96]{3,2,1,0:T(8,128)S(1)} %bitcast.176, bf16[2,2,8,16,1280]{4,3,2,1,0:T(8,128)(2,1)S(1)} %bitcast.155), kind=kOutput, calls=%fused_computation | convolution fusion | flops 69697536 | bytes 1908736 | tf_op jit(solution)/shard_map/jbch,jbcd->jbhd/dot_general | solution.py:168
  145.9 4.5 %all-to-all-done.1 = f32[8,3,16]{2,1,0:T(4,128)} async-done(((f32[8,3,16]{2,1,0:T(4,128)}), f32[8,3,16]{2,1,0:T(4,128)}, u32[]{:S(2)}, u32[]{:S(2)}) %all-to-all-start.1) | async-done | bytes 1568 | tf_op jit(solution)/shard_map/all_to_all | solution.py:180
  151.2 1.1 convolution_reduce_fusion.1
  153.1 0.9 convolution_reduce_fusion
  (118 shorter events, 15.9 us)
Async XLA Ops:
  7.2 48.8 %copy-start = (bf16[1,768,1280]{2,1,0:T(8,128)(2,1)S(1)}, bf16[1,768,1280]{2,1,0:T(8,128)(2,1)}, u32[]{:S(2)}) copy-start(bf16[1,768,1280]{2,1,0:T(8,128)(2,1)} %param.18) | copy-start | bytes 5898244
  7.2 6.1 %copy-start.6 = (bf16[256,1280]{1,0:T(8,128)(2,1)S(1)}, bf16[256,1280]{1,0:T(8,128)(2,1)}, u32[]{:S(2)}) copy-start(bf16[256,1280]{1,0:T(8,128)(2,1)} %param.11) | copy-start | bytes 1966084
  7.2 6.4 %copy-start.5 = (bf16[256,1280]{1,0:T(8,128)(2,1)S(1)}, bf16[256,1280]{1,0:T(8,128)(2,1)}, u32[]{:S(2)}) copy-start(bf16[256,1280]{1,0:T(8,128)(2,1)} %param.12) | copy-start | bytes 1966084
  12.4 2.6 %copy-start.21 = (pred[1536]{0:T(1024)(128)(4,1)}, pred[1536]{0:T(1024)(128)(4,1)S(1)}, u32[]{:S(2)}) copy-start(pred[1536]{0:T(1024)(128)(4,1)S(1)} %broadcast_compare_fusion.1) | copy-start | bytes 4612
  12.6 2.4 %copy-start.18 = (s32[1536]{0:T(1024)}, s32[1536]{0:T(1024)S(1)}, u32[]{:S(2)}) copy-start(s32[1536]{0:T(1024)S(1)} %multiply_add_fusion.1) | copy-start | bytes 18436
  13.9 8.4 %copy-start.23 = (s32[2]{0:T(128)S(1)}, s32[2]{0:T(128)}, u32[]{:S(2)}) copy-start(s32[2]{0:T(128)} %param.15) | copy-start | bytes 28
  14.9 37.1 %all-to-all-start = ((bf16[8,3,16,1280]{3,2,1,0:T(8,128)(2,1)}), bf16[8,3,16,1280]{3,2,1,0:T(8,128)(2,1)S(1)}, u32[]{:S(2)}, u32[]{:S(2)}) async-start(bf16[8,3,16,1280]{3,2,1,0:T(8,128)(2,1)} %pad_maximum_fusion), calls=%async_computation | async-start | bytes 1966080 | tf_op jit(solution)/shard_map/all_to_all | solution.py:106
  22.2 52.9 %all-gather.3.cloned.1.call-start = ((), (), s32[]{:S(2)}) async-start(), calls=%async_computation.2 | async-start | bytes 1658880 | tf_op jit(solution)/shard_map/all_gather | solution.py:89
  23.5 29.3 %copy-start.22 = (pred[1536]{0:T(1024)(128)(4,1)}, pred[1536]{0:T(1024)(128)(4,1)S(1)}, u32[]{:S(2)}) copy-start(pred[1536]{0:T(1024)(128)(4,1)S(1)} %broadcast_compare_fusion) | copy-start | bytes 4612
  23.8 1.6 copy-start.20
  27.7 86.0 %all-reduce.4.cloned.1.call-start = ((), (), s32[]{:S(2)}) async-start(), calls=%async_computation.3 | async-start | bytes 1474560 | tf_op jit(solution)/shard_map/psum | solution.py:120
  52.0 1.7 %copy-start.7 = (bf16[1,1280,768]{2,1,0:T(8,128)(2,1)S(1)}, bf16[1,1280,768]{2,1,0:T(8,128)(2,1)}, u32[]{:S(2)}) copy-start(bf16[1,1280,768]{2,1,0:T(8,128)(2,1)} %param.16) | copy-start | bytes 5898244
  52.0 2.8 %copy-start.8 = (bf16[1,1280,768]{2,1,0:T(8,128)(2,1)S(1)}, bf16[1,1280,768]{2,1,0:T(8,128)(2,1)}, u32[]{:S(2)}) copy-start(bf16[1,1280,768]{2,1,0:T(8,128)(2,1)} %param.17) | copy-start | bytes 5898244
  52.8 3.1 %copy-start.1 = (bf16[8,1,16,1280]{3,2,1,0:T(8,128)(2,1)}, bf16[8,1,16,1280]{3,2,1,0:T(8,128)(2,1)S(1)}, u32[]{:S(2)}) copy-start(bf16[8,1,16,1280]{3,2,1,0:T(8,128)(2,1)S(1)} %get-tuple-element.56) | copy-start | bytes 983044
  52.8 3.1 %copy-start.3 = (bf16[8,1,16,1280]{3,2,1,0:T(8,128)(2,1)}, bf16[8,1,16,1280]{3,2,1,0:T(8,128)(2,1)S(1)}, u32[]{:S(2)}) copy-start(bf16[8,1,16,1280]{3,2,1,0:T(8,128)(2,1)S(1)} %get-tuple-element.55) | copy-start | bytes 983044
  77.8 1.1 copy-start.13
  77.8 1.4 copy-start.14
  77.8 1.8 %copy-start.24 = (bf16[2,96,1280]{2,1,0:T(8,128)(2,1)S(1)}, bf16[2,96,1280]{2,1,0:T(8,128)(2,1)}, u32[]{:S(2)}) copy-start(bf16[2,96,1280]{2,1,0:T(8,128)(2,1)} %param.21) | copy-start | bytes 1474564
  77.9 1.6 %copy-start.12 = (bf16[1,2,8,16,1280]{4,3,2,1,0:T(8,128)(2,1)}, bf16[1,2,8,16,1280]{4,3,2,1,0:T(8,128)(2,1)S(1)}, u32[]{:S(2)}) copy-start(bf16[1,2,8,16,1280]{4,3,2,1,0:T(8,128)(2,1)S(1)} %get-tuple-element.53) | copy-start | bytes 1966084
  118.7 4.1 %copy-start.16 = (f32[8,1,16]{2,0,1:T(8,128)}, f32[8,1,16]{2,0,1:T(8,128)S(1)}, u32[]{:S(2)}) copy-start(f32[8,1,16]{2,0,1:T(8,128)S(1)} %reshape.188) | copy-start | bytes 1540
  121.0 12.1 %collective-permute-start = (f32[8,3,16]{2,0,1:T(8,128)}, f32[8,3,16]{2,0,1:T(8,128)}, u32[]{:S(2)}, u32[]{:S(2)}) collective-permute-start(f32[8,3,16]{2,0,1:T(8,128)} %pad_maximum_fusion.3), channel_id=1, source_target_pairs={{0,8},{8,0},{16,24},{24,16},{1,9},{9,1},{17,25},{25,17},{2,10},{10... | collective-permute-start | bytes 4616 | tf_op jit(solution)/shard_map/ppermute | solution.py:52
  123.8 3.2 %copy-start.15 = (f32[1,2,128,96]{3,2,1,0:T(8,128)S(1)}, f32[1,2,128,96]{3,2,1,0:T(8,128)}, u32[]{:S(2)}) copy-start(f32[1,2,128,96]{3,2,1,0:T(8,128)} %copy.84) | copy-start | bytes 294916
  126.9 2.2 %copy-start.2 = (bf16[8,1,16,1280]{3,2,1,0:T(8,128)(2,1)S(1)}, bf16[8,1,16,1280]{3,2,1,0:T(8,128)(2,1)}, u32[]{:S(2)}) copy-start(bf16[8,1,16,1280]{3,2,1,0:T(8,128)(2,1)} %copy-done.1) | copy-start | bytes 983044
  126.9 2.2 %copy-start.9 = (bf16[128,768]{1,0:T(8,128)(2,1)S(1)}, bf16[128,768]{1,0:T(8,128)(2,1)}, u32[]{:S(2)}) copy-start(bf16[128,768]{1,0:T(8,128)(2,1)} %get-tuple-element.50) | copy-start | bytes 589828
  126.9 2.2 %copy-start.10 = (bf16[128,768]{1,0:T(8,128)(2,1)S(1)}, bf16[128,768]{1,0:T(8,128)(2,1)}, u32[]{:S(2)}) copy-start(bf16[128,768]{1,0:T(8,128)(2,1)} %get-tuple-element.48) | copy-start | bytes 589828
  126.9 2.2 %copy-start.11 = (bf16[128,768]{1,0:T(8,128)(2,1)S(1)}, bf16[128,768]{1,0:T(8,128)(2,1)}, u32[]{:S(2)}) copy-start(bf16[128,768]{1,0:T(8,128)(2,1)} %get-tuple-element.49) | copy-start | bytes 589828
  131.1 2.0 %copy-start.17 = (f32[8,1,16]{2,0,1:T(8,128)S(1)}, f32[8,1,16]{2,0,1:T(8,128)}, u32[]{:S(2)}) copy-start(f32[8,1,16]{2,0,1:T(8,128)} %copy-done.16) | copy-start | bytes 1540
  131.1 3.3 %copy-start.4 = (bf16[8,1,16,1280]{3,2,1,0:T(8,128)(2,1)S(1)}, bf16[8,1,16,1280]{3,2,1,0:T(8,128)(2,1)}, u32[]{:S(2)}) copy-start(bf16[8,1,16,1280]{3,2,1,0:T(8,128)(2,1)} %copy-done.3) | copy-start | bytes 983044
  133.9 17.3 %copy-start.19 = (s32[1536]{0:T(1024)S(1)}, s32[1536]{0:T(1024)}, u32[]{:S(2)}) copy-start(s32[1536]{0:T(1024)} %copy-done.18) | copy-start | bytes 18436
  133.9 3.7 %collective-permute-start.1 = (f32[8,3,16]{2,0,1:T(8,128)S(1)}, f32[8,3,16]{2,0,1:T(8,128)S(1)}, u32[]{:S(2)}, u32[]{:S(2)}) collective-permute-start(f32[8,3,16]{2,0,1:T(8,128)S(1)} %fusion.87), channel_id=1, source_target_pairs={{0,16},{8,24},{16,0},{24,8},{1,17},{9,25},{17,1},{25,9},{2,18},{10... | collective-permute-start | bytes 4616 | tf_op jit(solution)/shard_map/ppermute | solution.py:52
  138.2 12.2 %all-to-all-start.1 = ((f32[8,3,16]{2,1,0:T(4,128)}), f32[8,3,16]{2,1,0:T(4,128)}, u32[]{:S(2)}, u32[]{:S(2)}) async-start(f32[8,3,16]{2,1,0:T(4,128)} %copy.88), calls=%async_computation.1 | async-start | bytes 32768 | tf_op jit(solution)/shard_map/all_to_all | solution.py:180
Sparse Core Ops, SparseCore 0:
  27.8 47.2 all-gather.2
  80.8 32.8 all-reduce.3

commit v4 on v3

--- a/solution.py
+++ b/solution.py
@@ -52,6 +52,42 @@
         x = x + lax.ppermute(x, axis_name, partner)
         bit *= 2
     return x
+
+
+def grp_sum_rounded(parts, axes, axis_name):
+    size = lax.axis_size(axis_name)
+    rounded = [p.astype(jnp.bfloat16) for p in parts]
+    if size == 1:
+        return [r.astype(jnp.float32) for r in rounded]
+    if size & (size - 1) or any(p.shape[a] % 2 for p, a in zip(parts, axes)):
+        return [lax.psum(r, axis_name).astype(jnp.float32) for r in rounded]
+    half_of = [p.shape[a] // 2 for p, a in zip(parts, axes)]
+    core = lax.axis_index(axis_name) % 2
+    keep = [
+        lax.dynamic_slice_in_dim(r, core * h, h, axis=a) for r, h, a in zip(rounded, half_of, axes)
+    ]
+    send = [
+        lax.dynamic_slice_in_dim(r, (1 - core) * h, h, axis=a)
+        for r, h, a in zip(rounded, half_of, axes)
+    ]
+    swap = [(i, i ^ 1) for i in range(size)]
+    got = lax.ppermute(send, axis_name, swap)
+    sums = [k.astype(jnp.float32) + g.astype(jnp.float32) for k, g in zip(keep, got)]
+    bit = 2
+    while bit < size:
+        partner = [(i, i ^ bit) for i in range(size)]
+        mine = [s.astype(jnp.bfloat16) for s in sums]
+        got = lax.ppermute(mine, axis_name, partner)
+        sums = [m.astype(jnp.float32) + g.astype(jnp.float32) for m, g in zip(mine, got)]
+        bit *= 2
+    other = lax.ppermute(sums, axis_name, swap)
+    full = []
+    for s, o, a in zip(sums, other, axes):
+        pair = jnp.stack([s, o])
+        first = lax.dynamic_index_in_dim(pair, core, axis=0, keepdims=False)
+        second = lax.dynamic_index_in_dim(pair, 1 - core, axis=0, keepdims=False)
+        full.append(jnp.concatenate([first, second], axis=a))
+    return full
 
 
 def body(
@@ -92,21 +128,27 @@
     cold_feats, cold_cotan, cold_scale = gather_rows(
         cold_map, tokens, cotangent, flat_weights, tok_rows, top_count
     )
-    cold_weighted = (
-        cold_scale.astype(jnp.float32)[:, None] * cold_cotan.astype(jnp.float32)
-    ).astype(jnp.bfloat16)
-    outgoing = jnp.stack(
+    cold_lines = -(-capacity // slice_width)
+    cold_lines = -(-cold_lines // 8) * 8
+    cold_scale_block = jnp.pad(
+        cold_scale.reshape(cold_count, capacity),
+        ((0, 0), (0, cold_lines * slice_width - capacity)),
+    ).reshape(cold_count, cold_lines, slice_width)
+    outgoing = jnp.concatenate(
         [
             cold_feats.reshape(cold_count, capacity, slice_width),
             cold_cotan.reshape(cold_count, capacity, slice_width),
-            cold_weighted.reshape(cold_count, capacity, slice_width),
+            cold_scale_block,
         ],
         axis=1,
     )
     received = lax.all_to_all(outgoing, "ep", split_axis=0, concat_axis=0, tiled=True)
-    recv_feats = received[:, 0].reshape(-1, slice_width)
-    recv_cotan = received[:, 1].reshape(-1, slice_width)
-    weighted = received[:, 2].reshape(-1, slice_width)
+    recv_feats = received[:, :capacity].reshape(-1, slice_width)
+    recv_cotan = received[:, capacity : 2 * capacity].reshape(-1, slice_width)
+    recv_scale = received[:, 2 * capacity :].reshape(cold_count, -1)[:, :capacity]
+    weighted = (
+        recv_scale.reshape(-1, 1).astype(jnp.float32) * recv_cotan.astype(jnp.float32)
+    ).astype(jnp.bfloat16)
     w_gate = gate_cold[0]
     w_up = up_cold[0]
     w_down = down_cold[0]
@@ -114,24 +156,6 @@
     part_up = jnp.dot(recv_feats, w_up, preferred_element_type=jnp.float32)
     part_hidden = lax.dot_general(
         weighted, w_down, (((1,), (1,)), ((), ())), preferred_element_type=jnp.float32
-    )
-    pre_gate, pre_up, grad_hidden = (
-        lax.psum(part_gate.astype(jnp.bfloat16), "grp").astype(jnp.float32),
-        lax.psum(part_up.astype(jnp.bfloat16), "grp").astype(jnp.float32),
-        lax.psum(part_hidden.astype(jnp.bfloat16), "grp").astype(jnp.float32),
-    )
-    hidden, back_gate, back_up = swiglu_back(pre_gate, pre_up, grad_hidden)
-    output_slice = jnp.dot(hidden, w_down, preferred_element_type=jnp.float32)
-    cold_route = jnp.sum(output_slice * recv_cotan.astype(jnp.float32), axis=1)
-    contract_rows = (((0,), (0,)), ((), ()))
-    grad_gate_cold = lax.dot_general(
-        recv_feats, back_gate, contract_rows, preferred_element_type=jnp.float32
-    )
-    grad_up_cold = lax.dot_general(
-        recv_feats, back_up, contract_rows, preferred_element_type=jnp.float32
-    )
-    grad_down_cold = lax.dot_general(
-        hidden, weighted, contract_rows, preferred_element_type=jnp.float32
     )
     all_rows = gathered[:, : 2 * hot_rows].reshape(blocks, 2, hot_count, capacity, slice_width)
     all_rows = jnp.transpose(all_rows, (1, 2, 0, 3, 4)).reshape(
@@ -152,10 +176,25 @@
         "jrd,jhd->jrh", rows_wt, down_hot, preferred_element_type=jnp.float32
     )
     cot_down = jnp.einsum("jrd,jhd->jrh", rows_cot, down_hot, preferred_element_type=jnp.float32)
-    hot_parts = lax.psum(
-        jnp.stack([part_gate_hot, part_up_hot, part_hidden_hot]).astype(jnp.bfloat16), "grp"
-    ).astype(jnp.float32)
-    hidden_hot, back_gate_hot, back_up_hot = swiglu_back(hot_parts[0], hot_parts[1], hot_parts[2])
+    (pre_gate, pre_up, grad_hidden, pre_gate_hot, pre_up_hot, grad_hidden_hot) = grp_sum_rounded(
+        [part_gate, part_up, part_hidden, part_gate_hot, part_up_hot, part_hidden_hot],
+        [0, 0, 0, 1, 1, 1],
+        "grp",
+    )
+    hidden, back_gate, back_up = swiglu_back(pre_gate, pre_up, grad_hidden)
+    output_slice = jnp.dot(hidden, w_down, preferred_element_type=jnp.float32)
+    cold_route = jnp.sum(output_slice * recv_cotan.astype(jnp.float32), axis=1)
+    contract_rows = (((0,), (0,)), ((), ()))
+    grad_gate_cold = lax.dot_general(
+        recv_feats, back_gate, contract_rows, preferred_element_type=jnp.float32
+    )
+    grad_up_cold = lax.dot_general(
+        recv_feats, back_up, contract_rows, preferred_element_type=jnp.float32
+    )
+    grad_down_cold = lax.dot_general(
+        hidden, weighted, contract_rows, preferred_element_type=jnp.float32
+    )
+    hidden_hot, back_gate_hot, back_up_hot = swiglu_back(pre_gate_hot, pre_up_hot, grad_hidden_hot)
     hot_route_part = jnp.sum(hidden_hot.astype(jnp.float32) * cot_down, axis=2)
     hidden_blk = hidden_hot.shape[2]
     feat_b = rows_feat.reshape(hot_count, blocks, capacity, slice_width)

time: 162 us -> 129 us (0.80)
  waiting for transfers between devices: 80.6 us -> 34.5 us
  starting transfers between devices: 13.5 us -> 22.6 us
  other arithmetic: 9.97 us -> 15.2 us
  matrix products: 27.2 us -> 22.1 us
  local copies, waits for them, and re-layouts: 15.9 us -> 19.2 us
    psum x1 -> x0, waiting for transfers between devices: 33 us -> none  [body(): lax.psum(part_up.astype(jnp.bfloat16), 'grp').astype(jnp.float32)]
    all_gather x1, waiting for transfers between devices: 17.7 us -> 1 us  [body(): lax.all_gather(jnp.concatenate([hot_feats, hot_cotan, scale_block], axis=...]
    ppermute x0 -> x18, starting transfers between devices: none -> 9.44 us  [the longest x6 7.67 us: grp_sum_rounded(): got = lax.ppermute(mine, axis_name, partner)]
    ppermute x0 -> x18, waiting for transfers between devices: none -> 8.87 us  [the longest x6 7.09 us: grp_sum_rounded(): got = lax.ppermute(mine, axis_name, partner)]
    slice x6 -> x1, local copies, waits for them, and re-layouts: 5.34 us -> 0.29 us  [the longest x2 2.52 us: body(): hot_parts[1]]
    all_to_all x1, waiting for transfers between devices: 24.3 us -> 20.1 us  [body(): lax.all_to_all(outgoing, 'ep', split_axis=0, concat_axis=0, tiled=True)]
    dynamic_slice x0 -> x8, local copies, waits for them, and re-layouts: none -> 3.53 us  [the longest x1 1.6 us: grp_sum_rounded(): first = lax.dynamic_index_in_dim(pair, core, axis=0, keepdims=False)]
    concatenate x0 -> x4, other arithmetic: none -> 2.01 us  [the longest x3 1.07 us: grp_sum_rounded(): full.append(jnp.concatenate([first, second], axis=a))]
  transfers between devices with their start and end apart: 6 -> 23, of which waited for: 5 -> 12; matrix products, arithmetic and copies ran while one was open for 16% -> 22% of each run, Pallas kernels for 0% -> 0%
where the time goes in v4:
time: 129 us; the launch traced here: 128 us
  waiting for transfers between devices  34.5 us (27%)
  starting transfers between devices  22.6 us (18%)
  matrix products  22.1 us (17%)
  local copies, waits for them, and re-layouts  19.2 us (15%)
  other arithmetic  15.2 us (12%)
  between operations  14.8 us (11%)
    all_to_all x1, waiting for transfers between devices, body(): lax.all_to_all(outgoing, 'ep', split_axis=0, concat_axis=0, tiled=True)  20.1 us
    ppermute x6, starting transfers between devices, grp_sum_rounded(): got = lax.ppermute(mine, axis_name, partner)  7.67 us
    all_to_all x1, starting transfers between devices, body(): lax.all_to_all(outgoing, 'ep', split_axis=0, concat_axis=0, tiled=True)  7.28 us
    ppermute x6, waiting for transfers between devices, grp_sum_rounded(): got = lax.ppermute(mine, axis_name, partner)  7.09 us
    unnamed x37, local copies, waits for them, and re-layouts  6.08 us
    all_to_all x1, waiting for transfers between devices, body(): lax.all_to_all(route_parts, 'ep', split_axis=0, concat_axis=0, tiled=True)  4.41 us
    all_to_all x1, starting transfers between devices, body(): lax.all_to_all(route_parts, 'ep', split_axis=0, concat_axis=0, tiled=True)  3.94 us
    another operation x4, other arithmetic  3.19 us
  transfers between devices with their start and end apart: 23, of which 12 were waited for; matrix products, arithmetic and copies ran while one was open for 22% of the time, Pallas kernels for 0%

profile of v4, /device:TPU:0, one launch (start us, length us, event | category | flops | bytes accessed | tf_op | source)
XLA Modules:
  0.0 128.4 jit_solution(8465822384356750033)
XLA Ops:
  7.2 1.0 copy.73
  11.2 2.3 %reduce-window.14 = s32[8,12,128]{2,1,0:T(8,128)S(1)} reduce-window(s32[8,12,128]{2,1,0:T(8,128)S(1)} %fusion.75, s32[]{:T(128)} %constant.67.clone.1), window={size=1x1x128 pad=0_0x0_0x127_0}, to_apply=%region_1.2 | reduce-window | flops 1560576 | bytes 98308 | tf_op jit(solution)/shard_map/reduce-window
  16.6 0.9 pad_maximum_fusion
  17.5 7.3 %all-to-all-start = ((bf16[8,40,1280]{2,1,0:T(8,128)(2,1)}), bf16[8,40,1280]{2,1,0:T(8,128)(2,1)S(1)}, u32[]{:S(2)}, u32[]{:S(2)}) async-start(bf16[8,40,1280]{2,1,0:T(8,128)(2,1)} %pad_maximum_fusion), calls=%async_computation | async-start | bytes 1638400 | tf_op jit(solution)/shard_map/all_to_all | solution.py:145
  26.3 1.0 copy.79
  27.6 1.3 %convolution_convert_fusion.9 = bf16[32,1280]{1,0:T(8,128)(2,1)S(1)} fusion(bf16[256,1280]{1,0:T(8,128)(2,1)} %param.11, bf16[32,256]{1,0:T(8,128)(2,1)S(1)} %convert_reduce_fusion.4), kind=kOutput, calls=%fused_computation.16 | convolution fusion | flops 21012480 | bytes 753664 | tf_op jit(solution)/shard_map/dot_general | solution.py:24
  29.7 20.1 %all-to-all-done = bf16[8,40,1280]{2,1,0:T(8,128)(2,1)S(1)} async-done(((bf16[8,40,1280]{2,1,0:T(8,128)(2,1)}), bf16[8,40,1280]{2,1,0:T(8,128)(2,1)S(1)}, u32[]{:S(2)}, u32[]{:S(2)}) %all-to-all-start) | async-done | bytes 819232 | tf_op jit(solution)/shard_map/all_to_all | solution.py:145
  54.1 1.8 %collective-permute-start.1 = (bf16[64,768]{1,0:T(8,128)(2,1)S(1)}, bf16[64,768]{1,0:T(8,128)(2,1)S(1)}, u32[]{:S(2)}, u32[]{:S(2)}) collective-permute-start(bf16[64,768]{1,0:T(8,128)(2,1)S(1)} %add_convert_fusion.2), channel_id=1, source_target_pairs={{0,16},{8,24},{16,0},{24,8},{1,17},{9,25},{17,1},{25,9},{2,18},{10... | collective-permute-start | bytes 294920 | tf_op jit(solution)/shard_map/ppermute | solution.py:80
  56.4 1.8 %collective-permute-start.4 = (bf16[64,768]{1,0:T(8,128)(2,1)S(1)}, bf16[64,768]{1,0:T(8,128)(2,1)S(1)}, u32[]{:S(2)}, u32[]{:S(2)}) collective-permute-start(bf16[64,768]{1,0:T(8,128)(2,1)S(1)} %add_convert_fusion.1), channel_id=1, source_target_pairs={{0,16},{8,24},{16,0},{24,8},{1,17},{9,25},{17,1},{25,9},{2,18},{10... | collective-permute-start | bytes 294920 | tf_op jit(solution)/shard_map/ppermute | solution.py:80
  58.2 3.7 %collective-permute-done.7 = bf16[64,768]{1,0:T(8,128)(2,1)S(1)} collective-permute-done((bf16[64,768]{1,0:T(8,128)(2,1)S(1)}, bf16[64,768]{1,0:T(8,128)(2,1)S(1)}, u32[]{:S(2)}, u32[]{:S(2)}) %collective-permute-start.7) | collective-permute-done | bytes 98336 | tf_op jit(solution)/shard_map/ppermute | solution.py:80
  62.0 1.5 %collective-permute-done.4 = bf16[64,768]{1,0:T(8,128)(2,1)S(1)} collective-permute-done((bf16[64,768]{1,0:T(8,128)(2,1)S(1)}, bf16[64,768]{1,0:T(8,128)(2,1)S(1)}, u32[]{:S(2)}, u32[]{:S(2)}) %collective-permute-start.4) | collective-permute-done | bytes 98336 | tf_op jit(solution)/shard_map/ppermute | solution.py:80
  66.5 1.0 fusion.53
  67.5 2.9 %fusion.2 = bf16[1,768,1280]{2,1,0:T(8,128)(2,1)} fusion(bf16[128,768]{1,0:T(8,128)(2,1)S(1)} %multiply_convert_fusion.3, bf16[128,1280]{1,0:T(8,128)(2,1)} %fusion.34), kind=kOutput, calls=%fused_computation.11 | convolution fusion | flops 252641280 | bytes 2490368 | tf_op jit(solution)/shard_map/dot_general | solution.py:194
  70.4 2.0 %fusion.1 = bf16[1,1280,768]{2,1,0:T(8,128)(2,1)} fusion(bf16[128,1280]{1,0:T(8,128)(2,1)S(1)} %bitcast.170, f32[64,768]{1,0:T(8,128)S(1)} %get-tuple-element.53, f32[64,768]{1,0:T(8,128)S(1)} %get-tuple-element.52, f32[64,768]{1,0:T(8,128)S(1)} %get-tuple-element.57, f32[64,768]{1,0:T(8,128)S(1)} %get-tuple-element.56), kind=kOutput, calls=%fused_computation.10 | convolution fusion | flops 253427712 | bytes 3080192 | tf_op jit(solution)/shard_map/dot_general | solution.py:191
  72.4 2.0 %fusion = bf16[1,1280,768]{2,1,0:T(8,128)(2,1)} fusion(bf16[128,1280]{1,0:T(8,128)(2,1)S(1)} %bitcast.171, f32[64,768]{1,0:T(8,128)S(1)} %get-tuple-element.57, f32[64,768]{1,0:T(8,128)S(1)} %get-tuple-element.56, f32[64,768]{1,0:T(8,128)S(1)} %get-tuple-element.55, f32[64,768]{1,0:T(8,128)S(1)} %get-tuple-element.54, f32[64,768]{1,0:T(8,128)S(1)} %get-tuple-element.53, ...), kind=kOutput, calls=%fused_computation.9 | convolution fusion | flops 253919232 | bytes 3473408 | tf_op jit(solution)/shard_map/dot_general | solution.py:188
  74.4 1.0 all-gather.3.cloned.1.call-done
  76.4 1.4 %slice.68 = bf16[8,64,1280]{2,1,0:T(8,128)(2,1)S(1)} slice(bf16[8,72,1280]{2,1,0:T(8,128)(2,1)} %bitcast.177), slice={[0:8], [0:64], [0:1280]} | slice | bytes 2621440 | tf_op jit(solution)/shard_map/slice | solution.py:160
  81.8 1.5 %collective-permute-start.10 = (bf16[2,64,96]{1,2,0:T(8,128)(2,1)S(1)}, bf16[2,64,96]{1,2,0:T(8,128)(2,1)S(1)}, u32[]{:S(2)}, u32[]{:S(2)}) collective-permute-start(bf16[2,64,96]{1,2,0:T(8,128)(2,1)S(1)} %add_convert_fusion.5), channel_id=1, source_target_pairs={{0,16},{8,24},{16,0},{24,8},{1,17},{9,25},{17,1},{25,9},{2,18},{10... | collective-permute-start | bytes 73736 | tf_op jit(solution)/shard_map/ppermute | solution.py:80
  84.2 1.6 %collective-permute-start.13 = (bf16[2,64,96]{1,2,0:T(8,128)(2,1)S(1)}, bf16[2,64,96]{1,2,0:T(8,128)(2,1)S(1)}, u32[]{:S(2)}, u32[]{:S(2)}) collective-permute-start(bf16[2,64,96]{1,2,0:T(8,128)(2,1)S(1)} %add_convert_fusion.4), channel_id=1, source_target_pairs={{0,16},{8,24},{16,0},{24,8},{1,17},{9,25},{17,1},{25,9},{2,18},{10... | collective-permute-start | bytes 73736 | tf_op jit(solution)/shard_map/ppermute | solution.py:80
  86.7 1.0 collective-permute-done.16
  90.5 0.9 fusion.23
  91.5 1.0 copy.85
  92.6 1.7 %fusion.69 = (f32[1,2,64,96]{2,3,1,0:T(8,128)}, f32[1,2,64,96]{2,3,1,0:T(8,128)}) fusion(s32[]{:T(128)S(6)} %select_n.44, f32[1,2,64,96]{2,3,1,0:T(8,128)} %get-tuple-element.73, f32[1,2,64,96]{2,3,1,0:T(8,128)} %bitcast.35, s32[]{:T(128)S(6)} %select_n.45), kind=kLoop, calls=%fused_computation.136 | loop fusion | flops 24576 | bytes 196616 | tf_op jit(solution)/shard_map/stack | solution.py:86
  94.2 1.6 %copy.83 = f32[1,2,64,96]{3,2,1,0:T(8,128)} copy(f32[1,2,64,96]{2,3,1,0:T(8,128)} %get-tuple-element.60) | data formatting | bytes 98304 | tf_op jit(solution)/shard_map/jit(dynamic_index_in_dim)/dynamic_slice | solution.py:87
  95.8 1.6 %copy.84 = f32[1,2,64,96]{3,2,1,0:T(8,128)} copy(f32[1,2,64,96]{2,3,1,0:T(8,128)} %get-tuple-element.61) | data formatting | bytes 98304 | tf_op jit(solution)/shard_map/jit(dynamic_index_in_dim)/dynamic_slice | solution.py:88
  100.0 2.2 %convert_reduce_fusion.2 = f32[2,1280,96]{1,2,0:T(8,128)} fusion(f32[2,8,16,96]{3,2,1,0:T(8,128)S(1)} %bitcast.184, f32[2,8,16,96]{3,2,1,0:T(8,128)S(1)} %bitcast.195, f32[2,8,16,96]{3,2,1,0:T(8,128)S(1)} %bitcast.187, bf16[2,2,8,16,1280]{4,3,2,1,0:T(8,128)(2,1)S(1)} %bitcast.165), kind=kOutput, calls=%fused_computation.2 | convolution fusion | flops 68812800 | bytes 2031616 | tf_op jit(solution)/shard_map/jbcd,jbch->jbdh/dot_general | solution.py:205
  102.2 1.6 %collective-permute-start.19 = (f32[8,3,16]{2,0,1:T(8,128)S(1)}, f32[8,3,16]{2,0,1:T(8,128)S(1)}, u32[]{:S(2)}, u32[]{:S(2)}) collective-permute-start(f32[8,3,16]{2,0,1:T(8,128)S(1)} %fusion.93), channel_id=1, source_target_pairs={{0,16},{8,24},{16,0},{24,8},{1,17},{9,25},{17,1},{25,9},{2,18},{10... | collective-permute-start | bytes 4616 | tf_op jit(solution)/shard_map/ppermute | solution.py:52
  103.7 2.2 %convert_reduce_fusion.1 = f32[2,1280,96]{1,2,0:T(8,128)} fusion(f32[2,8,16,96]{3,2,1,0:T(8,128)S(1)} %bitcast.196, f32[2,8,16,96]{3,2,1,0:T(8,128)S(1)} %bitcast.185, bf16[2,2,8,16,1280]{4,3,2,1,0:T(8,128)(2,1)S(1)} %bitcast.166), kind=kOutput, calls=%fused_computation.1 | convolution fusion | flops 68714496 | bytes 1900544 | tf_op jit(solution)/shard_map/jbcd,jbch->jbdh/dot_general | solution.py:206
  106.6 3.9 %all-to-all-start.1 = ((f32[8,3,16]{2,1,0:T(4,128)}), f32[8,3,16]{2,1,0:T(4,128)}, u32[]{:S(2)}, u32[]{:S(2)}) async-start(f32[8,3,16]{2,1,0:T(4,128)} %copy.88), calls=%async_computation.1 | async-start | bytes 32768 | tf_op jit(solution)/shard_map/all_to_all | solution.py:219
  110.5 2.2 %convert_reduce_fusion = f32[2,96,1280]{2,1,0:T(8,128)} fusion(f32[2,8,16]{2,1,0:T(8,128)S(1)} %copy.82, f32[2,8,16,96]{3,2,1,0:T(8,128)S(1)} %bitcast.188, f32[2,8,16,96]{3,2,1,0:T(8,128)S(1)} %bitcast.186, bf16[2,2,8,16,1280]{4,3,2,1,0:T(8,128)(2,1)S(1)} %bitcast.167), kind=kOutput, calls=%fused_computation | convolution fusion | flops 69697536 | bytes 1908736 | tf_op jit(solution)/shard_map/jbch,jbcd->jbhd/dot_general | solution.py:207
  112.7 4.4 %all-to-all-done.1 = f32[8,3,16]{2,1,0:T(4,128)} async-done(((f32[8,3,16]{2,1,0:T(4,128)}), f32[8,3,16]{2,1,0:T(4,128)}, u32[]{:S(2)}, u32[]{:S(2)}) %all-to-all-start.1) | async-done | bytes 1568 | tf_op jit(solution)/shard_map/all_to_all | solution.py:219
  117.9 1.1 convolution_reduce_fusion.1
  (165 shorter events, 32.1 us)
Async XLA Ops:
  7.2 43.0 %copy-start = (bf16[1,768,1280]{2,1,0:T(8,128)(2,1)S(1)}, bf16[1,768,1280]{2,1,0:T(8,128)(2,1)}, u32[]{:S(2)}) copy-start(bf16[1,768,1280]{2,1,0:T(8,128)(2,1)} %param.18) | copy-start | bytes 5898244
  7.2 8.8 %copy-start.1 = (bf16[256,1280]{1,0:T(8,128)(2,1)S(1)}, bf16[256,1280]{1,0:T(8,128)(2,1)}, u32[]{:S(2)}) copy-start(bf16[256,1280]{1,0:T(8,128)(2,1)} %param.12) | copy-start | bytes 1966084
  7.2 9.1 %copy-start.2 = (bf16[256,1280]{1,0:T(8,128)(2,1)S(1)}, bf16[256,1280]{1,0:T(8,128)(2,1)}, u32[]{:S(2)}) copy-start(bf16[256,1280]{1,0:T(8,128)(2,1)} %param.11) | copy-start | bytes 1966084
  14.9 2.6 %copy-start.13 = (pred[1536]{0:T(1024)(128)(4,1)}, pred[1536]{0:T(1024)(128)(4,1)S(1)}, u32[]{:S(2)}) copy-start(pred[1536]{0:T(1024)(128)(4,1)S(1)} %get-tuple-element.77) | copy-start | bytes 4612
  14.9 11.1 %copy-start.12 = (pred[1536]{0:T(1024)(128)(4,1)}, pred[1536]{0:T(1024)(128)(4,1)S(1)}, u32[]{:S(2)}) copy-start(pred[1536]{0:T(1024)(128)(4,1)S(1)} %get-tuple-element.76) | copy-start | bytes 4612
  15.1 2.4 %copy-start.9 = (s32[1536]{0:T(1024)}, s32[1536]{0:T(1024)S(1)}, u32[]{:S(2)}) copy-start(s32[1536]{0:T(1024)S(1)} %multiply_add_fusion.1) | copy-start | bytes 18436
  17.5 32.3 %all-to-all-start = ((bf16[8,40,1280]{2,1,0:T(8,128)(2,1)}), bf16[8,40,1280]{2,1,0:T(8,128)(2,1)S(1)}, u32[]{:S(2)}, u32[]{:S(2)}) async-start(bf16[8,40,1280]{2,1,0:T(8,128)(2,1)} %pad_maximum_fusion), calls=%async_computation | async-start | bytes 1638400 | tf_op jit(solution)/shard_map/all_to_all | solution.py:145
  24.8 50.6 %all-gather.3.cloned.1.call-start = ((), (), s32[]{:S(2)}) async-start(), calls=%async_computation.2 | async-start | bytes 1658880 | tf_op jit(solution)/shard_map/all_gather | solution.py:125
  51.0 3.1 %collective-permute-start = (bf16[64,768]{1,0:T(8,128)(2,1)S(1)}, bf16[64,768]{1,0:T(8,128)(2,1)S(1)}, u32[]{:S(2)}, u32[]{:S(2)}) collective-permute-start(bf16[64,768]{1,0:T(8,128)(2,1)S(1)} %constant_dynamic-slice_fusion.5), channel_id=1, source_target_pairs={{0,8},{8,0},{16,24},{24,16},{1,9},{9,1},{17,25},{25,17},{2,10},{10... | collective-permute-start | bytes 294920 | tf_op jit(solution)/shard_map/ppermute | solution.py:74
  52.2 3.8 %collective-permute-start.6 = (bf16[64,768]{1,0:T(8,128)(2,1)S(1)}, bf16[64,768]{1,0:T(8,128)(2,1)S(1)}, u32[]{:S(2)}, u32[]{:S(2)}) collective-permute-start(bf16[64,768]{1,0:T(8,128)(2,1)S(1)} %constant_dynamic-slice_fusion.3), channel_id=1, source_target_pairs={{0,8},{8,0},{16,24},{24,16},{1,9},{9,1},{17,25},{25,17},{2,10},{10... | collective-permute-start | bytes 294920 | tf_op jit(solution)/shard_map/ppermute | solution.py:74
  53.1 3.2 %collective-permute-start.3 = (bf16[64,768]{1,0:T(8,128)(2,1)S(1)}, bf16[64,768]{1,0:T(8,128)(2,1)S(1)}, u32[]{:S(2)}, u32[]{:S(2)}) collective-permute-start(bf16[64,768]{1,0:T(8,128)(2,1)S(1)} %constant_dynamic-slice_fusion.4), channel_id=1, source_target_pairs={{0,8},{8,0},{16,24},{24,16},{1,9},{9,1},{17,25},{25,17},{2,10},{10... | collective-permute-start | bytes 294920 | tf_op jit(solution)/shard_map/ppermute | solution.py:74
  54.1 9.5 %collective-permute-start.1 = (bf16[64,768]{1,0:T(8,128)(2,1)S(1)}, bf16[64,768]{1,0:T(8,128)(2,1)S(1)}, u32[]{:S(2)}, u32[]{:S(2)}) collective-permute-start(bf16[64,768]{1,0:T(8,128)(2,1)S(1)} %add_convert_fusion.2), channel_id=1, source_target_pairs={{0,16},{8,24},{16,0},{24,8},{1,17},{9,25},{17,1},{25,9},{2,18},{10... | collective-permute-start | bytes 294920 | tf_op jit(solution)/shard_map/ppermute | solution.py:80
  56.0 5.9 %collective-permute-start.7 = (bf16[64,768]{1,0:T(8,128)(2,1)S(1)}, bf16[64,768]{1,0:T(8,128)(2,1)S(1)}, u32[]{:S(2)}, u32[]{:S(2)}) collective-permute-start(bf16[64,768]{1,0:T(8,128)(2,1)S(1)} %add_convert_fusion), channel_id=1, source_target_pairs={{0,16},{8,24},{16,0},{24,8},{1,17},{9,25},{17,1},{25,9},{2,18},{10... | collective-permute-start | bytes 294920 | tf_op jit(solution)/shard_map/ppermute | solution.py:80
  56.4 7.2 %collective-permute-start.4 = (bf16[64,768]{1,0:T(8,128)(2,1)S(1)}, bf16[64,768]{1,0:T(8,128)(2,1)S(1)}, u32[]{:S(2)}, u32[]{:S(2)}) collective-permute-start(bf16[64,768]{1,0:T(8,128)(2,1)S(1)} %add_convert_fusion.1), channel_id=1, source_target_pairs={{0,16},{8,24},{16,0},{24,8},{1,17},{9,25},{17,1},{25,9},{2,18},{10... | collective-permute-start | bytes 294920 | tf_op jit(solution)/shard_map/ppermute | solution.py:80
  61.9 2.9 %collective-permute-start.8 = (f32[64,768]{1,0:T(8,128)S(1)}, f32[64,768]{1,0:T(8,128)S(1)}, u32[]{:S(2)}, u32[]{:S(2)}) collective-permute-start(f32[64,768]{1,0:T(8,128)S(1)} %get-tuple-element.68), channel_id=1, source_target_pairs={{0,8},{8,0},{16,24},{24,16},{1,9},{9,1},{17,25},{25,17},{2,10},{10... | collective-permute-start | bytes 589832 | tf_op jit(solution)/shard_map/ppermute | solution.py:83
  63.6 1.5 %collective-permute-start.5 = (f32[64,768]{1,0:T(8,128)S(1)}, f32[64,768]{1,0:T(8,128)S(1)}, u32[]{:S(2)}, u32[]{:S(2)}) collective-permute-start(f32[64,768]{1,0:T(8,128)S(1)} %get-tuple-element.66), channel_id=1, source_target_pairs={{0,8},{8,0},{16,24},{24,16},{1,9},{9,1},{17,25},{25,17},{2,10},{10... | collective-permute-start | bytes 589832 | tf_op jit(solution)/shard_map/ppermute | solution.py:83
  64.4 2.1 %collective-permute-start.2 = (f32[64,768]{1,0:T(8,128)}, f32[64,768]{1,0:T(8,128)}, u32[]{:S(2)}, u32[]{:S(2)}) collective-permute-start(f32[64,768]{1,0:T(8,128)} %get-tuple-element.64), channel_id=1, source_target_pairs={{0,8},{8,0},{16,24},{24,16},{1,9},{9,1},{17,25},{25,17},{2,10},{10... | collective-permute-start | bytes 589832 | tf_op jit(solution)/shard_map/ppermute | solution.py:83
  78.1 1.8 %copy-start.14 = (bf16[2,96,1280]{2,1,0:T(8,128)(2,1)S(1)}, bf16[2,96,1280]{2,1,0:T(8,128)(2,1)}, u32[]{:S(2)}) copy-start(bf16[2,96,1280]{2,1,0:T(8,128)(2,1)} %param.21) | copy-start | bytes 1474564
  80.4 1.3 %collective-permute-start.9 = (bf16[2,64,96]{1,2,0:T(8,128)(2,1)S(1)}, bf16[2,64,96]{1,2,0:T(8,128)(2,1)S(1)}, u32[]{:S(2)}, u32[]{:S(2)}) collective-permute-start(bf16[2,64,96]{1,2,0:T(8,128)(2,1)S(1)} %constant_dynamic-slice_fusion.2), channel_id=1, source_target_pairs={{0,8},{8,0},{16,24},{24,16},{1,9},{9,1},{17,25},{25,17},{2,10},{10... | collective-permute-start | bytes 73736 | tf_op jit(solution)/shard_map/ppermute | solution.py:74
  80.6 2.8 %collective-permute-start.15 = (bf16[2,64,96]{1,2,0:T(8,128)(2,1)S(1)}, bf16[2,64,96]{1,2,0:T(8,128)(2,1)S(1)}, u32[]{:S(2)}, u32[]{:S(2)}) collective-permute-start(bf16[2,64,96]{1,2,0:T(8,128)(2,1)S(1)} %constant_dynamic-slice_fusion), channel_id=1, source_target_pairs={{0,8},{8,0},{16,24},{24,16},{1,9},{9,1},{17,25},{25,17},{2,10},{10... | collective-permute-start | bytes 73736 | tf_op jit(solution)/shard_map/ppermute | solution.py:74
  81.2 2.9 %collective-permute-start.12 = (bf16[2,64,96]{1,2,0:T(8,128)(2,1)S(1)}, bf16[2,64,96]{1,2,0:T(8,128)(2,1)S(1)}, u32[]{:S(2)}, u32[]{:S(2)}) collective-permute-start(bf16[2,64,96]{1,2,0:T(8,128)(2,1)S(1)} %constant_dynamic-slice_fusion.1), channel_id=1, source_target_pairs={{0,8},{8,0},{16,24},{24,16},{1,9},{9,1},{17,25},{25,17},{2,10},{10... | collective-permute-start | bytes 73736 | tf_op jit(solution)/shard_map/ppermute | solution.py:74
  81.8 4.2 %collective-permute-start.10 = (bf16[2,64,96]{1,2,0:T(8,128)(2,1)S(1)}, bf16[2,64,96]{1,2,0:T(8,128)(2,1)S(1)}, u32[]{:S(2)}, u32[]{:S(2)}) collective-permute-start(bf16[2,64,96]{1,2,0:T(8,128)(2,1)S(1)} %add_convert_fusion.5), channel_id=1, source_target_pairs={{0,16},{8,24},{16,0},{24,8},{1,17},{9,25},{17,1},{25,9},{2,18},{10... | collective-permute-start | bytes 73736 | tf_op jit(solution)/shard_map/ppermute | solution.py:80
  83.5 4.2 %collective-permute-start.16 = (bf16[2,64,96]{1,2,0:T(8,128)(2,1)S(1)}, bf16[2,64,96]{1,2,0:T(8,128)(2,1)S(1)}, u32[]{:S(2)}, u32[]{:S(2)}) collective-permute-start(bf16[2,64,96]{1,2,0:T(8,128)(2,1)S(1)} %add_convert_fusion.3), channel_id=1, source_target_pairs={{0,16},{8,24},{16,0},{24,8},{1,17},{9,25},{17,1},{25,9},{2,18},{10... | collective-permute-start | bytes 73736 | tf_op jit(solution)/shard_map/ppermute | solution.py:80
  84.2 4.2 %collective-permute-start.13 = (bf16[2,64,96]{1,2,0:T(8,128)(2,1)S(1)}, bf16[2,64,96]{1,2,0:T(8,128)(2,1)S(1)}, u32[]{:S(2)}, u32[]{:S(2)}) collective-permute-start(bf16[2,64,96]{1,2,0:T(8,128)(2,1)S(1)} %add_convert_fusion.4), channel_id=1, source_target_pairs={{0,16},{8,24},{16,0},{24,8},{1,17},{9,25},{17,1},{25,9},{2,18},{10... | collective-permute-start | bytes 73736 | tf_op jit(solution)/shard_map/ppermute | solution.py:80
  86.7 5.9 %collective-permute-start.11 = (f32[2,64,96]{1,2,0:T(8,128)}, f32[2,64,96]{1,2,0:T(8,128)}, u32[]{:S(2)}, u32[]{:S(2)}) collective-permute-start(f32[2,64,96]{1,2,0:T(8,128)} %get-tuple-element.72), channel_id=1, source_target_pairs={{0,8},{8,0},{16,24},{24,16},{1,9},{9,1},{17,25},{25,17},{2,10},{10... | collective-permute-start | bytes 147464 | tf_op jit(solution)/shard_map/ppermute | solution.py:83
  87.7 1.4 %collective-permute-start.17 = (f32[2,64,96]{1,2,0:T(8,128)S(1)}, f32[2,64,96]{1,2,0:T(8,128)S(1)}, u32[]{:S(2)}, u32[]{:S(2)}) collective-permute-start(f32[2,64,96]{1,2,0:T(8,128)S(1)} %get-tuple-element.74), channel_id=1, source_target_pairs={{0,8},{8,0},{16,24},{24,16},{1,9},{9,1},{17,25},{25,17},{2,10},{10... | collective-permute-start | bytes 147464 | tf_op jit(solution)/shard_map/ppermute | solution.py:83
  88.4 1.4 %collective-permute-start.14 = (f32[2,64,96]{1,2,0:T(8,128)S(1)}, f32[2,64,96]{1,2,0:T(8,128)S(1)}, u32[]{:S(2)}, u32[]{:S(2)}) collective-permute-start(f32[2,64,96]{1,2,0:T(8,128)S(1)} %get-tuple-element.70), channel_id=1, source_target_pairs={{0,8},{8,0},{16,24},{24,16},{1,9},{9,1},{17,25},{25,17},{2,10},{10... | collective-permute-start | bytes 147464 | tf_op jit(solution)/shard_map/ppermute | solution.py:83
  98.2 4.0 %copy-start.8 = (f32[8,1,16]{2,0,1:T(8,128)S(1)}, f32[8,1,16]{2,0,1:T(8,128)}, u32[]{:S(2)}) copy-start(f32[8,1,16]{2,0,1:T(8,128)} %reshape.228) | copy-start | bytes 1540
  98.9 3.2 %collective-permute-start.18 = (f32[8,3,16]{2,0,1:T(8,128)S(1)}, f32[8,3,16]{2,0,1:T(8,128)S(1)}, u32[]{:S(2)}, u32[]{:S(2)}) collective-permute-start(f32[8,3,16]{2,0,1:T(8,128)S(1)} %pad_maximum_fusion.8), channel_id=1, source_target_pairs={{0,8},{8,0},{16,24},{24,16},{1,9},{9,1},{17,25},{25,17},{2,10},{10... | collective-permute-start | bytes 4616 | tf_op jit(solution)/shard_map/ppermute | solution.py:52
  102.2 15.7 %copy-start.10 = (s32[1536]{0:T(1024)S(1)}, s32[1536]{0:T(1024)}, u32[]{:S(2)}) copy-start(s32[1536]{0:T(1024)} %copy-done.9) | copy-start | bytes 18436
  102.2 3.8 %collective-permute-start.19 = (f32[8,3,16]{2,0,1:T(8,128)S(1)}, f32[8,3,16]{2,0,1:T(8,128)S(1)}, u32[]{:S(2)}, u32[]{:S(2)}) collective-permute-start(f32[8,3,16]{2,0,1:T(8,128)S(1)} %fusion.93), channel_id=1, source_target_pairs={{0,16},{8,24},{16,0},{24,8},{1,17},{9,25},{17,1},{25,9},{2,18},{10... | collective-permute-start | bytes 4616 | tf_op jit(solution)/shard_map/ppermute | solution.py:52
  106.6 10.5 %all-to-all-start.1 = ((f32[8,3,16]{2,1,0:T(4,128)}), f32[8,3,16]{2,1,0:T(4,128)}, u32[]{:S(2)}, u32[]{:S(2)}) async-start(f32[8,3,16]{2,1,0:T(4,128)} %copy.88), calls=%async_computation.1 | async-start | bytes 32768 | tf_op jit(solution)/shard_map/all_to_all | solution.py:219
  (6 other events, 7.3 us)
Sparse Core Ops, SparseCore 0:
  29.8 45.5 all-gather.2

commit v5 on v4

--- a/solution.py
+++ b/solution.py
@@ -4,31 +4,32 @@
 from jax.sharding import PartitionSpec as P
 
 
-def route_table(flat_ids, targets, capacity):
-    matches = (flat_ids[:, None] == targets[None, :]).astype(jnp.int32)
-    rank_of = jnp.cumsum(matches, axis=0) - 1
-    slot_of = jnp.sum(matches * rank_of, axis=1)
-    owner_of = jnp.sum(matches * jnp.arange(targets.shape[0], dtype=jnp.int32)[None, :], axis=1)
-    usable = jnp.sum(matches, axis=1) > 0
-    row_of = owner_of * capacity + slot_of
-    rows_total = targets.shape[0] * capacity
-    route_map = (row_of[None, :] == jnp.arange(rows_total, dtype=jnp.int32)[:, None]) & usable[
-        None, :
-    ]
-    return route_map.astype(jnp.float32)
-
-
-def gather_rows(route_map, tokens, cotangent, flat_weights, tok_rows, top_count):
-    per_token = jnp.sum(route_map.reshape(route_map.shape[0], tok_rows, top_count), axis=2)
-    token_map = per_token.astype(jnp.bfloat16)
+def token_table(expert_ids, targets, capacity):
+    hit = expert_ids[:, :, None] == targets[None, None, :]
+    tok_hit = jnp.any(hit, axis=1)
+    rank = jnp.cumsum(tok_hit.astype(jnp.int32), axis=0) - 1
+    slots = jnp.arange(capacity, dtype=jnp.int32)
+    sel = (rank[None, :, :] == slots[:, None, None]) & tok_hit[None, :, :]
+    return hit, sel
+
+
+def gather_rows(hit, sel, tokens, cotangent, gate_weights):
+    count, capacity = sel.shape[2], sel.shape[0]
+    token_map = jnp.transpose(sel, (2, 0, 1)).reshape(count * capacity, -1).astype(jnp.bfloat16)
     feat_rows = jnp.dot(token_map, tokens, preferred_element_type=jnp.float32).astype(jnp.bfloat16)
     cotan_rows = jnp.dot(token_map, cotangent, preferred_element_type=jnp.float32).astype(
         jnp.bfloat16
     )
-    scale_rows = jnp.dot(
-        route_map, flat_weights.astype(jnp.float32), precision=lax.Precision.HIGHEST
-    )
-    return (feat_rows, cotan_rows, scale_rows.astype(jnp.bfloat16))
+    per_token = jnp.sum(
+        jnp.where(hit, gate_weights.astype(jnp.float32)[:, :, None], 0.0), axis=1
+    )
+    scale = jnp.sum(jnp.where(sel, per_token[None, :, :], 0.0), axis=1)
+    return feat_rows, cotan_rows, jnp.transpose(scale).reshape(-1).astype(jnp.bfloat16)
+
+
+def scatter_routes(hit, sel, values):
+    per_token = jnp.sum(jnp.where(sel, jnp.transpose(values)[:, None, :], 0.0), axis=0)
+    return jnp.sum(jnp.where(hit, per_token[:, None, :], 0.0), axis=2)
 
 
 def swiglu_back(pre_gate, pre_up, grad_hidden):
@@ -106,27 +107,23 @@
     tok_rows, slice_width = tokens.shape
     top_count = expert_ids.shape[1]
     cold_count = lax.axis_size("ep")
+    blocks = lax.axis_size("ep")
     hot_count = hot_ids.shape[0]
     capacity = tok_rows // 16
-    flat_ids = expert_ids.reshape(-1)
-    flat_weights = gate_weights.reshape(-1)
-    cold_map = route_table(flat_ids, jnp.arange(cold_count, dtype=jnp.int32), capacity)
-    hot_map = route_table(flat_ids, hot_ids, capacity)
-    hot_feats, hot_cotan, hot_scale = gather_rows(
-        hot_map, tokens, cotangent, flat_weights, tok_rows, top_count
-    )
+    hot_hit, hot_sel = token_table(expert_ids, hot_ids, capacity)
+    hot_feats, hot_cotan, hot_scale = gather_rows(hot_hit, hot_sel, tokens, cotangent, gate_weights)
     hot_rows = hot_count * capacity
     scale_lines = -(-hot_rows // slice_width)
     scale_lines = -(-scale_lines // 8) * 8
     scale_block = jnp.pad(hot_scale, (0, scale_lines * slice_width - hot_rows)).reshape(
         scale_lines, slice_width
     )
-    blocks = lax.axis_size("ep")
-    gathered = lax.all_gather(
-        jnp.concatenate([hot_feats, hot_cotan, scale_block], axis=0), "ep", axis=0, tiled=False
+    hot_outgoing = jnp.concatenate([hot_feats, hot_cotan, scale_block], axis=0)
+    cold_hit, cold_sel = token_table(
+        expert_ids, jnp.arange(cold_count, dtype=jnp.int32), capacity
     )
     cold_feats, cold_cotan, cold_scale = gather_rows(
-        cold_map, tokens, cotangent, flat_weights, tok_rows, top_count
+        cold_hit, cold_sel, tokens, cotangent, gate_weights
     )
     cold_lines = -(-capacity // slice_width)
     cold_lines = -(-cold_lines // 8) * 8
@@ -142,6 +139,8 @@
         ],
         axis=1,
     )
+    hot_outgoing, outgoing = lax.optimization_barrier((hot_outgoing, outgoing))
+    gathered = lax.all_gather(hot_outgoing, "ep", axis=0, tiled=False)
     received = lax.all_to_all(outgoing, "ep", split_axis=0, concat_axis=0, tiled=True)
     recv_feats = received[:, :capacity].reshape(-1, slice_width)
     recv_cotan = received[:, capacity : 2 * capacity].reshape(-1, slice_width)
@@ -157,6 +156,24 @@
     part_hidden = lax.dot_general(
         weighted, w_down, (((1,), (1,)), ((), ())), preferred_element_type=jnp.float32
     )
+    pre_gate, pre_up, grad_hidden = grp_sum_rounded(
+        [part_gate, part_up, part_hidden], [0, 0, 0], "grp"
+    )
+    hidden, back_gate, back_up = swiglu_back(pre_gate, pre_up, grad_hidden)
+    output_slice = jnp.dot(hidden, w_down, preferred_element_type=jnp.float32)
+    cold_route = jnp.sum(output_slice * recv_cotan.astype(jnp.float32), axis=1)
+    cold_route = grp_sum_f32(cold_route.reshape(cold_count, capacity), "grp")
+    cold_back = lax.all_to_all(cold_route, "ep", split_axis=0, concat_axis=0, tiled=True)
+    contract_rows = (((0,), (0,)), ((), ()))
+    grad_gate_cold = lax.dot_general(
+        recv_feats, back_gate, contract_rows, preferred_element_type=jnp.float32
+    )
+    grad_up_cold = lax.dot_general(
+        recv_feats, back_up, contract_rows, preferred_element_type=jnp.float32
+    )
+    grad_down_cold = lax.dot_general(
+        hidden, weighted, contract_rows, preferred_element_type=jnp.float32
+    )
     all_rows = gathered[:, : 2 * hot_rows].reshape(blocks, 2, hot_count, capacity, slice_width)
     all_rows = jnp.transpose(all_rows, (1, 2, 0, 3, 4)).reshape(
         2, hot_count, blocks * capacity, slice_width
@@ -175,27 +192,22 @@
     part_hidden_hot = jnp.einsum(
         "jrd,jhd->jrh", rows_wt, down_hot, preferred_element_type=jnp.float32
     )
-    cot_down = jnp.einsum("jrd,jhd->jrh", rows_cot, down_hot, preferred_element_type=jnp.float32)
-    (pre_gate, pre_up, grad_hidden, pre_gate_hot, pre_up_hot, grad_hidden_hot) = grp_sum_rounded(
-        [part_gate, part_up, part_hidden, part_gate_hot, part_up_hot, part_hidden_hot],
-        [0, 0, 0, 1, 1, 1],
-        "grp",
-    )
-    hidden, back_gate, back_up = swiglu_back(pre_gate, pre_up, grad_hidden)
-    output_slice = jnp.dot(hidden, w_down, preferred_element_type=jnp.float32)
-    cold_route = jnp.sum(output_slice * recv_cotan.astype(jnp.float32), axis=1)
-    contract_rows = (((0,), (0,)), ((), ()))
-    grad_gate_cold = lax.dot_general(
-        recv_feats, back_gate, contract_rows, preferred_element_type=jnp.float32
-    )
-    grad_up_cold = lax.dot_general(
-        recv_feats, back_up, contract_rows, preferred_element_type=jnp.float32
-    )
-    grad_down_cold = lax.dot_general(
-        hidden, weighted, contract_rows, preferred_element_type=jnp.float32
+    part_cot_hot = jnp.einsum(
+        "jrd,jhd->jrh", rows_cot, down_hot, preferred_element_type=jnp.float32
+    )
+    pre_gate_hot, pre_up_hot, grad_hidden_hot, cot_down = grp_sum_rounded(
+        [part_gate_hot, part_up_hot, part_hidden_hot, part_cot_hot], [1, 1, 1, 1], "grp"
     )
     hidden_hot, back_gate_hot, back_up_hot = swiglu_back(pre_gate_hot, pre_up_hot, grad_hidden_hot)
     hot_route_part = jnp.sum(hidden_hot.astype(jnp.float32) * cot_down, axis=2)
+    hot_back = lax.all_to_all(
+        jnp.transpose(hot_route_part.reshape(hot_count, blocks, capacity), (1, 0, 2)),
+        "ep",
+        split_axis=0,
+        concat_axis=0,
+        tiled=True,
+    )
+    hot_route = jnp.sum(hot_back, axis=0)
     hidden_blk = hidden_hot.shape[2]
     feat_b = rows_feat.reshape(hot_count, blocks, capacity, slice_width)
     wt_b = rows_wt.reshape(hot_count, blocks, capacity, slice_width)
@@ -208,22 +220,9 @@
     grad_gate_hot = jnp.sum(blk_gate.astype(jnp.bfloat16).astype(jnp.float32), axis=1)
     grad_up_hot = jnp.sum(blk_up.astype(jnp.bfloat16).astype(jnp.float32), axis=1)
     grad_down_hot = jnp.sum(blk_down.astype(jnp.bfloat16).astype(jnp.float32), axis=1)
-    route_parts = jnp.concatenate(
-        [
-            cold_route.reshape(cold_count, 1, capacity),
-            jnp.transpose(hot_route_part.reshape(hot_count, blocks, capacity), (1, 0, 2)),
-        ],
-        axis=1,
-    )
-    route_parts = grp_sum_f32(route_parts, "grp")
-    route_back = lax.all_to_all(route_parts, "ep", split_axis=0, concat_axis=0, tiled=True)
-    cold_back = route_back[:, 0, :]
-    hot_route = jnp.sum(route_back[:, 1:, :], axis=0)
-    route_flat = jnp.dot(cold_back.reshape(-1), cold_map, precision=lax.Precision.HIGHEST)
-    route_flat = route_flat + jnp.dot(
-        hot_route.reshape(-1), hot_map, precision=lax.Precision.HIGHEST
-    )
-    gate_weight_grad = route_flat.reshape(tok_rows, top_count)
+    gate_weight_grad = scatter_routes(cold_hit, cold_sel, cold_back) + scatter_routes(
+        hot_hit, hot_sel, hot_route
+    )
     return (
         grad_gate_cold[None].astype(jnp.bfloat16),
         grad_up_cold[None].astype(jnp.bfloat16),

time: 129 us -> 145 us (1.12)
  other arithmetic: 15.2 us -> 21.5 us
  waiting for transfers between devices: 34.5 us -> 39.3 us
  starting transfers between devices: 22.6 us -> 26.8 us
  local copies, waits for them, and re-layouts: 19.2 us -> 21.8 us
  matrix products: 22.1 us -> 20 us
    all_to_all x1, waiting for transfers between devices: 20.1 us -> 24.8 us  [body(): lax.all_to_all(outgoing, 'ep', split_axis=0, concat_axis=0, tiled=True)]
    reduce_sum x5 -> x10, other arithmetic: 1.76 us -> 6.3 us  [the longest x1 1.68 us: body(): hot_route_part = jnp.sum(hidden_hot.astype(jnp.float32) * cot_down, axis=2)]
    all_to_all x1 -> x2, starting transfers between devices: 3.94 us -> 7.5 us  [the longest x1 4.11 us: body(): lax.all_to_all(jnp.transpose(hot_route_part.reshape(hot_count, blocks, ca...]
    unnamed x37 -> x31, local copies, waits for them, and re-layouts: 6.08 us -> 2.96 us
    dynamic_slice x1 -> x4, local copies, waits for them, and re-layouts: 1.6 us -> 4.62 us  [grp_sum_rounded(): second = lax.dynamic_index_in_dim(pair, 1 - core, axis=0, keepdims=False)]
    dynamic_slice x1 -> x4, local copies, waits for them, and re-layouts: 1.6 us -> 4.59 us  [grp_sum_rounded(): first = lax.dynamic_index_in_dim(pair, core, axis=0, keepdims=False)]
    add x5 -> x0, local copies, waits for them, and re-layouts: 2.61 us -> none  [the longest x4 2.01 us: route_table(): row_of = owner_of * capacity + slot_of]
    dot_general x4 -> x0, matrix products: 2.36 us -> none  [the longest x1 1.05 us: body(): jnp.dot(cold_back.reshape(-1), cold_map, precision=lax.Precision.HIGHEST)]
  transfers between devices with their start and end apart: 23 -> 27, of which waited for: 12 -> 11; matrix products, arithmetic and copies ran while one was open for 22% -> 21% of each run, Pallas kernels for 0% -> 0%
where the time goes in v5:
time: 145 us; the launch traced here: 144 us
  waiting for transfers between devices  39.3 us (27%)
  starting transfers between devices  26.8 us (18%)
  local copies, waits for them, and re-layouts  21.8 us (15%)
  other arithmetic  21.5 us (15%)
  matrix products  20 us (14%)
  between operations  14.6 us (10%)
    all_to_all x1, waiting for transfers between devices, body(): lax.all_to_all(outgoing, 'ep', split_axis=0, concat_axis=0, tiled=True)  24.8 us
    ppermute x7, waiting for transfers between devices, grp_sum_rounded(): got = lax.ppermute(mine, axis_name, partner)  8.81 us
    ppermute x7, starting transfers between devices, grp_sum_rounded(): got = lax.ppermute(mine, axis_name, partner)  8.02 us
    all_to_all x1, starting transfers between devices, body(): lax.all_to_all(outgoing, 'ep', split_axis=0, concat_axis=0, tiled=True)  7.28 us
    dynamic_slice x4, local copies, waits for them, and re-layouts, grp_sum_rounded(): second = lax.dynamic_index_in_dim(pair, 1 - core, axis=0, keepdims=False)  4.62 us
    dynamic_slice x4, local copies, waits for them, and re-layouts, grp_sum_rounded(): first = lax.dynamic_index_in_dim(pair, core, axis=0, keepdims=False)  4.59 us
    all_to_all x1, waiting for transfers between devices, body(): lax.all_to_all(cold_route, 'ep', split_axis=0, concat_axis=0, tiled=True)  4.41 us
    all_to_all x1, starting transfers between devices, body(): lax.all_to_all(jnp.transpose(hot_route_part.reshape(hot_count, blocks, ca...  4.11 us
  transfers between devices with their start and end apart: 27, of which 11 were waited for; matrix products, arithmetic and copies ran while one was open for 21% of the time, Pallas kernels for 0%

profile of v5, /device:TPU:0, one launch (start us, length us, event | category | flops | bytes accessed | tf_op | source)
XLA Modules:
  0.0 144.0 jit_solution(5027117538818606825)
XLA Ops:
  13.4 1.3 convolution_convert_fusion.8
  14.7 1.3 convolution_convert_fusion.9
  17.8 1.7 %pad.9 = bf16[8,10240]{0,1:T(8,128)(2,1)} pad(bf16[8,16]{0,1:T(8,128)(2,1)S(1)} %bitcast.222, bf16[]{:T(256)} %constant.72.clone.1), padding=0_0x0_10224 | pad | bytes 164098 | tf_op jit(solution)/shard_map/jit(_pad)/pad | solution.py:130
  19.5 2.2 %copy.131 = bf16[8,8,1280]{2,1,0:T(8,128)(2,1)S(1)} copy(bf16[8,8,1280]{0,2,1:T(8,128)(2,1)} %bitcast.173) | data formatting | bytes 327680 | tf_op jit(solution)/shard_map/reshape | solution.py:133
  23.3 7.3 %all-to-all-start = ((bf16[8,40,1280]{2,1,0:T(8,128)(2,1)}), bf16[8,40,1280]{2,1,0:T(8,128)(2,1)S(1)}, u32[]{:S(2)}, u32[]{:S(2)}) async-start(bf16[8,40,1280]{2,1,0:T(8,128)(2,1)} %pad_maximum_fusion), calls=%async_computation | async-start | bytes 1638400 | tf_op jit(solution)/shard_map/all_to_all | solution.py:144
  31.3 24.8 %all-to-all-done = bf16[8,40,1280]{2,1,0:T(8,128)(2,1)S(1)} async-done(((bf16[8,40,1280]{2,1,0:T(8,128)(2,1)}), bf16[8,40,1280]{2,1,0:T(8,128)(2,1)S(1)}, u32[]{:S(2)}, u32[]{:S(2)}) %all-to-all-start) | async-done | bytes 819232 | tf_op jit(solution)/shard_map/all_to_all | solution.py:144
  60.4 1.6 %collective-permute-start.1 = (bf16[64,768]{1,0:T(8,128)(2,1)S(1)}, bf16[64,768]{1,0:T(8,128)(2,1)S(1)}, u32[]{:S(2)}, u32[]{:S(2)}) collective-permute-start(bf16[64,768]{1,0:T(8,128)(2,1)S(1)} %add_convert_fusion.2), channel_id=1, source_target_pairs={{0,16},{8,24},{16,0},{24,8},{1,17},{9,25},{17,1},{25,9},{2,18},{10... | collective-permute-start | bytes 294920 | tf_op jit(solution)/shard_map/ppermute | solution.py:81
  62.6 1.6 %collective-permute-start.4 = (bf16[64,768]{1,0:T(8,128)(2,1)S(1)}, bf16[64,768]{1,0:T(8,128)(2,1)S(1)}, u32[]{:S(2)}, u32[]{:S(2)}) collective-permute-start(bf16[64,768]{1,0:T(8,128)(2,1)S(1)} %add_convert_fusion.1), channel_id=1, source_target_pairs={{0,16},{8,24},{16,0},{24,8},{1,17},{9,25},{17,1},{25,9},{2,18},{10... | collective-permute-start | bytes 294920 | tf_op jit(solution)/shard_map/ppermute | solution.py:81
  64.2 4.0 %collective-permute-done.7 = bf16[64,768]{1,0:T(8,128)(2,1)S(1)} collective-permute-done((bf16[64,768]{1,0:T(8,128)(2,1)S(1)}, bf16[64,768]{1,0:T(8,128)(2,1)S(1)}, u32[]{:S(2)}, u32[]{:S(2)}) %collective-permute-start.7) | collective-permute-done | bytes 98336 | tf_op jit(solution)/shard_map/ppermute | solution.py:81
  68.3 1.5 %collective-permute-done.4 = bf16[64,768]{1,0:T(8,128)(2,1)S(1)} collective-permute-done((bf16[64,768]{1,0:T(8,128)(2,1)S(1)}, bf16[64,768]{1,0:T(8,128)(2,1)S(1)}, u32[]{:S(2)}, u32[]{:S(2)}) %collective-permute-start.4) | collective-permute-done | bytes 98336 | tf_op jit(solution)/shard_map/ppermute | solution.py:81
  73.5 2.0 %fusion = bf16[1,1280,768]{2,1,0:T(8,128)(2,1)} fusion(bf16[128,1280]{1,0:T(8,128)(2,1)S(1)} %bitcast.180, f32[64,768]{1,0:T(8,128)S(1)} %get-tuple-element.20, f32[64,768]{1,0:T(8,128)S(1)} %get-tuple-element.19, f32[64,768]{1,0:T(8,128)S(1)} %get-tuple-element.18, f32[64,768]{1,0:T(8,128)S(1)} %get-tuple-element.17, f32[64,768]{1,0:T(8,128)S(1)} %get-tuple-element.16, ...), kind=kOutput, calls=%fused_computation.9 | convolution fusion | flops 253919232 | bytes 3473408 | tf_op jit(solution)/shard_map/dot_general | solution.py:168
  75.6 1.6 %collective-permute-start.19 = (f32[8,16]{1,0:T(8,128)S(1)}, f32[8,16]{1,0:T(8,128)S(1)}, u32[]{:S(2)}, u32[]{:S(2)}) collective-permute-start(f32[8,16]{1,0:T(8,128)S(1)} %add.148), channel_id=1, source_target_pairs={{0,16},{8,24},{16,0},{24,8},{1,17},{9,25},{17,1},{25,9},{2,18},{10... | collective-permute-start | bytes 1544 | tf_op jit(solution)/shard_map/ppermute | solution.py:53
  77.1 2.0 %fusion.1 = bf16[1,1280,768]{2,1,0:T(8,128)(2,1)} fusion(bf16[128,1280]{1,0:T(8,128)(2,1)S(1)} %bitcast.181, f32[64,768]{1,0:T(8,128)S(1)} %get-tuple-element.16, f32[64,768]{1,0:T(8,128)S(1)} %get-tuple-element.15, f32[64,768]{1,0:T(8,128)S(1)} %get-tuple-element.20, f32[64,768]{1,0:T(8,128)S(1)} %get-tuple-element.19), kind=kOutput, calls=%fused_computation.10 | convolution fusion | flops 253427712 | bytes 3080192 | tf_op jit(solution)/shard_map/dot_general | solution.py:171
  79.8 3.4 %all-to-all-start.1 = ((f32[8,1,16]{2,1,0:T(1,128)}), f32[8,1,16]{2,1,0:T(1,128)S(1)}, u32[]{:S(2)}, u32[]{:S(2)}) async-start(f32[8,1,16]{2,1,0:T(1,128)} %bitcast.60), calls=%async_computation.1 | async-start | bytes 8192 | tf_op jit(solution)/shard_map/all_to_all | solution.py:166
  83.2 2.0 %fusion.2 = bf16[1,768,1280]{2,1,0:T(8,128)(2,1)} fusion(bf16[128,768]{1,0:T(8,128)(2,1)S(1)} %multiply_convert_fusion.3, bf16[128,1280]{1,0:T(8,128)(2,1)S(1)} %copy-done.5), kind=kOutput, calls=%fused_computation.11 | convolution fusion | flops 252641280 | bytes 2490368 | tf_op jit(solution)/shard_map/dot_general | solution.py:174
  85.2 4.4 %all-to-all-done.1 = f32[8,1,16]{2,1,0:T(1,128)S(1)} async-done(((f32[8,1,16]{2,1,0:T(1,128)}), f32[8,1,16]{2,1,0:T(1,128)S(1)}, u32[]{:S(2)}, u32[]{:S(2)}) %all-to-all-start.1) | async-done | bytes 544 | tf_op jit(solution)/shard_map/all_to_all | solution.py:166
  91.4 1.4 slice.60
  97.3 1.6 %collective-permute-start.10 = (bf16[2,64,96]{1,2,0:T(8,128)(2,1)S(1)}, bf16[2,64,96]{1,2,0:T(8,128)(2,1)S(1)}, u32[]{:S(2)}, u32[]{:S(2)}) collective-permute-start(bf16[2,64,96]{1,2,0:T(8,128)(2,1)S(1)} %add_convert_fusion.6), channel_id=1, source_target_pairs={{0,16},{8,24},{16,0},{24,8},{1,17},{9,25},{17,1},{25,9},{2,18},{10... | collective-permute-start | bytes 73736 | tf_op jit(solution)/shard_map/ppermute | solution.py:81
  99.6 1.6 %collective-permute-start.16 = (bf16[2,64,96]{1,2,0:T(8,128)(2,1)S(1)}, bf16[2,64,96]{1,2,0:T(8,128)(2,1)S(1)}, u32[]{:S(2)}, u32[]{:S(2)}) collective-permute-start(bf16[2,64,96]{1,2,0:T(8,128)(2,1)S(1)} %add_convert_fusion.4), channel_id=1, source_target_pairs={{0,16},{8,24},{16,0},{24,8},{1,17},{9,25},{17,1},{25,9},{2,18},{10... | collective-permute-start | bytes 73736 | tf_op jit(solution)/shard_map/ppermute | solution.py:81
  102.0 1.1 collective-permute-done.21
  109.0 1.6 %copy.143 = f32[1,2,64,96]{3,2,1,0:T(8,128)} copy(f32[1,2,64,96]{2,3,1,0:T(8,128)} %get-tuple-element.21) | data formatting | bytes 98304 | tf_op jit(solution)/shard_map/jit(dynamic_index_in_dim)/dynamic_slice | solution.py:88
  110.6 1.6 %copy.144 = f32[1,2,64,96]{3,2,1,0:T(8,128)} copy(f32[1,2,64,96]{2,3,1,0:T(8,128)} %get-tuple-element.22) | data formatting | bytes 98304 | tf_op jit(solution)/shard_map/jit(dynamic_index_in_dim)/dynamic_slice | solution.py:89
  112.2 1.6 %copy.138 = f32[1,2,64,96]{3,2,1,0:T(8,128)} copy(f32[1,2,64,96]{2,3,1,0:T(8,128)} %get-tuple-element.27) | data formatting | bytes 98304 | tf_op jit(solution)/shard_map/jit(dynamic_index_in_dim)/dynamic_slice | solution.py:88
  113.8 1.6 %copy.139 = f32[1,2,64,96]{3,2,1,0:T(8,128)} copy(f32[1,2,64,96]{2,3,1,0:T(8,128)} %get-tuple-element.28) | data formatting | bytes 98304 | tf_op jit(solution)/shard_map/jit(dynamic_index_in_dim)/dynamic_slice | solution.py:89
  117.8 1.7 %fusion.44 = (f32[2,128]{1,0:T(2,128)}, f32[2,128,96]{2,1,0:T(8,128)S(1)}, f32[2,128,96]{2,1,0:T(8,128)S(1)}) fusion(f32[2,64,96]{2,1,0:T(8,128)} %bitcast.199, f32[2,64,96]{2,1,0:T(8,128)} %bitcast.198, f32[2,64,96]{2,1,0:T(8,128)} %bitcast.201, f32[2,64,96]{2,1,0:T(8,128)} %bitcast.200, f32[2,64,96]{2,1,0:T(8,128)} %bitcast.203, f32[2,64,96]{2,1,0:T(8,128)} %bitcast.202), kind=kLoop, calls=%fused_computation.108 | loop fusion | flops 294656 | bytes 492544 | tf_op jit(solution)/shard_map/reduce_sum | solution.py:202
  119.5 1.3 reshape.173
  120.8 1.3 copy.145
  122.1 4.1 %all-to-all-start.2 = ((f32[8,2,16]{2,1,0:T(2,128)}), f32[8,2,16]{2,1,0:T(2,128)}, u32[]{:S(2)}, u32[]{:S(2)}) async-start(f32[8,2,16]{2,1,0:T(2,128)} %copy.145), calls=%async_computation.2 | async-start | bytes 16384 | tf_op jit(solution)/shard_map/all_to_all | solution.py:203
  127.1 2.2 %convert_reduce_fusion.1 = f32[2,1280,96]{1,2,0:T(8,128)} fusion(f32[2,8,16,96]{3,2,1,0:T(8,128)S(1)} %bitcast.210, f32[2,8,16,96]{3,2,1,0:T(8,128)S(1)} %bitcast.195, bf16[2,2,8,16,1280]{4,3,2,1,0:T(8,128)(2,1)S(1)} %bitcast.175), kind=kOutput, calls=%fused_computation.1 | convolution fusion | flops 68714496 | bytes 1900544 | tf_op jit(solution)/shard_map/jbcd,jbch->jbdh/dot_general | solution.py:218
  129.3 2.2 %convert_reduce_fusion.2 = f32[2,1280,96]{1,2,0:T(8,128)} fusion(f32[2,8,16,96]{3,2,1,0:T(8,128)S(1)} %bitcast.196, f32[2,8,16,96]{3,2,1,0:T(8,128)S(1)} %bitcast.211, f32[2,8,16,96]{3,2,1,0:T(8,128)S(1)} %bitcast.193, bf16[2,2,8,16,1280]{4,3,2,1,0:T(8,128)(2,1)S(1)} %bitcast.176), kind=kOutput, calls=%fused_computation.2 | convolution fusion | flops 68812800 | bytes 2031616 | tf_op jit(solution)/shard_map/jbcd,jbch->jbdh/dot_general | solution.py:217
  131.5 2.2 %convert_reduce_fusion = f32[2,96,1280]{2,1,0:T(8,128)} fusion(f32[2,8,16]{2,1,0:T(8,128)S(1)} %copy.133, f32[2,8,16,96]{3,2,1,0:T(8,128)S(1)} %bitcast.194, f32[2,8,16,96]{3,2,1,0:T(8,128)S(1)} %bitcast.197, bf16[2,2,8,16,1280]{4,3,2,1,0:T(8,128)(2,1)S(1)} %bitcast.177), kind=kOutput, calls=%fused_computation | convolution fusion | flops 69697536 | bytes 1908736 | tf_op jit(solution)/shard_map/jbch,jbcd->jbhd/dot_general | solution.py:219
  135.9 1.3 add.153
  (167 shorter events, 38.6 us)
Async XLA Ops:
  7.2 49.2 %copy-start = (bf16[1,768,1280]{2,1,0:T(8,128)(2,1)S(1)}, bf16[1,768,1280]{2,1,0:T(8,128)(2,1)}, u32[]{:S(2)}) copy-start(bf16[1,768,1280]{2,1,0:T(8,128)(2,1)} %param.18) | copy-start | bytes 5898244
  7.2 9.0 %copy-start.1 = (bf16[256,1280]{1,0:T(8,128)(2,1)S(1)}, bf16[256,1280]{1,0:T(8,128)(2,1)}, u32[]{:S(2)}) copy-start(bf16[256,1280]{1,0:T(8,128)(2,1)} %param.12) | copy-start | bytes 1966084
  7.2 9.9 %copy-start.2 = (bf16[256,1280]{1,0:T(8,128)(2,1)S(1)}, bf16[256,1280]{1,0:T(8,128)(2,1)}, u32[]{:S(2)}) copy-start(bf16[256,1280]{1,0:T(8,128)(2,1)} %param.11) | copy-start | bytes 1966084
  8.9 10.6 %copy-start.12 = (pred[256,2]{0,1:T(4,128)(4,1)}, pred[256,2]{0,1:T(4,128)(4,1)S(1)}, u32[]{:S(2)}) copy-start(pred[256,2]{0,1:T(4,128)(4,1)S(1)} %compare_reduce_fusion) | copy-start | bytes 1540
  23.3 32.8 %all-to-all-start = ((bf16[8,40,1280]{2,1,0:T(8,128)(2,1)}), bf16[8,40,1280]{2,1,0:T(8,128)(2,1)S(1)}, u32[]{:S(2)}, u32[]{:S(2)}) async-start(bf16[8,40,1280]{2,1,0:T(8,128)(2,1)} %pad_maximum_fusion), calls=%async_computation | async-start | bytes 1638400 | tf_op jit(solution)/shard_map/all_to_all | solution.py:144
  30.6 59.8 %all-gather.3.cloned.1.call-start = ((), (), s32[]{:S(2)}) async-start(), calls=%async_computation.3 | async-start | bytes 1658880 | tf_op jit(solution)/shard_map/all_gather | solution.py:143
  57.2 3.1 %collective-permute-start = (bf16[64,768]{1,0:T(8,128)(2,1)S(1)}, bf16[64,768]{1,0:T(8,128)(2,1)S(1)}, u32[]{:S(2)}, u32[]{:S(2)}) collective-permute-start(bf16[64,768]{1,0:T(8,128)(2,1)S(1)} %constant_dynamic-slice_fusion.6), channel_id=1, source_target_pairs={{0,8},{8,0},{16,24},{24,16},{1,9},{9,1},{17,25},{25,17},{2,10},{10... | collective-permute-start | bytes 294920 | tf_op jit(solution)/shard_map/ppermute | solution.py:75
  58.4 3.5 %collective-permute-start.6 = (bf16[64,768]{1,0:T(8,128)(2,1)S(1)}, bf16[64,768]{1,0:T(8,128)(2,1)S(1)}, u32[]{:S(2)}, u32[]{:S(2)}) collective-permute-start(bf16[64,768]{1,0:T(8,128)(2,1)S(1)} %constant_dynamic-slice_fusion.4), channel_id=1, source_target_pairs={{0,8},{8,0},{16,24},{24,16},{1,9},{9,1},{17,25},{25,17},{2,10},{10... | collective-permute-start | bytes 294920 | tf_op jit(solution)/shard_map/ppermute | solution.py:75
  59.4 3.2 %collective-permute-start.3 = (bf16[64,768]{1,0:T(8,128)(2,1)S(1)}, bf16[64,768]{1,0:T(8,128)(2,1)S(1)}, u32[]{:S(2)}, u32[]{:S(2)}) collective-permute-start(bf16[64,768]{1,0:T(8,128)(2,1)S(1)} %constant_dynamic-slice_fusion.5), channel_id=1, source_target_pairs={{0,8},{8,0},{16,24},{24,16},{1,9},{9,1},{17,25},{25,17},{2,10},{10... | collective-permute-start | bytes 294920 | tf_op jit(solution)/shard_map/ppermute | solution.py:75
  60.4 9.5 %collective-permute-start.1 = (bf16[64,768]{1,0:T(8,128)(2,1)S(1)}, bf16[64,768]{1,0:T(8,128)(2,1)S(1)}, u32[]{:S(2)}, u32[]{:S(2)}) collective-permute-start(bf16[64,768]{1,0:T(8,128)(2,1)S(1)} %add_convert_fusion.2), channel_id=1, source_target_pairs={{0,16},{8,24},{16,0},{24,8},{1,17},{9,25},{17,1},{25,9},{2,18},{10... | collective-permute-start | bytes 294920 | tf_op jit(solution)/shard_map/ppermute | solution.py:81
  62.0 6.2 %collective-permute-start.7 = (bf16[64,768]{1,0:T(8,128)(2,1)S(1)}, bf16[64,768]{1,0:T(8,128)(2,1)S(1)}, u32[]{:S(2)}, u32[]{:S(2)}) collective-permute-start(bf16[64,768]{1,0:T(8,128)(2,1)S(1)} %add_convert_fusion), channel_id=1, source_target_pairs={{0,16},{8,24},{16,0},{24,8},{1,17},{9,25},{17,1},{25,9},{2,18},{10... | collective-permute-start | bytes 294920 | tf_op jit(solution)/shard_map/ppermute | solution.py:81
  62.6 7.2 %collective-permute-start.4 = (bf16[64,768]{1,0:T(8,128)(2,1)S(1)}, bf16[64,768]{1,0:T(8,128)(2,1)S(1)}, u32[]{:S(2)}, u32[]{:S(2)}) collective-permute-start(bf16[64,768]{1,0:T(8,128)(2,1)S(1)} %add_convert_fusion.1), channel_id=1, source_target_pairs={{0,16},{8,24},{16,0},{24,8},{1,17},{9,25},{17,1},{25,9},{2,18},{10... | collective-permute-start | bytes 294920 | tf_op jit(solution)/shard_map/ppermute | solution.py:81
  68.2 2.9 %collective-permute-start.8 = (f32[64,768]{1,0:T(8,128)S(1)}, f32[64,768]{1,0:T(8,128)S(1)}, u32[]{:S(2)}, u32[]{:S(2)}) collective-permute-start(f32[64,768]{1,0:T(8,128)S(1)} %get-tuple-element.33), channel_id=1, source_target_pairs={{0,8},{8,0},{16,24},{24,16},{1,9},{9,1},{17,25},{25,17},{2,10},{10... | collective-permute-start | bytes 589832 | tf_op jit(solution)/shard_map/ppermute | solution.py:84
  69.9 1.5 %collective-permute-start.5 = (f32[64,768]{1,0:T(8,128)S(1)}, f32[64,768]{1,0:T(8,128)S(1)}, u32[]{:S(2)}, u32[]{:S(2)}) collective-permute-start(f32[64,768]{1,0:T(8,128)S(1)} %get-tuple-element.31), channel_id=1, source_target_pairs={{0,8},{8,0},{16,24},{24,16},{1,9},{9,1},{17,25},{25,17},{2,10},{10... | collective-permute-start | bytes 589832 | tf_op jit(solution)/shard_map/ppermute | solution.py:84
  70.7 1.9 %collective-permute-start.2 = (f32[64,768]{1,0:T(8,128)}, f32[64,768]{1,0:T(8,128)}, u32[]{:S(2)}, u32[]{:S(2)}) collective-permute-start(f32[64,768]{1,0:T(8,128)} %get-tuple-element.29), channel_id=1, source_target_pairs={{0,8},{8,0},{16,24},{24,16},{1,9},{9,1},{17,25},{25,17},{2,10},{10... | collective-permute-start | bytes 589832 | tf_op jit(solution)/shard_map/ppermute | solution.py:84
  72.2 3.4 %collective-permute-start.18 = (f32[8,16]{1,0:T(8,128)S(1)}, f32[8,16]{1,0:T(8,128)S(1)}, u32[]{:S(2)}, u32[]{:S(2)}) collective-permute-start(f32[8,16]{1,0:T(8,128)S(1)} %reshape.172), channel_id=1, source_target_pairs={{0,8},{8,0},{16,24},{24,16},{1,9},{9,1},{17,25},{25,17},{2,10},{10... | collective-permute-start | bytes 1544 | tf_op jit(solution)/shard_map/ppermute | solution.py:53
  75.6 3.7 %collective-permute-start.19 = (f32[8,16]{1,0:T(8,128)S(1)}, f32[8,16]{1,0:T(8,128)S(1)}, u32[]{:S(2)}, u32[]{:S(2)}) collective-permute-start(f32[8,16]{1,0:T(8,128)S(1)} %add.148), channel_id=1, source_target_pairs={{0,16},{8,24},{16,0},{24,8},{1,17},{9,25},{17,1},{25,9},{2,18},{10... | collective-permute-start | bytes 1544 | tf_op jit(solution)/shard_map/ppermute | solution.py:53
  79.1 10.7 %copy-start.10 = (s32[256,6]{0,1:T(8,128)S(1)}, s32[256,6]{0,1:T(8,128)}, u32[]{:S(2)}) copy-start(s32[256,6]{0,1:T(8,128)} %param.14) | copy-start | bytes 18436
  79.8 9.8 %all-to-all-start.1 = ((f32[8,1,16]{2,1,0:T(1,128)}), f32[8,1,16]{2,1,0:T(1,128)S(1)}, u32[]{:S(2)}, u32[]{:S(2)}) async-start(f32[8,1,16]{2,1,0:T(1,128)} %bitcast.60), calls=%async_computation.1 | async-start | bytes 8192 | tf_op jit(solution)/shard_map/all_to_all | solution.py:166
  95.9 1.3 collective-permute-start.9
  96.0 2.8 %collective-permute-start.20 = (bf16[2,64,96]{1,2,0:T(8,128)(2,1)S(1)}, bf16[2,64,96]{1,2,0:T(8,128)(2,1)S(1)}, u32[]{:S(2)}, u32[]{:S(2)}) collective-permute-start(bf16[2,64,96]{1,2,0:T(8,128)(2,1)S(1)} %constant_dynamic-slice_fusion), channel_id=1, source_target_pairs={{0,8},{8,0},{16,24},{24,16},{1,9},{9,1},{17,25},{25,17},{2,10},{10... | collective-permute-start | bytes 73736 | tf_op jit(solution)/shard_map/ppermute | solution.py:75
  96.6 2.9 %collective-permute-start.15 = (bf16[2,64,96]{1,2,0:T(8,128)(2,1)S(1)}, bf16[2,64,96]{1,2,0:T(8,128)(2,1)S(1)}, u32[]{:S(2)}, u32[]{:S(2)}) collective-permute-start(bf16[2,64,96]{1,2,0:T(8,128)(2,1)S(1)} %constant_dynamic-slice_fusion.1), channel_id=1, source_target_pairs={{0,8},{8,0},{16,24},{24,16},{1,9},{9,1},{17,25},{25,17},{2,10},{10... | collective-permute-start | bytes 73736 | tf_op jit(solution)/shard_map/ppermute | solution.py:75
  96.7 4.5 %collective-permute-start.12 = (bf16[2,64,96]{1,2,0:T(8,128)(2,1)S(1)}, bf16[2,64,96]{1,2,0:T(8,128)(2,1)S(1)}, u32[]{:S(2)}, u32[]{:S(2)}) collective-permute-start(bf16[2,64,96]{1,2,0:T(8,128)(2,1)S(1)} %constant_dynamic-slice_fusion.2), channel_id=1, source_target_pairs={{0,8},{8,0},{16,24},{24,16},{1,9},{9,1},{17,25},{25,17},{2,10},{10... | collective-permute-start | bytes 73736 | tf_op jit(solution)/shard_map/ppermute | solution.py:75
  97.3 4.6 %collective-permute-start.10 = (bf16[2,64,96]{1,2,0:T(8,128)(2,1)S(1)}, bf16[2,64,96]{1,2,0:T(8,128)(2,1)S(1)}, u32[]{:S(2)}, u32[]{:S(2)}) collective-permute-start(bf16[2,64,96]{1,2,0:T(8,128)(2,1)S(1)} %add_convert_fusion.6), channel_id=1, source_target_pairs={{0,16},{8,24},{16,0},{24,8},{1,17},{9,25},{17,1},{25,9},{2,18},{10... | collective-permute-start | bytes 73736 | tf_op jit(solution)/shard_map/ppermute | solution.py:81
  98.9 4.2 %collective-permute-start.21 = (bf16[2,64,96]{1,2,0:T(8,128)(2,1)S(1)}, bf16[2,64,96]{1,2,0:T(8,128)(2,1)S(1)}, u32[]{:S(2)}, u32[]{:S(2)}) collective-permute-start(bf16[2,64,96]{1,2,0:T(8,128)(2,1)S(1)} %add_convert_fusion.3), channel_id=1, source_target_pairs={{0,16},{8,24},{16,0},{24,8},{1,17},{9,25},{17,1},{25,9},{2,18},{10... | collective-permute-start | bytes 73736 | tf_op jit(solution)/shard_map/ppermute | solution.py:81
  99.6 4.7 %collective-permute-start.16 = (bf16[2,64,96]{1,2,0:T(8,128)(2,1)S(1)}, bf16[2,64,96]{1,2,0:T(8,128)(2,1)S(1)}, u32[]{:S(2)}, u32[]{:S(2)}) collective-permute-start(bf16[2,64,96]{1,2,0:T(8,128)(2,1)S(1)} %add_convert_fusion.4), channel_id=1, source_target_pairs={{0,16},{8,24},{16,0},{24,8},{1,17},{9,25},{17,1},{25,9},{2,18},{10... | collective-permute-start | bytes 73736 | tf_op jit(solution)/shard_map/ppermute | solution.py:81
  101.3 4.2 %collective-permute-start.13 = (bf16[2,64,96]{1,2,0:T(8,128)(2,1)S(1)}, bf16[2,64,96]{1,2,0:T(8,128)(2,1)S(1)}, u32[]{:S(2)}, u32[]{:S(2)}) collective-permute-start(bf16[2,64,96]{1,2,0:T(8,128)(2,1)S(1)} %add_convert_fusion.5), channel_id=1, source_target_pairs={{0,16},{8,24},{16,0},{24,8},{1,17},{9,25},{17,1},{25,9},{2,18},{10... | collective-permute-start | bytes 73736 | tf_op jit(solution)/shard_map/ppermute | solution.py:81
  101.9 4.3 %collective-permute-start.11 = (f32[2,64,96]{1,2,0:T(8,128)S(1)}, f32[2,64,96]{1,2,0:T(8,128)S(1)}, u32[]{:S(2)}, u32[]{:S(2)}) collective-permute-start(f32[2,64,96]{1,2,0:T(8,128)S(1)} %get-tuple-element.42), channel_id=1, source_target_pairs={{0,8},{8,0},{16,24},{24,16},{1,9},{9,1},{17,25},{25,17},{2,10},{10... | collective-permute-start | bytes 147464 | tf_op jit(solution)/shard_map/ppermute | solution.py:84
  103.1 3.1 %collective-permute-start.22 = (f32[2,64,96]{1,2,0:T(8,128)S(1)}, f32[2,64,96]{1,2,0:T(8,128)S(1)}, u32[]{:S(2)}, u32[]{:S(2)}) collective-permute-start(f32[2,64,96]{1,2,0:T(8,128)S(1)} %get-tuple-element.38), channel_id=1, source_target_pairs={{0,8},{8,0},{16,24},{24,16},{1,9},{9,1},{17,25},{25,17},{2,10},{10... | collective-permute-start | bytes 147464 | tf_op jit(solution)/shard_map/ppermute | solution.py:84
  104.3 2.6 %collective-permute-start.17 = (f32[2,64,96]{1,2,0:T(8,128)S(1)}, f32[2,64,96]{1,2,0:T(8,128)S(1)}, u32[]{:S(2)}, u32[]{:S(2)}) collective-permute-start(f32[2,64,96]{1,2,0:T(8,128)S(1)} %get-tuple-element.44), channel_id=1, source_target_pairs={{0,8},{8,0},{16,24},{24,16},{1,9},{9,1},{17,25},{25,17},{2,10},{10... | collective-permute-start | bytes 147464 | tf_op jit(solution)/shard_map/ppermute | solution.py:84
  106.1 9.3 %collective-permute-start.14 = (f32[2,64,96]{1,2,0:T(8,128)}, f32[2,64,96]{1,2,0:T(8,128)}, u32[]{:S(2)}, u32[]{:S(2)}) collective-permute-start(f32[2,64,96]{1,2,0:T(8,128)} %get-tuple-element.40), channel_id=1, source_target_pairs={{0,8},{8,0},{16,24},{24,16},{1,9},{9,1},{17,25},{25,17},{2,10},{10... | collective-permute-start | bytes 147464 | tf_op jit(solution)/shard_map/ppermute | solution.py:84
  122.1 11.5 %all-to-all-start.2 = ((f32[8,2,16]{2,1,0:T(2,128)}), f32[8,2,16]{2,1,0:T(2,128)}, u32[]{:S(2)}, u32[]{:S(2)}) async-start(f32[8,2,16]{2,1,0:T(2,128)} %copy.145), calls=%async_computation.2 | async-start | bytes 16384 | tf_op jit(solution)/shard_map/all_to_all | solution.py:203
  (8 other events, 25.9 us)
Sparse Core Ops, SparseCore 0:
  34.2 46.5 all-gather.2

commit v6 on v5

--- a/solution.py
+++ b/solution.py
@@ -5,31 +5,40 @@
 
 
 def token_table(expert_ids, targets, capacity):
-    hit = expert_ids[:, :, None] == targets[None, None, :]
-    tok_hit = jnp.any(hit, axis=1)
-    rank = jnp.cumsum(tok_hit.astype(jnp.int32), axis=0) - 1
+    hit = expert_ids.T[:, None, :] == targets[None, :, None]
+    tok_hit = jnp.any(hit, axis=0)
+    rank = jnp.cumsum(tok_hit.astype(jnp.int32), axis=1) - 1
     slots = jnp.arange(capacity, dtype=jnp.int32)
-    sel = (rank[None, :, :] == slots[:, None, None]) & tok_hit[None, :, :]
+    sel = (rank[:, None, :] == slots[None, :, None]) & tok_hit[:, None, :]
     return hit, sel
 
 
 def gather_rows(hit, sel, tokens, cotangent, gate_weights):
-    count, capacity = sel.shape[2], sel.shape[0]
-    token_map = jnp.transpose(sel, (2, 0, 1)).reshape(count * capacity, -1).astype(jnp.bfloat16)
+    count, capacity = sel.shape[0], sel.shape[1]
+    token_map = sel.reshape(count * capacity, -1).astype(jnp.bfloat16)
     feat_rows = jnp.dot(token_map, tokens, preferred_element_type=jnp.float32).astype(jnp.bfloat16)
     cotan_rows = jnp.dot(token_map, cotangent, preferred_element_type=jnp.float32).astype(
         jnp.bfloat16
     )
     per_token = jnp.sum(
-        jnp.where(hit, gate_weights.astype(jnp.float32)[:, :, None], 0.0), axis=1
-    )
-    scale = jnp.sum(jnp.where(sel, per_token[None, :, :], 0.0), axis=1)
-    return feat_rows, cotan_rows, jnp.transpose(scale).reshape(-1).astype(jnp.bfloat16)
+        jnp.where(hit, gate_weights.T.astype(jnp.float32)[:, None, :], 0.0), axis=0
+    )
+    scale = jnp.sum(jnp.where(sel, per_token[:, None, :], 0.0), axis=2)
+    return feat_rows, cotan_rows, scale.reshape(-1).astype(jnp.bfloat16)
 
 
 def scatter_routes(hit, sel, values):
-    per_token = jnp.sum(jnp.where(sel, jnp.transpose(values)[:, None, :], 0.0), axis=0)
-    return jnp.sum(jnp.where(hit, per_token[:, None, :], 0.0), axis=2)
+    per_token = jnp.sum(jnp.where(sel, values[:, :, None], 0.0), axis=1)
+    return jnp.sum(jnp.where(hit, per_token[None, :, :], 0.0), axis=1).T
+
+
+def shift_exchange(chunks, axis_name, sign):
+    size = lax.axis_size(axis_name)
+    moved = [chunks[0]]
+    for k in range(1, size):
+        perm = [(i, (i + sign * k) % size) for i in range(size)]
+        moved.append(lax.ppermute(chunks[k], axis_name, perm))
+    return jnp.stack(moved)
 
 
 def swiglu_back(pre_gate, pre_up, grad_hidden):
@@ -119,9 +128,8 @@
         scale_lines, slice_width
     )
     hot_outgoing = jnp.concatenate([hot_feats, hot_cotan, scale_block], axis=0)
-    cold_hit, cold_sel = token_table(
-        expert_ids, jnp.arange(cold_count, dtype=jnp.int32), capacity
-    )
+    cold_targets = (lax.axis_index("ep") + jnp.arange(cold_count, dtype=jnp.int32)) % cold_count
+    cold_hit, cold_sel = token_table(expert_ids, cold_targets, capacity)
     cold_feats, cold_cotan, cold_scale = gather_rows(
         cold_hit, cold_sel, tokens, cotangent, gate_weights
     )
@@ -139,9 +147,8 @@
         ],
         axis=1,
     )
-    hot_outgoing, outgoing = lax.optimization_barrier((hot_outgoing, outgoing))
     gathered = lax.all_gather(hot_outgoing, "ep", axis=0, tiled=False)
-    received = lax.all_to_all(outgoing, "ep", split_axis=0, concat_axis=0, tiled=True)
+    received = shift_exchange(outgoing, "ep", 1)
     recv_feats = received[:, :capacity].reshape(-1, slice_width)
     recv_cotan = received[:, capacity : 2 * capacity].reshape(-1, slice_width)
     recv_scale = received[:, 2 * capacity :].reshape(cold_count, -1)[:, :capacity]
@@ -163,7 +170,7 @@
     output_slice = jnp.dot(hidden, w_down, preferred_element_type=jnp.float32)
     cold_route = jnp.sum(output_slice * recv_cotan.astype(jnp.float32), axis=1)
     cold_route = grp_sum_f32(cold_route.reshape(cold_count, capacity), "grp")
-    cold_back = lax.all_to_all(cold_route, "ep", split_axis=0, concat_axis=0, tiled=True)
+    cold_back = shift_exchange(cold_route, "ep", -1)
     contract_rows = (((0,), (0,)), ((), ()))
     grad_gate_cold = lax.dot_general(
         recv_feats, back_gate, contract_rows, preferred_element_type=jnp.float32

time: 145 us -> 152 us (1.048)
  starting transfers between devices: 26.8 us -> 46.3 us
  waiting for transfers between devices: 39.3 us -> 26.6 us
  local copies, waits for them, and re-layouts: 21.8 us -> 24.6 us
  matrix products: 20 us -> 18.2 us
    all_to_all x2 -> x0, waiting for transfers between devices: 29.2 us -> none  [the longest x1 24.8 us: body(): lax.all_to_all(outgoing, 'ep', split_axis=0, concat_axis=0, tiled=True)]
    ppermute x0 -> x14, starting transfers between devices: none -> 27.6 us  [shift_exchange(): moved.append(lax.ppermute(chunks[k], axis_name, perm))]
    ppermute x0 -> x14, waiting for transfers between devices: none -> 17.3 us  [shift_exchange(): moved.append(lax.ppermute(chunks[k], axis_name, perm))]
    all_to_all x2 -> x0, starting transfers between devices: 10.7 us -> none  [the longest x1 7.28 us: body(): lax.all_to_all(outgoing, 'ep', split_axis=0, concat_axis=0, tiled=True)]
    unnamed x31 -> x37, local copies, waits for them, and re-layouts: 2.96 us -> 8.11 us
    reshape x1, local copies, waits for them, and re-layouts: 2.2 us -> 0.03 us  [body(): cold_scale_block = jnp.pad(cold_scale.reshape(cold_count, capacity), ((0,...]
    all_to_all x1, starting transfers between devices: 4.11 us -> 6.22 us  [body(): lax.all_to_all(jnp.transpose(hot_route_part.reshape(hot_count, blocks, ca...]
    pad x1, local copies, waits for them, and re-layouts: 1.69 us -> 0.02 us  [body(): jnp.pad(cold_scale.reshape(cold_count, capacity), ((0, 0), (0, cold_lines...]
  transfers between devices with their start and end apart: 27 -> 39, of which waited for: 11 -> 12; matrix products, arithmetic and copies ran while one was open for 21% -> 28% of each run, Pallas kernels for 0% -> 0%
where the time goes in v6:
time: 152 us; the launch traced here: 151 us
  starting transfers between devices  46.3 us (30%)
  waiting for transfers between devices  26.6 us (18%)
  local copies, waits for them, and re-layouts  24.6 us (16%)
  other arithmetic  21 us (14%)
  matrix products  18.2 us (12%)
  between operations  14.6 us (10%)
    ppermute x14, starting transfers between devices, shift_exchange(): moved.append(lax.ppermute(chunks[k], axis_name, perm))  27.6 us
    ppermute x14, waiting for transfers between devices, shift_exchange(): moved.append(lax.ppermute(chunks[k], axis_name, perm))  17.3 us
    ppermute x7, waiting for transfers between devices, grp_sum_rounded(): got = lax.ppermute(mine, axis_name, partner)  8.82 us
    unnamed x37, local copies, waits for them, and re-layouts  8.11 us
    ppermute x7, starting transfers between devices, grp_sum_rounded(): got = lax.ppermute(mine, axis_name, partner)  8.07 us
    all_to_all x1, starting transfers between devices, body(): lax.all_to_all(jnp.transpose(hot_route_part.reshape(hot_count, blocks, ca...  6.22 us
    dynamic_slice x4, local copies, waits for them, and re-layouts, grp_sum_rounded(): second = lax.dynamic_index_in_dim(pair, 1 - core, axis=0, keepdims=False)  4.64 us
    dynamic_slice x4, local copies, waits for them, and re-layouts, grp_sum_rounded(): first = lax.dynamic_index_in_dim(pair, core, axis=0, keepdims=False)  4.62 us
  transfers between devices with their start and end apart: 39, of which 12 were waited for; matrix products, arithmetic and copies ran while one was open for 28% of the time, Pallas kernels for 0%

profile of v6, /device:TPU:0, one launch (start us, length us, event | category | flops | bytes accessed | tf_op | source)
XLA Modules:
  0.0 151.4 jit_solution(12439314699842082230)
XLA Ops:
  13.6 3.0 %collective-permute-start = (bf16[40,1280]{1,0:T(8,128)(2,1)}, bf16[40,1280]{1,0:T(8,128)(2,1)}, u32[]{:S(2)}, u32[]{:S(2)}) collective-permute-start(bf16[40,1280]{1,0:T(8,128)(2,1)} %get-tuple-element.17), channel_id=1, source_target_pairs={{0,1},{1,2},{2,3},{3,4},{4,5},{5,6},{6,7},{7,0},{8,9},{9,10},{10,1... | collective-permute-start | bytes 307208 | tf_op jit(solution)/shard_map/ppermute | solution.py:40
  19.4 3.1 %collective-permute-start.6 = (bf16[40,1280]{1,0:T(8,128)(2,1)S(1)}, bf16[40,1280]{1,0:T(8,128)(2,1)S(1)}, u32[]{:S(2)}, u32[]{:S(2)}) collective-permute-start(bf16[40,1280]{1,0:T(8,128)(2,1)S(1)} %get-tuple-element.11), channel_id=1, source_target_pairs={{0,7},{1,0},{2,1},{3,2},{4,3},{5,4},{6,5},{7,6},{8,15},{9,8},{10,9... | collective-permute-start | bytes 307208 | tf_op jit(solution)/shard_map/ppermute | solution.py:40
  22.5 2.0 %collective-permute-start.5 = (bf16[40,1280]{1,0:T(8,128)(2,1)}, bf16[40,1280]{1,0:T(8,128)(2,1)S(1)}, u32[]{:S(2)}, u32[]{:S(2)}) collective-permute-start(bf16[40,1280]{1,0:T(8,128)(2,1)} %get-tuple-element.12), channel_id=1, source_target_pairs={{0,6},{1,7},{2,0},{3,1},{4,2},{5,3},{6,4},{7,5},{8,14},{9,15},{10,... | collective-permute-start | bytes 307208 | tf_op jit(solution)/shard_map/ppermute | solution.py:40
  24.5 3.0 %collective-permute-start.3 = (bf16[40,1280]{1,0:T(8,128)(2,1)}, bf16[40,1280]{1,0:T(8,128)(2,1)S(1)}, u32[]{:S(2)}, u32[]{:S(2)}) collective-permute-start(bf16[40,1280]{1,0:T(8,128)(2,1)} %get-tuple-element.14), channel_id=1, source_target_pairs={{0,4},{1,5},{2,6},{3,7},{4,0},{5,1},{6,2},{7,3},{8,12},{9,13},{10,... | collective-permute-start | bytes 307208 | tf_op jit(solution)/shard_map/ppermute | solution.py:40
  27.5 1.5 %bitcast_dynamic-update-slice_fusion.6 = bf16[8,40,1280]{2,1,0:T(8,128)(2,1)} fusion(bf16[8,40,1280]{2,1,0:T(8,128)(2,1)} %get-tuple-element.18, bf16[40,1280]{1,0:T(8,128)(2,1)} %collective-permute-done), kind=kLoop, calls=%fused_computation.135 | loop fusion | bytes 204800
  29.0 11.4 %collective-permute-done.1 = bf16[40,1280]{1,0:T(8,128)(2,1)S(1)} collective-permute-done((bf16[40,1280]{1,0:T(8,128)(2,1)}, bf16[40,1280]{1,0:T(8,128)(2,1)S(1)}, u32[]{:S(2)}, u32[]{:S(2)}) %collective-permute-start.1) | collective-permute-done | bytes 102432 | tf_op jit(solution)/shard_map/ppermute | solution.py:40
  40.4 1.9 %collective-permute-start.2 = (bf16[40,1280]{1,0:T(8,128)(2,1)}, bf16[40,1280]{1,0:T(8,128)(2,1)S(1)}, u32[]{:S(2)}, u32[]{:S(2)}) collective-permute-start(bf16[40,1280]{1,0:T(8,128)(2,1)} %get-tuple-element.15), channel_id=1, source_target_pairs={{0,3},{1,4},{2,5},{3,6},{4,7},{5,0},{6,1},{7,2},{8,11},{9,12},{10,... | collective-permute-start | bytes 307208 | tf_op jit(solution)/shard_map/ppermute | solution.py:40
  42.9 4.6 %collective-permute-done.2 = bf16[40,1280]{1,0:T(8,128)(2,1)S(1)} collective-permute-done((bf16[40,1280]{1,0:T(8,128)(2,1)}, bf16[40,1280]{1,0:T(8,128)(2,1)S(1)}, u32[]{:S(2)}, u32[]{:S(2)}) %collective-permute-start.2) | collective-permute-done | bytes 102432 | tf_op jit(solution)/shard_map/ppermute | solution.py:40
  58.0 1.6 %collective-permute-start.8 = (bf16[64,768]{1,0:T(8,128)(2,1)S(1)}, bf16[64,768]{1,0:T(8,128)(2,1)S(1)}, u32[]{:S(2)}, u32[]{:S(2)}) collective-permute-start(bf16[64,768]{1,0:T(8,128)(2,1)S(1)} %add_convert_fusion.2), channel_id=1, source_target_pairs={{0,16},{8,24},{16,0},{24,8},{1,17},{9,25},{17,1},{25,9},{2,18},{10... | collective-permute-start | bytes 294920 | tf_op jit(solution)/shard_map/ppermute | solution.py:90
  60.3 1.6 %collective-permute-start.11 = (bf16[64,768]{1,0:T(8,128)(2,1)S(1)}, bf16[64,768]{1,0:T(8,128)(2,1)S(1)}, u32[]{:S(2)}, u32[]{:S(2)}) collective-permute-start(bf16[64,768]{1,0:T(8,128)(2,1)S(1)} %add_convert_fusion.1), channel_id=1, source_target_pairs={{0,16},{8,24},{16,0},{24,8},{1,17},{9,25},{17,1},{25,9},{2,18},{10... | collective-permute-start | bytes 294920 | tf_op jit(solution)/shard_map/ppermute | solution.py:90
  61.9 3.9 %collective-permute-done.14 = bf16[64,768]{1,0:T(8,128)(2,1)S(1)} collective-permute-done((bf16[64,768]{1,0:T(8,128)(2,1)S(1)}, bf16[64,768]{1,0:T(8,128)(2,1)S(1)}, u32[]{:S(2)}, u32[]{:S(2)}) %collective-permute-start.14) | collective-permute-done | bytes 98336 | tf_op jit(solution)/shard_map/ppermute | solution.py:90
  65.9 1.6 %collective-permute-done.11 = bf16[64,768]{1,0:T(8,128)(2,1)S(1)} collective-permute-done((bf16[64,768]{1,0:T(8,128)(2,1)S(1)}, bf16[64,768]{1,0:T(8,128)(2,1)S(1)}, u32[]{:S(2)}, u32[]{:S(2)}) %collective-permute-start.11) | collective-permute-done | bytes 98336 | tf_op jit(solution)/shard_map/ppermute | solution.py:90
  71.2 2.0 %fusion = bf16[1,1280,768]{2,1,0:T(8,128)(2,1)} fusion(bf16[128,1280]{1,0:T(8,128)(2,1)S(1)} %bitcast.209, f32[64,768]{1,0:T(8,128)S(1)} %get-tuple-element.24, f32[64,768]{1,0:T(8,128)S(1)} %get-tuple-element.23, f32[64,768]{1,0:T(8,128)S(1)} %get-tuple-element.22, f32[64,768]{1,0:T(8,128)S(1)} %get-tuple-element.21, f32[64,768]{1,0:T(8,128)S(1)} %get-tuple-element.20, ...), kind=kOutput, calls=%fused_computation.9 | convolution fusion | flops 253919232 | bytes 3473408 | tf_op jit(solution)/shard_map/dot_general | solution.py:175
  73.3 2.0 %fusion.1 = bf16[1,1280,768]{2,1,0:T(8,128)(2,1)} fusion(bf16[128,1280]{1,0:T(8,128)(2,1)S(1)} %bitcast.210, f32[64,768]{1,0:T(8,128)S(1)} %get-tuple-element.20, f32[64,768]{1,0:T(8,128)S(1)} %get-tuple-element.19, f32[64,768]{1,0:T(8,128)S(1)} %get-tuple-element.24, f32[64,768]{1,0:T(8,128)S(1)} %get-tuple-element.23), kind=kOutput, calls=%fused_computation.10 | convolution fusion | flops 253427712 | bytes 3080192 | tf_op jit(solution)/shard_map/dot_general | solution.py:178
  75.2 1.6 %collective-permute-start.26 = (f32[8,16]{1,0:T(8,128)S(1)}, f32[8,16]{1,0:T(8,128)S(1)}, u32[]{:S(2)}, u32[]{:S(2)}) collective-permute-start(f32[8,16]{1,0:T(8,128)S(1)} %add.176), channel_id=1, source_target_pairs={{0,16},{8,24},{16,0},{24,8},{1,17},{9,25},{17,1},{25,9},{2,18},{10... | collective-permute-start | bytes 1544 | tf_op jit(solution)/shard_map/ppermute | solution.py:62
  76.8 2.0 %fusion.2 = bf16[1,768,1280]{2,1,0:T(8,128)(2,1)} fusion(bf16[128,768]{1,0:T(8,128)(2,1)S(1)} %multiply_convert_fusion.3, bf16[128,1280]{1,0:T(8,128)(2,1)S(1)} %copy-done.5), kind=kOutput, calls=%fused_computation.11 | convolution fusion | flops 252641280 | bytes 2490368 | tf_op jit(solution)/shard_map/dot_general | solution.py:181
  78.9 2.3 %collective-permute-start.33 = (f32[16]{0:T(128)S(1)}, f32[16]{0:T(128)S(1)}, u32[]{:S(2)}, u32[]{:S(2)}) collective-permute-start(f32[16]{0:T(128)S(1)} %get-tuple-element.50), channel_id=1, source_target_pairs={{0,1},{1,2},{2,3},{3,4},{4,5},{5,6},{6,7},{7,0},{8,9},{9,10},{10,1... | collective-permute-start | bytes 200 | tf_op jit(solution)/shard_map/ppermute | solution.py:40
  82.2 3.2 %collective-permute-start.31 = (f32[16]{0:T(128)S(1)}, f32[16]{0:T(128)S(1)}, u32[]{:S(2)}, u32[]{:S(2)}) collective-permute-start(f32[16]{0:T(128)S(1)} %get-tuple-element.52), channel_id=1, source_target_pairs={{0,3},{1,4},{2,5},{3,6},{4,7},{5,0},{6,1},{7,2},{8,11},{9,12},{10,... | collective-permute-start | bytes 200 | tf_op jit(solution)/shard_map/ppermute | solution.py:40
  85.4 2.0 %collective-permute-start.30 = (f32[16]{0:T(128)S(1)}, f32[16]{0:T(128)S(1)}, u32[]{:S(2)}, u32[]{:S(2)}) collective-permute-start(f32[16]{0:T(128)S(1)} %get-tuple-element.53), channel_id=1, source_target_pairs={{0,4},{1,5},{2,6},{3,7},{4,0},{5,1},{6,2},{7,3},{8,12},{9,13},{10,... | collective-permute-start | bytes 200 | tf_op jit(solution)/shard_map/ppermute | solution.py:40
  88.3 2.4 %collective-permute-start.28 = (f32[16]{0:T(128)S(1)}, f32[16]{0:T(128)S(1)}, u32[]{:S(2)}, u32[]{:S(2)}) collective-permute-start(f32[16]{0:T(128)S(1)} %get-tuple-element.55), channel_id=1, source_target_pairs={{0,6},{1,7},{2,0},{3,1},{4,2},{5,3},{6,4},{7,5},{8,14},{9,15},{10,... | collective-permute-start | bytes 200 | tf_op jit(solution)/shard_map/ppermute | solution.py:40
  90.7 2.9 %collective-permute-start.27 = (f32[16]{0:T(128)S(1)}, f32[16]{0:T(128)S(1)}, u32[]{:S(2)}, u32[]{:S(2)}) collective-permute-start(f32[16]{0:T(128)S(1)} %get-tuple-element.56), channel_id=1, source_target_pairs={{0,7},{1,0},{2,1},{3,2},{4,3},{5,4},{6,5},{7,6},{8,15},{9,8},{10,9... | collective-permute-start | bytes 200 | tf_op jit(solution)/shard_map/ppermute | solution.py:40
  102.5 1.6 %collective-permute-start.17 = (bf16[2,64,96]{1,2,0:T(8,128)(2,1)S(1)}, bf16[2,64,96]{1,2,0:T(8,128)(2,1)S(1)}, u32[]{:S(2)}, u32[]{:S(2)}) collective-permute-start(bf16[2,64,96]{1,2,0:T(8,128)(2,1)S(1)} %add_convert_fusion.6), channel_id=1, source_target_pairs={{0,16},{8,24},{16,0},{24,8},{1,17},{9,25},{17,1},{25,9},{2,18},{10... | collective-permute-start | bytes 73736 | tf_op jit(solution)/shard_map/ppermute | solution.py:90
  104.9 1.6 %collective-permute-start.23 = (bf16[2,64,96]{1,2,0:T(8,128)(2,1)S(1)}, bf16[2,64,96]{1,2,0:T(8,128)(2,1)S(1)}, u32[]{:S(2)}, u32[]{:S(2)}) collective-permute-start(bf16[2,64,96]{1,2,0:T(8,128)(2,1)S(1)} %add_convert_fusion.4), channel_id=1, source_target_pairs={{0,16},{8,24},{16,0},{24,8},{1,17},{9,25},{17,1},{25,9},{2,18},{10... | collective-permute-start | bytes 73736 | tf_op jit(solution)/shard_map/ppermute | solution.py:90
  114.3 1.6 %copy.71 = f32[1,2,64,96]{3,2,1,0:T(8,128)} copy(f32[1,2,64,96]{2,3,1,0:T(8,128)} %get-tuple-element.25) | data formatting | bytes 98304 | tf_op jit(solution)/shard_map/jit(dynamic_index_in_dim)/dynamic_slice | solution.py:97
  115.9 1.6 %copy.72 = f32[1,2,64,96]{3,2,1,0:T(8,128)} copy(f32[1,2,64,96]{2,3,1,0:T(8,128)} %get-tuple-element.26) | data formatting | bytes 98304 | tf_op jit(solution)/shard_map/jit(dynamic_index_in_dim)/dynamic_slice | solution.py:98
  117.5 1.6 %copy.68 = f32[1,2,64,96]{3,2,1,0:T(8,128)} copy(f32[1,2,64,96]{2,3,1,0:T(8,128)} %get-tuple-element.31) | data formatting | bytes 98304 | tf_op jit(solution)/shard_map/jit(dynamic_index_in_dim)/dynamic_slice | solution.py:97
  119.1 1.6 %copy.69 = f32[1,2,64,96]{3,2,1,0:T(8,128)} copy(f32[1,2,64,96]{2,3,1,0:T(8,128)} %get-tuple-element.32) | data formatting | bytes 98304 | tf_op jit(solution)/shard_map/jit(dynamic_index_in_dim)/dynamic_slice | solution.py:98
  123.2 1.7 %fusion.44 = (f32[2,128]{1,0:T(2,128)}, f32[2,128,96]{2,1,0:T(8,128)S(1)}, f32[2,128,96]{2,1,0:T(8,128)S(1)}) fusion(f32[2,64,96]{2,1,0:T(8,128)} %bitcast.235, f32[2,64,96]{2,1,0:T(8,128)} %bitcast.234, f32[2,64,96]{2,1,0:T(8,128)} %bitcast.237, f32[2,64,96]{2,1,0:T(8,128)} %bitcast.236, f32[2,64,96]{2,1,0:T(8,128)} %bitcast.239, f32[2,64,96]{2,1,0:T(8,128)} %bitcast.238), kind=kLoop, calls=%fused_computation.108 | loop fusion | flops 294656 | bytes 492544 | tf_op jit(solution)/shard_map/reduce_sum | solution.py:209
  127.4 6.2 %all-to-all-start = ((f32[8,2,16]{2,1,0:T(2,128)}), f32[8,2,16]{2,1,0:T(2,128)}, u32[]{:S(2)}, u32[]{:S(2)}) async-start(f32[8,2,16]{2,1,0:T(2,128)} %copy.73), calls=%async_computation | async-start | bytes 16384 | tf_op jit(solution)/shard_map/all_to_all | solution.py:210
  134.5 2.2 %convert_reduce_fusion.1 = f32[2,1280,96]{1,2,0:T(8,128)} fusion(f32[2,8,16,96]{3,2,1,0:T(8,128)S(1)} %bitcast.246, f32[2,8,16,96]{3,2,1,0:T(8,128)S(1)} %bitcast.225, bf16[2,2,8,16,1280]{4,3,2,1,0:T(8,128)(2,1)S(1)} %bitcast.204), kind=kOutput, calls=%fused_computation.1 | convolution fusion | flops 68714496 | bytes 1900544 | tf_op jit(solution)/shard_map/jbcd,jbch->jbdh/dot_general | solution.py:225
  136.7 2.2 %convert_reduce_fusion.2 = f32[2,1280,96]{1,2,0:T(8,128)} fusion(f32[2,8,16,96]{3,2,1,0:T(8,128)S(1)} %bitcast.226, f32[2,8,16,96]{3,2,1,0:T(8,128)S(1)} %bitcast.247, f32[2,8,16,96]{3,2,1,0:T(8,128)S(1)} %bitcast.223, bf16[2,2,8,16,1280]{4,3,2,1,0:T(8,128)(2,1)S(1)} %bitcast.205), kind=kOutput, calls=%fused_computation.2 | convolution fusion | flops 68812800 | bytes 2031616 | tf_op jit(solution)/shard_map/jbcd,jbch->jbdh/dot_general | solution.py:224
  138.9 2.2 %convert_reduce_fusion = f32[2,96,1280]{2,1,0:T(8,128)} fusion(f32[2,8,16]{2,1,0:T(8,128)S(1)} %copy.63, f32[2,8,16,96]{3,2,1,0:T(8,128)S(1)} %bitcast.224, f32[2,8,16,96]{3,2,1,0:T(8,128)S(1)} %bitcast.227, bf16[2,2,8,16,1280]{4,3,2,1,0:T(8,128)(2,1)S(1)} %bitcast.206), kind=kOutput, calls=%fused_computation | convolution fusion | flops 69697536 | bytes 1908736 | tf_op jit(solution)/shard_map/jbch,jbcd->jbhd/dot_general | solution.py:226
  (201 shorter events, 53.4 us)
Async XLA Ops:
  7.2 88.5 %all-gather.3.cloned.1.call-start = ((), (), s32[]{:S(2)}) async-start(), calls=%async_computation.1 | async-start | bytes 1658880 | tf_op jit(solution)/shard_map/all_gather | solution.py:150
  13.6 13.9 %collective-permute-start = (bf16[40,1280]{1,0:T(8,128)(2,1)}, bf16[40,1280]{1,0:T(8,128)(2,1)}, u32[]{:S(2)}, u32[]{:S(2)}) collective-permute-start(bf16[40,1280]{1,0:T(8,128)(2,1)} %get-tuple-element.17), channel_id=1, source_target_pairs={{0,1},{1,2},{2,3},{3,4},{4,5},{5,6},{6,7},{7,0},{8,9},{9,10},{10,1... | collective-permute-start | bytes 307208 | tf_op jit(solution)/shard_map/ppermute | solution.py:40
  19.4 30.7 %collective-permute-start.6 = (bf16[40,1280]{1,0:T(8,128)(2,1)S(1)}, bf16[40,1280]{1,0:T(8,128)(2,1)S(1)}, u32[]{:S(2)}, u32[]{:S(2)}) collective-permute-start(bf16[40,1280]{1,0:T(8,128)(2,1)S(1)} %get-tuple-element.11), channel_id=1, source_target_pairs={{0,7},{1,0},{2,1},{3,2},{4,3},{5,4},{6,5},{7,6},{8,15},{9,8},{10,9... | collective-permute-start | bytes 307208 | tf_op jit(solution)/shard_map/ppermute | solution.py:40
  22.5 26.9 %collective-permute-start.5 = (bf16[40,1280]{1,0:T(8,128)(2,1)}, bf16[40,1280]{1,0:T(8,128)(2,1)S(1)}, u32[]{:S(2)}, u32[]{:S(2)}) collective-permute-start(bf16[40,1280]{1,0:T(8,128)(2,1)} %get-tuple-element.12), channel_id=1, source_target_pairs={{0,6},{1,7},{2,0},{3,1},{4,2},{5,3},{6,4},{7,5},{8,14},{9,15},{10,... | collective-permute-start | bytes 307208 | tf_op jit(solution)/shard_map/ppermute | solution.py:40
  24.5 24.3 %collective-permute-start.4 = (bf16[40,1280]{1,0:T(8,128)(2,1)}, bf16[40,1280]{1,0:T(8,128)(2,1)S(1)}, u32[]{:S(2)}, u32[]{:S(2)}) collective-permute-start(bf16[40,1280]{1,0:T(8,128)(2,1)} %get-tuple-element.13), channel_id=1, source_target_pairs={{0,5},{1,6},{2,7},{3,0},{4,1},{5,2},{6,3},{7,4},{8,13},{9,14},{10,... | collective-permute-start | bytes 307208 | tf_op jit(solution)/shard_map/ppermute | solution.py:40
  24.5 23.7 %collective-permute-start.3 = (bf16[40,1280]{1,0:T(8,128)(2,1)}, bf16[40,1280]{1,0:T(8,128)(2,1)S(1)}, u32[]{:S(2)}, u32[]{:S(2)}) collective-permute-start(bf16[40,1280]{1,0:T(8,128)(2,1)} %get-tuple-element.14), channel_id=1, source_target_pairs={{0,4},{1,5},{2,6},{3,7},{4,0},{5,1},{6,2},{7,3},{8,12},{9,13},{10,... | collective-permute-start | bytes 307208 | tf_op jit(solution)/shard_map/ppermute | solution.py:40
  27.5 12.9 %collective-permute-start.1 = (bf16[40,1280]{1,0:T(8,128)(2,1)}, bf16[40,1280]{1,0:T(8,128)(2,1)S(1)}, u32[]{:S(2)}, u32[]{:S(2)}) collective-permute-start(bf16[40,1280]{1,0:T(8,128)(2,1)} %get-tuple-element.16), channel_id=1, source_target_pairs={{0,2},{1,3},{2,4},{3,5},{4,6},{5,7},{6,0},{7,1},{8,10},{9,11},{10,... | collective-permute-start | bytes 307208 | tf_op jit(solution)/shard_map/ppermute | solution.py:40
  40.4 7.1 %collective-permute-start.2 = (bf16[40,1280]{1,0:T(8,128)(2,1)}, bf16[40,1280]{1,0:T(8,128)(2,1)S(1)}, u32[]{:S(2)}, u32[]{:S(2)}) collective-permute-start(bf16[40,1280]{1,0:T(8,128)(2,1)} %get-tuple-element.15), channel_id=1, source_target_pairs={{0,3},{1,4},{2,5},{3,6},{4,7},{5,0},{6,1},{7,2},{8,11},{9,12},{10,... | collective-permute-start | bytes 307208 | tf_op jit(solution)/shard_map/ppermute | solution.py:40
  55.7 4.0 %collective-permute-start.13 = (bf16[64,768]{1,0:T(8,128)(2,1)S(1)}, bf16[64,768]{1,0:T(8,128)(2,1)S(1)}, u32[]{:S(2)}, u32[]{:S(2)}) collective-permute-start(bf16[64,768]{1,0:T(8,128)(2,1)S(1)} %constant_dynamic-slice_fusion.4), channel_id=1, source_target_pairs={{0,8},{8,0},{16,24},{24,16},{1,9},{9,1},{17,25},{25,17},{2,10},{10... | collective-permute-start | bytes 294920 | tf_op jit(solution)/shard_map/ppermute | solution.py:84
  57.1 3.1 %collective-permute-start.10 = (bf16[64,768]{1,0:T(8,128)(2,1)S(1)}, bf16[64,768]{1,0:T(8,128)(2,1)S(1)}, u32[]{:S(2)}, u32[]{:S(2)}) collective-permute-start(bf16[64,768]{1,0:T(8,128)(2,1)S(1)} %constant_dynamic-slice_fusion.5), channel_id=1, source_target_pairs={{0,8},{8,0},{16,24},{24,16},{1,9},{9,1},{17,25},{25,17},{2,10},{10... | collective-permute-start | bytes 294920 | tf_op jit(solution)/shard_map/ppermute | solution.py:84
  58.0 9.6 %collective-permute-start.8 = (bf16[64,768]{1,0:T(8,128)(2,1)S(1)}, bf16[64,768]{1,0:T(8,128)(2,1)S(1)}, u32[]{:S(2)}, u32[]{:S(2)}) collective-permute-start(bf16[64,768]{1,0:T(8,128)(2,1)S(1)} %add_convert_fusion.2), channel_id=1, source_target_pairs={{0,16},{8,24},{16,0},{24,8},{1,17},{9,25},{17,1},{25,9},{2,18},{10... | collective-permute-start | bytes 294920 | tf_op jit(solution)/shard_map/ppermute | solution.py:90
  59.7 6.1 %collective-permute-start.14 = (bf16[64,768]{1,0:T(8,128)(2,1)S(1)}, bf16[64,768]{1,0:T(8,128)(2,1)S(1)}, u32[]{:S(2)}, u32[]{:S(2)}) collective-permute-start(bf16[64,768]{1,0:T(8,128)(2,1)S(1)} %add_convert_fusion), channel_id=1, source_target_pairs={{0,16},{8,24},{16,0},{24,8},{1,17},{9,25},{17,1},{25,9},{2,18},{10... | collective-permute-start | bytes 294920 | tf_op jit(solution)/shard_map/ppermute | solution.py:90
  60.3 7.2 %collective-permute-start.11 = (bf16[64,768]{1,0:T(8,128)(2,1)S(1)}, bf16[64,768]{1,0:T(8,128)(2,1)S(1)}, u32[]{:S(2)}, u32[]{:S(2)}) collective-permute-start(bf16[64,768]{1,0:T(8,128)(2,1)S(1)} %add_convert_fusion.1), channel_id=1, source_target_pairs={{0,16},{8,24},{16,0},{24,8},{1,17},{9,25},{17,1},{25,9},{2,18},{10... | collective-permute-start | bytes 294920 | tf_op jit(solution)/shard_map/ppermute | solution.py:90
  65.8 3.0 %collective-permute-start.15 = (f32[64,768]{1,0:T(8,128)S(1)}, f32[64,768]{1,0:T(8,128)S(1)}, u32[]{:S(2)}, u32[]{:S(2)}) collective-permute-start(f32[64,768]{1,0:T(8,128)S(1)} %get-tuple-element.37), channel_id=1, source_target_pairs={{0,8},{8,0},{16,24},{24,16},{1,9},{9,1},{17,25},{25,17},{2,10},{10... | collective-permute-start | bytes 589832 | tf_op jit(solution)/shard_map/ppermute | solution.py:93
  69.9 5.4 %collective-permute-start.25 = (f32[8,16]{1,0:T(8,128)S(1)}, f32[8,16]{1,0:T(8,128)S(1)}, u32[]{:S(2)}, u32[]{:S(2)}) collective-permute-start(f32[8,16]{1,0:T(8,128)S(1)} %reshape.197), channel_id=1, source_target_pairs={{0,8},{8,0},{16,24},{24,16},{1,9},{9,1},{17,25},{25,17},{2,10},{10... | collective-permute-start | bytes 1544 | tf_op jit(solution)/shard_map/ppermute | solution.py:62
  75.2 3.6 %collective-permute-start.26 = (f32[8,16]{1,0:T(8,128)S(1)}, f32[8,16]{1,0:T(8,128)S(1)}, u32[]{:S(2)}, u32[]{:S(2)}) collective-permute-start(f32[8,16]{1,0:T(8,128)S(1)} %add.176), channel_id=1, source_target_pairs={{0,16},{8,24},{16,0},{24,8},{1,17},{9,25},{17,1},{25,9},{2,18},{10... | collective-permute-start | bytes 1544 | tf_op jit(solution)/shard_map/ppermute | solution.py:62
  78.9 9.4 %collective-permute-start.33 = (f32[16]{0:T(128)S(1)}, f32[16]{0:T(128)S(1)}, u32[]{:S(2)}, u32[]{:S(2)}) collective-permute-start(f32[16]{0:T(128)S(1)} %get-tuple-element.50), channel_id=1, source_target_pairs={{0,1},{1,2},{2,3},{3,4},{4,5},{5,6},{6,7},{7,0},{8,9},{9,10},{10,1... | collective-permute-start | bytes 200 | tf_op jit(solution)/shard_map/ppermute | solution.py:40
  81.2 9.5 %collective-permute-start.32 = (f32[16]{0:T(128)S(1)}, f32[16]{0:T(128)S(1)}, u32[]{:S(2)}, u32[]{:S(2)}) collective-permute-start(f32[16]{0:T(128)S(1)} %get-tuple-element.51), channel_id=1, source_target_pairs={{0,2},{1,3},{2,4},{3,5},{4,6},{5,7},{6,0},{7,1},{8,10},{9,11},{10,... | collective-permute-start | bytes 200 | tf_op jit(solution)/shard_map/ppermute | solution.py:40
  82.2 11.4 %collective-permute-start.31 = (f32[16]{0:T(128)S(1)}, f32[16]{0:T(128)S(1)}, u32[]{:S(2)}, u32[]{:S(2)}) collective-permute-start(f32[16]{0:T(128)S(1)} %get-tuple-element.52), channel_id=1, source_target_pairs={{0,3},{1,4},{2,5},{3,6},{4,7},{5,0},{6,1},{7,2},{8,11},{9,12},{10,... | collective-permute-start | bytes 200 | tf_op jit(solution)/shard_map/ppermute | solution.py:40
  85.4 8.2 %collective-permute-start.30 = (f32[16]{0:T(128)S(1)}, f32[16]{0:T(128)S(1)}, u32[]{:S(2)}, u32[]{:S(2)}) collective-permute-start(f32[16]{0:T(128)S(1)} %get-tuple-element.53), channel_id=1, source_target_pairs={{0,4},{1,5},{2,6},{3,7},{4,0},{5,1},{6,2},{7,3},{8,12},{9,13},{10,... | collective-permute-start | bytes 200 | tf_op jit(solution)/shard_map/ppermute | solution.py:40
  87.4 6.2 %collective-permute-start.29 = (f32[16]{0:T(128)S(1)}, f32[16]{0:T(128)S(1)}, u32[]{:S(2)}, u32[]{:S(2)}) collective-permute-start(f32[16]{0:T(128)S(1)} %get-tuple-element.54), channel_id=1, source_target_pairs={{0,5},{1,6},{2,7},{3,0},{4,1},{5,2},{6,3},{7,4},{8,13},{9,14},{10,... | collective-permute-start | bytes 200 | tf_op jit(solution)/shard_map/ppermute | solution.py:40
  88.3 5.3 %collective-permute-start.28 = (f32[16]{0:T(128)S(1)}, f32[16]{0:T(128)S(1)}, u32[]{:S(2)}, u32[]{:S(2)}) collective-permute-start(f32[16]{0:T(128)S(1)} %get-tuple-element.55), channel_id=1, source_target_pairs={{0,6},{1,7},{2,0},{3,1},{4,2},{5,3},{6,4},{7,5},{8,14},{9,15},{10,... | collective-permute-start | bytes 200 | tf_op jit(solution)/shard_map/ppermute | solution.py:40
  90.7 4.2 %collective-permute-start.27 = (f32[16]{0:T(128)S(1)}, f32[16]{0:T(128)S(1)}, u32[]{:S(2)}, u32[]{:S(2)}) collective-permute-start(f32[16]{0:T(128)S(1)} %get-tuple-element.56), channel_id=1, source_target_pairs={{0,7},{1,0},{2,1},{3,2},{4,3},{5,4},{6,5},{7,6},{8,15},{9,8},{10,9... | collective-permute-start | bytes 200 | tf_op jit(solution)/shard_map/ppermute | solution.py:40
  102.0 4.5 %collective-permute-start.19 = (bf16[2,64,96]{1,2,0:T(8,128)(2,1)S(1)}, bf16[2,64,96]{1,2,0:T(8,128)(2,1)S(1)}, u32[]{:S(2)}, u32[]{:S(2)}) collective-permute-start(bf16[2,64,96]{1,2,0:T(8,128)(2,1)S(1)} %constant_dynamic-slice_fusion.2), channel_id=1, source_target_pairs={{0,8},{8,0},{16,24},{24,16},{1,9},{9,1},{17,25},{25,17},{2,10},{10... | collective-permute-start | bytes 73736 | tf_op jit(solution)/shard_map/ppermute | solution.py:84
  102.5 4.6 %collective-permute-start.17 = (bf16[2,64,96]{1,2,0:T(8,128)(2,1)S(1)}, bf16[2,64,96]{1,2,0:T(8,128)(2,1)S(1)}, u32[]{:S(2)}, u32[]{:S(2)}) collective-permute-start(bf16[2,64,96]{1,2,0:T(8,128)(2,1)S(1)} %add_convert_fusion.6), channel_id=1, source_target_pairs={{0,16},{8,24},{16,0},{24,8},{1,17},{9,25},{17,1},{25,9},{2,18},{10... | collective-permute-start | bytes 73736 | tf_op jit(solution)/shard_map/ppermute | solution.py:90
  104.2 4.2 %collective-permute-start.35 = (bf16[2,64,96]{1,2,0:T(8,128)(2,1)S(1)}, bf16[2,64,96]{1,2,0:T(8,128)(2,1)S(1)}, u32[]{:S(2)}, u32[]{:S(2)}) collective-permute-start(bf16[2,64,96]{1,2,0:T(8,128)(2,1)S(1)} %add_convert_fusion.3), channel_id=1, source_target_pairs={{0,16},{8,24},{16,0},{24,8},{1,17},{9,25},{17,1},{25,9},{2,18},{10... | collective-permute-start | bytes 73736 | tf_op jit(solution)/shard_map/ppermute | solution.py:90
  104.9 4.7 %collective-permute-start.23 = (bf16[2,64,96]{1,2,0:T(8,128)(2,1)S(1)}, bf16[2,64,96]{1,2,0:T(8,128)(2,1)S(1)}, u32[]{:S(2)}, u32[]{:S(2)}) collective-permute-start(bf16[2,64,96]{1,2,0:T(8,128)(2,1)S(1)} %add_convert_fusion.4), channel_id=1, source_target_pairs={{0,16},{8,24},{16,0},{24,8},{1,17},{9,25},{17,1},{25,9},{2,18},{10... | collective-permute-start | bytes 73736 | tf_op jit(solution)/shard_map/ppermute | solution.py:90
  106.6 4.2 %collective-permute-start.20 = (bf16[2,64,96]{1,2,0:T(8,128)(2,1)S(1)}, bf16[2,64,96]{1,2,0:T(8,128)(2,1)S(1)}, u32[]{:S(2)}, u32[]{:S(2)}) collective-permute-start(bf16[2,64,96]{1,2,0:T(8,128)(2,1)S(1)} %add_convert_fusion.5), channel_id=1, source_target_pairs={{0,16},{8,24},{16,0},{24,8},{1,17},{9,25},{17,1},{25,9},{2,18},{10... | collective-permute-start | bytes 73736 | tf_op jit(solution)/shard_map/ppermute | solution.py:90
  107.2 4.3 %collective-permute-start.18 = (f32[2,64,96]{1,2,0:T(8,128)S(1)}, f32[2,64,96]{1,2,0:T(8,128)S(1)}, u32[]{:S(2)}, u32[]{:S(2)}) collective-permute-start(f32[2,64,96]{1,2,0:T(8,128)S(1)} %get-tuple-element.46), channel_id=1, source_target_pairs={{0,8},{8,0},{16,24},{24,16},{1,9},{9,1},{17,25},{25,17},{2,10},{10... | collective-permute-start | bytes 147464 | tf_op jit(solution)/shard_map/ppermute | solution.py:93
  108.4 3.1 %collective-permute-start.36 = (f32[2,64,96]{1,2,0:T(8,128)S(1)}, f32[2,64,96]{1,2,0:T(8,128)S(1)}, u32[]{:S(2)}, u32[]{:S(2)}) collective-permute-start(f32[2,64,96]{1,2,0:T(8,128)S(1)} %get-tuple-element.42), channel_id=1, source_target_pairs={{0,8},{8,0},{16,24},{24,16},{1,9},{9,1},{17,25},{25,17},{2,10},{10... | collective-permute-start | bytes 147464 | tf_op jit(solution)/shard_map/ppermute | solution.py:93
  111.4 9.3 %collective-permute-start.21 = (f32[2,64,96]{1,2,0:T(8,128)}, f32[2,64,96]{1,2,0:T(8,128)}, u32[]{:S(2)}, u32[]{:S(2)}) collective-permute-start(f32[2,64,96]{1,2,0:T(8,128)} %get-tuple-element.44), channel_id=1, source_target_pairs={{0,8},{8,0},{16,24},{24,16},{1,9},{9,1},{17,25},{25,17},{2,10},{10... | collective-permute-start | bytes 147464 | tf_op jit(solution)/shard_map/ppermute | solution.py:93
  127.4 13.6 %all-to-all-start = ((f32[8,2,16]{2,1,0:T(2,128)}), f32[8,2,16]{2,1,0:T(2,128)}, u32[]{:S(2)}, u32[]{:S(2)}) async-start(f32[8,2,16]{2,1,0:T(2,128)} %copy.73), calls=%async_computation | async-start | bytes 16384 | tf_op jit(solution)/shard_map/all_to_all | solution.py:210
  (20 other events, 163.3 us)
Sparse Core Ops, SparseCore 0:
  19.5 50.1 all-gather.2

commit v7 on v4

--- a/solution.py
+++ b/solution.py
@@ -175,15 +175,37 @@
     part_hidden_hot = jnp.einsum(
         "jrd,jhd->jrh", rows_wt, down_hot, preferred_element_type=jnp.float32
     )
-    cot_down = jnp.einsum("jrd,jhd->jrh", rows_cot, down_hot, preferred_element_type=jnp.float32)
-    (pre_gate, pre_up, grad_hidden, pre_gate_hot, pre_up_hot, grad_hidden_hot) = grp_sum_rounded(
-        [part_gate, part_up, part_hidden, part_gate_hot, part_up_hot, part_hidden_hot],
-        [0, 0, 0, 1, 1, 1],
+    part_cot_hot = jnp.einsum(
+        "jrd,jhd->jrh", rows_cot, down_hot, preferred_element_type=jnp.float32
+    )
+    part_cot = lax.dot_general(
+        recv_cotan, w_down, (((1,), (1,)), ((), ())), preferred_element_type=jnp.float32
+    )
+    (
+        pre_gate,
+        pre_up,
+        grad_hidden,
+        cold_cot_down,
+        pre_gate_hot,
+        pre_up_hot,
+        grad_hidden_hot,
+        cot_down,
+    ) = grp_sum_rounded(
+        [
+            part_gate,
+            part_up,
+            part_hidden,
+            part_cot,
+            part_gate_hot,
+            part_up_hot,
+            part_hidden_hot,
+            part_cot_hot,
+        ],
+        [0, 0, 0, 0, 1, 1, 1, 1],
         "grp",
     )
     hidden, back_gate, back_up = swiglu_back(pre_gate, pre_up, grad_hidden)
-    output_slice = jnp.dot(hidden, w_down, preferred_element_type=jnp.float32)
-    cold_route = jnp.sum(output_slice * recv_cotan.astype(jnp.float32), axis=1)
+    cold_route = jnp.sum(hidden.astype(jnp.float32) * cold_cot_down, axis=1)
     contract_rows = (((0,), (0,)), ((), ()))
     grad_gate_cold = lax.dot_general(
         recv_feats, back_gate, contract_rows, preferred_element_type=jnp.float32
@@ -215,7 +237,6 @@
         ],
         axis=1,
     )
-    route_parts = grp_sum_f32(route_parts, "grp")
     route_back = lax.all_to_all(route_parts, "ep", split_axis=0, concat_axis=0, tiled=True)
     cold_back = route_back[:, 0, :]
     hot_route = jnp.sum(route_back[:, 1:, :], axis=0)

time: 129 us -> 133 us (1.031)
  local copies, waits for them, and re-layouts: 19.2 us -> 23.8 us
  waiting for transfers between devices: 34.5 us -> 30.8 us
  other arithmetic: 15.2 us -> 17.6 us
    all_to_all x1, waiting for transfers between devices: 4.41 us -> 0.01 us  [body(): lax.all_to_all(route_parts, 'ep', split_axis=0, concat_axis=0, tiled=True)]
    dynamic_slice x1 -> x4, local copies, waits for them, and re-layouts: 1.6 us -> 4.62 us  [grp_sum_rounded(): second = lax.dynamic_index_in_dim(pair, 1 - core, axis=0, keepdims=False)]
    dynamic_slice x1 -> x4, local copies, waits for them, and re-layouts: 1.6 us -> 4.59 us  [grp_sum_rounded(): first = lax.dynamic_index_in_dim(pair, core, axis=0, keepdims=False)]
    reduce_sum x0 -> x2, other arithmetic: none -> 2.49 us  [the longest x1 1.68 us: body(): hot_route_part = jnp.sum(hidden_hot.astype(jnp.float32) * cot_down, axis=2)]
    ppermute x6 -> x8, waiting for transfers between devices: 7.09 us -> 9.37 us  [grp_sum_rounded(): got = lax.ppermute(mine, axis_name, partner)]
    ppermute x2 -> x0, starting transfers between devices: 1.71 us -> none  [grp_sum_f32(): x = x + lax.ppermute(x, axis_name, partner)]
    unnamed x37 -> x29, local copies, waits for them, and re-layouts: 6.08 us -> 5 us
    ppermute x6 -> x8, starting transfers between devices: 7.67 us -> 8.63 us  [grp_sum_rounded(): got = lax.ppermute(mine, axis_name, partner)]
  transfers between devices with their start and end apart: 23 -> 27, of which waited for: 12 -> 10; matrix products, arithmetic and copies ran while one was open for 22% -> 27% of each run, Pallas kernels for 0% -> 0%
where the time goes in v7:
time: 133 us; the launch traced here: 132 us
  waiting for transfers between devices  30.8 us (23%)
  local copies, waits for them, and re-layouts  23.8 us (18%)
  starting transfers between devices  23 us (17%)
  matrix products  21.8 us (16%)
  other arithmetic  17.6 us (13%)
  between operations  14.8 us (11%)
    all_to_all x1, waiting for transfers between devices, body(): lax.all_to_all(outgoing, 'ep', split_axis=0, concat_axis=0, tiled=True)  20.1 us
    ppermute x8, waiting for transfers between devices, grp_sum_rounded(): got = lax.ppermute(mine, axis_name, partner)  9.37 us
    ppermute x8, starting transfers between devices, grp_sum_rounded(): got = lax.ppermute(mine, axis_name, partner)  8.63 us
    all_to_all x1, starting transfers between devices, body(): lax.all_to_all(outgoing, 'ep', split_axis=0, concat_axis=0, tiled=True)  7.28 us
    unnamed x29, local copies, waits for them, and re-layouts  5 us
    dynamic_slice x4, local copies, waits for them, and re-layouts, grp_sum_rounded(): second = lax.dynamic_index_in_dim(pair, 1 - core, axis=0, keepdims=False)  4.62 us
    dynamic_slice x4, local copies, waits for them, and re-layouts, grp_sum_rounded(): first = lax.dynamic_index_in_dim(pair, core, axis=0, keepdims=False)  4.59 us
    all_to_all x1, starting transfers between devices, body(): lax.all_to_all(route_parts, 'ep', split_axis=0, concat_axis=0, tiled=True)  4.16 us
  transfers between devices with their start and end apart: 27, of which 10 were waited for; matrix products, arithmetic and copies ran while one was open for 27% of the time, Pallas kernels for 0%

profile of v7, /device:TPU:0, one launch (start us, length us, event | category | flops | bytes accessed | tf_op | source)
XLA Modules:
  0.0 131.7 jit_solution(15104043156052433740)
XLA Ops:
  11.2 2.3 %reduce-window.14 = s32[8,12,128]{2,1,0:T(8,128)S(1)} reduce-window(s32[8,12,128]{2,1,0:T(8,128)S(1)} %fusion.79, s32[]{:T(128)} %constant.75.clone.1), window={size=1x1x128 pad=0_0x0_0x127_0}, to_apply=%region_1.2 | reduce-window | flops 1560576 | bytes 98308 | tf_op jit(solution)/shard_map/reduce-window
  17.5 7.3 %all-to-all-start = ((bf16[8,40,1280]{2,1,0:T(8,128)(2,1)}), bf16[8,40,1280]{2,1,0:T(8,128)(2,1)S(1)}, u32[]{:S(2)}, u32[]{:S(2)}) async-start(bf16[8,40,1280]{2,1,0:T(8,128)(2,1)} %pad_maximum_fusion), calls=%async_computation | async-start | bytes 1638400 | tf_op jit(solution)/shard_map/all_to_all | solution.py:145
  26.3 1.0 copy.88
  27.6 1.3 %convolution_convert_fusion.9 = bf16[32,1280]{1,0:T(8,128)(2,1)S(1)} fusion(bf16[256,1280]{1,0:T(8,128)(2,1)} %param.11, bf16[32,256]{1,0:T(8,128)(2,1)S(1)} %convert_reduce_fusion.4), kind=kOutput, calls=%fused_computation.15 | convolution fusion | flops 21012480 | bytes 753664 | tf_op jit(solution)/shard_map/dot_general | solution.py:24
  29.7 20.1 %all-to-all-done = bf16[8,40,1280]{2,1,0:T(8,128)(2,1)S(1)} async-done(((bf16[8,40,1280]{2,1,0:T(8,128)(2,1)}), bf16[8,40,1280]{2,1,0:T(8,128)(2,1)S(1)}, u32[]{:S(2)}, u32[]{:S(2)}) %all-to-all-start) | async-done | bytes 819232 | tf_op jit(solution)/shard_map/all_to_all | solution.py:145
  54.5 1.8 %collective-permute-start.1 = (bf16[64,768]{1,0:T(8,128)(2,1)S(1)}, bf16[64,768]{1,0:T(8,128)(2,1)S(1)}, u32[]{:S(2)}, u32[]{:S(2)}) collective-permute-start(bf16[64,768]{1,0:T(8,128)(2,1)S(1)} %add_convert_fusion.3), channel_id=1, source_target_pairs={{0,16},{8,24},{16,0},{24,8},{1,17},{9,25},{17,1},{25,9},{2,18},{10... | collective-permute-start | bytes 294920 | tf_op jit(solution)/shard_map/ppermute | solution.py:80
  56.7 1.8 %collective-permute-start.7 = (bf16[64,768]{1,0:T(8,128)(2,1)S(1)}, bf16[64,768]{1,0:T(8,128)(2,1)S(1)}, u32[]{:S(2)}, u32[]{:S(2)}) collective-permute-start(bf16[64,768]{1,0:T(8,128)(2,1)S(1)} %add_convert_fusion.1), channel_id=1, source_target_pairs={{0,16},{8,24},{16,0},{24,8},{1,17},{9,25},{17,1},{25,9},{2,18},{10... | collective-permute-start | bytes 294920 | tf_op jit(solution)/shard_map/ppermute | solution.py:80
  58.9 1.1 collective-permute-done.1
  60.7 1.3 %collective-permute-done.19 = bf16[64,768]{1,0:T(8,128)(2,1)S(1)} collective-permute-done((bf16[64,768]{1,0:T(8,128)(2,1)S(1)}, bf16[64,768]{1,0:T(8,128)(2,1)S(1)}, u32[]{:S(2)}, u32[]{:S(2)}) %collective-permute-start.19) | collective-permute-done | bytes 98336 | tf_op jit(solution)/shard_map/ppermute | solution.py:80
  62.2 2.0 %collective-permute-done.7 = bf16[64,768]{1,0:T(8,128)(2,1)S(1)} collective-permute-done((bf16[64,768]{1,0:T(8,128)(2,1)S(1)}, bf16[64,768]{1,0:T(8,128)(2,1)S(1)}, u32[]{:S(2)}, u32[]{:S(2)}) %collective-permute-start.7) | collective-permute-done | bytes 98336 | tf_op jit(solution)/shard_map/ppermute | solution.py:80
  64.3 1.4 %collective-permute-done.4 = bf16[64,768]{1,0:T(8,128)(2,1)S(1)} collective-permute-done((bf16[64,768]{1,0:T(8,128)(2,1)S(1)}, bf16[64,768]{1,0:T(8,128)(2,1)S(1)}, u32[]{:S(2)}, u32[]{:S(2)}) %collective-permute-start.4) | collective-permute-done | bytes 98336 | tf_op jit(solution)/shard_map/ppermute | solution.py:80
  66.0 1.2 collective-permute-done.5
  68.8 1.1 fusion.58
  69.9 3.0 %fusion.2 = bf16[1,768,1280]{2,1,0:T(8,128)(2,1)} fusion(bf16[128,768]{1,0:T(8,128)(2,1)} %get-tuple-element.49, bf16[128,1280]{1,0:T(8,128)(2,1)S(1)} %bitcast.180, f32[128]{0:T(128)S(1)} %reshape.233), kind=kOutput, calls=%fused_computation.11 | convolution fusion | flops 253132800 | bytes 2490880 | tf_op jit(solution)/shard_map/dot_general | solution.py:216
  72.8 2.0 %fusion.1 = bf16[1,1280,768]{2,1,0:T(8,128)(2,1)} fusion(bf16[128,1280]{1,0:T(8,128)(2,1)S(1)} %bitcast.170, f32[64,768]{1,0:T(8,128)S(1)} %get-tuple-element.57, f32[64,768]{1,0:T(8,128)S(1)} %get-tuple-element.56, f32[64,768]{1,0:T(8,128)S(1)} %get-tuple-element.61, f32[64,768]{1,0:T(8,128)S(1)} %get-tuple-element.60), kind=kOutput, calls=%fused_computation.10 | convolution fusion | flops 253427712 | bytes 3080192 | tf_op jit(solution)/shard_map/dot_general | solution.py:213
  74.8 2.0 %fusion = bf16[1,1280,768]{2,1,0:T(8,128)(2,1)} fusion(bf16[128,1280]{1,0:T(8,128)(2,1)S(1)} %bitcast.171, f32[64,768]{1,0:T(8,128)S(1)} %get-tuple-element.61, f32[64,768]{1,0:T(8,128)S(1)} %get-tuple-element.60, f32[64,768]{1,0:T(8,128)S(1)} %get-tuple-element.59, f32[64,768]{1,0:T(8,128)S(1)} %get-tuple-element.58, f32[64,768]{1,0:T(8,128)S(1)} %get-tuple-element.57, ...), kind=kOutput, calls=%fused_computation.9 | convolution fusion | flops 253919232 | bytes 3473408 | tf_op jit(solution)/shard_map/dot_general | solution.py:210
  77.8 1.4 %slice.68 = bf16[8,64,1280]{2,1,0:T(8,128)(2,1)S(1)} slice(bf16[8,72,1280]{2,1,0:T(8,128)(2,1)} %bitcast.184), slice={[0:8], [0:64], [0:1280]} | slice | bytes 2621440 | tf_op jit(solution)/shard_map/slice | solution.py:160
  83.7 1.8 %collective-permute-start.10 = (bf16[2,64,96]{1,2,0:T(8,128)(2,1)S(1)}, bf16[2,64,96]{1,2,0:T(8,128)(2,1)S(1)}, u32[]{:S(2)}, u32[]{:S(2)}) collective-permute-start(bf16[2,64,96]{1,2,0:T(8,128)(2,1)S(1)} %add_convert_fusion.7), channel_id=1, source_target_pairs={{0,16},{8,24},{16,0},{24,8},{1,17},{9,25},{17,1},{25,9},{2,18},{10... | collective-permute-start | bytes 73736 | tf_op jit(solution)/shard_map/ppermute | solution.py:80
  86.0 1.8 %collective-permute-start.16 = (bf16[2,64,96]{1,2,0:T(8,128)(2,1)S(1)}, bf16[2,64,96]{1,2,0:T(8,128)(2,1)S(1)}, u32[]{:S(2)}, u32[]{:S(2)}) collective-permute-start(bf16[2,64,96]{1,2,0:T(8,128)(2,1)S(1)} %add_convert_fusion.5), channel_id=1, source_target_pairs={{0,16},{8,24},{16,0},{24,8},{1,17},{9,25},{17,1},{25,9},{2,18},{10... | collective-permute-start | bytes 73736 | tf_op jit(solution)/shard_map/ppermute | solution.py:80
  88.4 1.4 %collective-permute-done.22 = bf16[2,64,96]{1,2,0:T(8,128)(2,1)S(1)} collective-permute-done((bf16[2,64,96]{1,2,0:T(8,128)(2,1)S(1)}, bf16[2,64,96]{1,2,0:T(8,128)(2,1)S(1)}, u32[]{:S(2)}, u32[]{:S(2)}) %collective-permute-start.22) | collective-permute-done | bytes 24608 | tf_op jit(solution)/shard_map/ppermute | solution.py:80
  90.8 1.3 collective-permute-done.13
  95.7 1.6 %copy.99 = f32[1,2,64,96]{3,2,1,0:T(8,128)} copy(f32[1,2,64,96]{2,3,1,0:T(8,128)} %get-tuple-element.62) | data formatting | bytes 98304 | tf_op jit(solution)/shard_map/jit(dynamic_index_in_dim)/dynamic_slice | solution.py:87
  97.3 1.6 %copy.100 = f32[1,2,64,96]{3,2,1,0:T(8,128)} copy(f32[1,2,64,96]{2,3,1,0:T(8,128)} %get-tuple-element.63) | data formatting | bytes 98304 | tf_op jit(solution)/shard_map/jit(dynamic_index_in_dim)/dynamic_slice | solution.py:88
  98.9 1.6 %copy.96 = f32[1,2,64,96]{3,2,1,0:T(8,128)} copy(f32[1,2,64,96]{2,3,1,0:T(8,128)} %get-tuple-element.68) | data formatting | bytes 98304 | tf_op jit(solution)/shard_map/jit(dynamic_index_in_dim)/dynamic_slice | solution.py:87
  100.5 1.6 %copy.97 = f32[1,2,64,96]{3,2,1,0:T(8,128)} copy(f32[1,2,64,96]{2,3,1,0:T(8,128)} %get-tuple-element.69) | data formatting | bytes 98304 | tf_op jit(solution)/shard_map/jit(dynamic_index_in_dim)/dynamic_slice | solution.py:88
  104.5 1.7 %fusion.64 = (f32[2,128]{1,0:T(2,128)}, f32[2,128,96]{2,1,0:T(8,128)S(1)}, f32[2,128,96]{2,1,0:T(8,128)S(1)}) fusion(f32[2,64,96]{2,1,0:T(8,128)} %bitcast.195, f32[2,64,96]{2,1,0:T(8,128)} %bitcast.194, f32[2,64,96]{2,1,0:T(8,128)} %bitcast.197, f32[2,64,96]{2,1,0:T(8,128)} %bitcast.196, f32[2,64,96]{2,1,0:T(8,128)} %bitcast.199, f32[2,64,96]{2,1,0:T(8,128)} %bitcast.198), kind=kLoop, calls=%fused_computation.139 | loop fusion | flops 294656 | bytes 492544 | tf_op jit(solution)/shard_map/reduce_sum | solution.py:220
  106.2 1.3 reshape.230
  108.8 4.2 %all-to-all-start.1 = ((f32[8,3,16]{2,1,0:T(4,128)}), f32[8,3,16]{2,1,0:T(4,128)}, u32[]{:S(2)}, u32[]{:S(2)}) async-start(f32[8,3,16]{2,1,0:T(4,128)} %copy.101), calls=%async_computation.1 | async-start | bytes 32768 | tf_op jit(solution)/shard_map/all_to_all | solution.py:240
  113.9 2.2 %convert_reduce_fusion.1 = f32[2,1280,96]{1,2,0:T(8,128)} fusion(f32[2,8,16,96]{3,2,1,0:T(8,128)S(1)} %bitcast.207, f32[2,8,16,96]{3,2,1,0:T(8,128)S(1)} %bitcast.191, bf16[2,2,8,16,1280]{4,3,2,1,0:T(8,128)(2,1)S(1)} %bitcast.173), kind=kOutput, calls=%fused_computation.1 | convolution fusion | flops 68714496 | bytes 1900544 | tf_op jit(solution)/shard_map/jbcd,jbch->jbdh/dot_general | solution.py:228
  116.1 2.2 %convert_reduce_fusion.2 = f32[2,1280,96]{1,2,0:T(8,128)} fusion(f32[2,8,16,96]{3,2,1,0:T(8,128)S(1)} %bitcast.192, f32[2,8,16,96]{3,2,1,0:T(8,128)S(1)} %bitcast.208, f32[2,8,16,96]{3,2,1,0:T(8,128)S(1)} %bitcast.189, bf16[2,2,8,16,1280]{4,3,2,1,0:T(8,128)(2,1)S(1)} %bitcast.174), kind=kOutput, calls=%fused_computation.2 | convolution fusion | flops 68812800 | bytes 2031616 | tf_op jit(solution)/shard_map/jbcd,jbch->jbdh/dot_general | solution.py:227
  118.2 2.2 %convert_reduce_fusion = f32[2,96,1280]{2,1,0:T(8,128)} fusion(f32[2,8,16]{2,1,0:T(8,128)S(1)} %copy.91, f32[2,8,16,96]{3,2,1,0:T(8,128)S(1)} %bitcast.190, f32[2,8,16,96]{3,2,1,0:T(8,128)S(1)} %bitcast.193, bf16[2,2,8,16,1280]{4,3,2,1,0:T(8,128)(2,1)S(1)} %bitcast.175), kind=kOutput, calls=%fused_computation | convolution fusion | flops 69697536 | bytes 1908736 | tf_op jit(solution)/shard_map/jbch,jbcd->jbhd/dot_general | solution.py:229
  121.2 1.1 convolution_reduce_fusion.1
  (173 shorter events, 37.4 us)
Async XLA Ops:
  7.2 42.9 %copy-start = (bf16[1,768,1280]{2,1,0:T(8,128)(2,1)S(1)}, bf16[1,768,1280]{2,1,0:T(8,128)(2,1)}, u32[]{:S(2)}) copy-start(bf16[1,768,1280]{2,1,0:T(8,128)(2,1)} %param.18) | copy-start | bytes 5898244
  7.2 8.8 %copy-start.1 = (bf16[256,1280]{1,0:T(8,128)(2,1)S(1)}, bf16[256,1280]{1,0:T(8,128)(2,1)}, u32[]{:S(2)}) copy-start(bf16[256,1280]{1,0:T(8,128)(2,1)} %param.12) | copy-start | bytes 1966084
  7.2 9.1 %copy-start.2 = (bf16[256,1280]{1,0:T(8,128)(2,1)S(1)}, bf16[256,1280]{1,0:T(8,128)(2,1)}, u32[]{:S(2)}) copy-start(bf16[256,1280]{1,0:T(8,128)(2,1)} %param.11) | copy-start | bytes 1966084
  14.9 11.1 %copy-start.9 = (pred[1536]{0:T(1024)(128)(4,1)}, pred[1536]{0:T(1024)(128)(4,1)S(1)}, u32[]{:S(2)}) copy-start(pred[1536]{0:T(1024)(128)(4,1)S(1)} %get-tuple-element.89) | copy-start | bytes 4612
  17.5 32.3 %all-to-all-start = ((bf16[8,40,1280]{2,1,0:T(8,128)(2,1)}), bf16[8,40,1280]{2,1,0:T(8,128)(2,1)S(1)}, u32[]{:S(2)}, u32[]{:S(2)}) async-start(bf16[8,40,1280]{2,1,0:T(8,128)(2,1)} %pad_maximum_fusion), calls=%async_computation | async-start | bytes 1638400 | tf_op jit(solution)/shard_map/all_to_all | solution.py:145
  24.8 52.1 %all-gather.3.cloned.1.call-start = ((), (), s32[]{:S(2)}) async-start(), calls=%async_computation.2 | async-start | bytes 1658880 | tf_op jit(solution)/shard_map/all_gather | solution.py:125
  50.9 3.5 %collective-permute-start = (bf16[64,768]{1,0:T(8,128)(2,1)S(1)}, bf16[64,768]{1,0:T(8,128)(2,1)S(1)}, u32[]{:S(2)}, u32[]{:S(2)}) collective-permute-start(bf16[64,768]{1,0:T(8,128)(2,1)S(1)} %constant_dynamic-slice_fusion.7), channel_id=1, source_target_pairs={{0,8},{8,0},{16,24},{24,16},{1,9},{9,1},{17,25},{25,17},{2,10},{10... | collective-permute-start | bytes 294920 | tf_op jit(solution)/shard_map/ppermute | solution.py:74
  51.9 4.4 %collective-permute-start.18 = (bf16[64,768]{1,0:T(8,128)(2,1)S(1)}, bf16[64,768]{1,0:T(8,128)(2,1)S(1)}, u32[]{:S(2)}, u32[]{:S(2)}) collective-permute-start(bf16[64,768]{1,0:T(8,128)(2,1)S(1)} %constant_dynamic-slice_fusion.1), channel_id=1, source_target_pairs={{0,8},{8,0},{16,24},{24,16},{1,9},{9,1},{17,25},{25,17},{2,10},{10... | collective-permute-start | bytes 294920 | tf_op jit(solution)/shard_map/ppermute | solution.py:74
  52.9 3.7 %collective-permute-start.6 = (bf16[64,768]{1,0:T(8,128)(2,1)S(1)}, bf16[64,768]{1,0:T(8,128)(2,1)S(1)}, u32[]{:S(2)}, u32[]{:S(2)}) collective-permute-start(bf16[64,768]{1,0:T(8,128)(2,1)S(1)} %constant_dynamic-slice_fusion.5), channel_id=1, source_target_pairs={{0,8},{8,0},{16,24},{24,16},{1,9},{9,1},{17,25},{25,17},{2,10},{10... | collective-permute-start | bytes 294920 | tf_op jit(solution)/shard_map/ppermute | solution.py:74
  54.0 4.5 %collective-permute-start.3 = (bf16[64,768]{1,0:T(8,128)(2,1)S(1)}, bf16[64,768]{1,0:T(8,128)(2,1)S(1)}, u32[]{:S(2)}, u32[]{:S(2)}) collective-permute-start(bf16[64,768]{1,0:T(8,128)(2,1)S(1)} %constant_dynamic-slice_fusion.6), channel_id=1, source_target_pairs={{0,8},{8,0},{16,24},{24,16},{1,9},{9,1},{17,25},{25,17},{2,10},{10... | collective-permute-start | bytes 294920 | tf_op jit(solution)/shard_map/ppermute | solution.py:74
  54.5 5.5 %collective-permute-start.1 = (bf16[64,768]{1,0:T(8,128)(2,1)S(1)}, bf16[64,768]{1,0:T(8,128)(2,1)S(1)}, u32[]{:S(2)}, u32[]{:S(2)}) collective-permute-start(bf16[64,768]{1,0:T(8,128)(2,1)S(1)} %add_convert_fusion.3), channel_id=1, source_target_pairs={{0,16},{8,24},{16,0},{24,8},{1,17},{9,25},{17,1},{25,9},{2,18},{10... | collective-permute-start | bytes 294920 | tf_op jit(solution)/shard_map/ppermute | solution.py:80
  56.3 5.8 %collective-permute-start.19 = (bf16[64,768]{1,0:T(8,128)(2,1)S(1)}, bf16[64,768]{1,0:T(8,128)(2,1)S(1)}, u32[]{:S(2)}, u32[]{:S(2)}) collective-permute-start(bf16[64,768]{1,0:T(8,128)(2,1)S(1)} %add_convert_fusion), channel_id=1, source_target_pairs={{0,16},{8,24},{16,0},{24,8},{1,17},{9,25},{17,1},{25,9},{2,18},{10... | collective-permute-start | bytes 294920 | tf_op jit(solution)/shard_map/ppermute | solution.py:80
  56.7 7.5 %collective-permute-start.7 = (bf16[64,768]{1,0:T(8,128)(2,1)S(1)}, bf16[64,768]{1,0:T(8,128)(2,1)S(1)}, u32[]{:S(2)}, u32[]{:S(2)}) collective-permute-start(bf16[64,768]{1,0:T(8,128)(2,1)S(1)} %add_convert_fusion.1), channel_id=1, source_target_pairs={{0,16},{8,24},{16,0},{24,8},{1,17},{9,25},{17,1},{25,9},{2,18},{10... | collective-permute-start | bytes 294920 | tf_op jit(solution)/shard_map/ppermute | solution.py:80
  58.5 7.2 %collective-permute-start.4 = (bf16[64,768]{1,0:T(8,128)(2,1)S(1)}, bf16[64,768]{1,0:T(8,128)(2,1)S(1)}, u32[]{:S(2)}, u32[]{:S(2)}) collective-permute-start(bf16[64,768]{1,0:T(8,128)(2,1)S(1)} %add_convert_fusion.2), channel_id=1, source_target_pairs={{0,16},{8,24},{16,0},{24,8},{1,17},{9,25},{17,1},{25,9},{2,18},{10... | collective-permute-start | bytes 294920 | tf_op jit(solution)/shard_map/ppermute | solution.py:80
  60.7 8.1 %collective-permute-start.2 = (f32[64,768]{1,0:T(8,128)}, f32[64,768]{1,0:T(8,128)}, u32[]{:S(2)}, u32[]{:S(2)}) collective-permute-start(f32[64,768]{1,0:T(8,128)} %get-tuple-element.72), channel_id=1, source_target_pairs={{0,8},{8,0},{16,24},{24,16},{1,9},{9,1},{17,25},{25,17},{2,10},{10... | collective-permute-start | bytes 589832 | tf_op jit(solution)/shard_map/ppermute | solution.py:83
  62.1 3.7 %collective-permute-start.20 = (f32[64,768]{1,0:T(8,128)S(1)}, f32[64,768]{1,0:T(8,128)S(1)}, u32[]{:S(2)}, u32[]{:S(2)}) collective-permute-start(f32[64,768]{1,0:T(8,128)S(1)} %get-tuple-element.70), channel_id=1, source_target_pairs={{0,8},{8,0},{16,24},{24,16},{1,9},{9,1},{17,25},{25,17},{2,10},{10... | collective-permute-start | bytes 589832 | tf_op jit(solution)/shard_map/ppermute | solution.py:83
  64.2 1.7 %collective-permute-start.8 = (f32[64,768]{1,0:T(8,128)S(1)}, f32[64,768]{1,0:T(8,128)S(1)}, u32[]{:S(2)}, u32[]{:S(2)}) collective-permute-start(f32[64,768]{1,0:T(8,128)S(1)} %get-tuple-element.76), channel_id=1, source_target_pairs={{0,8},{8,0},{16,24},{24,16},{1,9},{9,1},{17,25},{25,17},{2,10},{10... | collective-permute-start | bytes 589832 | tf_op jit(solution)/shard_map/ppermute | solution.py:83
  65.7 1.5 %collective-permute-start.5 = (f32[64,768]{1,0:T(8,128)S(1)}, f32[64,768]{1,0:T(8,128)S(1)}, u32[]{:S(2)}, u32[]{:S(2)}) collective-permute-start(f32[64,768]{1,0:T(8,128)S(1)} %get-tuple-element.74), channel_id=1, source_target_pairs={{0,8},{8,0},{16,24},{24,16},{1,9},{9,1},{17,25},{25,17},{2,10},{10... | collective-permute-start | bytes 589832 | tf_op jit(solution)/shard_map/ppermute | solution.py:83
  79.6 2.0 %copy-start.7 = (bf16[2,1280,96]{1,2,0:T(8,128)(2,1)S(1)}, bf16[2,1280,96]{1,2,0:T(8,128)(2,1)}, u32[]{:S(2)}) copy-start(bf16[2,1280,96]{1,2,0:T(8,128)(2,1)} %param.20) | copy-start | bytes 1474564
  82.3 1.3 collective-permute-start.9
  82.6 2.9 %collective-permute-start.21 = (bf16[2,64,96]{1,2,0:T(8,128)(2,1)S(1)}, bf16[2,64,96]{1,2,0:T(8,128)(2,1)S(1)}, u32[]{:S(2)}, u32[]{:S(2)}) collective-permute-start(bf16[2,64,96]{1,2,0:T(8,128)(2,1)S(1)} %constant_dynamic-slice_fusion), channel_id=1, source_target_pairs={{0,8},{8,0},{16,24},{24,16},{1,9},{9,1},{17,25},{25,17},{2,10},{10... | collective-permute-start | bytes 73736 | tf_op jit(solution)/shard_map/ppermute | solution.py:74
  83.0 2.9 %collective-permute-start.15 = (bf16[2,64,96]{1,2,0:T(8,128)(2,1)S(1)}, bf16[2,64,96]{1,2,0:T(8,128)(2,1)S(1)}, u32[]{:S(2)}, u32[]{:S(2)}) collective-permute-start(bf16[2,64,96]{1,2,0:T(8,128)(2,1)S(1)} %constant_dynamic-slice_fusion.2), channel_id=1, source_target_pairs={{0,8},{8,0},{16,24},{24,16},{1,9},{9,1},{17,25},{25,17},{2,10},{10... | collective-permute-start | bytes 73736 | tf_op jit(solution)/shard_map/ppermute | solution.py:74
  83.2 4.7 %collective-permute-start.12 = (bf16[2,64,96]{1,2,0:T(8,128)(2,1)S(1)}, bf16[2,64,96]{1,2,0:T(8,128)(2,1)S(1)}, u32[]{:S(2)}, u32[]{:S(2)}) collective-permute-start(bf16[2,64,96]{1,2,0:T(8,128)(2,1)S(1)} %constant_dynamic-slice_fusion.3), channel_id=1, source_target_pairs={{0,8},{8,0},{16,24},{24,16},{1,9},{9,1},{17,25},{25,17},{2,10},{10... | collective-permute-start | bytes 73736 | tf_op jit(solution)/shard_map/ppermute | solution.py:74
  83.7 4.6 %collective-permute-start.10 = (bf16[2,64,96]{1,2,0:T(8,128)(2,1)S(1)}, bf16[2,64,96]{1,2,0:T(8,128)(2,1)S(1)}, u32[]{:S(2)}, u32[]{:S(2)}) collective-permute-start(bf16[2,64,96]{1,2,0:T(8,128)(2,1)S(1)} %add_convert_fusion.7), channel_id=1, source_target_pairs={{0,16},{8,24},{16,0},{24,8},{1,17},{9,25},{17,1},{25,9},{2,18},{10... | collective-permute-start | bytes 73736 | tf_op jit(solution)/shard_map/ppermute | solution.py:80
  85.6 4.2 %collective-permute-start.22 = (bf16[2,64,96]{1,2,0:T(8,128)(2,1)S(1)}, bf16[2,64,96]{1,2,0:T(8,128)(2,1)S(1)}, u32[]{:S(2)}, u32[]{:S(2)}) collective-permute-start(bf16[2,64,96]{1,2,0:T(8,128)(2,1)S(1)} %add_convert_fusion.4), channel_id=1, source_target_pairs={{0,16},{8,24},{16,0},{24,8},{1,17},{9,25},{17,1},{25,9},{2,18},{10... | collective-permute-start | bytes 73736 | tf_op jit(solution)/shard_map/ppermute | solution.py:80
  86.0 4.7 %collective-permute-start.16 = (bf16[2,64,96]{1,2,0:T(8,128)(2,1)S(1)}, bf16[2,64,96]{1,2,0:T(8,128)(2,1)S(1)}, u32[]{:S(2)}, u32[]{:S(2)}) collective-permute-start(bf16[2,64,96]{1,2,0:T(8,128)(2,1)S(1)} %add_convert_fusion.5), channel_id=1, source_target_pairs={{0,16},{8,24},{16,0},{24,8},{1,17},{9,25},{17,1},{25,9},{2,18},{10... | collective-permute-start | bytes 73736 | tf_op jit(solution)/shard_map/ppermute | solution.py:80
  88.0 4.2 %collective-permute-start.13 = (bf16[2,64,96]{1,2,0:T(8,128)(2,1)S(1)}, bf16[2,64,96]{1,2,0:T(8,128)(2,1)S(1)}, u32[]{:S(2)}, u32[]{:S(2)}) collective-permute-start(bf16[2,64,96]{1,2,0:T(8,128)(2,1)S(1)} %add_convert_fusion.6), channel_id=1, source_target_pairs={{0,16},{8,24},{16,0},{24,8},{1,17},{9,25},{17,1},{25,9},{2,18},{10... | collective-permute-start | bytes 73736 | tf_op jit(solution)/shard_map/ppermute | solution.py:80
  88.3 4.5 %collective-permute-start.11 = (f32[2,64,96]{1,2,0:T(8,128)S(1)}, f32[2,64,96]{1,2,0:T(8,128)S(1)}, u32[]{:S(2)}, u32[]{:S(2)}) collective-permute-start(f32[2,64,96]{1,2,0:T(8,128)S(1)} %get-tuple-element.85), channel_id=1, source_target_pairs={{0,8},{8,0},{16,24},{24,16},{1,9},{9,1},{17,25},{25,17},{2,10},{10... | collective-permute-start | bytes 147464 | tf_op jit(solution)/shard_map/ppermute | solution.py:83
  89.8 3.1 %collective-permute-start.23 = (f32[2,64,96]{1,2,0:T(8,128)S(1)}, f32[2,64,96]{1,2,0:T(8,128)S(1)}, u32[]{:S(2)}, u32[]{:S(2)}) collective-permute-start(f32[2,64,96]{1,2,0:T(8,128)S(1)} %get-tuple-element.81), channel_id=1, source_target_pairs={{0,8},{8,0},{16,24},{24,16},{1,9},{9,1},{17,25},{25,17},{2,10},{10... | collective-permute-start | bytes 147464 | tf_op jit(solution)/shard_map/ppermute | solution.py:83
  90.7 2.9 %collective-permute-start.17 = (f32[2,64,96]{1,2,0:T(8,128)S(1)}, f32[2,64,96]{1,2,0:T(8,128)S(1)}, u32[]{:S(2)}, u32[]{:S(2)}) collective-permute-start(f32[2,64,96]{1,2,0:T(8,128)S(1)} %get-tuple-element.87), channel_id=1, source_target_pairs={{0,8},{8,0},{16,24},{24,16},{1,9},{9,1},{17,25},{25,17},{2,10},{10... | collective-permute-start | bytes 147464 | tf_op jit(solution)/shard_map/ppermute | solution.py:83
  92.8 9.3 %collective-permute-start.14 = (f32[2,64,96]{1,2,0:T(8,128)}, f32[2,64,96]{1,2,0:T(8,128)}, u32[]{:S(2)}, u32[]{:S(2)}) collective-permute-start(f32[2,64,96]{1,2,0:T(8,128)} %get-tuple-element.83), channel_id=1, source_target_pairs={{0,8},{8,0},{16,24},{24,16},{1,9},{9,1},{17,25},{25,17},{2,10},{10... | collective-permute-start | bytes 147464 | tf_op jit(solution)/shard_map/ppermute | solution.py:83
  108.8 11.6 %all-to-all-start.1 = ((f32[8,3,16]{2,1,0:T(4,128)}), f32[8,3,16]{2,1,0:T(4,128)}, u32[]{:S(2)}, u32[]{:S(2)}) async-start(f32[8,3,16]{2,1,0:T(4,128)} %copy.101), calls=%async_computation.1 | async-start | bytes 32768 | tf_op jit(solution)/shard_map/all_to_all | solution.py:240
  (6 other events, 7.7 us)
Sparse Core Ops, SparseCore 0:
  29.8 45.5 all-gather.2

commit v8 on v4

--- a/solution.py
+++ b/solution.py
@@ -4,31 +4,32 @@
 from jax.sharding import PartitionSpec as P
 
 
-def route_table(flat_ids, targets, capacity):
-    matches = (flat_ids[:, None] == targets[None, :]).astype(jnp.int32)
-    rank_of = jnp.cumsum(matches, axis=0) - 1
-    slot_of = jnp.sum(matches * rank_of, axis=1)
-    owner_of = jnp.sum(matches * jnp.arange(targets.shape[0], dtype=jnp.int32)[None, :], axis=1)
-    usable = jnp.sum(matches, axis=1) > 0
-    row_of = owner_of * capacity + slot_of
-    rows_total = targets.shape[0] * capacity
-    route_map = (row_of[None, :] == jnp.arange(rows_total, dtype=jnp.int32)[:, None]) & usable[
-        None, :
-    ]
-    return route_map.astype(jnp.float32)
-
-
-def gather_rows(route_map, tokens, cotangent, flat_weights, tok_rows, top_count):
-    per_token = jnp.sum(route_map.reshape(route_map.shape[0], tok_rows, top_count), axis=2)
-    token_map = per_token.astype(jnp.bfloat16)
+def token_table(expert_ids, targets, capacity):
+    hit = expert_ids.T[:, None, :] == targets[None, :, None]
+    tok_hit = jnp.any(hit, axis=0)
+    rank = jnp.cumsum(tok_hit.astype(jnp.int32), axis=1) - 1
+    slots = jnp.arange(capacity, dtype=jnp.int32)
+    sel = (rank[:, None, :] == slots[None, :, None]) & tok_hit[:, None, :]
+    return hit, sel
+
+
+def gather_rows(hit, sel, tokens, cotangent, gate_weights):
+    count, capacity = sel.shape[0], sel.shape[1]
+    token_map = sel.reshape(count * capacity, -1).astype(jnp.bfloat16)
     feat_rows = jnp.dot(token_map, tokens, preferred_element_type=jnp.float32).astype(jnp.bfloat16)
     cotan_rows = jnp.dot(token_map, cotangent, preferred_element_type=jnp.float32).astype(
         jnp.bfloat16
     )
-    scale_rows = jnp.dot(
-        route_map, flat_weights.astype(jnp.float32), precision=lax.Precision.HIGHEST
-    )
-    return (feat_rows, cotan_rows, scale_rows.astype(jnp.bfloat16))
+    per_token = jnp.sum(
+        jnp.where(hit, gate_weights.T.astype(jnp.float32)[:, None, :], 0.0), axis=0
+    )
+    scale = jnp.sum(jnp.where(sel, per_token[:, None, :], 0.0), axis=2)
+    return feat_rows, cotan_rows, scale.reshape(-1).astype(jnp.bfloat16)
+
+
+def scatter_routes(hit, sel, values):
+    per_token = jnp.sum(jnp.where(sel, values[:, :, None], 0.0), axis=1)
+    return jnp.sum(jnp.where(hit, per_token[None, :, :], 0.0), axis=1).T
 
 
 def swiglu_back(pre_gate, pre_up, grad_hidden):
@@ -61,15 +62,10 @@
         return [r.astype(jnp.float32) for r in rounded]
     if size & (size - 1) or any(p.shape[a] % 2 for p, a in zip(parts, axes)):
         return [lax.psum(r, axis_name).astype(jnp.float32) for r in rounded]
-    half_of = [p.shape[a] // 2 for p, a in zip(parts, axes)]
-    core = lax.axis_index(axis_name) % 2
-    keep = [
-        lax.dynamic_slice_in_dim(r, core * h, h, axis=a) for r, h, a in zip(rounded, half_of, axes)
-    ]
-    send = [
-        lax.dynamic_slice_in_dim(r, (1 - core) * h, h, axis=a)
-        for r, h, a in zip(rounded, half_of, axes)
-    ]
+    first_core = lax.axis_index(axis_name) % 2 == 0
+    halves = [jnp.split(r, 2, axis=a) for r, a in zip(rounded, axes)]
+    keep = [jnp.where(first_core, lo, hi) for lo, hi in halves]
+    send = [jnp.where(first_core, hi, lo) for lo, hi in halves]
     swap = [(i, i ^ 1) for i in range(size)]
     got = lax.ppermute(send, axis_name, swap)
     sums = [k.astype(jnp.float32) + g.astype(jnp.float32) for k, g in zip(keep, got)]
@@ -83,9 +79,8 @@
     other = lax.ppermute(sums, axis_name, swap)
     full = []
     for s, o, a in zip(sums, other, axes):
-        pair = jnp.stack([s, o])
-        first = lax.dynamic_index_in_dim(pair, core, axis=0, keepdims=False)
-        second = lax.dynamic_index_in_dim(pair, 1 - core, axis=0, keepdims=False)
+        first = jnp.where(first_core, s, o)
+        second = jnp.where(first_core, o, s)
         full.append(jnp.concatenate([first, second], axis=a))
     return full
 
@@ -108,13 +103,8 @@
     cold_count = lax.axis_size("ep")
     hot_count = hot_ids.shape[0]
     capacity = tok_rows // 16
-    flat_ids = expert_ids.reshape(-1)
-    flat_weights = gate_weights.reshape(-1)
-    cold_map = route_table(flat_ids, jnp.arange(cold_count, dtype=jnp.int32), capacity)
-    hot_map = route_table(flat_ids, hot_ids, capacity)
-    hot_feats, hot_cotan, hot_scale = gather_rows(
-        hot_map, tokens, cotangent, flat_weights, tok_rows, top_count
-    )
+    hot_hit, hot_sel = token_table(expert_ids, hot_ids, capacity)
+    hot_feats, hot_cotan, hot_scale = gather_rows(hot_hit, hot_sel, tokens, cotangent, gate_weights)
     hot_rows = hot_count * capacity
     scale_lines = -(-hot_rows // slice_width)
     scale_lines = -(-scale_lines // 8) * 8
@@ -125,8 +115,11 @@
     gathered = lax.all_gather(
         jnp.concatenate([hot_feats, hot_cotan, scale_block], axis=0), "ep", axis=0, tiled=False
     )
+    cold_hit, cold_sel = token_table(
+        expert_ids, jnp.arange(cold_count, dtype=jnp.int32), capacity
+    )
     cold_feats, cold_cotan, cold_scale = gather_rows(
-        cold_map, tokens, cotangent, flat_weights, tok_rows, top_count
+        cold_hit, cold_sel, tokens, cotangent, gate_weights
     )
     cold_lines = -(-capacity // slice_width)
     cold_lines = -(-cold_lines // 8) * 8
@@ -219,11 +212,9 @@
     route_back = lax.all_to_all(route_parts, "ep", split_axis=0, concat_axis=0, tiled=True)
     cold_back = route_back[:, 0, :]
     hot_route = jnp.sum(route_back[:, 1:, :], axis=0)
-    route_flat = jnp.dot(cold_back.reshape(-1), cold_map, precision=lax.Precision.HIGHEST)
-    route_flat = route_flat + jnp.dot(
-        hot_route.reshape(-1), hot_map, precision=lax.Precision.HIGHEST
-    )
-    gate_weight_grad = route_flat.reshape(tok_rows, top_count)
+    gate_weight_grad = scatter_routes(cold_hit, cold_sel, cold_back) + scatter_routes(
+        hot_hit, hot_sel, hot_route
+    )
     return (
         grad_gate_cold[None].astype(jnp.bfloat16),
         grad_up_cold[None].astype(jnp.bfloat16),

time: 129 us -> 124 us (0.961)
  local copies, waits for them, and re-layouts: 19.2 us -> 12.6 us
  other arithmetic: 15.2 us -> 16.6 us
    dynamic_slice x8 -> x0, local copies, waits for them, and re-layouts: 3.53 us -> none  [the longest x1 1.6 us: grp_sum_rounded(): first = lax.dynamic_index_in_dim(pair, core, axis=0, keepdims=False)]
    another operation x5 -> x4, other arithmetic: 4.85 us -> 1.42 us
    dot_general x4 -> x0, matrix products: 2.36 us -> none  [the longest x1 1.05 us: body(): jnp.dot(cold_back.reshape(-1), cold_map, precision=lax.Precision.HIGHEST)]
    select_n x0 -> x12, other arithmetic: none -> 2.32 us  [the longest x6 2.02 us: grp_sum_rounded(): first = jnp.where(first_core, s, o)]
    reduce_sum x4 -> x8, other arithmetic: 1.02 us -> 3.31 us  [the longest x2 1.53 us: scatter_routes(): per_token = jnp.sum(jnp.where(sel, values[:, :, None], 0.0), axis=1)]
    unnamed x37 -> x49, local copies, waits for them, and re-layouts: 6.08 us -> 3.86 us
    add x4 -> x0, local copies, waits for them, and re-layouts: 2.01 us -> none  [route_table(): row_of = owner_of * capacity + slot_of]
    concatenate x2 -> x3, local copies, waits for them, and re-layouts: 1.08 us -> 2.73 us  [grp_sum_rounded(): full.append(jnp.concatenate([first, second], axis=a))]
  transfers between devices with their start and end apart: 23 -> 23, of which waited for: 12 -> 11; matrix products, arithmetic and copies ran while one was open for 22% -> 23% of each run, Pallas kernels for 0% -> 0%
where the time goes in v8:
time: 124 us; the launch traced here: 123 us
  waiting for transfers between devices  33.9 us (27%)
  starting transfers between devices  23 us (19%)
  matrix products  22.6 us (18%)
  other arithmetic  16.6 us (13%)
  between operations  14.7 us (12%)
  local copies, waits for them, and re-layouts  12.6 us (10%)
    all_to_all x1, waiting for transfers between devices, body(): lax.all_to_all(outgoing, 'ep', split_axis=0, concat_axis=0, tiled=True)  21 us
    ppermute x6, starting transfers between devices, grp_sum_rounded(): got = lax.ppermute(mine, axis_name, partner)  8.48 us
    all_to_all x1, starting transfers between devices, body(): lax.all_to_all(outgoing, 'ep', split_axis=0, concat_axis=0, tiled=True)  7.28 us
    ppermute x6, waiting for transfers between devices, grp_sum_rounded(): got = lax.ppermute(mine, axis_name, partner)  6.21 us
    all_to_all x1, starting transfers between devices, body(): lax.all_to_all(route_parts, 'ep', split_axis=0, concat_axis=0, tiled=True)  3.94 us
    unnamed x49, local copies, waits for them, and re-layouts  3.86 us
    all_to_all x1, waiting for transfers between devices, body(): lax.all_to_all(route_parts, 'ep', split_axis=0, concat_axis=0, tiled=True)  3.65 us
    dot_general x1, matrix products, body(): jnp.einsum('jbcd,jbch->jbdh', feat_b, bg_b, preferred_element_type=jnp.fl...  3.14 us
  transfers between devices with their start and end apart: 23, of which 11 were waited for; matrix products, arithmetic and copies ran while one was open for 23% of the time, Pallas kernels for 0%

profile of v8, /device:TPU:0, one launch (start us, length us, event | category | flops | bytes accessed | tf_op | source)
XLA Modules:
  0.0 123.4 jit_solution(5121440662834304058)
XLA Ops:
  10.8 1.3 %convolution_convert_fusion.6 = bf16[128,1280]{1,0:T(8,128)(2,1)S(1)} fusion(pred[128,256]{1,0:T(32,128)(4,1)S(1)} %fusion.35, bf16[256,1280]{1,0:T(8,128)(2,1)} %param.12), kind=kOutput, calls=%fused_computation.13 | convolution fusion | flops 84049920 | bytes 1015808 | tf_op jit(solution)/shard_map/dot_general | solution.py:20
  12.4 0.9 pad_maximum_fusion
  13.4 7.3 %all-to-all-start = ((bf16[8,40,1280]{2,1,0:T(8,128)(2,1)}), bf16[8,40,1280]{2,1,0:T(8,128)(2,1)S(1)}, u32[]{:S(2)}, u32[]{:S(2)}) async-start(bf16[8,40,1280]{2,1,0:T(8,128)(2,1)} %pad_maximum_fusion), calls=%async_computation | async-start | bytes 1638400 | tf_op jit(solution)/shard_map/all_to_all | solution.py:138
  22.9 1.3 %convolution_convert_fusion.9 = bf16[32,1280]{1,0:T(8,128)(2,1)S(1)} fusion(pred[32,256]{1,0:T(32,128)(4,1)S(1)} %fusion.39, bf16[256,1280]{1,0:T(8,128)(2,1)} %param.11), kind=kOutput, calls=%fused_computation.16 | convolution fusion | flops 21012480 | bytes 745472 | tf_op jit(solution)/shard_map/dot_general | solution.py:19
  25.0 21.0 %all-to-all-done = bf16[8,40,1280]{2,1,0:T(8,128)(2,1)S(1)} async-done(((bf16[8,40,1280]{2,1,0:T(8,128)(2,1)}), bf16[8,40,1280]{2,1,0:T(8,128)(2,1)S(1)}, u32[]{:S(2)}, u32[]{:S(2)}) %all-to-all-start) | async-done | bytes 819232 | tf_op jit(solution)/shard_map/all_to_all | solution.py:138
  50.3 2.3 %collective-permute-start.1 = (bf16[64,768]{1,0:T(8,128)(2,1)S(1)}, bf16[64,768]{1,0:T(8,128)(2,1)S(1)}, u32[]{:S(2)}, u32[]{:S(2)}) collective-permute-start(bf16[64,768]{1,0:T(8,128)(2,1)S(1)} %add_convert_fusion.2), channel_id=1, source_target_pairs={{0,16},{8,24},{16,0},{24,8},{1,17},{9,25},{17,1},{25,9},{2,18},{10... | collective-permute-start | bytes 294920 | tf_op jit(solution)/shard_map/ppermute | solution.py:76
  52.8 2.1 %collective-permute-start.4 = (bf16[64,768]{1,0:T(8,128)(2,1)S(1)}, bf16[64,768]{1,0:T(8,128)(2,1)S(1)}, u32[]{:S(2)}, u32[]{:S(2)}) collective-permute-start(bf16[64,768]{1,0:T(8,128)(2,1)S(1)} %add_convert_fusion.1), channel_id=1, source_target_pairs={{0,16},{8,24},{16,0},{24,8},{1,17},{9,25},{17,1},{25,9},{2,18},{10... | collective-permute-start | bytes 294920 | tf_op jit(solution)/shard_map/ppermute | solution.py:76
  54.9 1.4 %collective-permute-done.1 = bf16[64,768]{1,0:T(8,128)(2,1)S(1)} collective-permute-done((bf16[64,768]{1,0:T(8,128)(2,1)S(1)}, bf16[64,768]{1,0:T(8,128)(2,1)S(1)}, u32[]{:S(2)}, u32[]{:S(2)}) %collective-permute-start.1) | collective-permute-done | bytes 98336 | tf_op jit(solution)/shard_map/ppermute | solution.py:76
  57.0 1.5 %collective-permute-done.7 = bf16[64,768]{1,0:T(8,128)(2,1)S(1)} collective-permute-done((bf16[64,768]{1,0:T(8,128)(2,1)S(1)}, bf16[64,768]{1,0:T(8,128)(2,1)S(1)}, u32[]{:S(2)}, u32[]{:S(2)}) %collective-permute-start.7) | collective-permute-done | bytes 98336 | tf_op jit(solution)/shard_map/ppermute | solution.py:76
  58.6 1.7 %collective-permute-done.4 = bf16[64,768]{1,0:T(8,128)(2,1)S(1)} collective-permute-done((bf16[64,768]{1,0:T(8,128)(2,1)S(1)}, bf16[64,768]{1,0:T(8,128)(2,1)S(1)}, u32[]{:S(2)}, u32[]{:S(2)}) %collective-permute-start.4) | collective-permute-done | bytes 98336 | tf_op jit(solution)/shard_map/ppermute | solution.py:76
  60.4 1.4 %collective-permute-done.5 = f32[64,768]{1,0:T(8,128)S(1)} collective-permute-done((f32[64,768]{1,0:T(8,128)S(1)}, f32[64,768]{1,0:T(8,128)S(1)}, u32[]{:S(2)}, u32[]{:S(2)}) %collective-permute-start.5) | collective-permute-done | bytes 196640 | tf_op jit(solution)/shard_map/ppermute | solution.py:79
  63.1 2.9 %fusion.2 = bf16[1,768,1280]{2,1,0:T(8,128)(2,1)} fusion(bf16[128,768]{1,0:T(8,128)(2,1)S(1)} %multiply_convert_fusion.3, bf16[128,1280]{1,0:T(8,128)(2,1)} %fusion.28), kind=kOutput, calls=%fused_computation.11 | convolution fusion | flops 252641280 | bytes 2490368 | tf_op jit(solution)/shard_map/dot_general | solution.py:187
  66.1 1.0 broadcast_select_fusion.7
  67.1 2.0 %fusion.1 = bf16[1,1280,768]{2,1,0:T(8,128)(2,1)} fusion(bf16[128,1280]{1,0:T(8,128)(2,1)S(1)} %bitcast.122, f32[64,768]{1,0:T(8,128)S(1)} %get-tuple-element.12, f32[64,768]{1,0:T(8,128)S(1)} %get-tuple-element.11, f32[64,768]{1,0:T(8,128)S(1)} %get-tuple-element.16, f32[64,768]{1,0:T(8,128)S(1)} %get-tuple-element.15), kind=kOutput, calls=%fused_computation.10 | convolution fusion | flops 253427712 | bytes 3080192 | tf_op jit(solution)/shard_map/dot_general | solution.py:184
  69.0 2.0 %fusion = bf16[1,1280,768]{2,1,0:T(8,128)(2,1)} fusion(bf16[128,1280]{1,0:T(8,128)(2,1)S(1)} %bitcast.123, f32[64,768]{1,0:T(8,128)S(1)} %get-tuple-element.16, f32[64,768]{1,0:T(8,128)S(1)} %get-tuple-element.15, f32[64,768]{1,0:T(8,128)S(1)} %get-tuple-element.14, f32[64,768]{1,0:T(8,128)S(1)} %get-tuple-element.13, f32[64,768]{1,0:T(8,128)S(1)} %get-tuple-element.12, ...), kind=kOutput, calls=%fused_computation.9 | convolution fusion | flops 253919232 | bytes 3473408 | tf_op jit(solution)/shard_map/dot_general | solution.py:181
  71.1 0.9 slice_bitcast_fusion
  72.0 1.4 %slice.68 = bf16[8,64,1280]{2,1,0:T(8,128)(2,1)S(1)} slice(bf16[8,72,1280]{2,1,0:T(8,128)(2,1)} %bitcast.129), slice={[0:8], [0:64], [0:1280]} | slice | bytes 2621440 | tf_op jit(solution)/shard_map/slice | solution.py:153
  73.8 0.9 copy-done.5
  77.5 1.8 %collective-permute-start.10 = (bf16[2,64,96]{1,2,0:T(8,128)(2,1)S(1)}, bf16[2,64,96]{1,2,0:T(8,128)(2,1)S(1)}, u32[]{:S(2)}, u32[]{:S(2)}) collective-permute-start(bf16[2,64,96]{1,2,0:T(8,128)(2,1)S(1)} %add_convert_fusion.5), channel_id=1, source_target_pairs={{0,16},{8,24},{16,0},{24,8},{1,17},{9,25},{17,1},{25,9},{2,18},{10... | collective-permute-start | bytes 73736 | tf_op jit(solution)/shard_map/ppermute | solution.py:76
  79.8 1.8 %collective-permute-start.13 = (bf16[2,64,96]{1,2,0:T(8,128)(2,1)S(1)}, bf16[2,64,96]{1,2,0:T(8,128)(2,1)S(1)}, u32[]{:S(2)}, u32[]{:S(2)}) collective-permute-start(bf16[2,64,96]{1,2,0:T(8,128)(2,1)S(1)} %add_convert_fusion.4), channel_id=1, source_target_pairs={{0,16},{8,24},{16,0},{24,8},{1,17},{9,25},{17,1},{25,9},{2,18},{10... | collective-permute-start | bytes 73736 | tf_op jit(solution)/shard_map/ppermute | solution.py:76
  82.3 1.2 %collective-permute-done.16 = bf16[2,64,96]{1,2,0:T(8,128)(2,1)S(1)} collective-permute-done((bf16[2,64,96]{1,2,0:T(8,128)(2,1)S(1)}, bf16[2,64,96]{1,2,0:T(8,128)(2,1)S(1)}, u32[]{:S(2)}, u32[]{:S(2)}) %collective-permute-start.16) | collective-permute-done | bytes 24608 | tf_op jit(solution)/shard_map/ppermute | solution.py:76
  86.3 0.9 fusion.23
  87.3 1.0 copy.57
  88.3 0.9 broadcast_select_fusion.16
  90.0 1.6 %copy.56 = f32[2,128,96]{2,1,0:T(8,128)} copy(f32[2,128,96]{1,2,0:T(8,128)} %pad_maximum_fusion.5) | data formatting | bytes 196608 | tf_op jit(solution)/shard_map/concatenate | solution.py:84
  91.6 1.3 %reshape.183 = f32[2,8,16]{2,1,0:T(8,128)} reshape(f32[2,128]{1,0:T(2,128)} %fusion.23) | data formatting | bytes 2048 | tf_op jit(solution)/shard_map/reshape | solution.py:207
  93.9 3.1 %convert_reduce_fusion.2 = f32[2,1280,96]{1,2,0:T(8,128)} fusion(f32[2,8,16,96]{3,2,1,0:T(8,128)S(1)} %bitcast.136, f32[2,8,16,96]{3,2,1,0:T(8,128)} %bitcast.149, f32[2,8,16,96]{3,2,1,0:T(8,128)S(1)} %bitcast.139, bf16[2,2,8,16,1280]{4,3,2,1,0:T(8,128)(2,1)S(1)} %bitcast.117), kind=kOutput, calls=%fused_computation.2 | convolution fusion | flops 68812800 | bytes 1998848 | tf_op jit(solution)/shard_map/jbcd,jbch->jbdh/dot_general | solution.py:198
  97.1 1.7 %collective-permute-start.19 = (f32[8,3,16]{2,0,1:T(8,128)S(1)}, f32[8,3,16]{2,0,1:T(8,128)S(1)}, u32[]{:S(2)}, u32[]{:S(2)}) collective-permute-start(f32[8,3,16]{2,0,1:T(8,128)S(1)} %fusion.50), channel_id=1, source_target_pairs={{0,16},{8,24},{16,0},{24,8},{1,17},{9,25},{17,1},{25,9},{2,18},{10... | collective-permute-start | bytes 4616 | tf_op jit(solution)/shard_map/ppermute | solution.py:53
  98.8 2.2 %convert_reduce_fusion.1 = f32[2,1280,96]{1,2,0:T(8,128)} fusion(f32[2,8,16,96]{3,2,1,0:T(8,128)S(1)} %bitcast.150, f32[2,8,16,96]{3,2,1,0:T(8,128)S(1)} %bitcast.137, bf16[2,2,8,16,1280]{4,3,2,1,0:T(8,128)(2,1)S(1)} %bitcast.118), kind=kOutput, calls=%fused_computation.1 | convolution fusion | flops 68714496 | bytes 1900544 | tf_op jit(solution)/shard_map/jbcd,jbch->jbdh/dot_general | solution.py:199
  101.6 3.9 %all-to-all-start.1 = ((f32[8,3,16]{2,1,0:T(4,128)}), f32[8,3,16]{2,1,0:T(4,128)}, u32[]{:S(2)}, u32[]{:S(2)}) async-start(f32[8,3,16]{2,1,0:T(4,128)} %copy.60), calls=%async_computation.1 | async-start | bytes 32768 | tf_op jit(solution)/shard_map/all_to_all | solution.py:212
  105.6 2.9 %convert_reduce_fusion = f32[2,96,1280]{2,1,0:T(8,128)} fusion(f32[2,8,16]{2,1,0:T(8,128)} %copy-done.14, f32[2,8,16,96]{3,2,1,0:T(8,128)S(1)} %bitcast.140, f32[2,8,16,96]{3,2,1,0:T(8,128)S(1)} %bitcast.138, bf16[2,2,8,16,1280]{4,3,2,1,0:T(8,128)(2,1)S(1)} %bitcast.119), kind=kOutput, calls=%fused_computation | convolution fusion | flops 69697536 | bytes 1901568 | tf_op jit(solution)/shard_map/jbch,jbcd->jbhd/dot_general | solution.py:200
  108.5 3.7 %all-to-all-done.1 = f32[8,3,16]{2,1,0:T(4,128)} async-done(((f32[8,3,16]{2,1,0:T(4,128)}), f32[8,3,16]{2,1,0:T(4,128)}, u32[]{:S(2)}, u32[]{:S(2)}) %all-to-all-start.1) | async-done | bytes 1568 | tf_op jit(solution)/shard_map/all_to_all | solution.py:212
  (169 shorter events, 27.0 us)
Async XLA Ops:
  7.2 39.1 %copy-start = (bf16[1,768,1280]{2,1,0:T(8,128)(2,1)S(1)}, bf16[1,768,1280]{2,1,0:T(8,128)(2,1)}, u32[]{:S(2)}) copy-start(bf16[1,768,1280]{2,1,0:T(8,128)(2,1)} %param.18) | copy-start | bytes 5898244
  7.2 4.9 %copy-start.2 = (bf16[256,1280]{1,0:T(8,128)(2,1)S(1)}, bf16[256,1280]{1,0:T(8,128)(2,1)}, u32[]{:S(2)}) copy-start(bf16[256,1280]{1,0:T(8,128)(2,1)} %param.11) | copy-start | bytes 1966084
  8.1 5.3 %copy-start.16 = (pred[8,256]{1,0:T(8,128)(4,1)}, pred[8,256]{1,0:T(8,128)(4,1)S(1)}, u32[]{:S(2)}) copy-start(pred[8,256]{1,0:T(8,128)(4,1)S(1)} %fusion.37) | copy-start | bytes 6148
  12.1 8.7 %copy-start.11 = (s32[256,6]{0,1:T(8,128)S(1)}, s32[256,6]{0,1:T(8,128)}, u32[]{:S(2)}) copy-start(s32[256,6]{0,1:T(8,128)} %param.14) | copy-start | bytes 18436
  12.2 8.7 %copy-start.20 = (s32[2]{0:T(128)S(1)}, s32[2]{0:T(128)}, u32[]{:S(2)}) copy-start(s32[2]{0:T(128)} %param.15) | copy-start | bytes 28
  12.4 10.3 %copy-start.1 = (bf16[256,1280]{1,0:T(8,128)(2,1)S(1)}, bf16[256,1280]{1,0:T(8,128)(2,1)}, u32[]{:S(2)}) copy-start(bf16[256,1280]{1,0:T(8,128)(2,1)} %param.12) | copy-start | bytes 1966084
  13.4 32.6 %all-to-all-start = ((bf16[8,40,1280]{2,1,0:T(8,128)(2,1)}), bf16[8,40,1280]{2,1,0:T(8,128)(2,1)S(1)}, u32[]{:S(2)}, u32[]{:S(2)}) async-start(bf16[8,40,1280]{2,1,0:T(8,128)(2,1)} %pad_maximum_fusion), calls=%async_computation | async-start | bytes 1638400 | tf_op jit(solution)/shard_map/all_to_all | solution.py:138
  20.7 50.4 %all-gather.3.cloned.1.call-start = ((), (), s32[]{:S(2)}) async-start(), calls=%async_computation.2 | async-start | bytes 1658880 | tf_op jit(solution)/shard_map/all_gather | solution.py:115
  47.1 3.1 %collective-permute-start = (bf16[64,768]{1,0:T(8,128)(2,1)S(1)}, bf16[64,768]{1,0:T(8,128)(2,1)S(1)}, u32[]{:S(2)}, u32[]{:S(2)}) collective-permute-start(bf16[64,768]{1,0:T(8,128)(2,1)S(1)} %broadcast_select_fusion.8), channel_id=1, source_target_pairs={{0,8},{8,0},{16,24},{24,16},{1,9},{9,1},{17,25},{25,17},{2,10},{10... | collective-permute-start | bytes 294920 | tf_op jit(solution)/shard_map/ppermute | solution.py:70
  48.3 4.3 %collective-permute-start.6 = (bf16[64,768]{1,0:T(8,128)(2,1)S(1)}, bf16[64,768]{1,0:T(8,128)(2,1)S(1)}, u32[]{:S(2)}, u32[]{:S(2)}) collective-permute-start(bf16[64,768]{1,0:T(8,128)(2,1)S(1)} %broadcast_select_fusion.2), channel_id=1, source_target_pairs={{0,8},{8,0},{16,24},{24,16},{1,9},{9,1},{17,25},{25,17},{2,10},{10... | collective-permute-start | bytes 294920 | tf_op jit(solution)/shard_map/ppermute | solution.py:70
  49.3 3.5 %collective-permute-start.3 = (bf16[64,768]{1,0:T(8,128)(2,1)S(1)}, bf16[64,768]{1,0:T(8,128)(2,1)S(1)}, u32[]{:S(2)}, u32[]{:S(2)}) collective-permute-start(bf16[64,768]{1,0:T(8,128)(2,1)S(1)} %broadcast_select_fusion.5), channel_id=1, source_target_pairs={{0,8},{8,0},{16,24},{24,16},{1,9},{9,1},{17,25},{25,17},{2,10},{10... | collective-permute-start | bytes 294920 | tf_op jit(solution)/shard_map/ppermute | solution.py:70
  50.3 6.0 %collective-permute-start.1 = (bf16[64,768]{1,0:T(8,128)(2,1)S(1)}, bf16[64,768]{1,0:T(8,128)(2,1)S(1)}, u32[]{:S(2)}, u32[]{:S(2)}) collective-permute-start(bf16[64,768]{1,0:T(8,128)(2,1)S(1)} %add_convert_fusion.2), channel_id=1, source_target_pairs={{0,16},{8,24},{16,0},{24,8},{1,17},{9,25},{17,1},{25,9},{2,18},{10... | collective-permute-start | bytes 294920 | tf_op jit(solution)/shard_map/ppermute | solution.py:76
  52.7 5.8 %collective-permute-start.7 = (bf16[64,768]{1,0:T(8,128)(2,1)S(1)}, bf16[64,768]{1,0:T(8,128)(2,1)S(1)}, u32[]{:S(2)}, u32[]{:S(2)}) collective-permute-start(bf16[64,768]{1,0:T(8,128)(2,1)S(1)} %add_convert_fusion), channel_id=1, source_target_pairs={{0,16},{8,24},{16,0},{24,8},{1,17},{9,25},{17,1},{25,9},{2,18},{10... | collective-permute-start | bytes 294920 | tf_op jit(solution)/shard_map/ppermute | solution.py:76
  52.8 7.4 %collective-permute-start.4 = (bf16[64,768]{1,0:T(8,128)(2,1)S(1)}, bf16[64,768]{1,0:T(8,128)(2,1)S(1)}, u32[]{:S(2)}, u32[]{:S(2)}) collective-permute-start(bf16[64,768]{1,0:T(8,128)(2,1)S(1)} %add_convert_fusion.1), channel_id=1, source_target_pairs={{0,16},{8,24},{16,0},{24,8},{1,17},{9,25},{17,1},{25,9},{2,18},{10... | collective-permute-start | bytes 294920 | tf_op jit(solution)/shard_map/ppermute | solution.py:76
  57.0 9.1 %collective-permute-start.2 = (f32[64,768]{1,0:T(8,128)}, f32[64,768]{1,0:T(8,128)}, u32[]{:S(2)}, u32[]{:S(2)}) collective-permute-start(f32[64,768]{1,0:T(8,128)} %convert_add_fusion.2), channel_id=1, source_target_pairs={{0,8},{8,0},{16,24},{24,16},{1,9},{9,1},{17,25},{25,17},{2,10},{10... | collective-permute-start | bytes 589832 | tf_op jit(solution)/shard_map/ppermute | solution.py:79
  58.5 1.8 %collective-permute-start.8 = (f32[64,768]{1,0:T(8,128)S(1)}, f32[64,768]{1,0:T(8,128)S(1)}, u32[]{:S(2)}, u32[]{:S(2)}) collective-permute-start(f32[64,768]{1,0:T(8,128)S(1)} %convert_add_fusion), channel_id=1, source_target_pairs={{0,8},{8,0},{16,24},{24,16},{1,9},{9,1},{17,25},{25,17},{2,10},{10... | collective-permute-start | bytes 589832 | tf_op jit(solution)/shard_map/ppermute | solution.py:79
  60.2 1.5 %collective-permute-start.5 = (f32[64,768]{1,0:T(8,128)S(1)}, f32[64,768]{1,0:T(8,128)S(1)}, u32[]{:S(2)}, u32[]{:S(2)}) collective-permute-start(f32[64,768]{1,0:T(8,128)S(1)} %convert_add_fusion.1), channel_id=1, source_target_pairs={{0,8},{8,0},{16,24},{24,16},{1,9},{9,1},{17,25},{25,17},{2,10},{10... | collective-permute-start | bytes 589832 | tf_op jit(solution)/shard_map/ppermute | solution.py:79
  61.9 4.2 %copy-start.10 = (bf16[64,768]{1,0:T(8,128)(2,1)S(1)}, bf16[64,768]{1,0:T(8,128)(2,1)}, u32[]{:S(2)}) copy-start(bf16[64,768]{1,0:T(8,128)(2,1)} %copy-done.9) | copy-start | bytes 294916
  76.1 1.3 %collective-permute-start.9 = (bf16[2,64,96]{1,2,0:T(8,128)(2,1)S(1)}, bf16[2,64,96]{1,2,0:T(8,128)(2,1)S(1)}, u32[]{:S(2)}, u32[]{:S(2)}) collective-permute-start(bf16[2,64,96]{1,2,0:T(8,128)(2,1)S(1)} %broadcast_select_fusion.17), channel_id=1, source_target_pairs={{0,8},{8,0},{16,24},{24,16},{1,9},{9,1},{17,25},{25,17},{2,10},{10... | collective-permute-start | bytes 73736 | tf_op jit(solution)/shard_map/ppermute | solution.py:70
  76.4 2.9 %collective-permute-start.15 = (bf16[2,64,96]{1,2,0:T(8,128)(2,1)S(1)}, bf16[2,64,96]{1,2,0:T(8,128)(2,1)S(1)}, u32[]{:S(2)}, u32[]{:S(2)}) collective-permute-start(bf16[2,64,96]{1,2,0:T(8,128)(2,1)S(1)} %broadcast_select_fusion.11), channel_id=1, source_target_pairs={{0,8},{8,0},{16,24},{24,16},{1,9},{9,1},{17,25},{25,17},{2,10},{10... | collective-permute-start | bytes 73736 | tf_op jit(solution)/shard_map/ppermute | solution.py:70
  76.8 2.9 %collective-permute-start.12 = (bf16[2,64,96]{1,2,0:T(8,128)(2,1)S(1)}, bf16[2,64,96]{1,2,0:T(8,128)(2,1)S(1)}, u32[]{:S(2)}, u32[]{:S(2)}) collective-permute-start(bf16[2,64,96]{1,2,0:T(8,128)(2,1)S(1)} %broadcast_select_fusion.14), channel_id=1, source_target_pairs={{0,8},{8,0},{16,24},{24,16},{1,9},{9,1},{17,25},{25,17},{2,10},{10... | collective-permute-start | bytes 73736 | tf_op jit(solution)/shard_map/ppermute | solution.py:70
  77.5 8.2 %copy-start.7 = (bf16[2,64,96]{1,2,0:T(8,128)(2,1)}, bf16[2,64,96]{1,2,0:T(8,128)(2,1)S(1)}, u32[]{:S(2)}) copy-start(bf16[2,64,96]{1,2,0:T(8,128)(2,1)S(1)} %add_convert_fusion.5) | copy-start | bytes 73732
  77.5 4.2 %collective-permute-start.10 = (bf16[2,64,96]{1,2,0:T(8,128)(2,1)S(1)}, bf16[2,64,96]{1,2,0:T(8,128)(2,1)S(1)}, u32[]{:S(2)}, u32[]{:S(2)}) collective-permute-start(bf16[2,64,96]{1,2,0:T(8,128)(2,1)S(1)} %add_convert_fusion.5), channel_id=1, source_target_pairs={{0,16},{8,24},{16,0},{24,8},{1,17},{9,25},{17,1},{25,9},{2,18},{10... | collective-permute-start | bytes 73736 | tf_op jit(solution)/shard_map/ppermute | solution.py:76
  79.4 4.2 %collective-permute-start.16 = (bf16[2,64,96]{1,2,0:T(8,128)(2,1)S(1)}, bf16[2,64,96]{1,2,0:T(8,128)(2,1)S(1)}, u32[]{:S(2)}, u32[]{:S(2)}) collective-permute-start(bf16[2,64,96]{1,2,0:T(8,128)(2,1)S(1)} %add_convert_fusion.3), channel_id=1, source_target_pairs={{0,16},{8,24},{16,0},{24,8},{1,17},{9,25},{17,1},{25,9},{2,18},{10... | collective-permute-start | bytes 73736 | tf_op jit(solution)/shard_map/ppermute | solution.py:76
  79.8 4.3 %collective-permute-start.13 = (bf16[2,64,96]{1,2,0:T(8,128)(2,1)S(1)}, bf16[2,64,96]{1,2,0:T(8,128)(2,1)S(1)}, u32[]{:S(2)}, u32[]{:S(2)}) collective-permute-start(bf16[2,64,96]{1,2,0:T(8,128)(2,1)S(1)} %add_convert_fusion.4), channel_id=1, source_target_pairs={{0,16},{8,24},{16,0},{24,8},{1,17},{9,25},{17,1},{25,9},{2,18},{10... | collective-permute-start | bytes 73736 | tf_op jit(solution)/shard_map/ppermute | solution.py:76
  82.3 6.0 %collective-permute-start.11 = (f32[2,64,96]{1,2,0:T(8,128)}, f32[2,64,96]{1,2,0:T(8,128)}, u32[]{:S(2)}, u32[]{:S(2)}) collective-permute-start(f32[2,64,96]{1,2,0:T(8,128)} %convert_add_fusion.5), channel_id=1, source_target_pairs={{0,8},{8,0},{16,24},{24,16},{1,9},{9,1},{17,25},{25,17},{2,10},{10... | collective-permute-start | bytes 147464 | tf_op jit(solution)/shard_map/ppermute | solution.py:79
  83.6 1.4 %collective-permute-start.17 = (f32[2,64,96]{1,2,0:T(8,128)S(1)}, f32[2,64,96]{1,2,0:T(8,128)S(1)}, u32[]{:S(2)}, u32[]{:S(2)}) collective-permute-start(f32[2,64,96]{1,2,0:T(8,128)S(1)} %convert_add_fusion.3), channel_id=1, source_target_pairs={{0,8},{8,0},{16,24},{24,16},{1,9},{9,1},{17,25},{25,17},{2,10},{10... | collective-permute-start | bytes 147464 | tf_op jit(solution)/shard_map/ppermute | solution.py:79
  84.1 1.4 %collective-permute-start.14 = (f32[2,64,96]{1,2,0:T(8,128)S(1)}, f32[2,64,96]{1,2,0:T(8,128)S(1)}, u32[]{:S(2)}, u32[]{:S(2)}) collective-permute-start(f32[2,64,96]{1,2,0:T(8,128)S(1)} %convert_add_fusion.4), channel_id=1, source_target_pairs={{0,8},{8,0},{16,24},{24,16},{1,9},{9,1},{17,25},{25,17},{2,10},{10... | collective-permute-start | bytes 147464 | tf_op jit(solution)/shard_map/ppermute | solution.py:79
  93.0 5.8 %copy-start.13 = (f32[2,128,96]{2,1,0:T(8,128)S(1)}, f32[2,128,96]{2,1,0:T(8,128)}, u32[]{:S(2)}) copy-start(f32[2,128,96]{2,1,0:T(8,128)} %copy.56) | copy-start | bytes 294916
  93.8 3.3 %collective-permute-start.18 = (f32[8,3,16]{2,0,1:T(8,128)S(1)}, f32[8,3,16]{2,0,1:T(8,128)S(1)}, u32[]{:S(2)}, u32[]{:S(2)}) collective-permute-start(f32[8,3,16]{2,0,1:T(8,128)S(1)} %pad_maximum_fusion.8), channel_id=1, source_target_pairs={{0,8},{8,0},{16,24},{24,16},{1,9},{9,1},{17,25},{25,17},{2,10},{10... | collective-permute-start | bytes 4616 | tf_op jit(solution)/shard_map/ppermute | solution.py:53
  97.1 3.9 %collective-permute-start.19 = (f32[8,3,16]{2,0,1:T(8,128)S(1)}, f32[8,3,16]{2,0,1:T(8,128)S(1)}, u32[]{:S(2)}, u32[]{:S(2)}) collective-permute-start(f32[8,3,16]{2,0,1:T(8,128)S(1)} %fusion.50), channel_id=1, source_target_pairs={{0,16},{8,24},{16,0},{24,8},{1,17},{9,25},{17,1},{25,9},{2,18},{10... | collective-permute-start | bytes 4616 | tf_op jit(solution)/shard_map/ppermute | solution.py:53
  101.6 10.5 %all-to-all-start.1 = ((f32[8,3,16]{2,1,0:T(4,128)}), f32[8,3,16]{2,1,0:T(4,128)}, u32[]{:S(2)}, u32[]{:S(2)}) async-start(f32[8,3,16]{2,1,0:T(4,128)} %copy.60), calls=%async_computation.1 | async-start | bytes 32768 | tf_op jit(solution)/shard_map/all_to_all | solution.py:212
  (13 other events, 26.9 us)
Sparse Core Ops, SparseCore 0:
  25.1 45.6 all-gather.2

commit v9 on v8

--- a/solution.py
+++ b/solution.py
@@ -112,9 +112,11 @@
         scale_lines, slice_width
     )
     blocks = lax.axis_size("ep")
-    gathered = lax.all_gather(
-        jnp.concatenate([hot_feats, hot_cotan, scale_block], axis=0), "ep", axis=0, tiled=False
-    )
+    hot_outgoing = jnp.concatenate([hot_feats, hot_cotan, scale_block], axis=0)
+    hot_outgoing, expert_ids, tokens, cotangent, gate_weights = lax.optimization_barrier(
+        (hot_outgoing, expert_ids, tokens, cotangent, gate_weights)
+    )
+    gathered = lax.all_gather(hot_outgoing, "ep", axis=0, tiled=False)
     cold_hit, cold_sel = token_table(
         expert_ids, jnp.arange(cold_count, dtype=jnp.int32), capacity
     )
@@ -168,15 +170,19 @@
     part_hidden_hot = jnp.einsum(
         "jrd,jhd->jrh", rows_wt, down_hot, preferred_element_type=jnp.float32
     )
-    cot_down = jnp.einsum("jrd,jhd->jrh", rows_cot, down_hot, preferred_element_type=jnp.float32)
-    (pre_gate, pre_up, grad_hidden, pre_gate_hot, pre_up_hot, grad_hidden_hot) = grp_sum_rounded(
-        [part_gate, part_up, part_hidden, part_gate_hot, part_up_hot, part_hidden_hot],
-        [0, 0, 0, 1, 1, 1],
-        "grp",
+    part_cot_hot = jnp.einsum(
+        "jrd,jhd->jrh", rows_cot, down_hot, preferred_element_type=jnp.float32
+    )
+    pre_gate, pre_up, grad_hidden = grp_sum_rounded(
+        [part_gate, part_up, part_hidden], [0, 0, 0], "grp"
+    )
+    pre_gate_hot, pre_up_hot, grad_hidden_hot, cot_down = grp_sum_rounded(
+        [part_gate_hot, part_up_hot, part_hidden_hot, part_cot_hot], [1, 1, 1, 1], "grp"
     )
     hidden, back_gate, back_up = swiglu_back(pre_gate, pre_up, grad_hidden)
     output_slice = jnp.dot(hidden, w_down, preferred_element_type=jnp.float32)
     cold_route = jnp.sum(output_slice * recv_cotan.astype(jnp.float32), axis=1)
+    cold_route = grp_sum_f32(cold_route.reshape(cold_count, 1, capacity), "grp")
     contract_rows = (((0,), (0,)), ((), ()))
     grad_gate_cold = lax.dot_general(
         recv_feats, back_gate, contract_rows, preferred_element_type=jnp.float32
@@ -203,12 +209,11 @@
     grad_down_hot = jnp.sum(blk_down.astype(jnp.bfloat16).astype(jnp.float32), axis=1)
     route_parts = jnp.concatenate(
         [
-            cold_route.reshape(cold_count, 1, capacity),
+            cold_route,
             jnp.transpose(hot_route_part.reshape(hot_count, blocks, capacity), (1, 0, 2)),
         ],
         axis=1,
     )
-    route_parts = grp_sum_f32(route_parts, "grp")
     route_back = lax.all_to_all(route_parts, "ep", split_axis=0, concat_axis=0, tiled=True)
     cold_back = route_back[:, 0, :]
     hot_route = jnp.sum(route_back[:, 1:, :], axis=0)

time: 124 us -> 121 us (0.976)
  local copies, waits for them, and re-layouts: 12.6 us -> 8.96 us
  matrix products: 22.6 us -> 20.2 us
  other arithmetic: 16.6 us -> 18.4 us
  waiting for transfers between devices: 33.9 us -> 35.2 us
    all_to_all x1, waiting for transfers between devices: 21 us -> 24.8 us  [body(): lax.all_to_all(outgoing, 'ep', split_axis=0, concat_axis=0, tiled=True)]
    all_to_all x1, waiting for transfers between devices: 3.65 us -> 0.01 us  [body(): lax.all_to_all(route_parts, 'ep', split_axis=0, concat_axis=0, tiled=True)]
    ppermute x6 -> x7, waiting for transfers between devices: 6.21 us -> 8.09 us  [grp_sum_rounded(): got = lax.ppermute(mine, axis_name, partner)]
    reduce_sum x0 -> x1, other arithmetic: none -> 1.78 us  [body(): hot_route_part = jnp.sum(hidden_hot.astype(jnp.float32) * cot_down, axis=2)]
    select_n x6 -> x7, other arithmetic: 2.02 us -> 3.36 us  [grp_sum_rounded(): first = jnp.where(first_core, s, o)]
    reshape x1, local copies, waits for them, and re-layouts: 1.34 us -> 0.08 us  [body(): hot_route_part.reshape(hot_count, blocks, capacity)]
    ppermute x6 -> x7, waiting for transfers between devices: 2.58 us -> 1.39 us  [grp_sum_rounded(): other = lax.ppermute(sums, axis_name, swap)]
    unnamed x49 -> x39, local copies, waits for them, and re-layouts: 3.86 us -> 2.99 us
  transfers between devices with their start and end apart: 23 -> 26, of which waited for: 11 -> 10; matrix products, arithmetic and copies ran while one was open for 23% -> 19% of each run, Pallas kernels for 0% -> 0%
where the time goes in v9:
time: 121 us; the launch traced here: 120 us
  waiting for transfers between devices  35.2 us (29%)
  starting transfers between devices  22.9 us (19%)
  matrix products  20.2 us (17%)
  other arithmetic  18.4 us (15%)
  between operations  14.7 us (12%)
  local copies, waits for them, and re-layouts  8.96 us (7%)
    all_to_all x1, waiting for transfers between devices, body(): lax.all_to_all(outgoing, 'ep', split_axis=0, concat_axis=0, tiled=True)  24.8 us
    ppermute x7, waiting for transfers between devices, grp_sum_rounded(): got = lax.ppermute(mine, axis_name, partner)  8.09 us
    ppermute x7, starting transfers between devices, grp_sum_rounded(): got = lax.ppermute(mine, axis_name, partner)  8.02 us
    all_to_all x1, starting transfers between devices, body(): lax.all_to_all(outgoing, 'ep', split_axis=0, concat_axis=0, tiled=True)  7.28 us
    all_to_all x1, starting transfers between devices, body(): lax.all_to_all(route_parts, 'ep', split_axis=0, concat_axis=0, tiled=True)  4.12 us
    select_n x7, other arithmetic, grp_sum_rounded(): first = jnp.where(first_core, s, o)  3.36 us
    dot_general x1, matrix products, body(): jnp.einsum('jbcd,jbch->jbdh', feat_b, bu_b, preferred_element_type=jnp.fl...  3.14 us
    unnamed x39, local copies, waits for them, and re-layouts  2.99 us
  transfers between devices with their start and end apart: 26, of which 10 were waited for; matrix products, arithmetic and copies ran while one was open for 19% of the time, Pallas kernels for 0%

profile of v9, /device:TPU:0, one launch (start us, length us, event | category | flops | bytes accessed | tf_op | source)
XLA Modules:
  0.0 120.3 jit_solution(12354822154580976628)
XLA Ops:
  7.3 0.9 compare_reduce_fusion
  11.3 1.3 %convolution_convert_fusion.8 = bf16[32,1280]{1,0:T(8,128)(2,1)S(1)} fusion(pred[32,256]{1,0:T(32,128)(4,1)S(1)} %fusion.39, bf16[256,1280]{1,0:T(8,128)(2,1)} %param.12), kind=kOutput, calls=%fused_computation.15 | convolution fusion | flops 21012480 | bytes 745472 | tf_op jit(solution)/shard_map/dot_general | solution.py:20
  12.6 1.3 %convolution_convert_fusion.9 = bf16[32,1280]{1,0:T(8,128)(2,1)S(1)} fusion(pred[32,256]{1,0:T(32,128)(4,1)S(1)} %fusion.39, bf16[256,1280]{1,0:T(8,128)(2,1)} %param.11), kind=kOutput, calls=%fused_computation.16 | convolution fusion | flops 21012480 | bytes 745472 | tf_op jit(solution)/shard_map/dot_general | solution.py:19
  16.4 0.9 pad_maximum_fusion
  17.4 7.3 %all-to-all-start = ((bf16[8,40,1280]{2,1,0:T(8,128)(2,1)}), bf16[8,40,1280]{2,1,0:T(8,128)(2,1)S(1)}, u32[]{:S(2)}, u32[]{:S(2)}) async-start(bf16[8,40,1280]{2,1,0:T(8,128)(2,1)} %pad_maximum_fusion), calls=%async_computation | async-start | bytes 1638400 | tf_op jit(solution)/shard_map/all_to_all | solution.py:140
  25.4 24.8 %all-to-all-done = bf16[8,40,1280]{2,1,0:T(8,128)(2,1)S(1)} async-done(((bf16[8,40,1280]{2,1,0:T(8,128)(2,1)}), bf16[8,40,1280]{2,1,0:T(8,128)(2,1)S(1)}, u32[]{:S(2)}, u32[]{:S(2)}) %all-to-all-start) | async-done | bytes 819232 | tf_op jit(solution)/shard_map/all_to_all | solution.py:140
  54.5 1.6 %collective-permute-start.1 = (bf16[64,768]{1,0:T(8,128)(2,1)S(1)}, bf16[64,768]{1,0:T(8,128)(2,1)S(1)}, u32[]{:S(2)}, u32[]{:S(2)}) collective-permute-start(bf16[64,768]{1,0:T(8,128)(2,1)S(1)} %add_convert_fusion.2), channel_id=1, source_target_pairs={{0,16},{8,24},{16,0},{24,8},{1,17},{9,25},{17,1},{25,9},{2,18},{10... | collective-permute-start | bytes 294920 | tf_op jit(solution)/shard_map/ppermute | solution.py:76
  56.8 1.6 %collective-permute-start.4 = (bf16[64,768]{1,0:T(8,128)(2,1)S(1)}, bf16[64,768]{1,0:T(8,128)(2,1)S(1)}, u32[]{:S(2)}, u32[]{:S(2)}) collective-permute-start(bf16[64,768]{1,0:T(8,128)(2,1)S(1)} %add_convert_fusion.1), channel_id=1, source_target_pairs={{0,16},{8,24},{16,0},{24,8},{1,17},{9,25},{17,1},{25,9},{2,18},{10... | collective-permute-start | bytes 294920 | tf_op jit(solution)/shard_map/ppermute | solution.py:76
  58.3 1.9 %collective-permute-done.1 = bf16[64,768]{1,0:T(8,128)(2,1)S(1)} collective-permute-done((bf16[64,768]{1,0:T(8,128)(2,1)S(1)}, bf16[64,768]{1,0:T(8,128)(2,1)S(1)}, u32[]{:S(2)}, u32[]{:S(2)}) %collective-permute-start.1) | collective-permute-done | bytes 98336 | tf_op jit(solution)/shard_map/ppermute | solution.py:76
  60.9 1.4 %collective-permute-done.7 = bf16[64,768]{1,0:T(8,128)(2,1)S(1)} collective-permute-done((bf16[64,768]{1,0:T(8,128)(2,1)S(1)}, bf16[64,768]{1,0:T(8,128)(2,1)S(1)}, u32[]{:S(2)}, u32[]{:S(2)}) %collective-permute-start.7) | collective-permute-done | bytes 98336 | tf_op jit(solution)/shard_map/ppermute | solution.py:76
  62.4 1.5 %collective-permute-done.4 = bf16[64,768]{1,0:T(8,128)(2,1)S(1)} collective-permute-done((bf16[64,768]{1,0:T(8,128)(2,1)S(1)}, bf16[64,768]{1,0:T(8,128)(2,1)S(1)}, u32[]{:S(2)}, u32[]{:S(2)}) %collective-permute-start.4) | collective-permute-done | bytes 98336 | tf_op jit(solution)/shard_map/ppermute | solution.py:76
  64.1 1.4 %collective-permute-done.5 = f32[64,768]{1,0:T(8,128)S(1)} collective-permute-done((f32[64,768]{1,0:T(8,128)S(1)}, f32[64,768]{1,0:T(8,128)S(1)}, u32[]{:S(2)}, u32[]{:S(2)}) %collective-permute-start.5) | collective-permute-done | bytes 196640 | tf_op jit(solution)/shard_map/ppermute | solution.py:79
  66.4 1.0 broadcast_select_fusion.7
  67.3 2.0 %fusion = bf16[1,1280,768]{2,1,0:T(8,128)(2,1)} fusion(bf16[128,1280]{1,0:T(8,128)(2,1)S(1)} %bitcast.125, f32[64,768]{1,0:T(8,128)S(1)} %get-tuple-element.29, f32[64,768]{1,0:T(8,128)S(1)} %get-tuple-element.28, f32[64,768]{1,0:T(8,128)S(1)} %get-tuple-element.27, f32[64,768]{1,0:T(8,128)S(1)} %get-tuple-element.26, f32[64,768]{1,0:T(8,128)S(1)} %get-tuple-element.25, ...), kind=kOutput, calls=%fused_computation.9 | convolution fusion | flops 253919232 | bytes 3473408 | tf_op jit(solution)/shard_map/dot_general | solution.py:187
  69.4 2.0 %fusion.1 = bf16[1,1280,768]{2,1,0:T(8,128)(2,1)} fusion(bf16[128,1280]{1,0:T(8,128)(2,1)S(1)} %bitcast.126, f32[64,768]{1,0:T(8,128)S(1)} %get-tuple-element.25, f32[64,768]{1,0:T(8,128)S(1)} %get-tuple-element.24, f32[64,768]{1,0:T(8,128)S(1)} %get-tuple-element.29, f32[64,768]{1,0:T(8,128)S(1)} %get-tuple-element.28), kind=kOutput, calls=%fused_computation.10 | convolution fusion | flops 253427712 | bytes 3080192 | tf_op jit(solution)/shard_map/dot_general | solution.py:190
  71.3 1.5 %collective-permute-start.19 = (f32[8,1,16]{2,0,1:T(8,128)S(1)}, f32[8,1,16]{2,0,1:T(8,128)S(1)}, u32[]{:S(2)}, u32[]{:S(2)}) collective-permute-start(f32[8,1,16]{2,0,1:T(8,128)S(1)} %add.110), channel_id=1, source_target_pairs={{0,16},{8,24},{16,0},{24,8},{1,17},{9,25},{17,1},{25,9},{2,18},{10... | collective-permute-start | bytes 1544 | tf_op jit(solution)/shard_map/ppermute | solution.py:53
  72.9 2.0 %fusion.2 = bf16[1,768,1280]{2,1,0:T(8,128)(2,1)} fusion(bf16[128,768]{1,0:T(8,128)(2,1)S(1)} %multiply_convert_fusion.3, bf16[128,1280]{1,0:T(8,128)(2,1)S(1)} %copy-done.5), kind=kOutput, calls=%fused_computation.11 | convolution fusion | flops 252641280 | bytes 2490368 | tf_op jit(solution)/shard_map/dot_general | solution.py:193
  75.0 0.9 slice_bitcast_fusion
  75.9 1.4 %slice.68 = bf16[8,64,1280]{2,1,0:T(8,128)(2,1)S(1)} slice(bf16[8,72,1280]{2,1,0:T(8,128)(2,1)} %bitcast.134), slice={[0:8], [0:64], [0:1280]} | slice | bytes 2621440 | tf_op jit(solution)/shard_map/slice | solution.py:155
  77.8 0.9 copy-done.6
  81.8 1.6 %collective-permute-start.10 = (bf16[2,64,96]{1,2,0:T(8,128)(2,1)S(1)}, bf16[2,64,96]{1,2,0:T(8,128)(2,1)S(1)}, u32[]{:S(2)}, u32[]{:S(2)}) collective-permute-start(bf16[2,64,96]{1,2,0:T(8,128)(2,1)S(1)} %add_convert_fusion.6), channel_id=1, source_target_pairs={{0,16},{8,24},{16,0},{24,8},{1,17},{9,25},{17,1},{25,9},{2,18},{10... | collective-permute-start | bytes 73736 | tf_op jit(solution)/shard_map/ppermute | solution.py:76
  84.2 1.6 %collective-permute-start.16 = (bf16[2,64,96]{1,2,0:T(8,128)(2,1)S(1)}, bf16[2,64,96]{1,2,0:T(8,128)(2,1)S(1)}, u32[]{:S(2)}, u32[]{:S(2)}) collective-permute-start(bf16[2,64,96]{1,2,0:T(8,128)(2,1)S(1)} %add_convert_fusion.4), channel_id=1, source_target_pairs={{0,16},{8,24},{16,0},{24,8},{1,17},{9,25},{17,1},{25,9},{2,18},{10... | collective-permute-start | bytes 73736 | tf_op jit(solution)/shard_map/ppermute | solution.py:76
  86.5 1.1 collective-permute-done.21
  87.7 1.1 collective-permute-done.16
  88.9 1.1 collective-permute-done.13
  92.9 0.9 broadcast_select_fusion.16
  93.9 1.8 %fusion.35 = (f32[2,128]{1,0:T(2,128)S(1)}, f32[2,128,96]{1,2,0:T(8,128)S(1)}, f32[2,128,96]{1,2,0:T(8,128)}) fusion(f32[2,64,96]{1,2,0:T(8,128)} %get-tuple-element.37, f32[2,64,96]{1,2,0:T(8,128)} %get-tuple-element.36, f32[2,64,96]{1,2,0:T(8,128)S(1)} %get-tuple-element.35, f32[2,64,96]{1,2,0:T(8,128)S(1)} %get-tuple-element.34, ...), kind=kLoop, calls=%fused_computation.79 | loop fusion | flops 294656 | bytes 492544 | tf_op jit(solution)/shard_map/reduce_sum | solution.py:197
  96.3 4.1 %all-to-all-start.1 = ((f32[8,3,16]{2,1,0:T(4,128)}), f32[8,3,16]{2,1,0:T(4,128)}, u32[]{:S(2)}, u32[]{:S(2)}) async-start(f32[8,3,16]{2,1,0:T(4,128)} %copy.60), calls=%async_computation.1 | async-start | bytes 32768 | tf_op jit(solution)/shard_map/all_to_all | solution.py:217
  100.6 1.0 copy.58
  101.6 3.1 %convert_reduce_fusion.1 = f32[2,1280,96]{1,2,0:T(8,128)} fusion(f32[2,8,16,96]{3,2,1,0:T(8,128)} %bitcast.152, f32[2,8,16,96]{3,2,1,0:T(8,128)S(1)} %bitcast.141, bf16[2,2,8,16,1280]{4,3,2,1,0:T(8,128)(2,1)S(1)} %bitcast.120), kind=kOutput, calls=%fused_computation.1 | convolution fusion | flops 68714496 | bytes 1867776 | tf_op jit(solution)/shard_map/jbcd,jbch->jbdh/dot_general | solution.py:205
  104.7 2.2 %convert_reduce_fusion.2 = f32[2,1280,96]{1,2,0:T(8,128)} fusion(f32[2,8,16,96]{3,2,1,0:T(8,128)S(1)} %bitcast.142, f32[2,8,16,96]{3,2,1,0:T(8,128)S(1)} %bitcast.153, f32[2,8,16,96]{3,2,1,0:T(8,128)S(1)} %bitcast.139, bf16[2,2,8,16,1280]{4,3,2,1,0:T(8,128)(2,1)S(1)} %bitcast.121), kind=kOutput, calls=%fused_computation.2 | convolution fusion | flops 68812800 | bytes 2031616 | tf_op jit(solution)/shard_map/jbcd,jbch->jbdh/dot_general | solution.py:204
  106.9 2.2 %convert_reduce_fusion = f32[2,96,1280]{2,1,0:T(8,128)} fusion(f32[2,8,16]{2,1,0:T(8,128)S(1)} %copy-done.12, f32[2,8,16,96]{3,2,1,0:T(8,128)S(1)} %bitcast.140, f32[2,8,16,96]{3,2,1,0:T(8,128)S(1)} %bitcast.143, bf16[2,2,8,16,1280]{4,3,2,1,0:T(8,128)(2,1)S(1)} %bitcast.122), kind=kOutput, calls=%fused_computation | convolution fusion | flops 69697536 | bytes 1908736 | tf_op jit(solution)/shard_map/jbch,jbcd->jbhd/dot_general | solution.py:206
  (170 shorter events, 26.4 us)
Async XLA Ops:
  7.2 43.3 %copy-start = (bf16[1,768,1280]{2,1,0:T(8,128)(2,1)S(1)}, bf16[1,768,1280]{2,1,0:T(8,128)(2,1)}, u32[]{:S(2)}) copy-start(bf16[1,768,1280]{2,1,0:T(8,128)(2,1)} %param.18) | copy-start | bytes 5898244
  7.2 7.5 %copy-start.9 = (s32[256,6]{0,1:T(8,128)S(1)}, s32[256,6]{0,1:T(8,128)}, u32[]{:S(2)}) copy-start(s32[256,6]{0,1:T(8,128)} %param.14) | copy-start | bytes 18436
  7.2 8.4 %copy-start.16 = (bf16[256,6]{0,1:T(8,128)(2,1)S(1)}, bf16[256,6]{0,1:T(8,128)(2,1)}, u32[]{:S(2)}) copy-start(bf16[256,6]{0,1:T(8,128)(2,1)} %param.13) | copy-start | bytes 9220
  7.2 8.7 %copy-start.1 = (bf16[256,1280]{1,0:T(8,128)(2,1)S(1)}, bf16[256,1280]{1,0:T(8,128)(2,1)}, u32[]{:S(2)}) copy-start(bf16[256,1280]{1,0:T(8,128)(2,1)} %param.12) | copy-start | bytes 1966084
  7.2 9.0 %copy-start.2 = (bf16[256,1280]{1,0:T(8,128)(2,1)S(1)}, bf16[256,1280]{1,0:T(8,128)(2,1)}, u32[]{:S(2)}) copy-start(bf16[256,1280]{1,0:T(8,128)(2,1)} %param.11) | copy-start | bytes 1966084
  17.4 32.8 %all-to-all-start = ((bf16[8,40,1280]{2,1,0:T(8,128)(2,1)}), bf16[8,40,1280]{2,1,0:T(8,128)(2,1)S(1)}, u32[]{:S(2)}, u32[]{:S(2)}) async-start(bf16[8,40,1280]{2,1,0:T(8,128)(2,1)} %pad_maximum_fusion), calls=%async_computation | async-start | bytes 1638400 | tf_op jit(solution)/shard_map/all_to_all | solution.py:140
  24.7 50.3 %all-gather.3.cloned.1.call-start = ((), (), s32[]{:S(2)}) async-start(), calls=%async_computation.2 | async-start | bytes 1658880 | tf_op jit(solution)/shard_map/all_gather | solution.py:119
  51.3 3.1 %collective-permute-start = (bf16[64,768]{1,0:T(8,128)(2,1)S(1)}, bf16[64,768]{1,0:T(8,128)(2,1)S(1)}, u32[]{:S(2)}, u32[]{:S(2)}) collective-permute-start(bf16[64,768]{1,0:T(8,128)(2,1)S(1)} %broadcast_select_fusion.8), channel_id=1, source_target_pairs={{0,8},{8,0},{16,24},{24,16},{1,9},{9,1},{17,25},{25,17},{2,10},{10... | collective-permute-start | bytes 294920 | tf_op jit(solution)/shard_map/ppermute | solution.py:70
  52.5 3.5 %collective-permute-start.6 = (bf16[64,768]{1,0:T(8,128)(2,1)S(1)}, bf16[64,768]{1,0:T(8,128)(2,1)S(1)}, u32[]{:S(2)}, u32[]{:S(2)}) collective-permute-start(bf16[64,768]{1,0:T(8,128)(2,1)S(1)} %broadcast_select_fusion.2), channel_id=1, source_target_pairs={{0,8},{8,0},{16,24},{24,16},{1,9},{9,1},{17,25},{25,17},{2,10},{10... | collective-permute-start | bytes 294920 | tf_op jit(solution)/shard_map/ppermute | solution.py:70
  53.5 3.2 %collective-permute-start.3 = (bf16[64,768]{1,0:T(8,128)(2,1)S(1)}, bf16[64,768]{1,0:T(8,128)(2,1)S(1)}, u32[]{:S(2)}, u32[]{:S(2)}) collective-permute-start(bf16[64,768]{1,0:T(8,128)(2,1)S(1)} %broadcast_select_fusion.5), channel_id=1, source_target_pairs={{0,8},{8,0},{16,24},{24,16},{1,9},{9,1},{17,25},{25,17},{2,10},{10... | collective-permute-start | bytes 294920 | tf_op jit(solution)/shard_map/ppermute | solution.py:70
  54.5 5.7 %collective-permute-start.1 = (bf16[64,768]{1,0:T(8,128)(2,1)S(1)}, bf16[64,768]{1,0:T(8,128)(2,1)S(1)}, u32[]{:S(2)}, u32[]{:S(2)}) collective-permute-start(bf16[64,768]{1,0:T(8,128)(2,1)S(1)} %add_convert_fusion.2), channel_id=1, source_target_pairs={{0,16},{8,24},{16,0},{24,8},{1,17},{9,25},{17,1},{25,9},{2,18},{10... | collective-permute-start | bytes 294920 | tf_op jit(solution)/shard_map/ppermute | solution.py:76
  56.1 6.2 %collective-permute-start.7 = (bf16[64,768]{1,0:T(8,128)(2,1)S(1)}, bf16[64,768]{1,0:T(8,128)(2,1)S(1)}, u32[]{:S(2)}, u32[]{:S(2)}) collective-permute-start(bf16[64,768]{1,0:T(8,128)(2,1)S(1)} %add_convert_fusion), channel_id=1, source_target_pairs={{0,16},{8,24},{16,0},{24,8},{1,17},{9,25},{17,1},{25,9},{2,18},{10... | collective-permute-start | bytes 294920 | tf_op jit(solution)/shard_map/ppermute | solution.py:76
  56.8 7.2 %collective-permute-start.4 = (bf16[64,768]{1,0:T(8,128)(2,1)S(1)}, bf16[64,768]{1,0:T(8,128)(2,1)S(1)}, u32[]{:S(2)}, u32[]{:S(2)}) collective-permute-start(bf16[64,768]{1,0:T(8,128)(2,1)S(1)} %add_convert_fusion.1), channel_id=1, source_target_pairs={{0,16},{8,24},{16,0},{24,8},{1,17},{9,25},{17,1},{25,9},{2,18},{10... | collective-permute-start | bytes 294920 | tf_op jit(solution)/shard_map/ppermute | solution.py:76
  60.9 5.5 %collective-permute-start.2 = (f32[64,768]{1,0:T(8,128)}, f32[64,768]{1,0:T(8,128)}, u32[]{:S(2)}, u32[]{:S(2)}) collective-permute-start(f32[64,768]{1,0:T(8,128)} %convert_add_fusion.2), channel_id=1, source_target_pairs={{0,8},{8,0},{16,24},{24,16},{1,9},{9,1},{17,25},{25,17},{2,10},{10... | collective-permute-start | bytes 589832 | tf_op jit(solution)/shard_map/ppermute | solution.py:79
  62.3 1.7 %collective-permute-start.8 = (f32[64,768]{1,0:T(8,128)S(1)}, f32[64,768]{1,0:T(8,128)S(1)}, u32[]{:S(2)}, u32[]{:S(2)}) collective-permute-start(f32[64,768]{1,0:T(8,128)S(1)} %convert_add_fusion), channel_id=1, source_target_pairs={{0,8},{8,0},{16,24},{24,16},{1,9},{9,1},{17,25},{25,17},{2,10},{10... | collective-permute-start | bytes 589832 | tf_op jit(solution)/shard_map/ppermute | solution.py:79
  64.0 1.5 %collective-permute-start.5 = (f32[64,768]{1,0:T(8,128)S(1)}, f32[64,768]{1,0:T(8,128)S(1)}, u32[]{:S(2)}, u32[]{:S(2)}) collective-permute-start(f32[64,768]{1,0:T(8,128)S(1)} %convert_add_fusion.1), channel_id=1, source_target_pairs={{0,8},{8,0},{16,24},{24,16},{1,9},{9,1},{17,25},{25,17},{2,10},{10... | collective-permute-start | bytes 589832 | tf_op jit(solution)/shard_map/ppermute | solution.py:79
  66.2 5.1 %collective-permute-start.18 = (f32[8,1,16]{2,0,1:T(8,128)S(1)}, f32[8,1,16]{2,0,1:T(8,128)S(1)}, u32[]{:S(2)}, u32[]{:S(2)}) collective-permute-start(f32[8,1,16]{2,0,1:T(8,128)S(1)} %reshape.184), channel_id=1, source_target_pairs={{0,8},{8,0},{16,24},{24,16},{1,9},{9,1},{17,25},{25,17},{2,10},{10... | collective-permute-start | bytes 1544 | tf_op jit(solution)/shard_map/ppermute | solution.py:53
  69.4 3.5 %copy-start.5 = (bf16[128,1280]{1,0:T(8,128)(2,1)S(1)}, bf16[128,1280]{1,0:T(8,128)(2,1)}, u32[]{:S(2)}) copy-start(bf16[128,1280]{1,0:T(8,128)(2,1)} %fusion.27) | copy-start | bytes 983044
  71.3 3.6 %collective-permute-start.19 = (f32[8,1,16]{2,0,1:T(8,128)S(1)}, f32[8,1,16]{2,0,1:T(8,128)S(1)}, u32[]{:S(2)}, u32[]{:S(2)}) collective-permute-start(f32[8,1,16]{2,0,1:T(8,128)S(1)} %add.110), channel_id=1, source_target_pairs={{0,16},{8,24},{16,0},{24,8},{1,17},{9,25},{17,1},{25,9},{2,18},{10... | collective-permute-start | bytes 1544 | tf_op jit(solution)/shard_map/ppermute | solution.py:53
  80.4 1.3 %collective-permute-start.9 = (bf16[2,64,96]{1,2,0:T(8,128)(2,1)S(1)}, bf16[2,64,96]{1,2,0:T(8,128)(2,1)S(1)}, u32[]{:S(2)}, u32[]{:S(2)}) collective-permute-start(bf16[2,64,96]{1,2,0:T(8,128)(2,1)S(1)} %broadcast_select_fusion.20), channel_id=1, source_target_pairs={{0,8},{8,0},{16,24},{24,16},{1,9},{9,1},{17,25},{25,17},{2,10},{10... | collective-permute-start | bytes 73736 | tf_op jit(solution)/shard_map/ppermute | solution.py:70
  80.6 2.8 %collective-permute-start.20 = (bf16[2,64,96]{1,2,0:T(8,128)(2,1)S(1)}, bf16[2,64,96]{1,2,0:T(8,128)(2,1)S(1)}, u32[]{:S(2)}, u32[]{:S(2)}) collective-permute-start(bf16[2,64,96]{1,2,0:T(8,128)(2,1)S(1)} %broadcast_select_fusion.11), channel_id=1, source_target_pairs={{0,8},{8,0},{16,24},{24,16},{1,9},{9,1},{17,25},{25,17},{2,10},{10... | collective-permute-start | bytes 73736 | tf_op jit(solution)/shard_map/ppermute | solution.py:70
  81.2 2.9 %collective-permute-start.15 = (bf16[2,64,96]{1,2,0:T(8,128)(2,1)S(1)}, bf16[2,64,96]{1,2,0:T(8,128)(2,1)S(1)}, u32[]{:S(2)}, u32[]{:S(2)}) collective-permute-start(bf16[2,64,96]{1,2,0:T(8,128)(2,1)S(1)} %broadcast_select_fusion.14), channel_id=1, source_target_pairs={{0,8},{8,0},{16,24},{24,16},{1,9},{9,1},{17,25},{25,17},{2,10},{10... | collective-permute-start | bytes 73736 | tf_op jit(solution)/shard_map/ppermute | solution.py:70
  81.2 4.5 %collective-permute-start.12 = (bf16[2,64,96]{1,2,0:T(8,128)(2,1)S(1)}, bf16[2,64,96]{1,2,0:T(8,128)(2,1)S(1)}, u32[]{:S(2)}, u32[]{:S(2)}) collective-permute-start(bf16[2,64,96]{1,2,0:T(8,128)(2,1)S(1)} %broadcast_select_fusion.17), channel_id=1, source_target_pairs={{0,8},{8,0},{16,24},{24,16},{1,9},{9,1},{17,25},{25,17},{2,10},{10... | collective-permute-start | bytes 73736 | tf_op jit(solution)/shard_map/ppermute | solution.py:70
  81.8 4.6 %collective-permute-start.10 = (bf16[2,64,96]{1,2,0:T(8,128)(2,1)S(1)}, bf16[2,64,96]{1,2,0:T(8,128)(2,1)S(1)}, u32[]{:S(2)}, u32[]{:S(2)}) collective-permute-start(bf16[2,64,96]{1,2,0:T(8,128)(2,1)S(1)} %add_convert_fusion.6), channel_id=1, source_target_pairs={{0,16},{8,24},{16,0},{24,8},{1,17},{9,25},{17,1},{25,9},{2,18},{10... | collective-permute-start | bytes 73736 | tf_op jit(solution)/shard_map/ppermute | solution.py:76
  83.5 4.2 %collective-permute-start.21 = (bf16[2,64,96]{1,2,0:T(8,128)(2,1)S(1)}, bf16[2,64,96]{1,2,0:T(8,128)(2,1)S(1)}, u32[]{:S(2)}, u32[]{:S(2)}) collective-permute-start(bf16[2,64,96]{1,2,0:T(8,128)(2,1)S(1)} %add_convert_fusion.3), channel_id=1, source_target_pairs={{0,16},{8,24},{16,0},{24,8},{1,17},{9,25},{17,1},{25,9},{2,18},{10... | collective-permute-start | bytes 73736 | tf_op jit(solution)/shard_map/ppermute | solution.py:76
  84.2 4.7 %collective-permute-start.16 = (bf16[2,64,96]{1,2,0:T(8,128)(2,1)S(1)}, bf16[2,64,96]{1,2,0:T(8,128)(2,1)S(1)}, u32[]{:S(2)}, u32[]{:S(2)}) collective-permute-start(bf16[2,64,96]{1,2,0:T(8,128)(2,1)S(1)} %add_convert_fusion.4), channel_id=1, source_target_pairs={{0,16},{8,24},{16,0},{24,8},{1,17},{9,25},{17,1},{25,9},{2,18},{10... | collective-permute-start | bytes 73736 | tf_op jit(solution)/shard_map/ppermute | solution.py:76
  85.8 4.2 %collective-permute-start.13 = (bf16[2,64,96]{1,2,0:T(8,128)(2,1)S(1)}, bf16[2,64,96]{1,2,0:T(8,128)(2,1)S(1)}, u32[]{:S(2)}, u32[]{:S(2)}) collective-permute-start(bf16[2,64,96]{1,2,0:T(8,128)(2,1)S(1)} %add_convert_fusion.5), channel_id=1, source_target_pairs={{0,16},{8,24},{16,0},{24,8},{1,17},{9,25},{17,1},{25,9},{2,18},{10... | collective-permute-start | bytes 73736 | tf_op jit(solution)/shard_map/ppermute | solution.py:76
  86.4 4.2 %collective-permute-start.11 = (f32[2,64,96]{1,2,0:T(8,128)S(1)}, f32[2,64,96]{1,2,0:T(8,128)S(1)}, u32[]{:S(2)}, u32[]{:S(2)}) collective-permute-start(f32[2,64,96]{1,2,0:T(8,128)S(1)} %convert_add_fusion.6), channel_id=1, source_target_pairs={{0,8},{8,0},{16,24},{24,16},{1,9},{9,1},{17,25},{25,17},{2,10},{10... | collective-permute-start | bytes 147464 | tf_op jit(solution)/shard_map/ppermute | solution.py:79
  87.7 3.0 %collective-permute-start.22 = (f32[2,64,96]{1,2,0:T(8,128)S(1)}, f32[2,64,96]{1,2,0:T(8,128)S(1)}, u32[]{:S(2)}, u32[]{:S(2)}) collective-permute-start(f32[2,64,96]{1,2,0:T(8,128)S(1)} %convert_add_fusion.3), channel_id=1, source_target_pairs={{0,8},{8,0},{16,24},{24,16},{1,9},{9,1},{17,25},{25,17},{2,10},{10... | collective-permute-start | bytes 147464 | tf_op jit(solution)/shard_map/ppermute | solution.py:79
  88.9 2.5 %collective-permute-start.17 = (f32[2,64,96]{1,2,0:T(8,128)S(1)}, f32[2,64,96]{1,2,0:T(8,128)S(1)}, u32[]{:S(2)}, u32[]{:S(2)}) collective-permute-start(f32[2,64,96]{1,2,0:T(8,128)S(1)} %convert_add_fusion.4), channel_id=1, source_target_pairs={{0,8},{8,0},{16,24},{24,16},{1,9},{9,1},{17,25},{25,17},{2,10},{10... | collective-permute-start | bytes 147464 | tf_op jit(solution)/shard_map/ppermute | solution.py:79
  90.6 2.3 %collective-permute-start.14 = (f32[2,64,96]{1,2,0:T(8,128)}, f32[2,64,96]{1,2,0:T(8,128)}, u32[]{:S(2)}, u32[]{:S(2)}) collective-permute-start(f32[2,64,96]{1,2,0:T(8,128)} %convert_add_fusion.5), channel_id=1, source_target_pairs={{0,8},{8,0},{16,24},{24,16},{1,9},{9,1},{17,25},{25,17},{2,10},{10... | collective-permute-start | bytes 147464 | tf_op jit(solution)/shard_map/ppermute | solution.py:79
  96.3 12.7 %all-to-all-start.1 = ((f32[8,3,16]{2,1,0:T(4,128)}), f32[8,3,16]{2,1,0:T(4,128)}, u32[]{:S(2)}, u32[]{:S(2)}) async-start(f32[8,3,16]{2,1,0:T(4,128)} %copy.60), calls=%async_computation.1 | async-start | bytes 32768 | tf_op jit(solution)/shard_map/all_to_all | solution.py:217
  (11 other events, 22.9 us)
Sparse Core Ops, SparseCore 0:
  28.3 46.5 all-gather.2

commit v10 on v9

--- a/solution.py
+++ b/solution.py
@@ -173,11 +173,16 @@
     part_cot_hot = jnp.einsum(
         "jrd,jhd->jrh", rows_cot, down_hot, preferred_element_type=jnp.float32
     )
-    pre_gate, pre_up, grad_hidden = grp_sum_rounded(
-        [part_gate, part_up, part_hidden], [0, 0, 0], "grp"
-    )
-    pre_gate_hot, pre_up_hot, grad_hidden_hot, cot_down = grp_sum_rounded(
-        [part_gate_hot, part_up_hot, part_hidden_hot, part_cot_hot], [1, 1, 1, 1], "grp"
+    (cold_sums,) = grp_sum_rounded([jnp.stack([part_gate, part_up, part_hidden])], [1], "grp")
+    pre_gate, pre_up, grad_hidden = cold_sums[0], cold_sums[1], cold_sums[2]
+    (hot_sums,) = grp_sum_rounded(
+        [jnp.stack([part_gate_hot, part_up_hot, part_hidden_hot, part_cot_hot])], [2], "grp"
+    )
+    pre_gate_hot, pre_up_hot, grad_hidden_hot, cot_down = (
+        hot_sums[0],
+        hot_sums[1],
+        hot_sums[2],
+        hot_sums[3],
     )
     hidden, back_gate, back_up = swiglu_back(pre_gate, pre_up, grad_hidden)
     output_slice = jnp.dot(hidden, w_down, preferred_element_type=jnp.float32)
@@ -217,8 +222,10 @@
     route_back = lax.all_to_all(route_parts, "ep", split_axis=0, concat_axis=0, tiled=True)
     cold_back = route_back[:, 0, :]
     hot_route = jnp.sum(route_back[:, 1:, :], axis=0)
-    gate_weight_grad = scatter_routes(cold_hit, cold_sel, cold_back) + scatter_routes(
-        hot_hit, hot_sel, hot_route
+    gate_weight_grad = scatter_routes(
+        jnp.concatenate([cold_hit, hot_hit], axis=1),
+        jnp.concatenate([cold_sel, hot_sel], axis=0),
+        jnp.concatenate([cold_back, hot_route], axis=0),
     )
     return (
         grad_gate_cold[None].astype(jnp.bfloat16),

time: 121 us -> 130 us (1.074)
  waiting for transfers between devices: 35.2 us -> 44.9 us
  starting transfers between devices: 22.9 us -> 16.4 us
  matrix products: 20.2 us -> 24.2 us
  local copies, waits for them, and re-layouts: 8.96 us -> 10.5 us
    all_gather x1, waiting for transfers between devices: 0.01 us -> 9.02 us  [body(): gathered = lax.all_gather(hot_outgoing, 'ep', axis=0, tiled=False)]
    ppermute x7 -> x2, starting transfers between devices: 8.02 us -> 3.09 us  [grp_sum_rounded(): got = lax.ppermute(mine, axis_name, partner)]
    eq x0 -> x2, other arithmetic: none -> 2.14 us  [token_table(): hit = expert_ids.T[:, None, :] == targets[None, :, None]]
    select_n x7 -> x2, other arithmetic: 3.36 us -> 1.48 us  [grp_sum_rounded(): first = jnp.where(first_core, s, o)]
    concatenate x3 -> x0, local copies, waits for them, and re-layouts: 1.84 us -> none  [grp_sum_rounded(): full.append(jnp.concatenate([first, second], axis=a))]
    slice x1 -> x4, local copies, waits for them, and re-layouts: 0.21 us -> 2.05 us  [the longest x1 0.99 us: body(): hot_sums[0]]
    unnamed x39 -> x51, local copies, waits for them, and re-layouts: 2.99 us -> 4.61 us
    ppermute x7 -> x2, waiting for transfers between devices: 0.07 us -> 1.57 us  [grp_sum_rounded(): got = lax.ppermute(send, axis_name, swap)]
  transfers between devices with their start and end apart: 26 -> 11, of which waited for: 10 -> 6; matrix products, arithmetic and copies ran while one was open for 19% -> 26% of each run, Pallas kernels for 0% -> 0%
where the time goes in v10:
time: 130 us; the launch traced here: 129 us
  waiting for transfers between devices  44.9 us (35%)
  matrix products  24.2 us (19%)
  other arithmetic  18.9 us (15%)
  starting transfers between devices  16.4 us (13%)
  between operations  14.5 us (11%)
  local copies, waits for them, and re-layouts  10.5 us (8%)
    all_to_all x1, waiting for transfers between devices, body(): lax.all_to_all(outgoing, 'ep', split_axis=0, concat_axis=0, tiled=True)  24.8 us
    all_gather x1, waiting for transfers between devices, body(): gathered = lax.all_gather(hot_outgoing, 'ep', axis=0, tiled=False)  9.02 us
    ppermute x2, waiting for transfers between devices, grp_sum_rounded(): got = lax.ppermute(mine, axis_name, partner)  8.66 us
    all_to_all x1, starting transfers between devices, body(): lax.all_to_all(outgoing, 'ep', split_axis=0, concat_axis=0, tiled=True)  7.28 us
    unnamed x51, local copies, waits for them, and re-layouts  4.61 us
    all_to_all x1, starting transfers between devices, body(): lax.all_to_all(route_parts, 'ep', split_axis=0, concat_axis=0, tiled=True)  3.93 us
    dot_general x1, matrix products, body(): jnp.einsum('jbcd,jbch->jbdh', feat_b, bu_b, preferred_element_type=jnp.fl...  3.14 us
    ppermute x2, starting transfers between devices, grp_sum_rounded(): got = lax.ppermute(mine, axis_name, partner)  3.09 us
  transfers between devices with their start and end apart: 11, of which 6 were waited for; matrix products, arithmetic and copies ran while one was open for 26% of the time, Pallas kernels for 0%

profile of v10, /device:TPU:0, one launch (start us, length us, event | category | flops | bytes accessed | tf_op | source)
XLA Modules:
  0.0 129.4 jit_solution(8077313935698493644)
XLA Ops:
  7.4 1.5 %broadcast_compare_fusion = (pred[6,2,256]{2,0,1:T(8,128)(4,1)}, pred[2,256]{1,0:T(4,128)(4,1)S(1)}) fusion(s32[6,256]{1,0:T(8,128)} %bitcast.200, s32[2]{0:T(128)} %param.15), kind=kLoop, calls=%fused_computation.132 | loop fusion | flops 5632 | bytes 9736 | tf_op jit(solution)/shard_map/eq | solution.py:8
  11.8 1.3 %convolution_convert_fusion.8 = bf16[32,1280]{1,0:T(8,128)(2,1)S(1)} fusion(pred[32,256]{1,0:T(32,128)(4,1)S(1)} %fusion.66, bf16[256,1280]{1,0:T(8,128)(2,1)} %param.12), kind=kOutput, calls=%fused_computation.15 | convolution fusion | flops 21012480 | bytes 745472 | tf_op jit(solution)/shard_map/dot_general | solution.py:20
  13.2 1.3 %convolution_convert_fusion.9 = bf16[32,1280]{1,0:T(8,128)(2,1)S(1)} fusion(pred[32,256]{1,0:T(32,128)(4,1)S(1)} %fusion.66, bf16[256,1280]{1,0:T(8,128)(2,1)} %param.11), kind=kOutput, calls=%fused_computation.16 | convolution fusion | flops 21012480 | bytes 745472 | tf_op jit(solution)/shard_map/dot_general | solution.py:19
  17.6 0.9 pad_maximum_fusion
  18.6 7.3 %all-to-all-start = ((bf16[8,40,1280]{2,1,0:T(8,128)(2,1)}), bf16[8,40,1280]{2,1,0:T(8,128)(2,1)S(1)}, u32[]{:S(2)}, u32[]{:S(2)}) async-start(bf16[8,40,1280]{2,1,0:T(8,128)(2,1)} %pad_maximum_fusion), calls=%async_computation | async-start | bytes 1638400 | tf_op jit(solution)/shard_map/all_to_all | solution.py:140
  26.6 24.8 %all-to-all-done = bf16[8,40,1280]{2,1,0:T(8,128)(2,1)S(1)} async-done(((bf16[8,40,1280]{2,1,0:T(8,128)(2,1)}), bf16[8,40,1280]{2,1,0:T(8,128)(2,1)S(1)}, u32[]{:S(2)}, u32[]{:S(2)}) %all-to-all-start) | async-done | bytes 819232 | tf_op jit(solution)/shard_map/all_to_all | solution.py:140
  51.4 0.9 slice_convert_fusion
  55.4 1.6 %collective-permute-done = bf16[3,64,768]{2,1,0:T(8,128)(2,1)S(1)} collective-permute-done((bf16[3,64,768]{2,1,0:T(8,128)(2,1)S(1)}, bf16[3,64,768]{2,1,0:T(8,128)(2,1)S(1)}, u32[]{:S(2)}, u32[]{:S(2)}) %collective-permute-start) | collective-permute-done | bytes 294944 | tf_op jit(solution)/shard_map/ppermute | solution.py:70
  57.1 1.6 %collective-permute-start.1 = (bf16[3,64,768]{2,1,0:T(8,128)(2,1)S(1)}, bf16[3,64,768]{2,1,0:T(8,128)(2,1)S(1)}, u32[]{:S(2)}, u32[]{:S(2)}) collective-permute-start(bf16[3,64,768]{2,1,0:T(8,128)(2,1)S(1)} %add_convert_fusion), channel_id=1, source_target_pairs={{0,16},{8,24},{16,0},{24,8},{1,17},{9,25},{17,1},{25,9},{2,18},{10... | collective-permute-start | bytes 884744 | tf_op jit(solution)/shard_map/ppermute | solution.py:76
  59.9 6.3 %collective-permute-done.1 = bf16[3,64,768]{2,1,0:T(8,128)(2,1)S(1)} collective-permute-done((bf16[3,64,768]{2,1,0:T(8,128)(2,1)S(1)}, bf16[3,64,768]{2,1,0:T(8,128)(2,1)S(1)}, u32[]{:S(2)}, u32[]{:S(2)}) %collective-permute-start.1) | collective-permute-done | bytes 294944 | tf_op jit(solution)/shard_map/ppermute | solution.py:76
  66.9 9.0 %all-gather.3.cloned.1.call-done = bf16[576,1280]{1,0:T(8,128)(2,1)} async-done(((bf16[72,1280]{1,0:T(8,128)(2,1)}), bf16[576,1280]{1,0:T(8,128)(2,1)}) %all-gather.3.cloned.1.call-update) | async-done | bytes 1474576 | tf_op jit(solution)/shard_map/all_gather | solution.py:119
  75.9 0.9 slice_bitcast_fusion
  76.8 1.4 %slice.100 = bf16[8,64,1280]{2,1,0:T(8,128)(2,1)S(1)} slice(bf16[8,72,1280]{2,1,0:T(8,128)(2,1)} %bitcast.187), slice={[0:8], [0:64], [0:1280]} | slice | bytes 2621440 | tf_op jit(solution)/shard_map/slice | solution.py:155
  78.6 1.2 copy-done.16
  79.8 1.0 fusion.33
  80.7 1.0 fusion.32
  81.7 1.0 fusion.35
  82.8 1.4 %fusion.34 = bf16[1,2,128,96]{2,3,1,0:T(8,128)(2,1)S(1)} fusion(bf16[2,96,1280]{2,1,0:T(8,128)(2,1)} %param.21, bf16[2,128,1280]{2,1,0:T(8,128)(2,1)S(1)} %bitcast.184, f32[2,128]{1,0:T(2,128)S(1)} %reshape.193), kind=kOutput, calls=%fused_computation.45 | convolution fusion | flops 63922176 | bytes 1197056 | tf_op jit(solution)/shard_map/jrd,jhd->jrh/dot_general | solution.py:170
  86.0 1.4 %broadcast_select_fusion.1 = (f32[3,64,768]{2,1,0:T(8,128)S(1)}, f32[3,64,768]{2,1,0:T(8,128)S(1)}) fusion(f32[3,64,768]{2,1,0:T(8,128)} %collective-permute-done.2, pred[]{:T(512)S(6)} %eq.103, bf16[3,64,768]{2,1,0:T(8,128)(2,1)} %copy-done.15, bf16[3,64,768]{2,1,0:T(8,128)(2,1)} %copy-done.7), kind=kLoop, calls=%fused_computation.75 | loop fusion | flops 737280 | bytes 2359297 | tf_op jit(solution)/shard_map/jit(_where)/select_n | solution.py:82
  89.9 1.3 add_convert_fusion.1
  91.2 1.5 %collective-permute-start.4 = (bf16[4,2,64,96]{2,3,1,0:T(8,128)(2,1)S(1)}, bf16[4,2,64,96]{2,3,1,0:T(8,128)(2,1)S(1)}, u32[]{:S(2)}, u32[]{:S(2)}) collective-permute-start(bf16[4,2,64,96]{2,3,1,0:T(8,128)(2,1)S(1)} %add_convert_fusion.1), channel_id=1, source_target_pairs={{0,16},{8,24},{16,0},{24,8},{1,17},{9,25},{17,1},{25,9},{2,18},{10... | collective-permute-start | bytes 294920 | tf_op jit(solution)/shard_map/ppermute | solution.py:76
  92.7 3.1 %fusion = bf16[1,1280,768]{2,1,0:T(8,128)(2,1)} fusion(bf16[128,1280]{1,0:T(8,128)(2,1)S(1)} %bitcast.176, f32[1,128,768]{2,1,0:T(8,128)} %get-tuple-element.21, f32[3,64,768]{2,1,0:T(8,128)S(1)} %get-tuple-element.24, f32[3,64,768]{2,1,0:T(8,128)S(1)} %get-tuple-element.25), kind=kOutput, calls=%fused_computation.9 | convolution fusion | flops 253820928 | bytes 3866624 | tf_op jit(solution)/shard_map/dot_general | solution.py:192
  95.8 2.4 %collective-permute-done.4 = bf16[4,2,64,96]{2,3,1,0:T(8,128)(2,1)S(1)} collective-permute-done((bf16[4,2,64,96]{2,3,1,0:T(8,128)(2,1)S(1)}, bf16[4,2,64,96]{2,3,1,0:T(8,128)(2,1)S(1)}, u32[]{:S(2)}, u32[]{:S(2)}) %collective-permute-start.4) | collective-permute-done | bytes 98336 | tf_op jit(solution)/shard_map/ppermute | solution.py:76
  98.3 2.0 %fusion.1 = bf16[1,1280,768]{2,1,0:T(8,128)(2,1)} fusion(bf16[128,1280]{1,0:T(8,128)(2,1)S(1)} %bitcast.177, f32[1,128,768]{2,1,0:T(8,128)S(1)} %copy-done.4, f32[3,64,768]{2,1,0:T(8,128)S(1)} %get-tuple-element.24, f32[3,64,768]{2,1,0:T(8,128)S(1)} %get-tuple-element.25), kind=kOutput, calls=%fused_computation.10 | convolution fusion | flops 253329408 | bytes 3866624 | tf_op jit(solution)/shard_map/dot_general | solution.py:195
  100.3 1.5 %collective-permute-start.7 = (f32[8,1,16]{2,0,1:T(8,128)S(1)}, f32[8,1,16]{2,0,1:T(8,128)S(1)}, u32[]{:S(2)}, u32[]{:S(2)}) collective-permute-start(f32[8,1,16]{2,0,1:T(8,128)S(1)} %add.71), channel_id=1, source_target_pairs={{0,16},{8,24},{16,0},{24,8},{1,17},{9,25},{17,1},{25,9},{2,18},{10... | collective-permute-start | bytes 1544 | tf_op jit(solution)/shard_map/ppermute | solution.py:53
  101.8 2.0 %fusion.2 = bf16[1,768,1280]{2,1,0:T(8,128)(2,1)} fusion(bf16[128,768]{1,0:T(8,128)(2,1)S(1)} %copy-done.14, bf16[128,1280]{1,0:T(8,128)(2,1)S(1)} %bitcast.182), kind=kOutput, calls=%fused_computation.11 | convolution fusion | flops 252641280 | bytes 2490368 | tf_op jit(solution)/shard_map/dot_general | solution.py:198
  105.6 3.9 %all-to-all-start.1 = ((f32[8,3,16]{2,1,0:T(4,128)}), f32[8,3,16]{2,1,0:T(4,128)}, u32[]{:S(2)}, u32[]{:S(2)}) async-start(f32[8,3,16]{2,1,0:T(4,128)} %copy.62), calls=%async_computation.1 | async-start | bytes 32768 | tf_op jit(solution)/shard_map/all_to_all | solution.py:222
  110.3 1.0 copy.60
  111.4 3.1 %convert_reduce_fusion.1 = f32[2,1280,96]{1,2,0:T(8,128)} fusion(f32[2,8,16,96]{3,2,1,0:T(8,128)} %bitcast.198, f32[2,8,16,96]{3,2,1,0:T(8,128)S(1)} %bitcast.193, bf16[2,2,8,16,1280]{4,3,2,1,0:T(8,128)(2,1)S(1)} %bitcast.171), kind=kOutput, calls=%fused_computation.1 | convolution fusion | flops 68714496 | bytes 1867776 | tf_op jit(solution)/shard_map/jbcd,jbch->jbdh/dot_general | solution.py:210
  114.5 2.2 %convert_reduce_fusion.2 = f32[2,1280,96]{1,2,0:T(8,128)} fusion(f32[2,8,16,96]{3,2,1,0:T(8,128)S(1)} %bitcast.194, f32[2,8,16,96]{3,2,1,0:T(8,128)S(1)} %bitcast.199, f32[2,8,16,96]{3,2,1,0:T(8,128)S(1)} %bitcast.191, bf16[2,2,8,16,1280]{4,3,2,1,0:T(8,128)(2,1)S(1)} %bitcast.172), kind=kOutput, calls=%fused_computation.2 | convolution fusion | flops 68812800 | bytes 2031616 | tf_op jit(solution)/shard_map/jbcd,jbch->jbdh/dot_general | solution.py:209
  116.7 2.2 %convert_reduce_fusion = f32[2,96,1280]{2,1,0:T(8,128)} fusion(f32[2,8,16]{2,1,0:T(8,128)S(1)} %copy.57, f32[2,8,16,96]{3,2,1,0:T(8,128)S(1)} %bitcast.192, f32[2,8,16,96]{3,2,1,0:T(8,128)S(1)} %bitcast.195, bf16[2,2,8,16,1280]{4,3,2,1,0:T(8,128)(2,1)S(1)} %bitcast.173), kind=kOutput, calls=%fused_computation | convolution fusion | flops 69697536 | bytes 1908736 | tf_op jit(solution)/shard_map/jbch,jbcd->jbhd/dot_general | solution.py:211
  121.2 1.3 %select_reduce_fusion.2 = f32[6,256]{1,0:T(8,128)} fusion(pred[6,2,256]{2,0,1:T(8,128)(4,1)} %get-tuple-element.30, pred[6,8,256]{2,0,1:T(8,128)(4,1)} %get-tuple-element.32, f32[10,256]{1,0:T(8,128)S(1)} %select_reduce_fusion), kind=kLoop, calls=%fused_computation.112 | loop fusion | flops 44544 | bytes 31744 | tf_op jit(solution)/shard_map/reduce_sum | solution.py:32
  (132 shorter events, 21.7 us)
Async XLA Ops:
  7.2 47.2 %copy-start = (bf16[1,768,1280]{2,1,0:T(8,128)(2,1)S(1)}, bf16[1,768,1280]{2,1,0:T(8,128)(2,1)}, u32[]{:S(2)}) copy-start(bf16[1,768,1280]{2,1,0:T(8,128)(2,1)} %param.18) | copy-start | bytes 5898244
  7.2 8.0 %copy-start.20 = (s32[256,6]{0,1:T(8,128)S(1)}, s32[256,6]{0,1:T(8,128)}, u32[]{:S(2)}) copy-start(s32[256,6]{0,1:T(8,128)} %param.14) | copy-start | bytes 18436
  7.2 8.0 %copy-start.22 = (bf16[256,6]{0,1:T(8,128)(2,1)S(1)}, bf16[256,6]{0,1:T(8,128)(2,1)}, u32[]{:S(2)}) copy-start(bf16[256,6]{0,1:T(8,128)(2,1)} %param.13) | copy-start | bytes 9220
  7.2 9.9 %copy-start.8 = (bf16[256,1280]{1,0:T(8,128)(2,1)S(1)}, bf16[256,1280]{1,0:T(8,128)(2,1)}, u32[]{:S(2)}) copy-start(bf16[256,1280]{1,0:T(8,128)(2,1)} %param.12) | copy-start | bytes 1966084
  7.2 10.1 %copy-start.9 = (bf16[256,1280]{1,0:T(8,128)(2,1)S(1)}, bf16[256,1280]{1,0:T(8,128)(2,1)}, u32[]{:S(2)}) copy-start(bf16[256,1280]{1,0:T(8,128)(2,1)} %param.11) | copy-start | bytes 1966084
  18.6 32.8 %all-to-all-start = ((bf16[8,40,1280]{2,1,0:T(8,128)(2,1)}), bf16[8,40,1280]{2,1,0:T(8,128)(2,1)S(1)}, u32[]{:S(2)}, u32[]{:S(2)}) async-start(bf16[8,40,1280]{2,1,0:T(8,128)(2,1)} %pad_maximum_fusion), calls=%async_computation | async-start | bytes 1638400 | tf_op jit(solution)/shard_map/all_to_all | solution.py:140
  25.8 50.1 %all-gather.3.cloned.1.call-start = ((), (), s32[]{:S(2)}) async-start(), calls=%async_computation.2 | async-start | bytes 1658880 | tf_op jit(solution)/shard_map/all_gather | solution.py:119
  51.4 1.8 %copy-start.11 = (bf16[1,1280,768]{2,1,0:T(8,128)(2,1)S(1)}, bf16[1,1280,768]{2,1,0:T(8,128)(2,1)}, u32[]{:S(2)}) copy-start(bf16[1,1280,768]{2,1,0:T(8,128)(2,1)} %param.17) | copy-start | bytes 5898244
  51.4 2.3 %copy-start.12 = (bf16[1,1280,768]{2,1,0:T(8,128)(2,1)S(1)}, bf16[1,1280,768]{2,1,0:T(8,128)(2,1)}, u32[]{:S(2)}) copy-start(bf16[1,1280,768]{2,1,0:T(8,128)(2,1)} %param.16) | copy-start | bytes 5898244
  54.3 0.9 copy-start.5
  55.3 1.6 %collective-permute-start = (bf16[3,64,768]{2,1,0:T(8,128)(2,1)S(1)}, bf16[3,64,768]{2,1,0:T(8,128)(2,1)S(1)}, u32[]{:S(2)}, u32[]{:S(2)}) collective-permute-start(bf16[3,64,768]{2,1,0:T(8,128)(2,1)S(1)} %broadcast_select_fusion.2), channel_id=1, source_target_pairs={{0,8},{8,0},{16,24},{24,16},{1,9},{9,1},{17,25},{25,17},{2,10},{10... | collective-permute-start | bytes 884744 | tf_op jit(solution)/shard_map/ppermute | solution.py:70
  57.0 9.1 %copy-start.7 = (bf16[3,64,768]{2,1,0:T(8,128)(2,1)}, bf16[3,64,768]{2,1,0:T(8,128)(2,1)S(1)}, u32[]{:S(2)}) copy-start(bf16[3,64,768]{2,1,0:T(8,128)(2,1)S(1)} %add_convert_fusion) | copy-start | bytes 884740
  57.1 9.1 %collective-permute-start.1 = (bf16[3,64,768]{2,1,0:T(8,128)(2,1)S(1)}, bf16[3,64,768]{2,1,0:T(8,128)(2,1)S(1)}, u32[]{:S(2)}, u32[]{:S(2)}) collective-permute-start(bf16[3,64,768]{2,1,0:T(8,128)(2,1)S(1)} %add_convert_fusion), channel_id=1, source_target_pairs={{0,16},{8,24},{16,0},{24,8},{1,17},{9,25},{17,1},{25,9},{2,18},{10... | collective-permute-start | bytes 884744 | tf_op jit(solution)/shard_map/ppermute | solution.py:76
  66.9 19.1 %collective-permute-start.2 = (f32[3,64,768]{2,1,0:T(8,128)S(1)}, f32[3,64,768]{2,1,0:T(8,128)}, u32[]{:S(2)}, u32[]{:S(2)}) collective-permute-start(f32[3,64,768]{2,1,0:T(8,128)S(1)} %convert_add_fusion), channel_id=1, source_target_pairs={{0,8},{8,0},{16,24},{24,16},{1,9},{9,1},{17,25},{25,17},{2,10},{10... | collective-permute-start | bytes 1769480 | tf_op jit(solution)/shard_map/ppermute | solution.py:79
  78.4 2.4 %copy-start.1 = (bf16[8,2,2,16,1280]{4,3,0,2,1:T(8,128)(2,1)}, bf16[8,2,2,16,1280]{4,3,0,2,1:T(8,128)(2,1)S(1)}, u32[]{:S(2)}) copy-start(bf16[8,2,2,16,1280]{4,3,0,2,1:T(8,128)(2,1)S(1)} %copy.73) | copy-start | bytes 3932164
  78.4 1.4 %copy-start.16 = (bf16[2,1280,96]{1,2,0:T(8,128)(2,1)S(1)}, bf16[2,1280,96]{1,2,0:T(8,128)(2,1)}, u32[]{:S(2)}) copy-start(bf16[2,1280,96]{1,2,0:T(8,128)(2,1)} %param.20) | copy-start | bytes 1474564
  78.4 2.3 %copy-start.17 = (bf16[2,1280,96]{1,2,0:T(8,128)(2,1)S(1)}, bf16[2,1280,96]{1,2,0:T(8,128)(2,1)}, u32[]{:S(2)}) copy-start(bf16[2,1280,96]{1,2,0:T(8,128)(2,1)} %param.19) | copy-start | bytes 1474564
  78.5 3.2 %copy-start.18 = (bf16[2,96,1280]{2,1,0:T(8,128)(2,1)S(1)}, bf16[2,96,1280]{2,1,0:T(8,128)(2,1)}, u32[]{:S(2)}) copy-start(bf16[2,96,1280]{2,1,0:T(8,128)(2,1)} %param.21) | copy-start | bytes 1474564
  85.2 0.8 copy-start.3
  86.0 2.9 %copy-start.10 = (f32[8,16,1280]{2,1,0:T(8,128)S(1)}, f32[8,16,1280]{2,1,0:T(8,128)}, u32[]{:S(2)}) copy-start(f32[8,16,1280]{2,1,0:T(8,128)} %get-tuple-element.26) | copy-start | bytes 1966084
  86.0 4.0 %collective-permute-start.3 = (bf16[4,2,64,96]{2,3,1,0:T(8,128)(2,1)}, bf16[4,2,64,96]{2,3,1,0:T(8,128)(2,1)}, u32[]{:S(2)}, u32[]{:S(2)}) collective-permute-start(bf16[4,2,64,96]{2,3,1,0:T(8,128)(2,1)} %broadcast_select_fusion.5), channel_id=1, source_target_pairs={{0,8},{8,0},{16,24},{24,16},{1,9},{9,1},{17,25},{25,17},{2,10},{10... | collective-permute-start | bytes 294920 | tf_op jit(solution)/shard_map/ppermute | solution.py:70
  89.5 10.8 %collective-permute-start.6 = (f32[8,1,16]{2,0,1:T(8,128)S(1)}, f32[8,1,16]{2,0,1:T(8,128)S(1)}, u32[]{:S(2)}, u32[]{:S(2)}) collective-permute-start(f32[8,1,16]{2,0,1:T(8,128)S(1)} %reshape.189), channel_id=1, source_target_pairs={{0,8},{8,0},{16,24},{24,16},{1,9},{9,1},{17,25},{25,17},{2,10},{10... | collective-permute-start | bytes 1544 | tf_op jit(solution)/shard_map/ppermute | solution.py:53
  91.2 6.9 %collective-permute-start.4 = (bf16[4,2,64,96]{2,3,1,0:T(8,128)(2,1)S(1)}, bf16[4,2,64,96]{2,3,1,0:T(8,128)(2,1)S(1)}, u32[]{:S(2)}, u32[]{:S(2)}) collective-permute-start(bf16[4,2,64,96]{2,3,1,0:T(8,128)(2,1)S(1)} %add_convert_fusion.1), channel_id=1, source_target_pairs={{0,16},{8,24},{16,0},{24,8},{1,17},{9,25},{17,1},{25,9},{2,18},{10... | collective-permute-start | bytes 294920 | tf_op jit(solution)/shard_map/ppermute | solution.py:76
  92.7 5.6 %copy-start.4 = (f32[1,128,768]{2,1,0:T(8,128)S(1)}, f32[1,128,768]{2,1,0:T(8,128)}, u32[]{:S(2)}) copy-start(f32[1,128,768]{2,1,0:T(8,128)} %get-tuple-element.21) | copy-start | bytes 1179652
  98.2 3.6 %copy-start.6 = (bf16[8,16,1280]{2,1,0:T(8,128)(2,1)S(1)}, bf16[8,16,1280]{2,1,0:T(8,128)(2,1)}, u32[]{:S(2)}) copy-start(bf16[8,16,1280]{2,1,0:T(8,128)(2,1)} %copy-done.5) | copy-start | bytes 983044
  98.2 3.6 %copy-start.14 = (bf16[128,768]{1,0:T(8,128)(2,1)S(1)}, bf16[128,768]{1,0:T(8,128)(2,1)}, u32[]{:S(2)}) copy-start(bf16[128,768]{1,0:T(8,128)(2,1)} %copy-done.13) | copy-start | bytes 589828
  98.2 5.7 %collective-permute-start.5 = (f32[4,2,64,96]{2,3,1,0:T(8,128)S(1)}, f32[4,2,64,96]{2,3,1,0:T(8,128)S(1)}, u32[]{:S(2)}, u32[]{:S(2)}) collective-permute-start(f32[4,2,64,96]{2,3,1,0:T(8,128)S(1)} %convert_add_fusion.1), channel_id=1, source_target_pairs={{0,8},{8,0},{16,24},{24,16},{1,9},{9,1},{17,25},{25,17},{2,10},{10... | collective-permute-start | bytes 589832 | tf_op jit(solution)/shard_map/ppermute | solution.py:79
  100.3 3.6 %collective-permute-start.7 = (f32[8,1,16]{2,0,1:T(8,128)S(1)}, f32[8,1,16]{2,0,1:T(8,128)S(1)}, u32[]{:S(2)}, u32[]{:S(2)}) collective-permute-start(f32[8,1,16]{2,0,1:T(8,128)S(1)} %add.71), channel_id=1, source_target_pairs={{0,16},{8,24},{16,0},{24,8},{1,17},{9,25},{17,1},{25,9},{2,18},{10... | collective-permute-start | bytes 1544 | tf_op jit(solution)/shard_map/ppermute | solution.py:53
  103.9 7.4 %copy-start.2 = (bf16[8,2,2,16,1280]{4,3,0,2,1:T(8,128)(2,1)S(1)}, bf16[8,2,2,16,1280]{4,3,0,2,1:T(8,128)(2,1)}, u32[]{:S(2)}) copy-start(bf16[8,2,2,16,1280]{4,3,0,2,1:T(8,128)(2,1)} %copy-done.1) | copy-start | bytes 3932164
  105.6 13.3 %all-to-all-start.1 = ((f32[8,3,16]{2,1,0:T(4,128)}), f32[8,3,16]{2,1,0:T(4,128)}, u32[]{:S(2)}, u32[]{:S(2)}) async-start(f32[8,3,16]{2,1,0:T(4,128)} %copy.62), calls=%async_computation.1 | async-start | bytes 32768 | tf_op jit(solution)/shard_map/all_to_all | solution.py:222
  111.3 3.2 %copy-start.19 = (f32[1,2,128,96]{3,2,1,0:T(8,128)S(1)}, f32[1,2,128,96]{3,2,1,0:T(8,128)}, u32[]{:S(2)}) copy-start(f32[1,2,128,96]{3,2,1,0:T(8,128)} %copy.58) | copy-start | bytes 294916
  114.5 5.8 %copy-start.21 = (pred[2,16,256]{2,1,0:T(8,128)(4,1)S(1)}, pred[2,16,256]{2,1,0:T(8,128)(4,1)}, u32[]{:S(2)}) copy-start(pred[2,16,256]{2,1,0:T(8,128)(4,1)} %fusion.65) | copy-start | bytes 24580
  (2 other events, 1.4 us)
Sparse Core Ops, SparseCore 0:
  29.4 46.4 all-gather.2

commit v11 on v9

--- a/solution.py
+++ b/solution.py
@@ -195,18 +195,13 @@
     )
     hidden_hot, back_gate_hot, back_up_hot = swiglu_back(pre_gate_hot, pre_up_hot, grad_hidden_hot)
     hot_route_part = jnp.sum(hidden_hot.astype(jnp.float32) * cot_down, axis=2)
-    hidden_blk = hidden_hot.shape[2]
-    feat_b = rows_feat.reshape(hot_count, blocks, capacity, slice_width)
-    wt_b = rows_wt.reshape(hot_count, blocks, capacity, slice_width)
-    bg_b = back_gate_hot.reshape(hot_count, blocks, capacity, hidden_blk)
-    bu_b = back_up_hot.reshape(hot_count, blocks, capacity, hidden_blk)
-    hid_b = hidden_hot.reshape(hot_count, blocks, capacity, hidden_blk)
-    blk_gate = jnp.einsum("jbcd,jbch->jbdh", feat_b, bg_b, preferred_element_type=jnp.float32)
-    blk_up = jnp.einsum("jbcd,jbch->jbdh", feat_b, bu_b, preferred_element_type=jnp.float32)
-    blk_down = jnp.einsum("jbch,jbcd->jbhd", hid_b, wt_b, preferred_element_type=jnp.float32)
-    grad_gate_hot = jnp.sum(blk_gate.astype(jnp.bfloat16).astype(jnp.float32), axis=1)
-    grad_up_hot = jnp.sum(blk_up.astype(jnp.bfloat16).astype(jnp.float32), axis=1)
-    grad_down_hot = jnp.sum(blk_down.astype(jnp.bfloat16).astype(jnp.float32), axis=1)
+    grad_gate_hot = jnp.einsum(
+        "jrd,jrh->jdh", rows_feat, back_gate_hot, preferred_element_type=jnp.float32
+    )
+    grad_up_hot = jnp.einsum("jrd,jrh->jdh", rows_feat, back_up_hot, preferred_element_type=jnp.float32)
+    grad_down_hot = jnp.einsum(
+        "jrh,jrd->jhd", hidden_hot, rows_wt, preferred_element_type=jnp.float32
+    )
     route_parts = jnp.concatenate(
         [
             cold_route,
@@ -217,8 +212,10 @@
     route_back = lax.all_to_all(route_parts, "ep", split_axis=0, concat_axis=0, tiled=True)
     cold_back = route_back[:, 0, :]
     hot_route = jnp.sum(route_back[:, 1:, :], axis=0)
-    gate_weight_grad = scatter_routes(cold_hit, cold_sel, cold_back) + scatter_routes(
-        hot_hit, hot_sel, hot_route
+    gate_weight_grad = scatter_routes(
+        jnp.concatenate([cold_hit, hot_hit], axis=1),
+        jnp.concatenate([cold_sel, hot_sel], axis=0),
+        jnp.concatenate([cold_back, hot_route], axis=0),
     )
     return (
         grad_gate_cold[None].astype(jnp.bfloat16),

time: 121 us -> 120 us (level)
  waiting for transfers between devices: 35.2 us -> 37.2 us
  other arithmetic: 18.4 us -> 16.7 us
  local copies, waits for them, and re-layouts: 8.96 us -> 7.39 us
    eq x0 -> x2, other arithmetic: none -> 2.14 us  [token_table(): hit = expert_ids.T[:, None, :] == targets[None, :, None]]
    all_to_all x1, waiting for transfers between devices: 0.01 us -> 2.06 us  [body(): lax.all_to_all(route_parts, 'ep', split_axis=0, concat_axis=0, tiled=True)]
    dot_general x3, matrix products: 7.49 us -> 5.65 us  [the longest x1 2.25 us: body(): jnp.einsum('jrd,jrh->jdh', rows_feat, back_gate_hot, preferred_element_ty...]
    concatenate x3 -> x0, local copies, waits for them, and re-layouts: 1.84 us -> none  [grp_sum_rounded(): full.append(jnp.concatenate([first, second], axis=a))]
    reduce_sum x2 -> x1, other arithmetic: 1.57 us -> 0.11 us  [scatter_routes(): per_token = jnp.sum(jnp.where(sel, values[:, :, None], 0.0), axis=1)]
    select_n x7, other arithmetic: 3.36 us -> 2.02 us  [grp_sum_rounded(): first = jnp.where(first_core, s, o)]
    reshape x1, local copies, waits for them, and re-layouts: 0.08 us -> 1.35 us  [body(): hot_route_part.reshape(hot_count, blocks, capacity)]
  transfers between devices with their start and end apart: 26 -> 26, of which waited for: 10 -> 13; matrix products, arithmetic and copies ran while one was open for 19% -> 21% of each run, Pallas kernels for 0% -> 0%
where the time goes in v11:
time: 120 us; the launch traced here: 119 us
  waiting for transfers between devices  37.2 us (31%)
  starting transfers between devices  22.2 us (18%)
  matrix products  20.6 us (17%)
  other arithmetic  16.7 us (14%)
  between operations  14.7 us (12%)
  local copies, waits for them, and re-layouts  7.39 us (6%)
    all_to_all x1, waiting for transfers between devices, body(): lax.all_to_all(outgoing, 'ep', split_axis=0, concat_axis=0, tiled=True)  24.2 us
    ppermute x7, starting transfers between devices, grp_sum_rounded(): got = lax.ppermute(mine, axis_name, partner)  8.02 us
    ppermute x7, waiting for transfers between devices, grp_sum_rounded(): got = lax.ppermute(mine, axis_name, partner)  7.52 us
    all_to_all x1, starting transfers between devices, body(): lax.all_to_all(outgoing, 'ep', split_axis=0, concat_axis=0, tiled=True)  7.28 us
    all_to_all x1, starting transfers between devices, body(): lax.all_to_all(route_parts, 'ep', split_axis=0, concat_axis=0, tiled=True)  3.4 us
    unnamed x39, local copies, waits for them, and re-layouts  2.69 us
    ppermute x7, waiting for transfers between devices, grp_sum_rounded(): other = lax.ppermute(sums, axis_name, swap)  2.6 us
  transfers between devices with their start and end apart: 26, of which 13 were waited for; matrix products, arithmetic and copies ran while one was open for 21% of the time, Pallas kernels for 0%

profile of v11, /device:TPU:0, one launch (start us, length us, event | category | flops | bytes accessed | tf_op | source)
XLA Modules:
  0.0 118.7 jit_solution(6597973956429527232)
XLA Ops:
  7.4 1.5 %broadcast_compare_fusion = (pred[6,2,256]{2,0,1:T(8,128)(4,1)}, pred[2,256]{1,0:T(4,128)(4,1)S(1)}) fusion(s32[6,256]{1,0:T(8,128)} %bitcast.131, s32[2]{0:T(128)} %param.15), kind=kLoop, calls=%fused_computation.120 | loop fusion | flops 5632 | bytes 9736 | tf_op jit(solution)/shard_map/eq | solution.py:8
  11.9 1.3 %convolution_convert_fusion.5 = bf16[32,1280]{1,0:T(8,128)(2,1)S(1)} fusion(pred[32,256]{1,0:T(32,128)(4,1)S(1)} %fusion.35, bf16[256,1280]{1,0:T(8,128)(2,1)} %param.12), kind=kOutput, calls=%fused_computation.9 | convolution fusion | flops 21012480 | bytes 745472 | tf_op jit(solution)/shard_map/dot_general | solution.py:20
  13.2 1.3 %convolution_convert_fusion.6 = bf16[32,1280]{1,0:T(8,128)(2,1)S(1)} fusion(pred[32,256]{1,0:T(32,128)(4,1)S(1)} %fusion.35, bf16[256,1280]{1,0:T(8,128)(2,1)} %param.11), kind=kOutput, calls=%fused_computation.10 | convolution fusion | flops 21012480 | bytes 745472 | tf_op jit(solution)/shard_map/dot_general | solution.py:19
  17.6 0.9 pad_maximum_fusion
  18.6 7.3 %all-to-all-start = ((bf16[8,40,1280]{2,1,0:T(8,128)(2,1)}), bf16[8,40,1280]{2,1,0:T(8,128)(2,1)S(1)}, u32[]{:S(2)}, u32[]{:S(2)}) async-start(bf16[8,40,1280]{2,1,0:T(8,128)(2,1)} %pad_maximum_fusion), calls=%async_computation | async-start | bytes 1638400 | tf_op jit(solution)/shard_map/all_to_all | solution.py:140
  27.2 24.2 %all-to-all-done = bf16[8,40,1280]{2,1,0:T(8,128)(2,1)S(1)} async-done(((bf16[8,40,1280]{2,1,0:T(8,128)(2,1)}), bf16[8,40,1280]{2,1,0:T(8,128)(2,1)S(1)}, u32[]{:S(2)}, u32[]{:S(2)}) %all-to-all-start) | async-done | bytes 819232 | tf_op jit(solution)/shard_map/all_to_all | solution.py:140
  55.7 1.6 %collective-permute-start.1 = (bf16[64,768]{1,0:T(8,128)(2,1)S(1)}, bf16[64,768]{1,0:T(8,128)(2,1)S(1)}, u32[]{:S(2)}, u32[]{:S(2)}) collective-permute-start(bf16[64,768]{1,0:T(8,128)(2,1)S(1)} %add_convert_fusion.2), channel_id=1, source_target_pairs={{0,16},{8,24},{16,0},{24,8},{1,17},{9,25},{17,1},{25,9},{2,18},{10... | collective-permute-start | bytes 294920 | tf_op jit(solution)/shard_map/ppermute | solution.py:76
  57.9 1.6 %collective-permute-start.4 = (bf16[64,768]{1,0:T(8,128)(2,1)S(1)}, bf16[64,768]{1,0:T(8,128)(2,1)S(1)}, u32[]{:S(2)}, u32[]{:S(2)}) collective-permute-start(bf16[64,768]{1,0:T(8,128)(2,1)S(1)} %add_convert_fusion.1), channel_id=1, source_target_pairs={{0,16},{8,24},{16,0},{24,8},{1,17},{9,25},{17,1},{25,9},{2,18},{10... | collective-permute-start | bytes 294920 | tf_op jit(solution)/shard_map/ppermute | solution.py:76
  59.5 1.9 %collective-permute-done.1 = bf16[64,768]{1,0:T(8,128)(2,1)S(1)} collective-permute-done((bf16[64,768]{1,0:T(8,128)(2,1)S(1)}, bf16[64,768]{1,0:T(8,128)(2,1)S(1)}, u32[]{:S(2)}, u32[]{:S(2)}) %collective-permute-start.1) | collective-permute-done | bytes 98336 | tf_op jit(solution)/shard_map/ppermute | solution.py:76
  62.0 1.4 %collective-permute-done.7 = bf16[64,768]{1,0:T(8,128)(2,1)S(1)} collective-permute-done((bf16[64,768]{1,0:T(8,128)(2,1)S(1)}, bf16[64,768]{1,0:T(8,128)(2,1)S(1)}, u32[]{:S(2)}, u32[]{:S(2)}) %collective-permute-start.7) | collective-permute-done | bytes 98336 | tf_op jit(solution)/shard_map/ppermute | solution.py:76
  63.5 1.5 %collective-permute-done.4 = bf16[64,768]{1,0:T(8,128)(2,1)S(1)} collective-permute-done((bf16[64,768]{1,0:T(8,128)(2,1)S(1)}, bf16[64,768]{1,0:T(8,128)(2,1)S(1)}, u32[]{:S(2)}, u32[]{:S(2)}) %collective-permute-start.4) | collective-permute-done | bytes 98336 | tf_op jit(solution)/shard_map/ppermute | solution.py:76
  65.2 1.4 %collective-permute-done.5 = f32[64,768]{1,0:T(8,128)S(1)} collective-permute-done((f32[64,768]{1,0:T(8,128)S(1)}, f32[64,768]{1,0:T(8,128)S(1)}, u32[]{:S(2)}, u32[]{:S(2)}) %collective-permute-start.5) | collective-permute-done | bytes 196640 | tf_op jit(solution)/shard_map/ppermute | solution.py:79
  67.5 1.0 broadcast_select_fusion.7
  68.5 2.0 %fusion = bf16[1,1280,768]{2,1,0:T(8,128)(2,1)} fusion(bf16[128,1280]{1,0:T(8,128)(2,1)S(1)} %bitcast.115, f32[64,768]{1,0:T(8,128)S(1)} %get-tuple-element.28, f32[64,768]{1,0:T(8,128)S(1)} %get-tuple-element.27, f32[64,768]{1,0:T(8,128)S(1)} %get-tuple-element.26, f32[64,768]{1,0:T(8,128)S(1)} %get-tuple-element.25, f32[64,768]{1,0:T(8,128)S(1)} %get-tuple-element.24, ...), kind=kOutput, calls=%fused_computation.3 | convolution fusion | flops 253919232 | bytes 3473408 | tf_op jit(solution)/shard_map/dot_general | solution.py:187
  70.5 2.0 %fusion.1 = bf16[1,1280,768]{2,1,0:T(8,128)(2,1)} fusion(bf16[128,1280]{1,0:T(8,128)(2,1)S(1)} %bitcast.116, f32[64,768]{1,0:T(8,128)S(1)} %get-tuple-element.24, f32[64,768]{1,0:T(8,128)S(1)} %get-tuple-element.23, f32[64,768]{1,0:T(8,128)S(1)} %get-tuple-element.28, f32[64,768]{1,0:T(8,128)S(1)} %get-tuple-element.27), kind=kOutput, calls=%fused_computation.4 | convolution fusion | flops 253427712 | bytes 3080192 | tf_op jit(solution)/shard_map/dot_general | solution.py:190
  72.5 1.5 %collective-permute-start.19 = (f32[8,1,16]{2,0,1:T(8,128)S(1)}, f32[8,1,16]{2,0,1:T(8,128)S(1)}, u32[]{:S(2)}, u32[]{:S(2)}) collective-permute-start(f32[8,1,16]{2,0,1:T(8,128)S(1)} %add.98), channel_id=1, source_target_pairs={{0,16},{8,24},{16,0},{24,8},{1,17},{9,25},{17,1},{25,9},{2,18},{10... | collective-permute-start | bytes 1544 | tf_op jit(solution)/shard_map/ppermute | solution.py:53
  74.0 2.0 %fusion.2 = bf16[1,768,1280]{2,1,0:T(8,128)(2,1)} fusion(bf16[128,768]{1,0:T(8,128)(2,1)S(1)} %multiply_convert_fusion.4, bf16[128,1280]{1,0:T(8,128)(2,1)S(1)} %copy-done.5), kind=kOutput, calls=%fused_computation.5 | convolution fusion | flops 252641280 | bytes 2490368 | tf_op jit(solution)/shard_map/dot_general | solution.py:193
  77.7 1.4 %slice.70 = bf16[8,64,1280]{2,1,0:T(8,128)(2,1)S(1)} slice(bf16[8,72,1280]{2,1,0:T(8,128)(2,1)} %bitcast.124), slice={[0:8], [0:64], [0:1280]} | slice | bytes 2621440 | tf_op jit(solution)/shard_map/slice | solution.py:155
  79.5 1.5 %convolution_convert_fusion.7 = bf16[2,128,96]{1,2,0:T(8,128)(2,1)S(1)} fusion(bf16[2,128,1280]{2,1,0:T(8,128)(2,1)S(1)} %bitcast.117, bf16[2,96,1280]{2,1,0:T(8,128)(2,1)} %param.21), kind=kOutput, calls=%fused_computation.24 | convolution fusion | flops 62939136 | bytes 1196032 | tf_op jit(solution)/shard_map/jrd,jhd->jrh/dot_general | solution.py:173
  81.0 1.4 %convolution_convert_fusion.10 = bf16[2,128,96]{1,2,0:T(8,128)(2,1)S(1)} fusion(bf16[2,96,1280]{2,1,0:T(8,128)(2,1)} %param.21, bf16[2,128,1280]{2,1,0:T(8,128)(2,1)S(1)} %bitcast.118, f32[2,128]{1,0:T(2,128)S(1)} %reshape.169), kind=kOutput, calls=%fused_computation.27 | convolution fusion | flops 63922176 | bytes 1197056 | tf_op jit(solution)/shard_map/jrd,jhd->jrh/dot_general | solution.py:170
  84.8 1.6 %collective-permute-start.10 = (bf16[2,64,96]{1,2,0:T(8,128)(2,1)S(1)}, bf16[2,64,96]{1,2,0:T(8,128)(2,1)S(1)}, u32[]{:S(2)}, u32[]{:S(2)}) collective-permute-start(bf16[2,64,96]{1,2,0:T(8,128)(2,1)S(1)} %add_convert_fusion.6), channel_id=1, source_target_pairs={{0,16},{8,24},{16,0},{24,8},{1,17},{9,25},{17,1},{25,9},{2,18},{10... | collective-permute-start | bytes 73736 | tf_op jit(solution)/shard_map/ppermute | solution.py:76
  87.2 1.6 %collective-permute-start.16 = (bf16[2,64,96]{1,2,0:T(8,128)(2,1)S(1)}, bf16[2,64,96]{1,2,0:T(8,128)(2,1)S(1)}, u32[]{:S(2)}, u32[]{:S(2)}) collective-permute-start(bf16[2,64,96]{1,2,0:T(8,128)(2,1)S(1)} %add_convert_fusion.4), channel_id=1, source_target_pairs={{0,16},{8,24},{16,0},{24,8},{1,17},{9,25},{17,1},{25,9},{2,18},{10... | collective-permute-start | bytes 73736 | tf_op jit(solution)/shard_map/ppermute | solution.py:76
  90.7 1.1 collective-permute-done.16
  91.9 1.1 collective-permute-done.13
  93.2 1.1 collective-permute-done.14
  95.0 1.3 %fusion.28 = (f32[2,128]{1,0:T(2,128)}, bf16[2,128,96]{1,2,0:T(8,128)(2,1)}) fusion(f32[2,64,96]{1,2,0:T(8,128)S(1)} %get-tuple-element.30, f32[2,64,96]{1,2,0:T(8,128)S(1)} %get-tuple-element.29, f32[2,64,96]{1,2,0:T(8,128)S(1)} %get-tuple-element.34, f32[2,64,96]{1,2,0:T(8,128)S(1)} %get-tuple-element.33, f32[2,64,96]{1,2,0:T(8,128)S(1)} %get-tuple-element.36, ...), kind=kLoop, calls=%fused_computation.62 | loop fusion | flops 294656 | bytes 345088 | tf_op jit(solution)/shard_map/reduce_sum | solution.py:197
  96.4 1.4 %reshape.164 = f32[2,8,16]{2,1,0:T(8,128)} reshape(f32[2,128]{1,0:T(2,128)} %get-tuple-element.17) | data formatting | bytes 2048 | tf_op jit(solution)/shard_map/reshape | solution.py:208
  97.7 2.1 %fusion.23 = f32[2,96,1280]{2,1,0:T(8,128)} fusion(bf16[2,128,96]{1,2,0:T(8,128)(2,1)} %get-tuple-element.18, bf16[2,128,1280]{2,1,0:T(8,128)(2,1)S(1)} %bitcast.119, f32[2,128]{1,0:T(2,128)} %copy-done.16), kind=kOutput, calls=%fused_computation.32 | convolution fusion | flops 63897600 | bytes 1688576 | tf_op jit(solution)/shard_map/jrh,jrd->jhd/dot_general | solution.py:202
  101.1 3.4 %all-to-all-start.1 = ((f32[8,3,16]{2,1,0:T(4,128)}), f32[8,3,16]{2,1,0:T(4,128)S(1)}, u32[]{:S(2)}, u32[]{:S(2)}) async-start(f32[8,3,16]{2,1,0:T(4,128)} %copy.36), calls=%async_computation.1 | async-start | bytes 32768 | tf_op jit(solution)/shard_map/all_to_all | solution.py:212
  105.5 2.3 %fusion.30 = f32[2,1280,96]{1,2,0:T(8,128)} fusion(bf16[2,128,1280]{2,1,0:T(8,128)(2,1)S(1)} %bitcast.111, f32[2,64,96]{1,2,0:T(8,128)S(1)} %get-tuple-element.36, f32[2,64,96]{1,2,0:T(8,128)S(1)} %get-tuple-element.35, f32[2,64,96]{1,2,0:T(8,128)} %copy-done.7, f32[2,64,96]{1,2,0:T(8,128)} %copy-done.6, f32[2,64,96]{1,2,0:T(8,128)S(1)} %get-tuple-element.32, ...), kind=kOutput, calls=%fused_computation.88 | convolution fusion | flops 63234048 | bytes 1933312 | tf_op jit(solution)/shard_map/jrd,jrh->jdh/dot_general | solution.py:198
  107.7 1.3 %fusion.31 = f32[2,1280,96]{1,2,0:T(8,128)} fusion(bf16[2,128,1280]{2,1,0:T(8,128)(2,1)S(1)} %bitcast.112, f32[2,64,96]{1,2,0:T(8,128)S(1)} %get-tuple-element.32, f32[2,64,96]{1,2,0:T(8,128)S(1)} %get-tuple-element.31, f32[2,64,96]{1,2,0:T(8,128)S(1)} %get-tuple-element.36, f32[2,64,96]{1,2,0:T(8,128)S(1)} %get-tuple-element.35), kind=kOutput, calls=%fused_computation.89 | convolution fusion | flops 63111168 | bytes 1835008 | tf_op jit(solution)/shard_map/jrd,jrh->jdh/dot_general | solution.py:201
  109.0 2.1 %all-to-all-done.1 = f32[8,3,16]{2,1,0:T(4,128)S(1)} async-done(((f32[8,3,16]{2,1,0:T(4,128)}), f32[8,3,16]{2,1,0:T(4,128)S(1)}, u32[]{:S(2)}, u32[]{:S(2)}) %all-to-all-start.1) | async-done | bytes 1568 | tf_op jit(solution)/shard_map/all_to_all | solution.py:212
  (166 shorter events, 25.3 us)
Async XLA Ops:
  7.2 44.5 %copy-start = (bf16[1,768,1280]{2,1,0:T(8,128)(2,1)S(1)}, bf16[1,768,1280]{2,1,0:T(8,128)(2,1)}, u32[]{:S(2)}) copy-start(bf16[1,768,1280]{2,1,0:T(8,128)(2,1)} %param.18) | copy-start | bytes 5898244
  7.2 8.0 %copy-start.11 = (s32[256,6]{0,1:T(8,128)S(1)}, s32[256,6]{0,1:T(8,128)}, u32[]{:S(2)}) copy-start(s32[256,6]{0,1:T(8,128)} %param.14) | copy-start | bytes 18436
  7.2 8.0 %copy-start.14 = (bf16[256,6]{0,1:T(8,128)(2,1)S(1)}, bf16[256,6]{0,1:T(8,128)(2,1)}, u32[]{:S(2)}) copy-start(bf16[256,6]{0,1:T(8,128)(2,1)} %param.13) | copy-start | bytes 9220
  7.2 9.9 %copy-start.1 = (bf16[256,1280]{1,0:T(8,128)(2,1)S(1)}, bf16[256,1280]{1,0:T(8,128)(2,1)}, u32[]{:S(2)}) copy-start(bf16[256,1280]{1,0:T(8,128)(2,1)} %param.12) | copy-start | bytes 1966084
  7.2 10.1 %copy-start.2 = (bf16[256,1280]{1,0:T(8,128)(2,1)S(1)}, bf16[256,1280]{1,0:T(8,128)(2,1)}, u32[]{:S(2)}) copy-start(bf16[256,1280]{1,0:T(8,128)(2,1)} %param.11) | copy-start | bytes 1966084
  18.6 32.8 %all-to-all-start = ((bf16[8,40,1280]{2,1,0:T(8,128)(2,1)}), bf16[8,40,1280]{2,1,0:T(8,128)(2,1)S(1)}, u32[]{:S(2)}, u32[]{:S(2)}) async-start(bf16[8,40,1280]{2,1,0:T(8,128)(2,1)} %pad_maximum_fusion), calls=%async_computation | async-start | bytes 1638400 | tf_op jit(solution)/shard_map/all_to_all | solution.py:140
  25.8 50.9 %all-gather.3.cloned.1.call-start = ((), (), s32[]{:S(2)}) async-start(), calls=%async_computation.2 | async-start | bytes 1658880 | tf_op jit(solution)/shard_map/all_gather | solution.py:119
  52.5 3.1 %collective-permute-start = (bf16[64,768]{1,0:T(8,128)(2,1)S(1)}, bf16[64,768]{1,0:T(8,128)(2,1)S(1)}, u32[]{:S(2)}, u32[]{:S(2)}) collective-permute-start(bf16[64,768]{1,0:T(8,128)(2,1)S(1)} %broadcast_select_fusion.8), channel_id=1, source_target_pairs={{0,8},{8,0},{16,24},{24,16},{1,9},{9,1},{17,25},{25,17},{2,10},{10... | collective-permute-start | bytes 294920 | tf_op jit(solution)/shard_map/ppermute | solution.py:70
  53.7 3.5 %collective-permute-start.6 = (bf16[64,768]{1,0:T(8,128)(2,1)S(1)}, bf16[64,768]{1,0:T(8,128)(2,1)S(1)}, u32[]{:S(2)}, u32[]{:S(2)}) collective-permute-start(bf16[64,768]{1,0:T(8,128)(2,1)S(1)} %broadcast_select_fusion.2), channel_id=1, source_target_pairs={{0,8},{8,0},{16,24},{24,16},{1,9},{9,1},{17,25},{25,17},{2,10},{10... | collective-permute-start | bytes 294920 | tf_op jit(solution)/shard_map/ppermute | solution.py:70
  54.7 3.2 %collective-permute-start.3 = (bf16[64,768]{1,0:T(8,128)(2,1)S(1)}, bf16[64,768]{1,0:T(8,128)(2,1)S(1)}, u32[]{:S(2)}, u32[]{:S(2)}) collective-permute-start(bf16[64,768]{1,0:T(8,128)(2,1)S(1)} %broadcast_select_fusion.5), channel_id=1, source_target_pairs={{0,8},{8,0},{16,24},{24,16},{1,9},{9,1},{17,25},{25,17},{2,10},{10... | collective-permute-start | bytes 294920 | tf_op jit(solution)/shard_map/ppermute | solution.py:70
  55.7 5.7 %collective-permute-start.1 = (bf16[64,768]{1,0:T(8,128)(2,1)S(1)}, bf16[64,768]{1,0:T(8,128)(2,1)S(1)}, u32[]{:S(2)}, u32[]{:S(2)}) collective-permute-start(bf16[64,768]{1,0:T(8,128)(2,1)S(1)} %add_convert_fusion.2), channel_id=1, source_target_pairs={{0,16},{8,24},{16,0},{24,8},{1,17},{9,25},{17,1},{25,9},{2,18},{10... | collective-permute-start | bytes 294920 | tf_op jit(solution)/shard_map/ppermute | solution.py:76
  57.3 6.2 %collective-permute-start.7 = (bf16[64,768]{1,0:T(8,128)(2,1)S(1)}, bf16[64,768]{1,0:T(8,128)(2,1)S(1)}, u32[]{:S(2)}, u32[]{:S(2)}) collective-permute-start(bf16[64,768]{1,0:T(8,128)(2,1)S(1)} %add_convert_fusion), channel_id=1, source_target_pairs={{0,16},{8,24},{16,0},{24,8},{1,17},{9,25},{17,1},{25,9},{2,18},{10... | collective-permute-start | bytes 294920 | tf_op jit(solution)/shard_map/ppermute | solution.py:76
  57.9 7.2 %collective-permute-start.4 = (bf16[64,768]{1,0:T(8,128)(2,1)S(1)}, bf16[64,768]{1,0:T(8,128)(2,1)S(1)}, u32[]{:S(2)}, u32[]{:S(2)}) collective-permute-start(bf16[64,768]{1,0:T(8,128)(2,1)S(1)} %add_convert_fusion.1), channel_id=1, source_target_pairs={{0,16},{8,24},{16,0},{24,8},{1,17},{9,25},{17,1},{25,9},{2,18},{10... | collective-permute-start | bytes 294920 | tf_op jit(solution)/shard_map/ppermute | solution.py:76
  62.0 5.5 %collective-permute-start.2 = (f32[64,768]{1,0:T(8,128)}, f32[64,768]{1,0:T(8,128)}, u32[]{:S(2)}, u32[]{:S(2)}) collective-permute-start(f32[64,768]{1,0:T(8,128)} %convert_add_fusion.2), channel_id=1, source_target_pairs={{0,8},{8,0},{16,24},{24,16},{1,9},{9,1},{17,25},{25,17},{2,10},{10... | collective-permute-start | bytes 589832 | tf_op jit(solution)/shard_map/ppermute | solution.py:79
  63.5 1.7 %collective-permute-start.8 = (f32[64,768]{1,0:T(8,128)S(1)}, f32[64,768]{1,0:T(8,128)S(1)}, u32[]{:S(2)}, u32[]{:S(2)}) collective-permute-start(f32[64,768]{1,0:T(8,128)S(1)} %convert_add_fusion), channel_id=1, source_target_pairs={{0,8},{8,0},{16,24},{24,16},{1,9},{9,1},{17,25},{25,17},{2,10},{10... | collective-permute-start | bytes 589832 | tf_op jit(solution)/shard_map/ppermute | solution.py:79
  65.1 1.5 %collective-permute-start.5 = (f32[64,768]{1,0:T(8,128)S(1)}, f32[64,768]{1,0:T(8,128)S(1)}, u32[]{:S(2)}, u32[]{:S(2)}) collective-permute-start(f32[64,768]{1,0:T(8,128)S(1)} %convert_add_fusion.1), channel_id=1, source_target_pairs={{0,8},{8,0},{16,24},{24,16},{1,9},{9,1},{17,25},{25,17},{2,10},{10... | collective-permute-start | bytes 589832 | tf_op jit(solution)/shard_map/ppermute | solution.py:79
  67.4 5.1 %collective-permute-start.18 = (f32[8,1,16]{2,0,1:T(8,128)S(1)}, f32[8,1,16]{2,0,1:T(8,128)S(1)}, u32[]{:S(2)}, u32[]{:S(2)}) collective-permute-start(f32[8,1,16]{2,0,1:T(8,128)S(1)} %reshape.163), channel_id=1, source_target_pairs={{0,8},{8,0},{16,24},{24,16},{1,9},{9,1},{17,25},{25,17},{2,10},{10... | collective-permute-start | bytes 1544 | tf_op jit(solution)/shard_map/ppermute | solution.py:53
  72.5 3.6 %collective-permute-start.19 = (f32[8,1,16]{2,0,1:T(8,128)S(1)}, f32[8,1,16]{2,0,1:T(8,128)S(1)}, u32[]{:S(2)}, u32[]{:S(2)}) collective-permute-start(f32[8,1,16]{2,0,1:T(8,128)S(1)} %add.98), channel_id=1, source_target_pairs={{0,16},{8,24},{16,0},{24,8},{1,17},{9,25},{17,1},{25,9},{2,18},{10... | collective-permute-start | bytes 1544 | tf_op jit(solution)/shard_map/ppermute | solution.py:53
  83.4 1.3 %collective-permute-start.9 = (bf16[2,64,96]{1,2,0:T(8,128)(2,1)S(1)}, bf16[2,64,96]{1,2,0:T(8,128)(2,1)S(1)}, u32[]{:S(2)}, u32[]{:S(2)}) collective-permute-start(bf16[2,64,96]{1,2,0:T(8,128)(2,1)S(1)} %broadcast_select_fusion.20), channel_id=1, source_target_pairs={{0,8},{8,0},{16,24},{24,16},{1,9},{9,1},{17,25},{25,17},{2,10},{10... | collective-permute-start | bytes 73736 | tf_op jit(solution)/shard_map/ppermute | solution.py:70
  83.6 2.8 %collective-permute-start.20 = (bf16[2,64,96]{1,2,0:T(8,128)(2,1)S(1)}, bf16[2,64,96]{1,2,0:T(8,128)(2,1)S(1)}, u32[]{:S(2)}, u32[]{:S(2)}) collective-permute-start(bf16[2,64,96]{1,2,0:T(8,128)(2,1)S(1)} %broadcast_select_fusion.11), channel_id=1, source_target_pairs={{0,8},{8,0},{16,24},{24,16},{1,9},{9,1},{17,25},{25,17},{2,10},{10... | collective-permute-start | bytes 73736 | tf_op jit(solution)/shard_map/ppermute | solution.py:70
  84.1 2.9 %collective-permute-start.15 = (bf16[2,64,96]{1,2,0:T(8,128)(2,1)S(1)}, bf16[2,64,96]{1,2,0:T(8,128)(2,1)S(1)}, u32[]{:S(2)}, u32[]{:S(2)}) collective-permute-start(bf16[2,64,96]{1,2,0:T(8,128)(2,1)S(1)} %broadcast_select_fusion.14), channel_id=1, source_target_pairs={{0,8},{8,0},{16,24},{24,16},{1,9},{9,1},{17,25},{25,17},{2,10},{10... | collective-permute-start | bytes 73736 | tf_op jit(solution)/shard_map/ppermute | solution.py:70
  84.2 4.5 %collective-permute-start.12 = (bf16[2,64,96]{1,2,0:T(8,128)(2,1)S(1)}, bf16[2,64,96]{1,2,0:T(8,128)(2,1)S(1)}, u32[]{:S(2)}, u32[]{:S(2)}) collective-permute-start(bf16[2,64,96]{1,2,0:T(8,128)(2,1)S(1)} %broadcast_select_fusion.17), channel_id=1, source_target_pairs={{0,8},{8,0},{16,24},{24,16},{1,9},{9,1},{17,25},{25,17},{2,10},{10... | collective-permute-start | bytes 73736 | tf_op jit(solution)/shard_map/ppermute | solution.py:70
  84.8 4.6 %collective-permute-start.10 = (bf16[2,64,96]{1,2,0:T(8,128)(2,1)S(1)}, bf16[2,64,96]{1,2,0:T(8,128)(2,1)S(1)}, u32[]{:S(2)}, u32[]{:S(2)}) collective-permute-start(bf16[2,64,96]{1,2,0:T(8,128)(2,1)S(1)} %add_convert_fusion.6), channel_id=1, source_target_pairs={{0,16},{8,24},{16,0},{24,8},{1,17},{9,25},{17,1},{25,9},{2,18},{10... | collective-permute-start | bytes 73736 | tf_op jit(solution)/shard_map/ppermute | solution.py:76
  86.5 4.2 %collective-permute-start.21 = (bf16[2,64,96]{1,2,0:T(8,128)(2,1)S(1)}, bf16[2,64,96]{1,2,0:T(8,128)(2,1)S(1)}, u32[]{:S(2)}, u32[]{:S(2)}) collective-permute-start(bf16[2,64,96]{1,2,0:T(8,128)(2,1)S(1)} %add_convert_fusion.3), channel_id=1, source_target_pairs={{0,16},{8,24},{16,0},{24,8},{1,17},{9,25},{17,1},{25,9},{2,18},{10... | collective-permute-start | bytes 73736 | tf_op jit(solution)/shard_map/ppermute | solution.py:76
  87.2 4.7 %collective-permute-start.16 = (bf16[2,64,96]{1,2,0:T(8,128)(2,1)S(1)}, bf16[2,64,96]{1,2,0:T(8,128)(2,1)S(1)}, u32[]{:S(2)}, u32[]{:S(2)}) collective-permute-start(bf16[2,64,96]{1,2,0:T(8,128)(2,1)S(1)} %add_convert_fusion.4), channel_id=1, source_target_pairs={{0,16},{8,24},{16,0},{24,8},{1,17},{9,25},{17,1},{25,9},{2,18},{10... | collective-permute-start | bytes 73736 | tf_op jit(solution)/shard_map/ppermute | solution.py:76
  88.8 4.2 %collective-permute-start.13 = (bf16[2,64,96]{1,2,0:T(8,128)(2,1)S(1)}, bf16[2,64,96]{1,2,0:T(8,128)(2,1)S(1)}, u32[]{:S(2)}, u32[]{:S(2)}) collective-permute-start(bf16[2,64,96]{1,2,0:T(8,128)(2,1)S(1)} %add_convert_fusion.5), channel_id=1, source_target_pairs={{0,16},{8,24},{16,0},{24,8},{1,17},{9,25},{17,1},{25,9},{2,18},{10... | collective-permute-start | bytes 73736 | tf_op jit(solution)/shard_map/ppermute | solution.py:76
  90.1 14.5 %collective-permute-start.11 = (f32[2,64,96]{1,2,0:T(8,128)}, f32[2,64,96]{1,2,0:T(8,128)}, u32[]{:S(2)}, u32[]{:S(2)}) collective-permute-start(f32[2,64,96]{1,2,0:T(8,128)} %convert_add_fusion.6), channel_id=1, source_target_pairs={{0,8},{8,0},{16,24},{24,16},{1,9},{9,1},{17,25},{25,17},{2,10},{10... | collective-permute-start | bytes 147464 | tf_op jit(solution)/shard_map/ppermute | solution.py:79
  90.7 2.4 %collective-permute-start.22 = (f32[2,64,96]{1,2,0:T(8,128)S(1)}, f32[2,64,96]{1,2,0:T(8,128)S(1)}, u32[]{:S(2)}, u32[]{:S(2)}) collective-permute-start(f32[2,64,96]{1,2,0:T(8,128)S(1)} %convert_add_fusion.3), channel_id=1, source_target_pairs={{0,8},{8,0},{16,24},{24,16},{1,9},{9,1},{17,25},{25,17},{2,10},{10... | collective-permute-start | bytes 147464 | tf_op jit(solution)/shard_map/ppermute | solution.py:79
  91.8 1.4 %collective-permute-start.17 = (f32[2,64,96]{1,2,0:T(8,128)S(1)}, f32[2,64,96]{1,2,0:T(8,128)S(1)}, u32[]{:S(2)}, u32[]{:S(2)}) collective-permute-start(f32[2,64,96]{1,2,0:T(8,128)S(1)} %convert_add_fusion.4), channel_id=1, source_target_pairs={{0,8},{8,0},{16,24},{24,16},{1,9},{9,1},{17,25},{25,17},{2,10},{10... | collective-permute-start | bytes 147464 | tf_op jit(solution)/shard_map/ppermute | solution.py:79
  93.0 1.4 %collective-permute-start.14 = (f32[2,64,96]{1,2,0:T(8,128)S(1)}, f32[2,64,96]{1,2,0:T(8,128)S(1)}, u32[]{:S(2)}, u32[]{:S(2)}) collective-permute-start(f32[2,64,96]{1,2,0:T(8,128)S(1)} %convert_add_fusion.5), channel_id=1, source_target_pairs={{0,8},{8,0},{16,24},{24,16},{1,9},{9,1},{17,25},{25,17},{2,10},{10... | collective-permute-start | bytes 147464 | tf_op jit(solution)/shard_map/ppermute | solution.py:79
  101.1 10.0 %all-to-all-start.1 = ((f32[8,3,16]{2,1,0:T(4,128)}), f32[8,3,16]{2,1,0:T(4,128)S(1)}, u32[]{:S(2)}, u32[]{:S(2)}) async-start(f32[8,3,16]{2,1,0:T(4,128)} %copy.36), calls=%async_computation.1 | async-start | bytes 32768 | tf_op jit(solution)/shard_map/all_to_all | solution.py:212
  105.5 5.8 %copy-start.12 = (pred[6,8,256]{2,0,1:T(8,128)(4,1)S(1)}, pred[6,8,256]{2,0,1:T(8,128)(4,1)}, u32[]{:S(2)}) copy-start(pred[6,8,256]{2,0,1:T(8,128)(4,1)} %get-tuple-element.39) | copy-start | bytes 36868
  (11 other events, 34.4 us)
Sparse Core Ops, SparseCore 0:
  29.4 46.5 all-gather.2

commit v12 on v11

--- a/solution.py
+++ b/solution.py
@@ -53,6 +53,22 @@
         x = x + lax.ppermute(x, axis_name, partner)
         bit *= 2
     return x
+
+
+def grp_sum_doubling(parts, axis_name):
+    size = lax.axis_size(axis_name)
+    mine = [p.astype(jnp.bfloat16) for p in parts]
+    if size & (size - 1):
+        return [lax.psum(r, axis_name).astype(jnp.float32) for r in mine]
+    sums = [r.astype(jnp.float32) for r in mine]
+    bit = 1
+    while bit < size:
+        partner = [(i, i ^ bit) for i in range(size)]
+        got = lax.ppermute(mine, axis_name, partner)
+        sums = [m.astype(jnp.float32) + g.astype(jnp.float32) for m, g in zip(mine, got)]
+        mine = [s.astype(jnp.bfloat16) for s in sums]
+        bit *= 2
+    return sums
 
 
 def grp_sum_rounded(parts, axes, axis_name):
@@ -176,8 +192,8 @@
     pre_gate, pre_up, grad_hidden = grp_sum_rounded(
         [part_gate, part_up, part_hidden], [0, 0, 0], "grp"
     )
-    pre_gate_hot, pre_up_hot, grad_hidden_hot, cot_down = grp_sum_rounded(
-        [part_gate_hot, part_up_hot, part_hidden_hot, part_cot_hot], [1, 1, 1, 1], "grp"
+    pre_gate_hot, pre_up_hot, grad_hidden_hot, cot_down = grp_sum_doubling(
+        [part_gate_hot, part_up_hot, part_hidden_hot, part_cot_hot], "grp"
     )
     hidden, back_gate, back_up = swiglu_back(pre_gate, pre_up, grad_hidden)
     output_slice = jnp.dot(hidden, w_down, preferred_element_type=jnp.float32)

time: 120 us -> 115 us (0.958)
  waiting for transfers between devices: 37.2 us -> 34.7 us
  other arithmetic: 16.7 us -> 14.5 us
    ppermute x0 -> x8, starting transfers between devices: none -> 5.45 us  [grp_sum_doubling(): got = lax.ppermute(mine, axis_name, partner)]
    ppermute x7 -> x3, starting transfers between devices: 8.02 us -> 3.71 us  [grp_sum_rounded(): got = lax.ppermute(mine, axis_name, partner)]
    ppermute x7 -> x3, waiting for transfers between devices: 7.52 us -> 4.81 us  [grp_sum_rounded(): got = lax.ppermute(mine, axis_name, partner)]
    ppermute x0 -> x8, waiting for transfers between devices: none -> 2.41 us  [grp_sum_doubling(): got = lax.ppermute(mine, axis_name, partner)]
    ppermute x7 -> x3, waiting for transfers between devices: 2.6 us -> 1.38 us  [grp_sum_rounded(): other = lax.ppermute(sums, axis_name, swap)]
    unnamed x39 -> x37, local copies, waits for them, and re-layouts: 2.69 us -> 2.07 us
  transfers between devices with their start and end apart: 26 -> 22, of which waited for: 13 -> 9; matrix products, arithmetic and copies ran while one was open for 21% -> 19% of each run, Pallas kernels for 0% -> 0%
where the time goes in v12:
time: 115 us; the launch traced here: 114 us
  waiting for transfers between devices  34.7 us (30%)
  starting transfers between devices  22.5 us (20%)
  matrix products  20.3 us (18%)
  other arithmetic  14.5 us (13%)
  between operations  14.5 us (13%)
  local copies, waits for them, and re-layouts  7.49 us (7%)
    all_to_all x1, waiting for transfers between devices, body(): lax.all_to_all(outgoing, 'ep', split_axis=0, concat_axis=0, tiled=True)  24.2 us
    all_to_all x1, starting transfers between devices, body(): lax.all_to_all(outgoing, 'ep', split_axis=0, concat_axis=0, tiled=True)  7.29 us
    ppermute x8, starting transfers between devices, grp_sum_doubling(): got = lax.ppermute(mine, axis_name, partner)  5.45 us
    ppermute x3, waiting for transfers between devices, grp_sum_rounded(): got = lax.ppermute(mine, axis_name, partner)  4.81 us
    all_to_all x1, starting transfers between devices, body(): lax.all_to_all(route_parts, 'ep', split_axis=0, concat_axis=0, tiled=True)  3.91 us
    ppermute x3, starting transfers between devices, grp_sum_rounded(): got = lax.ppermute(mine, axis_name, partner)  3.71 us
    ppermute x8, waiting for transfers between devices, grp_sum_doubling(): got = lax.ppermute(mine, axis_name, partner)  2.41 us
  transfers between devices with their start and end apart: 22, of which 9 were waited for; matrix products, arithmetic and copies ran while one was open for 19% of the time, Pallas kernels for 0%

profile of v12, /device:TPU:0, one launch (start us, length us, event | category | flops | bytes accessed | tf_op | source)
XLA Modules:
  0.0 114.0 jit_solution(7324505918030075768)
XLA Ops:
  7.4 1.5 %broadcast_compare_fusion = (pred[6,2,256]{2,0,1:T(8,128)(4,1)}, pred[2,256]{1,0:T(4,128)(4,1)S(1)}) fusion(s32[6,256]{1,0:T(8,128)} %bitcast.131, s32[2]{0:T(128)} %param.15), kind=kLoop, calls=%fused_computation.103 | loop fusion | flops 5632 | bytes 9736 | tf_op jit(solution)/shard_map/eq | solution.py:8
  11.9 1.3 %convolution_convert_fusion.5 = bf16[32,1280]{1,0:T(8,128)(2,1)S(1)} fusion(pred[32,256]{1,0:T(32,128)(4,1)S(1)} %fusion.34, bf16[256,1280]{1,0:T(8,128)(2,1)} %param.12), kind=kOutput, calls=%fused_computation.9 | convolution fusion | flops 21012480 | bytes 745472 | tf_op jit(solution)/shard_map/dot_general | solution.py:20
  13.2 1.3 %convolution_convert_fusion.6 = bf16[32,1280]{1,0:T(8,128)(2,1)S(1)} fusion(pred[32,256]{1,0:T(32,128)(4,1)S(1)} %fusion.34, bf16[256,1280]{1,0:T(8,128)(2,1)} %param.11), kind=kOutput, calls=%fused_computation.10 | convolution fusion | flops 21012480 | bytes 745472 | tf_op jit(solution)/shard_map/dot_general | solution.py:19
  17.6 0.9 pad_maximum_fusion
  18.6 7.3 %all-to-all-start = ((bf16[8,40,1280]{2,1,0:T(8,128)(2,1)}), bf16[8,40,1280]{2,1,0:T(8,128)(2,1)S(1)}, u32[]{:S(2)}, u32[]{:S(2)}) async-start(bf16[8,40,1280]{2,1,0:T(8,128)(2,1)} %pad_maximum_fusion), calls=%async_computation | async-start | bytes 1638400 | tf_op jit(solution)/shard_map/all_to_all | solution.py:156
  27.2 24.2 %all-to-all-done = bf16[8,40,1280]{2,1,0:T(8,128)(2,1)S(1)} async-done(((bf16[8,40,1280]{2,1,0:T(8,128)(2,1)}), bf16[8,40,1280]{2,1,0:T(8,128)(2,1)S(1)}, u32[]{:S(2)}, u32[]{:S(2)}) %all-to-all-start) | async-done | bytes 819232 | tf_op jit(solution)/shard_map/all_to_all | solution.py:156
  54.8 0.8 fusion.22
  55.7 1.6 %collective-permute-start.1 = (bf16[64,768]{1,0:T(8,128)(2,1)S(1)}, bf16[64,768]{1,0:T(8,128)(2,1)S(1)}, u32[]{:S(2)}, u32[]{:S(2)}) collective-permute-start(bf16[64,768]{1,0:T(8,128)(2,1)S(1)} %add_convert_fusion.2), channel_id=1, source_target_pairs={{0,16},{8,24},{16,0},{24,8},{1,17},{9,25},{17,1},{25,9},{2,18},{10... | collective-permute-start | bytes 294920 | tf_op jit(solution)/shard_map/ppermute | solution.py:92
  57.9 1.6 %collective-permute-start.4 = (bf16[64,768]{1,0:T(8,128)(2,1)S(1)}, bf16[64,768]{1,0:T(8,128)(2,1)S(1)}, u32[]{:S(2)}, u32[]{:S(2)}) collective-permute-start(bf16[64,768]{1,0:T(8,128)(2,1)S(1)} %add_convert_fusion.1), channel_id=1, source_target_pairs={{0,16},{8,24},{16,0},{24,8},{1,17},{9,25},{17,1},{25,9},{2,18},{10... | collective-permute-start | bytes 294920 | tf_op jit(solution)/shard_map/ppermute | solution.py:92
  59.5 1.9 %collective-permute-done.1 = bf16[64,768]{1,0:T(8,128)(2,1)S(1)} collective-permute-done((bf16[64,768]{1,0:T(8,128)(2,1)S(1)}, bf16[64,768]{1,0:T(8,128)(2,1)S(1)}, u32[]{:S(2)}, u32[]{:S(2)}) %collective-permute-start.1) | collective-permute-done | bytes 98336 | tf_op jit(solution)/shard_map/ppermute | solution.py:92
  62.0 1.4 %collective-permute-done.7 = bf16[64,768]{1,0:T(8,128)(2,1)S(1)} collective-permute-done((bf16[64,768]{1,0:T(8,128)(2,1)S(1)}, bf16[64,768]{1,0:T(8,128)(2,1)S(1)}, u32[]{:S(2)}, u32[]{:S(2)}) %collective-permute-start.7) | collective-permute-done | bytes 98336 | tf_op jit(solution)/shard_map/ppermute | solution.py:92
  63.5 1.6 %collective-permute-done.4 = bf16[64,768]{1,0:T(8,128)(2,1)S(1)} collective-permute-done((bf16[64,768]{1,0:T(8,128)(2,1)S(1)}, bf16[64,768]{1,0:T(8,128)(2,1)S(1)}, u32[]{:S(2)}, u32[]{:S(2)}) %collective-permute-start.4) | collective-permute-done | bytes 98336 | tf_op jit(solution)/shard_map/ppermute | solution.py:92
  65.3 1.4 %collective-permute-done.5 = f32[64,768]{1,0:T(8,128)S(1)} collective-permute-done((f32[64,768]{1,0:T(8,128)S(1)}, f32[64,768]{1,0:T(8,128)S(1)}, u32[]{:S(2)}, u32[]{:S(2)}) %collective-permute-start.5) | collective-permute-done | bytes 196640 | tf_op jit(solution)/shard_map/ppermute | solution.py:95
  67.6 1.0 broadcast_select_fusion.7
  68.5 2.0 %fusion = bf16[1,1280,768]{2,1,0:T(8,128)(2,1)} fusion(bf16[128,1280]{1,0:T(8,128)(2,1)S(1)} %bitcast.115, f32[64,768]{1,0:T(8,128)S(1)} %get-tuple-element.28, f32[64,768]{1,0:T(8,128)S(1)} %get-tuple-element.27, f32[64,768]{1,0:T(8,128)S(1)} %get-tuple-element.26, f32[64,768]{1,0:T(8,128)S(1)} %get-tuple-element.25, f32[64,768]{1,0:T(8,128)S(1)} %get-tuple-element.24, ...), kind=kOutput, calls=%fused_computation.3 | convolution fusion | flops 253919232 | bytes 3473408 | tf_op jit(solution)/shard_map/dot_general | solution.py:203
  70.5 2.0 %fusion.1 = bf16[1,1280,768]{2,1,0:T(8,128)(2,1)} fusion(bf16[128,1280]{1,0:T(8,128)(2,1)S(1)} %bitcast.116, f32[64,768]{1,0:T(8,128)S(1)} %get-tuple-element.24, f32[64,768]{1,0:T(8,128)S(1)} %get-tuple-element.23, f32[64,768]{1,0:T(8,128)S(1)} %get-tuple-element.28, f32[64,768]{1,0:T(8,128)S(1)} %get-tuple-element.27), kind=kOutput, calls=%fused_computation.4 | convolution fusion | flops 253427712 | bytes 3080192 | tf_op jit(solution)/shard_map/dot_general | solution.py:206
  72.5 1.5 %collective-permute-start.16 = (f32[8,1,16]{2,0,1:T(8,128)S(1)}, f32[8,1,16]{2,0,1:T(8,128)S(1)}, u32[]{:S(2)}, u32[]{:S(2)}) collective-permute-start(f32[8,1,16]{2,0,1:T(8,128)S(1)} %add.97), channel_id=1, source_target_pairs={{0,16},{8,24},{16,0},{24,8},{1,17},{9,25},{17,1},{25,9},{2,18},{10... | collective-permute-start | bytes 1544 | tf_op jit(solution)/shard_map/ppermute | solution.py:53
  74.0 2.0 %fusion.2 = bf16[1,768,1280]{2,1,0:T(8,128)(2,1)} fusion(bf16[128,768]{1,0:T(8,128)(2,1)S(1)} %multiply_convert_fusion.4, bf16[128,1280]{1,0:T(8,128)(2,1)S(1)} %copy-done.5), kind=kOutput, calls=%fused_computation.5 | convolution fusion | flops 252641280 | bytes 2490368 | tf_op jit(solution)/shard_map/dot_general | solution.py:209
  76.7 0.9 slice_bitcast_fusion
  77.7 1.4 %slice.70 = bf16[8,64,1280]{2,1,0:T(8,128)(2,1)S(1)} slice(bf16[8,72,1280]{2,1,0:T(8,128)(2,1)} %bitcast.124), slice={[0:8], [0:64], [0:1280]} | slice | bytes 2621440 | tf_op jit(solution)/shard_map/slice | solution.py:171
  79.5 1.5 %convolution_convert_fusion.7 = bf16[2,128,96]{1,2,0:T(8,128)(2,1)S(1)} fusion(bf16[2,128,1280]{2,1,0:T(8,128)(2,1)S(1)} %bitcast.117, bf16[2,96,1280]{2,1,0:T(8,128)(2,1)} %param.21), kind=kOutput, calls=%fused_computation.24 | convolution fusion | flops 62939136 | bytes 1196032 | tf_op jit(solution)/shard_map/jrd,jhd->jrh/dot_general | solution.py:189
  81.0 1.4 %convolution_convert_fusion.10 = bf16[2,128,96]{1,2,0:T(8,128)(2,1)S(1)} fusion(bf16[2,96,1280]{2,1,0:T(8,128)(2,1)} %param.21, bf16[2,128,1280]{2,1,0:T(8,128)(2,1)S(1)} %bitcast.118, f32[2,128]{1,0:T(2,128)S(1)} %reshape.169), kind=kOutput, calls=%fused_computation.27 | convolution fusion | flops 63922176 | bytes 1197056 | tf_op jit(solution)/shard_map/jrd,jhd->jrh/dot_general | solution.py:186
  84.3 1.6 %collective-permute-start.12 = (bf16[2,128,96]{1,2,0:T(8,128)(2,1)S(1)}, bf16[2,128,96]{1,2,0:T(8,128)(2,1)S(1)}, u32[]{:S(2)}, u32[]{:S(2)}) collective-permute-start(bf16[2,128,96]{1,2,0:T(8,128)(2,1)S(1)} %add_convert_fusion.5), channel_id=1, source_target_pairs={{0,16},{8,24},{16,0},{24,8},{1,17},{9,25},{17,1},{25,9},{2,18},{10... | collective-permute-start | bytes 147464 | tf_op jit(solution)/shard_map/ppermute | solution.py:67
  86.5 1.6 %collective-permute-start.18 = (bf16[2,128,96]{1,2,0:T(8,128)(2,1)S(1)}, bf16[2,128,96]{1,2,0:T(8,128)(2,1)S(1)}, u32[]{:S(2)}, u32[]{:S(2)}) collective-permute-start(bf16[2,128,96]{1,2,0:T(8,128)(2,1)S(1)} %add_convert_fusion.3), channel_id=1, source_target_pairs={{0,16},{8,24},{16,0},{24,8},{1,17},{9,25},{17,1},{25,9},{2,18},{10... | collective-permute-start | bytes 147464 | tf_op jit(solution)/shard_map/ppermute | solution.py:67
  88.7 1.5 %collective-permute-done.14 = bf16[2,128,96]{1,2,0:T(8,128)(2,1)S(1)} collective-permute-done((bf16[2,128,96]{1,2,0:T(8,128)(2,1)S(1)}, bf16[2,128,96]{1,2,0:T(8,128)(2,1)S(1)}, u32[]{:S(2)}, u32[]{:S(2)}) %collective-permute-start.14) | collective-permute-done | bytes 49184 | tf_op jit(solution)/shard_map/ppermute | solution.py:67
  90.2 0.9 collective-permute-done.18
  91.8 1.4 %reshape.164 = f32[2,8,16]{2,1,0:T(8,128)} reshape(f32[2,128]{1,0:T(2,128)} %get-tuple-element.17) | data formatting | bytes 2048 | tf_op jit(solution)/shard_map/reshape | solution.py:224
  94.4 3.9 %all-to-all-start.1 = ((f32[8,3,16]{2,1,0:T(4,128)}), f32[8,3,16]{2,1,0:T(4,128)}, u32[]{:S(2)}, u32[]{:S(2)}) async-start(f32[8,3,16]{2,1,0:T(4,128)} %copy.36), calls=%async_computation.1 | async-start | bytes 32768 | tf_op jit(solution)/shard_map/all_to_all | solution.py:228
  98.4 2.1 %fusion.29 = f32[2,1280,96]{1,2,0:T(8,128)} fusion(bf16[2,128,1280]{2,1,0:T(8,128)(2,1)S(1)} %bitcast.111, bf16[2,128,96]{1,2,0:T(8,128)(2,1)} %collective-permute-done.10, bf16[2,128,96]{1,2,0:T(8,128)(2,1)S(1)} %add_convert_fusion.6, bf16[2,128,96]{1,2,0:T(8,128)(2,1)} %copy-done.8, bf16[2,128,96]{1,2,0:T(8,128)(2,1)S(1)} %add_convert_fusion.5, ...), kind=kOutput, calls=%fused_computation.83 | convolution fusion | flops 63381504 | bytes 1933312 | tf_op jit(solution)/shard_map/jrd,jrh->jdh/dot_general | solution.py:214
  100.4 2.1 %fusion.30 = f32[2,1280,96]{1,2,0:T(8,128)} fusion(bf16[2,128,1280]{2,1,0:T(8,128)(2,1)S(1)} %bitcast.112, bf16[2,128,96]{1,2,0:T(8,128)(2,1)} %collective-permute-done.10, bf16[2,128,96]{1,2,0:T(8,128)(2,1)S(1)} %add_convert_fusion.6, bf16[2,128,96]{1,2,0:T(8,128)(2,1)S(1)} %collective-permute-done.14, bf16[2,128,96]{1,2,0:T(8,128)(2,1)S(1)} %add_convert_fusion.4), kind=kOutput, calls=%fused_computation.84 | convolution fusion | flops 63209472 | bytes 1835008 | tf_op jit(solution)/shard_map/jrd,jrh->jdh/dot_general | solution.py:217
  102.5 1.3 %fusion.23 = f32[2,96,1280]{2,1,0:T(8,128)} fusion(bf16[2,128,96]{1,2,0:T(8,128)(2,1)S(1)} %get-tuple-element.18, bf16[2,128,1280]{2,1,0:T(8,128)(2,1)S(1)} %bitcast.119, f32[2,128]{1,0:T(2,128)S(1)} %copy-done.15), kind=kOutput, calls=%fused_computation.32 | convolution fusion | flops 63897600 | bytes 1688576 | tf_op jit(solution)/shard_map/jrh,jrd->jhd/dot_general | solution.py:218
  103.8 1.1 all-to-all-done.1
  (144 shorter events, 21.8 us)
Async XLA Ops:
  7.2 44.5 %copy-start = (bf16[1,768,1280]{2,1,0:T(8,128)(2,1)S(1)}, bf16[1,768,1280]{2,1,0:T(8,128)(2,1)}, u32[]{:S(2)}) copy-start(bf16[1,768,1280]{2,1,0:T(8,128)(2,1)} %param.18) | copy-start | bytes 5898244
  7.2 8.0 %copy-start.9 = (s32[256,6]{0,1:T(8,128)S(1)}, s32[256,6]{0,1:T(8,128)}, u32[]{:S(2)}) copy-start(s32[256,6]{0,1:T(8,128)} %param.14) | copy-start | bytes 18436
  7.2 8.0 %copy-start.12 = (bf16[256,6]{0,1:T(8,128)(2,1)S(1)}, bf16[256,6]{0,1:T(8,128)(2,1)}, u32[]{:S(2)}) copy-start(bf16[256,6]{0,1:T(8,128)(2,1)} %param.13) | copy-start | bytes 9220
  7.2 9.9 %copy-start.1 = (bf16[256,1280]{1,0:T(8,128)(2,1)S(1)}, bf16[256,1280]{1,0:T(8,128)(2,1)}, u32[]{:S(2)}) copy-start(bf16[256,1280]{1,0:T(8,128)(2,1)} %param.12) | copy-start | bytes 1966084
  7.2 10.1 %copy-start.2 = (bf16[256,1280]{1,0:T(8,128)(2,1)S(1)}, bf16[256,1280]{1,0:T(8,128)(2,1)}, u32[]{:S(2)}) copy-start(bf16[256,1280]{1,0:T(8,128)(2,1)} %param.11) | copy-start | bytes 1966084
  18.6 32.8 %all-to-all-start = ((bf16[8,40,1280]{2,1,0:T(8,128)(2,1)}), bf16[8,40,1280]{2,1,0:T(8,128)(2,1)S(1)}, u32[]{:S(2)}, u32[]{:S(2)}) async-start(bf16[8,40,1280]{2,1,0:T(8,128)(2,1)} %pad_maximum_fusion), calls=%async_computation | async-start | bytes 1638400 | tf_op jit(solution)/shard_map/all_to_all | solution.py:156
  25.8 50.9 %all-gather.3.cloned.1.call-start = ((), (), s32[]{:S(2)}) async-start(), calls=%async_computation.2 | async-start | bytes 1658880 | tf_op jit(solution)/shard_map/all_gather | solution.py:135
  52.5 3.1 %collective-permute-start = (bf16[64,768]{1,0:T(8,128)(2,1)S(1)}, bf16[64,768]{1,0:T(8,128)(2,1)S(1)}, u32[]{:S(2)}, u32[]{:S(2)}) collective-permute-start(bf16[64,768]{1,0:T(8,128)(2,1)S(1)} %broadcast_select_fusion.8), channel_id=1, source_target_pairs={{0,8},{8,0},{16,24},{24,16},{1,9},{9,1},{17,25},{25,17},{2,10},{10... | collective-permute-start | bytes 294920 | tf_op jit(solution)/shard_map/ppermute | solution.py:86
  53.7 3.5 %collective-permute-start.6 = (bf16[64,768]{1,0:T(8,128)(2,1)S(1)}, bf16[64,768]{1,0:T(8,128)(2,1)S(1)}, u32[]{:S(2)}, u32[]{:S(2)}) collective-permute-start(bf16[64,768]{1,0:T(8,128)(2,1)S(1)} %broadcast_select_fusion.2), channel_id=1, source_target_pairs={{0,8},{8,0},{16,24},{24,16},{1,9},{9,1},{17,25},{25,17},{2,10},{10... | collective-permute-start | bytes 294920 | tf_op jit(solution)/shard_map/ppermute | solution.py:86
  54.6 3.2 %collective-permute-start.3 = (bf16[64,768]{1,0:T(8,128)(2,1)S(1)}, bf16[64,768]{1,0:T(8,128)(2,1)S(1)}, u32[]{:S(2)}, u32[]{:S(2)}) collective-permute-start(bf16[64,768]{1,0:T(8,128)(2,1)S(1)} %broadcast_select_fusion.5), channel_id=1, source_target_pairs={{0,8},{8,0},{16,24},{24,16},{1,9},{9,1},{17,25},{25,17},{2,10},{10... | collective-permute-start | bytes 294920 | tf_op jit(solution)/shard_map/ppermute | solution.py:86
  55.7 5.7 %collective-permute-start.1 = (bf16[64,768]{1,0:T(8,128)(2,1)S(1)}, bf16[64,768]{1,0:T(8,128)(2,1)S(1)}, u32[]{:S(2)}, u32[]{:S(2)}) collective-permute-start(bf16[64,768]{1,0:T(8,128)(2,1)S(1)} %add_convert_fusion.2), channel_id=1, source_target_pairs={{0,16},{8,24},{16,0},{24,8},{1,17},{9,25},{17,1},{25,9},{2,18},{10... | collective-permute-start | bytes 294920 | tf_op jit(solution)/shard_map/ppermute | solution.py:92
  57.3 6.2 %collective-permute-start.7 = (bf16[64,768]{1,0:T(8,128)(2,1)S(1)}, bf16[64,768]{1,0:T(8,128)(2,1)S(1)}, u32[]{:S(2)}, u32[]{:S(2)}) collective-permute-start(bf16[64,768]{1,0:T(8,128)(2,1)S(1)} %add_convert_fusion), channel_id=1, source_target_pairs={{0,16},{8,24},{16,0},{24,8},{1,17},{9,25},{17,1},{25,9},{2,18},{10... | collective-permute-start | bytes 294920 | tf_op jit(solution)/shard_map/ppermute | solution.py:92
  57.9 7.2 %collective-permute-start.4 = (bf16[64,768]{1,0:T(8,128)(2,1)S(1)}, bf16[64,768]{1,0:T(8,128)(2,1)S(1)}, u32[]{:S(2)}, u32[]{:S(2)}) collective-permute-start(bf16[64,768]{1,0:T(8,128)(2,1)S(1)} %add_convert_fusion.1), channel_id=1, source_target_pairs={{0,16},{8,24},{16,0},{24,8},{1,17},{9,25},{17,1},{25,9},{2,18},{10... | collective-permute-start | bytes 294920 | tf_op jit(solution)/shard_map/ppermute | solution.py:92
  62.0 5.5 %collective-permute-start.2 = (f32[64,768]{1,0:T(8,128)}, f32[64,768]{1,0:T(8,128)}, u32[]{:S(2)}, u32[]{:S(2)}) collective-permute-start(f32[64,768]{1,0:T(8,128)} %convert_add_fusion.2), channel_id=1, source_target_pairs={{0,8},{8,0},{16,24},{24,16},{1,9},{9,1},{17,25},{25,17},{2,10},{10... | collective-permute-start | bytes 589832 | tf_op jit(solution)/shard_map/ppermute | solution.py:95
  63.5 1.7 %collective-permute-start.8 = (f32[64,768]{1,0:T(8,128)S(1)}, f32[64,768]{1,0:T(8,128)S(1)}, u32[]{:S(2)}, u32[]{:S(2)}) collective-permute-start(f32[64,768]{1,0:T(8,128)S(1)} %convert_add_fusion), channel_id=1, source_target_pairs={{0,8},{8,0},{16,24},{24,16},{1,9},{9,1},{17,25},{25,17},{2,10},{10... | collective-permute-start | bytes 589832 | tf_op jit(solution)/shard_map/ppermute | solution.py:95
  65.1 1.5 %collective-permute-start.5 = (f32[64,768]{1,0:T(8,128)S(1)}, f32[64,768]{1,0:T(8,128)S(1)}, u32[]{:S(2)}, u32[]{:S(2)}) collective-permute-start(f32[64,768]{1,0:T(8,128)S(1)} %convert_add_fusion.1), channel_id=1, source_target_pairs={{0,8},{8,0},{16,24},{24,16},{1,9},{9,1},{17,25},{25,17},{2,10},{10... | collective-permute-start | bytes 589832 | tf_op jit(solution)/shard_map/ppermute | solution.py:95
  67.4 5.1 %collective-permute-start.15 = (f32[8,1,16]{2,0,1:T(8,128)S(1)}, f32[8,1,16]{2,0,1:T(8,128)S(1)}, u32[]{:S(2)}, u32[]{:S(2)}) collective-permute-start(f32[8,1,16]{2,0,1:T(8,128)S(1)} %reshape.163), channel_id=1, source_target_pairs={{0,8},{8,0},{16,24},{24,16},{1,9},{9,1},{17,25},{25,17},{2,10},{10... | collective-permute-start | bytes 1544 | tf_op jit(solution)/shard_map/ppermute | solution.py:53
  72.5 3.6 %collective-permute-start.16 = (f32[8,1,16]{2,0,1:T(8,128)S(1)}, f32[8,1,16]{2,0,1:T(8,128)S(1)}, u32[]{:S(2)}, u32[]{:S(2)}) collective-permute-start(f32[8,1,16]{2,0,1:T(8,128)S(1)} %add.97), channel_id=1, source_target_pairs={{0,16},{8,24},{16,0},{24,8},{1,17},{9,25},{17,1},{25,9},{2,18},{10... | collective-permute-start | bytes 1544 | tf_op jit(solution)/shard_map/ppermute | solution.py:53
  79.5 3.7 %copy-start.14 = (f32[2,128]{1,0:T(2,128)}, f32[2,128]{1,0:T(2,128)S(1)}, u32[]{:S(2)}) copy-start(f32[2,128]{1,0:T(2,128)S(1)} %reshape.169) | copy-start | bytes 3076
  82.8 1.5 %collective-permute-start.11 = (bf16[2,128,96]{1,2,0:T(8,128)(2,1)S(1)}, bf16[2,128,96]{1,2,0:T(8,128)(2,1)S(1)}, u32[]{:S(2)}, u32[]{:S(2)}) collective-permute-start(bf16[2,128,96]{1,2,0:T(8,128)(2,1)S(1)} %convolution_convert_fusion.9), channel_id=1, source_target_pairs={{0,8},{8,0},{16,24},{24,16},{1,9},{9,1},{17,25},{25,17},{2,10},{10... | collective-permute-start | bytes 147464 | tf_op jit(solution)/shard_map/ppermute | solution.py:67
  83.2 2.6 %collective-permute-start.13 = (bf16[2,128,96]{1,2,0:T(8,128)(2,1)S(1)}, bf16[2,128,96]{1,2,0:T(8,128)(2,1)S(1)}, u32[]{:S(2)}, u32[]{:S(2)}) collective-permute-start(bf16[2,128,96]{1,2,0:T(8,128)(2,1)S(1)} %convolution_convert_fusion.8), channel_id=1, source_target_pairs={{0,8},{8,0},{16,24},{24,16},{1,9},{9,1},{17,25},{25,17},{2,10},{10... | collective-permute-start | bytes 147464 | tf_op jit(solution)/shard_map/ppermute | solution.py:67
  83.8 2.7 %collective-permute-start.17 = (bf16[2,128,96]{1,2,0:T(8,128)(2,1)S(1)}, bf16[2,128,96]{1,2,0:T(8,128)(2,1)S(1)}, u32[]{:S(2)}, u32[]{:S(2)}) collective-permute-start(bf16[2,128,96]{1,2,0:T(8,128)(2,1)S(1)} %convolution_convert_fusion.7), channel_id=1, source_target_pairs={{0,8},{8,0},{16,24},{24,16},{1,9},{9,1},{17,25},{25,17},{2,10},{10... | collective-permute-start | bytes 147464 | tf_op jit(solution)/shard_map/ppermute | solution.py:67
  83.9 4.2 %collective-permute-start.9 = (bf16[2,128,96]{1,2,0:T(8,128)(2,1)S(1)}, bf16[2,128,96]{1,2,0:T(8,128)(2,1)S(1)}, u32[]{:S(2)}, u32[]{:S(2)}) collective-permute-start(bf16[2,128,96]{1,2,0:T(8,128)(2,1)S(1)} %convolution_convert_fusion.10), channel_id=1, source_target_pairs={{0,8},{8,0},{16,24},{24,16},{1,9},{9,1},{17,25},{25,17},{2,10},{10... | collective-permute-start | bytes 147464 | tf_op jit(solution)/shard_map/ppermute | solution.py:67
  84.3 4.4 %collective-permute-start.12 = (bf16[2,128,96]{1,2,0:T(8,128)(2,1)S(1)}, bf16[2,128,96]{1,2,0:T(8,128)(2,1)S(1)}, u32[]{:S(2)}, u32[]{:S(2)}) collective-permute-start(bf16[2,128,96]{1,2,0:T(8,128)(2,1)S(1)} %add_convert_fusion.5), channel_id=1, source_target_pairs={{0,16},{8,24},{16,0},{24,8},{1,17},{9,25},{17,1},{25,9},{2,18},{10... | collective-permute-start | bytes 147464 | tf_op jit(solution)/shard_map/ppermute | solution.py:67
  85.9 4.3 %collective-permute-start.14 = (bf16[2,128,96]{1,2,0:T(8,128)(2,1)S(1)}, bf16[2,128,96]{1,2,0:T(8,128)(2,1)S(1)}, u32[]{:S(2)}, u32[]{:S(2)}) collective-permute-start(bf16[2,128,96]{1,2,0:T(8,128)(2,1)S(1)} %add_convert_fusion.4), channel_id=1, source_target_pairs={{0,16},{8,24},{16,0},{24,8},{1,17},{9,25},{17,1},{25,9},{2,18},{10... | collective-permute-start | bytes 147464 | tf_op jit(solution)/shard_map/ppermute | solution.py:67
  86.5 4.6 %collective-permute-start.18 = (bf16[2,128,96]{1,2,0:T(8,128)(2,1)S(1)}, bf16[2,128,96]{1,2,0:T(8,128)(2,1)S(1)}, u32[]{:S(2)}, u32[]{:S(2)}) collective-permute-start(bf16[2,128,96]{1,2,0:T(8,128)(2,1)S(1)} %add_convert_fusion.3), channel_id=1, source_target_pairs={{0,16},{8,24},{16,0},{24,8},{1,17},{9,25},{17,1},{25,9},{2,18},{10... | collective-permute-start | bytes 147464 | tf_op jit(solution)/shard_map/ppermute | solution.py:67
  88.1 10.3 %collective-permute-start.10 = (bf16[2,128,96]{1,2,0:T(8,128)(2,1)S(1)}, bf16[2,128,96]{1,2,0:T(8,128)(2,1)}, u32[]{:S(2)}, u32[]{:S(2)}) collective-permute-start(bf16[2,128,96]{1,2,0:T(8,128)(2,1)S(1)} %add_convert_fusion.6), channel_id=1, source_target_pairs={{0,16},{8,24},{16,0},{24,8},{1,17},{9,25},{17,1},{25,9},{2,18},{10... | collective-permute-start | bytes 147464 | tf_op jit(solution)/shard_map/ppermute | solution.py:67
  94.4 10.5 %all-to-all-start.1 = ((f32[8,3,16]{2,1,0:T(4,128)}), f32[8,3,16]{2,1,0:T(4,128)}, u32[]{:S(2)}, u32[]{:S(2)}) async-start(f32[8,3,16]{2,1,0:T(4,128)} %copy.36), calls=%async_computation.1 | async-start | bytes 32768 | tf_op jit(solution)/shard_map/all_to_all | solution.py:228
  98.3 4.2 %copy-start.15 = (f32[2,128]{1,0:T(2,128)S(1)}, f32[2,128]{1,0:T(2,128)}, u32[]{:S(2)}) copy-start(f32[2,128]{1,0:T(2,128)} %copy-done.14) | copy-start | bytes 3076
  100.4 6.0 %copy-start.11 = (pred[2,16,256]{2,1,0:T(8,128)(4,1)S(1)}, pred[2,16,256]{2,1,0:T(8,128)(4,1)}, u32[]{:S(2)}) copy-start(pred[2,16,256]{2,1,0:T(8,128)(4,1)} %fusion.33) | copy-start | bytes 24580
  100.4 6.1 %copy-start.10 = (pred[6,8,256]{2,0,1:T(8,128)(4,1)S(1)}, pred[6,8,256]{2,0,1:T(8,128)(4,1)}, u32[]{:S(2)}) copy-start(pred[6,8,256]{2,0,1:T(8,128)(4,1)} %get-tuple-element.31) | copy-start | bytes 36868
  100.4 6.1 %copy-start.13 = (pred[6,2,256]{2,0,1:T(8,128)(4,1)S(1)}, pred[6,2,256]{2,0,1:T(8,128)(4,1)}, u32[]{:S(2)}) copy-start(pred[6,2,256]{2,0,1:T(8,128)(4,1)} %get-tuple-element.29) | copy-start | bytes 9220
  (6 other events, 16.1 us)
Sparse Core Ops, SparseCore 0:
  29.4 46.5 all-gather.2

commit v13 on v12

--- a/solution.py
+++ b/solution.py
@@ -119,26 +119,29 @@
     cold_count = lax.axis_size("ep")
     hot_count = hot_ids.shape[0]
     capacity = tok_rows // 16
-    hot_hit, hot_sel = token_table(expert_ids, hot_ids, capacity)
-    hot_feats, hot_cotan, hot_scale = gather_rows(hot_hit, hot_sel, tokens, cotangent, gate_weights)
+    blocks = lax.axis_size("ep")
+    targets = jnp.concatenate([jnp.arange(cold_count, dtype=jnp.int32), hot_ids])
+    all_hit, all_sel = token_table(expert_ids, targets, capacity)
+    feats_all, cotan_all, scale_all = gather_rows(all_hit, all_sel, tokens, cotangent, gate_weights)
+    cold_total = cold_count * capacity
+    hot_feats, hot_cotan, hot_scale = (
+        feats_all[cold_total:],
+        cotan_all[cold_total:],
+        scale_all[cold_total:],
+    )
+    cold_feats, cold_cotan, cold_scale = (
+        feats_all[:cold_total],
+        cotan_all[:cold_total],
+        scale_all[:cold_total],
+    )
     hot_rows = hot_count * capacity
     scale_lines = -(-hot_rows // slice_width)
     scale_lines = -(-scale_lines // 8) * 8
     scale_block = jnp.pad(hot_scale, (0, scale_lines * slice_width - hot_rows)).reshape(
         scale_lines, slice_width
     )
-    blocks = lax.axis_size("ep")
     hot_outgoing = jnp.concatenate([hot_feats, hot_cotan, scale_block], axis=0)
-    hot_outgoing, expert_ids, tokens, cotangent, gate_weights = lax.optimization_barrier(
-        (hot_outgoing, expert_ids, tokens, cotangent, gate_weights)
-    )
     gathered = lax.all_gather(hot_outgoing, "ep", axis=0, tiled=False)
-    cold_hit, cold_sel = token_table(
-        expert_ids, jnp.arange(cold_count, dtype=jnp.int32), capacity
-    )
-    cold_feats, cold_cotan, cold_scale = gather_rows(
-        cold_hit, cold_sel, tokens, cotangent, gate_weights
-    )
     cold_lines = -(-capacity // slice_width)
     cold_lines = -(-cold_lines // 8) * 8
     cold_scale_block = jnp.pad(
@@ -229,9 +232,7 @@
     cold_back = route_back[:, 0, :]
     hot_route = jnp.sum(route_back[:, 1:, :], axis=0)
     gate_weight_grad = scatter_routes(
-        jnp.concatenate([cold_hit, hot_hit], axis=1),
-        jnp.concatenate([cold_sel, hot_sel], axis=0),
-        jnp.concatenate([cold_back, hot_route], axis=0),
+        all_hit, all_sel, jnp.concatenate([cold_back, hot_route], axis=0)
     )
     return (
         grad_gate_cold[None].astype(jnp.bfloat16),

time: 115 us -> 110 us (0.957)
  other arithmetic: 14.5 us -> 11 us
  matrix products: 20.3 us -> 18.8 us
    eq x2 -> x0, other arithmetic: 2.14 us -> none  [token_table(): hit = expert_ids.T[:, None, :] == targets[None, :, None]]
    dot_general x2 -> x1, matrix products: 1.58 us -> 0.28 us  [gather_rows(): jnp.dot(token_map, tokens, preferred_element_type=jnp.float32)]
    unnamed x37 -> x34, local copies, waits for them, and re-layouts: 2.07 us -> 2.8 us
  transfers between devices with their start and end apart: 22 -> 22, of which waited for: 9 -> 9; matrix products, arithmetic and copies ran while one was open for 19% -> 18% of each run, Pallas kernels for 0% -> 0%
where the time goes in v13:
time: 110 us; the launch traced here: 109 us
  waiting for transfers between devices  34.5 us (31%)
  starting transfers between devices  22.5 us (20%)
  matrix products  18.8 us (17%)
  between operations  14.6 us (13%)
  other arithmetic  11 us (10%)
  local copies, waits for them, and re-layouts  7.37 us (7%)
    all_to_all x1, waiting for transfers between devices, body(): lax.all_to_all(outgoing, 'ep', split_axis=0, concat_axis=0, tiled=True)  24.6 us
    all_to_all x1, starting transfers between devices, body(): lax.all_to_all(outgoing, 'ep', split_axis=0, concat_axis=0, tiled=True)  7.28 us
    ppermute x8, starting transfers between devices, grp_sum_doubling(): got = lax.ppermute(mine, axis_name, partner)  5.45 us
    ppermute x3, waiting for transfers between devices, grp_sum_rounded(): got = lax.ppermute(mine, axis_name, partner)  4.8 us
    all_to_all x1, starting transfers between devices, body(): lax.all_to_all(route_parts, 'ep', split_axis=0, concat_axis=0, tiled=True)  3.95 us
    ppermute x3, starting transfers between devices, grp_sum_rounded(): got = lax.ppermute(mine, axis_name, partner)  3.71 us
    unnamed x34, local copies, waits for them, and re-layouts  2.8 us
    ppermute x8, waiting for transfers between devices, grp_sum_doubling(): got = lax.ppermute(mine, axis_name, partner)  2.41 us
  transfers between devices with their start and end apart: 22, of which 9 were waited for; matrix products, arithmetic and copies ran while one was open for 18% of the time, Pallas kernels for 0%

profile of v13, /device:TPU:0, one launch (start us, length us, event | category | flops | bytes accessed | tf_op | source)
XLA Modules:
  0.0 108.8 jit_solution(13271502282075157526)
XLA Ops:
  7.2 0.8 convert_bitcast_fusion
  8.7 0.8 compare_reduce_fusion
  9.6 0.8 fusion.29
  11.7 1.4 %convolution_convert_fusion.3 = bf16[160,1280]{1,0:T(8,128)(2,1)S(1)} fusion(pred[160,256]{1,0:T(32,128)(4,1)S(1)} %fusion.27, bf16[256,1280]{1,0:T(8,128)(2,1)} %param.12), kind=kOutput, calls=%fused_computation.7 | convolution fusion | flops 105062400 | bytes 1105920 | tf_op jit(solution)/shard_map/dot_general | solution.py:20
  14.2 0.9 pad_maximum_fusion
  15.2 7.3 %all-to-all-start = ((bf16[8,40,1280]{2,1,0:T(8,128)(2,1)}), bf16[8,40,1280]{2,1,0:T(8,128)(2,1)S(1)}, u32[]{:S(2)}, u32[]{:S(2)}) async-start(bf16[8,40,1280]{2,1,0:T(8,128)(2,1)} %pad_maximum_fusion), calls=%async_computation | async-start | bytes 1638400 | tf_op jit(solution)/shard_map/all_to_all | solution.py:159
  23.4 24.6 %all-to-all-done = bf16[8,40,1280]{2,1,0:T(8,128)(2,1)S(1)} async-done(((bf16[8,40,1280]{2,1,0:T(8,128)(2,1)}), bf16[8,40,1280]{2,1,0:T(8,128)(2,1)S(1)}, u32[]{:S(2)}, u32[]{:S(2)}) %all-to-all-start) | async-done | bytes 819232 | tf_op jit(solution)/shard_map/all_to_all | solution.py:159
  51.4 0.8 fusion.22
  52.3 1.6 %collective-permute-start.1 = (bf16[64,768]{1,0:T(8,128)(2,1)S(1)}, bf16[64,768]{1,0:T(8,128)(2,1)S(1)}, u32[]{:S(2)}, u32[]{:S(2)}) collective-permute-start(bf16[64,768]{1,0:T(8,128)(2,1)S(1)} %add_convert_fusion.2), channel_id=1, source_target_pairs={{0,16},{8,24},{16,0},{24,8},{1,17},{9,25},{17,1},{25,9},{2,18},{10... | collective-permute-start | bytes 294920 | tf_op jit(solution)/shard_map/ppermute | solution.py:92
  54.5 1.6 %collective-permute-start.4 = (bf16[64,768]{1,0:T(8,128)(2,1)S(1)}, bf16[64,768]{1,0:T(8,128)(2,1)S(1)}, u32[]{:S(2)}, u32[]{:S(2)}) collective-permute-start(bf16[64,768]{1,0:T(8,128)(2,1)S(1)} %add_convert_fusion.1), channel_id=1, source_target_pairs={{0,16},{8,24},{16,0},{24,8},{1,17},{9,25},{17,1},{25,9},{2,18},{10... | collective-permute-start | bytes 294920 | tf_op jit(solution)/shard_map/ppermute | solution.py:92
  56.1 1.9 %collective-permute-done.1 = bf16[64,768]{1,0:T(8,128)(2,1)S(1)} collective-permute-done((bf16[64,768]{1,0:T(8,128)(2,1)S(1)}, bf16[64,768]{1,0:T(8,128)(2,1)S(1)}, u32[]{:S(2)}, u32[]{:S(2)}) %collective-permute-start.1) | collective-permute-done | bytes 98336 | tf_op jit(solution)/shard_map/ppermute | solution.py:92
  58.6 1.4 %collective-permute-done.7 = bf16[64,768]{1,0:T(8,128)(2,1)S(1)} collective-permute-done((bf16[64,768]{1,0:T(8,128)(2,1)S(1)}, bf16[64,768]{1,0:T(8,128)(2,1)S(1)}, u32[]{:S(2)}, u32[]{:S(2)}) %collective-permute-start.7) | collective-permute-done | bytes 98336 | tf_op jit(solution)/shard_map/ppermute | solution.py:92
  60.1 1.5 %collective-permute-done.4 = bf16[64,768]{1,0:T(8,128)(2,1)S(1)} collective-permute-done((bf16[64,768]{1,0:T(8,128)(2,1)S(1)}, bf16[64,768]{1,0:T(8,128)(2,1)S(1)}, u32[]{:S(2)}, u32[]{:S(2)}) %collective-permute-start.4) | collective-permute-done | bytes 98336 | tf_op jit(solution)/shard_map/ppermute | solution.py:92
  61.8 1.4 %collective-permute-done.5 = f32[64,768]{1,0:T(8,128)S(1)} collective-permute-done((f32[64,768]{1,0:T(8,128)S(1)}, f32[64,768]{1,0:T(8,128)S(1)}, u32[]{:S(2)}, u32[]{:S(2)}) %collective-permute-start.5) | collective-permute-done | bytes 196640 | tf_op jit(solution)/shard_map/ppermute | solution.py:95
  64.1 1.0 broadcast_select_fusion.7
  65.1 2.0 %fusion = bf16[1,1280,768]{2,1,0:T(8,128)(2,1)} fusion(bf16[128,1280]{1,0:T(8,128)(2,1)S(1)} %bitcast.95, f32[64,768]{1,0:T(8,128)S(1)} %get-tuple-element.18, f32[64,768]{1,0:T(8,128)S(1)} %get-tuple-element.17, f32[64,768]{1,0:T(8,128)S(1)} %get-tuple-element.16, f32[64,768]{1,0:T(8,128)S(1)} %get-tuple-element.15, f32[64,768]{1,0:T(8,128)S(1)} %get-tuple-element.14, ...), kind=kOutput, calls=%fused_computation.3 | convolution fusion | flops 253919232 | bytes 3473408 | tf_op jit(solution)/shard_map/dot_general | solution.py:206
  67.1 2.0 %fusion.1 = bf16[1,1280,768]{2,1,0:T(8,128)(2,1)} fusion(bf16[128,1280]{1,0:T(8,128)(2,1)S(1)} %bitcast.96, f32[64,768]{1,0:T(8,128)S(1)} %get-tuple-element.14, f32[64,768]{1,0:T(8,128)S(1)} %get-tuple-element.13, f32[64,768]{1,0:T(8,128)S(1)} %get-tuple-element.18, f32[64,768]{1,0:T(8,128)S(1)} %get-tuple-element.17), kind=kOutput, calls=%fused_computation.4 | convolution fusion | flops 253427712 | bytes 3080192 | tf_op jit(solution)/shard_map/dot_general | solution.py:209
  69.1 1.5 %collective-permute-start.16 = (f32[8,1,16]{2,0,1:T(8,128)S(1)}, f32[8,1,16]{2,0,1:T(8,128)S(1)}, u32[]{:S(2)}, u32[]{:S(2)}) collective-permute-start(f32[8,1,16]{2,0,1:T(8,128)S(1)} %add.91), channel_id=1, source_target_pairs={{0,16},{8,24},{16,0},{24,8},{1,17},{9,25},{17,1},{25,9},{2,18},{10... | collective-permute-start | bytes 1544 | tf_op jit(solution)/shard_map/ppermute | solution.py:53
  70.6 2.0 %fusion.2 = bf16[1,768,1280]{2,1,0:T(8,128)(2,1)} fusion(bf16[128,768]{1,0:T(8,128)(2,1)S(1)} %multiply_convert_fusion.4, bf16[128,1280]{1,0:T(8,128)(2,1)S(1)} %copy-done.4), kind=kOutput, calls=%fused_computation.5 | convolution fusion | flops 252641280 | bytes 2490368 | tf_op jit(solution)/shard_map/dot_general | solution.py:212
  72.7 0.9 slice_bitcast_fusion
  73.7 1.4 %slice.96 = bf16[8,64,1280]{2,1,0:T(8,128)(2,1)S(1)} slice(bf16[8,72,1280]{2,1,0:T(8,128)(2,1)} %bitcast.104), slice={[0:8], [0:64], [0:1280]} | slice | bytes 2621440 | tf_op jit(solution)/shard_map/slice | solution.py:174
  75.5 1.5 %convolution_convert_fusion.5 = bf16[2,128,96]{1,2,0:T(8,128)(2,1)S(1)} fusion(bf16[2,128,1280]{2,1,0:T(8,128)(2,1)S(1)} %bitcast.97, bf16[2,96,1280]{2,1,0:T(8,128)(2,1)} %param.21), kind=kOutput, calls=%fused_computation.22 | convolution fusion | flops 62939136 | bytes 1196032 | tf_op jit(solution)/shard_map/jrd,jhd->jrh/dot_general | solution.py:192
  77.0 1.4 %convolution_convert_fusion.8 = bf16[2,128,96]{1,2,0:T(8,128)(2,1)S(1)} fusion(bf16[2,96,1280]{2,1,0:T(8,128)(2,1)} %param.21, bf16[2,128,1280]{2,1,0:T(8,128)(2,1)S(1)} %bitcast.98, f32[2,128]{1,0:T(2,128)S(1)} %reshape.137), kind=kOutput, calls=%fused_computation.25 | convolution fusion | flops 63922176 | bytes 1197056 | tf_op jit(solution)/shard_map/jrd,jhd->jrh/dot_general | solution.py:189
  80.3 1.6 %collective-permute-start.12 = (bf16[2,128,96]{1,2,0:T(8,128)(2,1)S(1)}, bf16[2,128,96]{1,2,0:T(8,128)(2,1)S(1)}, u32[]{:S(2)}, u32[]{:S(2)}) collective-permute-start(bf16[2,128,96]{1,2,0:T(8,128)(2,1)S(1)} %add_convert_fusion.5), channel_id=1, source_target_pairs={{0,16},{8,24},{16,0},{24,8},{1,17},{9,25},{17,1},{25,9},{2,18},{10... | collective-permute-start | bytes 147464 | tf_op jit(solution)/shard_map/ppermute | solution.py:67
  82.5 1.6 %collective-permute-start.18 = (bf16[2,128,96]{1,2,0:T(8,128)(2,1)S(1)}, bf16[2,128,96]{1,2,0:T(8,128)(2,1)S(1)}, u32[]{:S(2)}, u32[]{:S(2)}) collective-permute-start(bf16[2,128,96]{1,2,0:T(8,128)(2,1)S(1)} %add_convert_fusion.3), channel_id=1, source_target_pairs={{0,16},{8,24},{16,0},{24,8},{1,17},{9,25},{17,1},{25,9},{2,18},{10... | collective-permute-start | bytes 147464 | tf_op jit(solution)/shard_map/ppermute | solution.py:67
  84.7 1.5 %collective-permute-done.14 = bf16[2,128,96]{1,2,0:T(8,128)(2,1)S(1)} collective-permute-done((bf16[2,128,96]{1,2,0:T(8,128)(2,1)S(1)}, bf16[2,128,96]{1,2,0:T(8,128)(2,1)S(1)}, u32[]{:S(2)}, u32[]{:S(2)}) %collective-permute-start.14) | collective-permute-done | bytes 49184 | tf_op jit(solution)/shard_map/ppermute | solution.py:67
  86.2 0.9 collective-permute-done.18
  89.1 3.9 %all-to-all-start.1 = ((f32[8,3,16]{2,1,0:T(4,128)}), f32[8,3,16]{2,1,0:T(4,128)}, u32[]{:S(2)}, u32[]{:S(2)}) async-start(f32[8,3,16]{2,1,0:T(4,128)} %copy.45), calls=%async_computation.1 | async-start | bytes 32768 | tf_op jit(solution)/shard_map/all_to_all | solution.py:231
  93.1 2.1 %fusion.31 = f32[2,1280,96]{1,2,0:T(8,128)} fusion(bf16[2,128,1280]{2,1,0:T(8,128)(2,1)S(1)} %bitcast.91, bf16[2,128,96]{1,2,0:T(8,128)(2,1)} %collective-permute-done.10, bf16[2,128,96]{1,2,0:T(8,128)(2,1)S(1)} %add_convert_fusion.6, bf16[2,128,96]{1,2,0:T(8,128)(2,1)} %copy-done.8, bf16[2,128,96]{1,2,0:T(8,128)(2,1)S(1)} %add_convert_fusion.5, ...), kind=kOutput, calls=%fused_computation.83 | convolution fusion | flops 63381504 | bytes 1933312 | tf_op jit(solution)/shard_map/jrd,jrh->jdh/dot_general | solution.py:217
  95.2 2.1 %fusion.32 = f32[2,1280,96]{1,2,0:T(8,128)} fusion(bf16[2,128,1280]{2,1,0:T(8,128)(2,1)S(1)} %bitcast.92, bf16[2,128,96]{1,2,0:T(8,128)(2,1)} %collective-permute-done.10, bf16[2,128,96]{1,2,0:T(8,128)(2,1)S(1)} %add_convert_fusion.6, bf16[2,128,96]{1,2,0:T(8,128)(2,1)S(1)} %collective-permute-done.14, bf16[2,128,96]{1,2,0:T(8,128)(2,1)S(1)} %add_convert_fusion.4), kind=kOutput, calls=%fused_computation.84 | convolution fusion | flops 63209472 | bytes 1835008 | tf_op jit(solution)/shard_map/jrd,jrh->jdh/dot_general | solution.py:220
  97.2 1.3 %fusion.23 = f32[2,96,1280]{2,1,0:T(8,128)} fusion(bf16[2,128,96]{1,2,0:T(8,128)(2,1)S(1)} %get-tuple-element.8, bf16[2,128,1280]{2,1,0:T(8,128)(2,1)S(1)} %bitcast.99, f32[2,128]{1,0:T(2,128)S(1)} %copy-done.13), kind=kOutput, calls=%fused_computation.30 | convolution fusion | flops 63897600 | bytes 1688576 | tf_op jit(solution)/shard_map/jrh,jrd->jhd/dot_general | solution.py:221
  98.5 1.2 %all-to-all-done.1 = f32[8,3,16]{2,1,0:T(4,128)} async-done(((f32[8,3,16]{2,1,0:T(4,128)}), f32[8,3,16]{2,1,0:T(4,128)}, u32[]{:S(2)}, u32[]{:S(2)}) %all-to-all-start.1) | async-done | bytes 1568 | tf_op jit(solution)/shard_map/all_to_all | solution.py:231
  (136 shorter events, 17.8 us)
Async XLA Ops:
  7.2 41.1 %copy-start = (bf16[1,768,1280]{2,1,0:T(8,128)(2,1)S(1)}, bf16[1,768,1280]{2,1,0:T(8,128)(2,1)}, u32[]{:S(2)}) copy-start(bf16[1,768,1280]{2,1,0:T(8,128)(2,1)} %param.18) | copy-start | bytes 5898244
  14.2 8.5 %slice-start = ((bf16[160,1280]{1,0:T(8,128)(2,1)}), bf16[32,1280]{1,0:T(8,128)(2,1)S(1)}, s32[]{:S(2)}) async-start(bf16[160,1280]{1,0:T(8,128)(2,1)} %copy-done.3), calls=%async_computation.3 | async-start | bytes 163840 | tf_op jit(solution)/shard_map/slice | solution.py:128
  15.2 32.8 %all-to-all-start = ((bf16[8,40,1280]{2,1,0:T(8,128)(2,1)}), bf16[8,40,1280]{2,1,0:T(8,128)(2,1)S(1)}, u32[]{:S(2)}, u32[]{:S(2)}) async-start(bf16[8,40,1280]{2,1,0:T(8,128)(2,1)} %pad_maximum_fusion), calls=%async_computation | async-start | bytes 1638400 | tf_op jit(solution)/shard_map/all_to_all | solution.py:159
  22.4 50.3 %all-gather.3.cloned.1.call-start = ((), (), s32[]{:S(2)}) async-start(), calls=%async_computation.2 | async-start | bytes 1658880 | tf_op jit(solution)/shard_map/all_gather | solution.py:144
  49.1 3.1 %collective-permute-start = (bf16[64,768]{1,0:T(8,128)(2,1)S(1)}, bf16[64,768]{1,0:T(8,128)(2,1)S(1)}, u32[]{:S(2)}, u32[]{:S(2)}) collective-permute-start(bf16[64,768]{1,0:T(8,128)(2,1)S(1)} %broadcast_select_fusion.8), channel_id=1, source_target_pairs={{0,8},{8,0},{16,24},{24,16},{1,9},{9,1},{17,25},{25,17},{2,10},{10... | collective-permute-start | bytes 294920 | tf_op jit(solution)/shard_map/ppermute | solution.py:86
  50.3 3.5 %collective-permute-start.6 = (bf16[64,768]{1,0:T(8,128)(2,1)S(1)}, bf16[64,768]{1,0:T(8,128)(2,1)S(1)}, u32[]{:S(2)}, u32[]{:S(2)}) collective-permute-start(bf16[64,768]{1,0:T(8,128)(2,1)S(1)} %broadcast_select_fusion.2), channel_id=1, source_target_pairs={{0,8},{8,0},{16,24},{24,16},{1,9},{9,1},{17,25},{25,17},{2,10},{10... | collective-permute-start | bytes 294920 | tf_op jit(solution)/shard_map/ppermute | solution.py:86
  51.3 3.2 %collective-permute-start.3 = (bf16[64,768]{1,0:T(8,128)(2,1)S(1)}, bf16[64,768]{1,0:T(8,128)(2,1)S(1)}, u32[]{:S(2)}, u32[]{:S(2)}) collective-permute-start(bf16[64,768]{1,0:T(8,128)(2,1)S(1)} %broadcast_select_fusion.5), channel_id=1, source_target_pairs={{0,8},{8,0},{16,24},{24,16},{1,9},{9,1},{17,25},{25,17},{2,10},{10... | collective-permute-start | bytes 294920 | tf_op jit(solution)/shard_map/ppermute | solution.py:86
  52.3 5.7 %collective-permute-start.1 = (bf16[64,768]{1,0:T(8,128)(2,1)S(1)}, bf16[64,768]{1,0:T(8,128)(2,1)S(1)}, u32[]{:S(2)}, u32[]{:S(2)}) collective-permute-start(bf16[64,768]{1,0:T(8,128)(2,1)S(1)} %add_convert_fusion.2), channel_id=1, source_target_pairs={{0,16},{8,24},{16,0},{24,8},{1,17},{9,25},{17,1},{25,9},{2,18},{10... | collective-permute-start | bytes 294920 | tf_op jit(solution)/shard_map/ppermute | solution.py:92
  53.9 6.2 %collective-permute-start.7 = (bf16[64,768]{1,0:T(8,128)(2,1)S(1)}, bf16[64,768]{1,0:T(8,128)(2,1)S(1)}, u32[]{:S(2)}, u32[]{:S(2)}) collective-permute-start(bf16[64,768]{1,0:T(8,128)(2,1)S(1)} %add_convert_fusion), channel_id=1, source_target_pairs={{0,16},{8,24},{16,0},{24,8},{1,17},{9,25},{17,1},{25,9},{2,18},{10... | collective-permute-start | bytes 294920 | tf_op jit(solution)/shard_map/ppermute | solution.py:92
  54.5 7.2 %collective-permute-start.4 = (bf16[64,768]{1,0:T(8,128)(2,1)S(1)}, bf16[64,768]{1,0:T(8,128)(2,1)S(1)}, u32[]{:S(2)}, u32[]{:S(2)}) collective-permute-start(bf16[64,768]{1,0:T(8,128)(2,1)S(1)} %add_convert_fusion.1), channel_id=1, source_target_pairs={{0,16},{8,24},{16,0},{24,8},{1,17},{9,25},{17,1},{25,9},{2,18},{10... | collective-permute-start | bytes 294920 | tf_op jit(solution)/shard_map/ppermute | solution.py:92
  58.6 5.5 %collective-permute-start.2 = (f32[64,768]{1,0:T(8,128)}, f32[64,768]{1,0:T(8,128)}, u32[]{:S(2)}, u32[]{:S(2)}) collective-permute-start(f32[64,768]{1,0:T(8,128)} %convert_add_fusion.2), channel_id=1, source_target_pairs={{0,8},{8,0},{16,24},{24,16},{1,9},{9,1},{17,25},{25,17},{2,10},{10... | collective-permute-start | bytes 589832 | tf_op jit(solution)/shard_map/ppermute | solution.py:95
  60.1 1.7 %collective-permute-start.8 = (f32[64,768]{1,0:T(8,128)S(1)}, f32[64,768]{1,0:T(8,128)S(1)}, u32[]{:S(2)}, u32[]{:S(2)}) collective-permute-start(f32[64,768]{1,0:T(8,128)S(1)} %convert_add_fusion), channel_id=1, source_target_pairs={{0,8},{8,0},{16,24},{24,16},{1,9},{9,1},{17,25},{25,17},{2,10},{10... | collective-permute-start | bytes 589832 | tf_op jit(solution)/shard_map/ppermute | solution.py:95
  61.7 1.5 %collective-permute-start.5 = (f32[64,768]{1,0:T(8,128)S(1)}, f32[64,768]{1,0:T(8,128)S(1)}, u32[]{:S(2)}, u32[]{:S(2)}) collective-permute-start(f32[64,768]{1,0:T(8,128)S(1)} %convert_add_fusion.1), channel_id=1, source_target_pairs={{0,8},{8,0},{16,24},{24,16},{1,9},{9,1},{17,25},{25,17},{2,10},{10... | collective-permute-start | bytes 589832 | tf_op jit(solution)/shard_map/ppermute | solution.py:95
  64.0 5.1 %collective-permute-start.15 = (f32[8,1,16]{2,0,1:T(8,128)S(1)}, f32[8,1,16]{2,0,1:T(8,128)S(1)}, u32[]{:S(2)}, u32[]{:S(2)}) collective-permute-start(f32[8,1,16]{2,0,1:T(8,128)S(1)} %reshape.132), channel_id=1, source_target_pairs={{0,8},{8,0},{16,24},{24,16},{1,9},{9,1},{17,25},{25,17},{2,10},{10... | collective-permute-start | bytes 1544 | tf_op jit(solution)/shard_map/ppermute | solution.py:53
  67.1 3.5 %copy-start.4 = (bf16[128,1280]{1,0:T(8,128)(2,1)S(1)}, bf16[128,1280]{1,0:T(8,128)(2,1)}, u32[]{:S(2)}) copy-start(bf16[128,1280]{1,0:T(8,128)(2,1)} %fusion.22) | copy-start | bytes 983044
  69.1 3.6 %collective-permute-start.16 = (f32[8,1,16]{2,0,1:T(8,128)S(1)}, f32[8,1,16]{2,0,1:T(8,128)S(1)}, u32[]{:S(2)}, u32[]{:S(2)}) collective-permute-start(f32[8,1,16]{2,0,1:T(8,128)S(1)} %add.91), channel_id=1, source_target_pairs={{0,16},{8,24},{16,0},{24,8},{1,17},{9,25},{17,1},{25,9},{2,18},{10... | collective-permute-start | bytes 1544 | tf_op jit(solution)/shard_map/ppermute | solution.py:53
  75.5 2.9 %copy-start.12 = (f32[2,128]{1,0:T(2,128)}, f32[2,128]{1,0:T(2,128)S(1)}, u32[]{:S(2)}) copy-start(f32[2,128]{1,0:T(2,128)S(1)} %reshape.137) | copy-start | bytes 3076
  75.5 2.9 %copy-start.6 = (bf16[2,1280,96]{1,2,0:T(8,128)(2,1)S(1)}, bf16[2,1280,96]{1,2,0:T(8,128)(2,1)}, u32[]{:S(2)}) copy-start(bf16[2,1280,96]{1,2,0:T(8,128)(2,1)} %param.20) | copy-start | bytes 1474564
  75.5 3.4 %copy-start.7 = (bf16[2,1280,96]{1,2,0:T(8,128)(2,1)S(1)}, bf16[2,1280,96]{1,2,0:T(8,128)(2,1)}, u32[]{:S(2)}) copy-start(bf16[2,1280,96]{1,2,0:T(8,128)(2,1)} %param.19) | copy-start | bytes 1474564
  78.8 1.5 %collective-permute-start.11 = (bf16[2,128,96]{1,2,0:T(8,128)(2,1)S(1)}, bf16[2,128,96]{1,2,0:T(8,128)(2,1)S(1)}, u32[]{:S(2)}, u32[]{:S(2)}) collective-permute-start(bf16[2,128,96]{1,2,0:T(8,128)(2,1)S(1)} %convolution_convert_fusion.7), channel_id=1, source_target_pairs={{0,8},{8,0},{16,24},{24,16},{1,9},{9,1},{17,25},{25,17},{2,10},{10... | collective-permute-start | bytes 147464 | tf_op jit(solution)/shard_map/ppermute | solution.py:67
  79.2 2.6 %collective-permute-start.13 = (bf16[2,128,96]{1,2,0:T(8,128)(2,1)S(1)}, bf16[2,128,96]{1,2,0:T(8,128)(2,1)S(1)}, u32[]{:S(2)}, u32[]{:S(2)}) collective-permute-start(bf16[2,128,96]{1,2,0:T(8,128)(2,1)S(1)} %convolution_convert_fusion.6), channel_id=1, source_target_pairs={{0,8},{8,0},{16,24},{24,16},{1,9},{9,1},{17,25},{25,17},{2,10},{10... | collective-permute-start | bytes 147464 | tf_op jit(solution)/shard_map/ppermute | solution.py:67
  79.8 2.7 %collective-permute-start.17 = (bf16[2,128,96]{1,2,0:T(8,128)(2,1)S(1)}, bf16[2,128,96]{1,2,0:T(8,128)(2,1)S(1)}, u32[]{:S(2)}, u32[]{:S(2)}) collective-permute-start(bf16[2,128,96]{1,2,0:T(8,128)(2,1)S(1)} %convolution_convert_fusion.5), channel_id=1, source_target_pairs={{0,8},{8,0},{16,24},{24,16},{1,9},{9,1},{17,25},{25,17},{2,10},{10... | collective-permute-start | bytes 147464 | tf_op jit(solution)/shard_map/ppermute | solution.py:67
  79.9 4.2 %collective-permute-start.9 = (bf16[2,128,96]{1,2,0:T(8,128)(2,1)S(1)}, bf16[2,128,96]{1,2,0:T(8,128)(2,1)S(1)}, u32[]{:S(2)}, u32[]{:S(2)}) collective-permute-start(bf16[2,128,96]{1,2,0:T(8,128)(2,1)S(1)} %convolution_convert_fusion.8), channel_id=1, source_target_pairs={{0,8},{8,0},{16,24},{24,16},{1,9},{9,1},{17,25},{25,17},{2,10},{10... | collective-permute-start | bytes 147464 | tf_op jit(solution)/shard_map/ppermute | solution.py:67
  80.3 4.4 %collective-permute-start.12 = (bf16[2,128,96]{1,2,0:T(8,128)(2,1)S(1)}, bf16[2,128,96]{1,2,0:T(8,128)(2,1)S(1)}, u32[]{:S(2)}, u32[]{:S(2)}) collective-permute-start(bf16[2,128,96]{1,2,0:T(8,128)(2,1)S(1)} %add_convert_fusion.5), channel_id=1, source_target_pairs={{0,16},{8,24},{16,0},{24,8},{1,17},{9,25},{17,1},{25,9},{2,18},{10... | collective-permute-start | bytes 147464 | tf_op jit(solution)/shard_map/ppermute | solution.py:67
  81.9 4.3 %collective-permute-start.14 = (bf16[2,128,96]{1,2,0:T(8,128)(2,1)S(1)}, bf16[2,128,96]{1,2,0:T(8,128)(2,1)S(1)}, u32[]{:S(2)}, u32[]{:S(2)}) collective-permute-start(bf16[2,128,96]{1,2,0:T(8,128)(2,1)S(1)} %add_convert_fusion.4), channel_id=1, source_target_pairs={{0,16},{8,24},{16,0},{24,8},{1,17},{9,25},{17,1},{25,9},{2,18},{10... | collective-permute-start | bytes 147464 | tf_op jit(solution)/shard_map/ppermute | solution.py:67
  82.5 4.6 %collective-permute-start.18 = (bf16[2,128,96]{1,2,0:T(8,128)(2,1)S(1)}, bf16[2,128,96]{1,2,0:T(8,128)(2,1)S(1)}, u32[]{:S(2)}, u32[]{:S(2)}) collective-permute-start(bf16[2,128,96]{1,2,0:T(8,128)(2,1)S(1)} %add_convert_fusion.3), channel_id=1, source_target_pairs={{0,16},{8,24},{16,0},{24,8},{1,17},{9,25},{17,1},{25,9},{2,18},{10... | collective-permute-start | bytes 147464 | tf_op jit(solution)/shard_map/ppermute | solution.py:67
  84.1 9.0 %collective-permute-start.10 = (bf16[2,128,96]{1,2,0:T(8,128)(2,1)S(1)}, bf16[2,128,96]{1,2,0:T(8,128)(2,1)}, u32[]{:S(2)}, u32[]{:S(2)}) collective-permute-start(bf16[2,128,96]{1,2,0:T(8,128)(2,1)S(1)} %add_convert_fusion.6), channel_id=1, source_target_pairs={{0,16},{8,24},{16,0},{24,8},{1,17},{9,25},{17,1},{25,9},{2,18},{10... | collective-permute-start | bytes 147464 | tf_op jit(solution)/shard_map/ppermute | solution.py:67
  84.7 3.0 %copy-start.8 = (bf16[2,128,96]{1,2,0:T(8,128)(2,1)}, bf16[2,128,96]{1,2,0:T(8,128)(2,1)S(1)}, u32[]{:S(2)}) copy-start(bf16[2,128,96]{1,2,0:T(8,128)(2,1)S(1)} %collective-permute-done.12) | copy-start | bytes 147460
  88.5 8.7 %copy-start.13 = (f32[2,128]{1,0:T(2,128)S(1)}, f32[2,128]{1,0:T(2,128)}, u32[]{:S(2)}) copy-start(f32[2,128]{1,0:T(2,128)} %copy-done.12) | copy-start | bytes 3076
  89.1 10.5 %all-to-all-start.1 = ((f32[8,3,16]{2,1,0:T(4,128)}), f32[8,3,16]{2,1,0:T(4,128)}, u32[]{:S(2)}, u32[]{:S(2)}) async-start(f32[8,3,16]{2,1,0:T(4,128)} %copy.45), calls=%async_computation.1 | async-start | bytes 32768 | tf_op jit(solution)/shard_map/all_to_all | solution.py:231
  95.2 6.1 %copy-start.9 = (s32[256,6]{0,1:T(8,128)S(1)}, s32[256,6]{0,1:T(8,128)}, u32[]{:S(2)}) copy-start(s32[256,6]{0,1:T(8,128)} %param.14) | copy-start | bytes 18436
  95.2 6.1 %copy-start.11 = (s32[10]{0:T(128)S(1)}, s32[10]{0:T(128)}, u32[]{:S(2)}) copy-start(s32[10]{0:T(128)} %copy-done.10) | copy-start | bytes 124
  (5 other events, 7.5 us)
Sparse Core Ops, SparseCore 0:
  26.0 46.5 all-gather.2

commit v14 on v13

--- a/solution.py
+++ b/solution.py
@@ -195,22 +195,25 @@
     pre_gate, pre_up, grad_hidden = grp_sum_rounded(
         [part_gate, part_up, part_hidden], [0, 0, 0], "grp"
     )
-    pre_gate_hot, pre_up_hot, grad_hidden_hot, cot_down = grp_sum_doubling(
-        [part_gate_hot, part_up_hot, part_hidden_hot, part_cot_hot], "grp"
-    )
     hidden, back_gate, back_up = swiglu_back(pre_gate, pre_up, grad_hidden)
     output_slice = jnp.dot(hidden, w_down, preferred_element_type=jnp.float32)
     cold_route = jnp.sum(output_slice * recv_cotan.astype(jnp.float32), axis=1)
     cold_route = grp_sum_f32(cold_route.reshape(cold_count, 1, capacity), "grp")
     contract_rows = (((0,), (0,)), ((), ()))
+    late_feats, back_gate, back_up, late_hidden, late_weighted, part_gate_hot = (
+        lax.optimization_barrier((recv_feats, back_gate, back_up, hidden, weighted, part_gate_hot))
+    )
+    pre_gate_hot, pre_up_hot, grad_hidden_hot, cot_down = grp_sum_doubling(
+        [part_gate_hot, part_up_hot, part_hidden_hot, part_cot_hot], "grp"
+    )
     grad_gate_cold = lax.dot_general(
-        recv_feats, back_gate, contract_rows, preferred_element_type=jnp.float32
+        late_feats, back_gate, contract_rows, preferred_element_type=jnp.float32
     )
     grad_up_cold = lax.dot_general(
-        recv_feats, back_up, contract_rows, preferred_element_type=jnp.float32
+        late_feats, back_up, contract_rows, preferred_element_type=jnp.float32
     )
     grad_down_cold = lax.dot_general(
-        hidden, weighted, contract_rows, preferred_element_type=jnp.float32
+        late_hidden, late_weighted, contract_rows, preferred_element_type=jnp.float32
     )
     hidden_hot, back_gate_hot, back_up_hot = swiglu_back(pre_gate_hot, pre_up_hot, grad_hidden_hot)
     hot_route_part = jnp.sum(hidden_hot.astype(jnp.float32) * cot_down, axis=2)

time: 110 us -> 113 us (1.027)
  waiting for transfers between devices: 34.5 us -> 41.4 us
  local copies, waits for them, and re-layouts: 7.37 us -> 5.85 us
  other arithmetic: 11 us -> 9.49 us
    all_gather x1, waiting for transfers between devices: 0.01 us -> 3.21 us  [body(): gathered = lax.all_gather(hot_outgoing, 'ep', axis=0, tiled=False)]
    ppermute x2, waiting for transfers between devices: 0.15 us -> 2.95 us  [grp_sum_f32(): x = x + lax.ppermute(x, axis_name, partner)]
    convert_element_type x1, other arithmetic: 0.07 us -> 1.27 us  [body(): recv_cotan.astype(jnp.float32)]
    unnamed x34 -> x28, local copies, waits for them, and re-layouts: 2.8 us -> 1.81 us
  transfers between devices with their start and end apart: 22 -> 22, of which waited for: 9 -> 11; matrix products, arithmetic and copies ran while one was open for 18% -> 16% of each run, Pallas kernels for 0% -> 0%
where the time goes in v14:
time: 113 us; the launch traced here: 112 us
  waiting for transfers between devices  41.4 us (37%)
  starting transfers between devices  22.3 us (20%)
  matrix products  18.7 us (17%)
  between operations  14.6 us (13%)
  other arithmetic  9.49 us (8%)
  local copies, waits for them, and re-layouts  5.85 us (5%)
    all_to_all x1, waiting for transfers between devices, body(): lax.all_to_all(outgoing, 'ep', split_axis=0, concat_axis=0, tiled=True)  24.6 us
    all_to_all x1, starting transfers between devices, body(): lax.all_to_all(outgoing, 'ep', split_axis=0, concat_axis=0, tiled=True)  7.28 us
    ppermute x8, starting transfers between devices, grp_sum_doubling(): got = lax.ppermute(mine, axis_name, partner)  5.39 us
    ppermute x3, waiting for transfers between devices, grp_sum_rounded(): got = lax.ppermute(mine, axis_name, partner)  5.31 us
    ppermute x3, starting transfers between devices, grp_sum_rounded(): got = lax.ppermute(mine, axis_name, partner)  3.72 us
    all_to_all x1, starting transfers between devices, body(): lax.all_to_all(route_parts, 'ep', split_axis=0, concat_axis=0, tiled=True)  3.33 us
    all_gather x1, waiting for transfers between devices, body(): gathered = lax.all_gather(hot_outgoing, 'ep', axis=0, tiled=False)  3.21 us
    ppermute x2, waiting for transfers between devices, grp_sum_f32(): x = x + lax.ppermute(x, axis_name, partner)  2.95 us
  transfers between devices with their start and end apart: 22, of which 11 were waited for; matrix products, arithmetic and copies ran while one was open for 16% of the time, Pallas kernels for 0%

profile of v14, /device:TPU:0, one launch (start us, length us, event | category | flops | bytes accessed | tf_op | source)
XLA Modules:
  0.0 112.4 jit_solution(9774392145568576478)
XLA Ops:
  11.7 1.4 %convolution_convert_fusion.3 = bf16[160,1280]{1,0:T(8,128)(2,1)S(1)} fusion(pred[160,256]{1,0:T(32,128)(4,1)S(1)} %fusion.26, bf16[256,1280]{1,0:T(8,128)(2,1)} %param.12), kind=kOutput, calls=%fused_computation.7 | convolution fusion | flops 105062400 | bytes 1105920 | tf_op jit(solution)/shard_map/dot_general | solution.py:20
  14.2 0.9 pad_maximum_fusion
  15.2 7.3 %all-to-all-start = ((bf16[8,40,1280]{2,1,0:T(8,128)(2,1)}), bf16[8,40,1280]{2,1,0:T(8,128)(2,1)S(1)}, u32[]{:S(2)}, u32[]{:S(2)}) async-start(bf16[8,40,1280]{2,1,0:T(8,128)(2,1)} %pad_maximum_fusion), calls=%async_computation | async-start | bytes 1638400 | tf_op jit(solution)/shard_map/all_to_all | solution.py:159
  23.4 24.6 %all-to-all-done = bf16[8,40,1280]{2,1,0:T(8,128)(2,1)S(1)} async-done(((bf16[8,40,1280]{2,1,0:T(8,128)(2,1)}), bf16[8,40,1280]{2,1,0:T(8,128)(2,1)S(1)}, u32[]{:S(2)}, u32[]{:S(2)}) %all-to-all-start) | async-done | bytes 819232 | tf_op jit(solution)/shard_map/all_to_all | solution.py:159
  49.1 1.3 %slice_convert_fusion = (f32[8,16,1280]{2,1,0:T(8,128)S(1)}, bf16[8,16,1280]{2,1,0:T(8,128)(2,1)S(1)}) fusion(bf16[8,40,1280]{2,1,0:T(8,128)(2,1)} %copy-done.1), kind=kLoop, calls=%fused_computation.38 | loop fusion | flops 163840 | bytes 1638400 | tf_op jit(solution)/shard_map/convert_element_type | solution.py:164
  52.0 1.6 %collective-permute-start.1 = (bf16[64,768]{1,0:T(8,128)(2,1)S(1)}, bf16[64,768]{1,0:T(8,128)(2,1)S(1)}, u32[]{:S(2)}, u32[]{:S(2)}) collective-permute-start(bf16[64,768]{1,0:T(8,128)(2,1)S(1)} %add_convert_fusion.2), channel_id=1, source_target_pairs={{0,16},{8,24},{16,0},{24,8},{1,17},{9,25},{17,1},{25,9},{2,18},{10... | collective-permute-start | bytes 294920 | tf_op jit(solution)/shard_map/ppermute | solution.py:92
  54.3 1.6 %collective-permute-start.4 = (bf16[64,768]{1,0:T(8,128)(2,1)S(1)}, bf16[64,768]{1,0:T(8,128)(2,1)S(1)}, u32[]{:S(2)}, u32[]{:S(2)}) collective-permute-start(bf16[64,768]{1,0:T(8,128)(2,1)S(1)} %add_convert_fusion.1), channel_id=1, source_target_pairs={{0,16},{8,24},{16,0},{24,8},{1,17},{9,25},{17,1},{25,9},{2,18},{10... | collective-permute-start | bytes 294920 | tf_op jit(solution)/shard_map/ppermute | solution.py:92
  55.8 1.9 %collective-permute-done.1 = bf16[64,768]{1,0:T(8,128)(2,1)S(1)} collective-permute-done((bf16[64,768]{1,0:T(8,128)(2,1)S(1)}, bf16[64,768]{1,0:T(8,128)(2,1)S(1)}, u32[]{:S(2)}, u32[]{:S(2)}) %collective-permute-start.1) | collective-permute-done | bytes 98336 | tf_op jit(solution)/shard_map/ppermute | solution.py:92
  57.8 2.0 %collective-permute-done.7 = bf16[64,768]{1,0:T(8,128)(2,1)S(1)} collective-permute-done((bf16[64,768]{1,0:T(8,128)(2,1)S(1)}, bf16[64,768]{1,0:T(8,128)(2,1)S(1)}, u32[]{:S(2)}, u32[]{:S(2)}) %collective-permute-start.7) | collective-permute-done | bytes 98336 | tf_op jit(solution)/shard_map/ppermute | solution.py:92
  59.9 1.4 %collective-permute-done.4 = bf16[64,768]{1,0:T(8,128)(2,1)S(1)} collective-permute-done((bf16[64,768]{1,0:T(8,128)(2,1)S(1)}, bf16[64,768]{1,0:T(8,128)(2,1)S(1)}, u32[]{:S(2)}, u32[]{:S(2)}) %collective-permute-start.4) | collective-permute-done | bytes 98336 | tf_op jit(solution)/shard_map/ppermute | solution.py:92
  61.6 1.3 %collective-permute-done.5 = f32[64,768]{1,0:T(8,128)S(1)} collective-permute-done((f32[64,768]{1,0:T(8,128)S(1)}, f32[64,768]{1,0:T(8,128)S(1)}, u32[]{:S(2)}, u32[]{:S(2)}) %collective-permute-start.5) | collective-permute-done | bytes 196640 | tf_op jit(solution)/shard_map/ppermute | solution.py:95
  62.9 1.0 multiply_convert_fusion.4
  64.7 0.9 collective-permute-done.15
  65.7 1.5 %collective-permute-start.16 = (f32[8,1,16]{2,0,1:T(8,128)S(1)}, f32[8,1,16]{2,0,1:T(8,128)S(1)}, u32[]{:S(2)}, u32[]{:S(2)}) collective-permute-start(f32[8,1,16]{2,0,1:T(8,128)S(1)} %add.91), channel_id=1, source_target_pairs={{0,16},{8,24},{16,0},{24,8},{1,17},{9,25},{17,1},{25,9},{2,18},{10... | collective-permute-start | bytes 1544 | tf_op jit(solution)/shard_map/ppermute | solution.py:53
  67.3 2.0 %collective-permute-done.16 = f32[8,1,16]{2,0,1:T(8,128)S(1)} collective-permute-done((f32[8,1,16]{2,0,1:T(8,128)S(1)}, f32[8,1,16]{2,0,1:T(8,128)S(1)}, u32[]{:S(2)}, u32[]{:S(2)}) %collective-permute-start.16) | collective-permute-done | bytes 544 | tf_op jit(solution)/shard_map/ppermute | solution.py:53
  69.3 3.2 %all-gather.3.cloned.1.call-done = bf16[576,1280]{1,0:T(8,128)(2,1)} async-done(((bf16[72,1280]{1,0:T(8,128)(2,1)}), bf16[576,1280]{1,0:T(8,128)(2,1)}) %all-gather.3.cloned.1.call-update) | async-done | bytes 1474576 | tf_op jit(solution)/shard_map/all_gather | solution.py:144
  72.5 0.9 slice_bitcast_fusion
  73.4 1.4 %slice.94 = bf16[8,64,1280]{2,1,0:T(8,128)(2,1)S(1)} slice(bf16[8,72,1280]{2,1,0:T(8,128)(2,1)} %bitcast.106), slice={[0:8], [0:64], [0:1280]} | slice | bytes 2621440 | tf_op jit(solution)/shard_map/slice | solution.py:174
  75.0 0.9 fusion.36
  76.1 1.7 %convolution_convert_fusion.5 = bf16[2,128,96]{1,2,0:T(8,128)(2,1)S(1)} fusion(bf16[2,128,1280]{2,1,0:T(8,128)(2,1)} %bitcast.99, bf16[2,96,1280]{2,1,0:T(8,128)(2,1)} %param.21), kind=kOutput, calls=%fused_computation.22 | convolution fusion | flops 62939136 | bytes 1196032 | tf_op jit(solution)/shard_map/jrd,jhd->jrh/dot_general | solution.py:192
  77.8 1.7 %convolution_convert_fusion.7 = bf16[2,128,96]{1,2,0:T(8,128)(2,1)S(1)} fusion(bf16[2,96,1280]{2,1,0:T(8,128)(2,1)} %param.21, bf16[2,128,1280]{2,1,0:T(8,128)(2,1)} %bitcast.100, f32[2,128]{1,0:T(2,128)S(1)} %reshape.137), kind=kOutput, calls=%fused_computation.24 | convolution fusion | flops 63922176 | bytes 1197056 | tf_op jit(solution)/shard_map/jrd,jhd->jrh/dot_general | solution.py:189
  81.3 2.0 %fusion = bf16[1,1280,768]{2,1,0:T(8,128)(2,1)} fusion(bf16[128,1280]{1,0:T(8,128)(2,1)S(1)} %bitcast.97, bf16[128,768]{1,0:T(8,128)(2,1)S(1)} %copy-done.6), kind=kOutput, calls=%fused_computation.3 | convolution fusion | flops 252641280 | bytes 2490368 | tf_op jit(solution)/shard_map/dot_general | solution.py:209
  83.3 2.0 %fusion.1 = bf16[1,1280,768]{2,1,0:T(8,128)(2,1)} fusion(bf16[128,1280]{1,0:T(8,128)(2,1)S(1)} %bitcast.98, bf16[128,768]{1,0:T(8,128)(2,1)S(1)} %copy-done.5), kind=kOutput, calls=%fused_computation.4 | convolution fusion | flops 252641280 | bytes 2490368 | tf_op jit(solution)/shard_map/dot_general | solution.py:212
  85.3 2.0 %fusion.2 = bf16[1,768,1280]{2,1,0:T(8,128)(2,1)} fusion(bf16[128,768]{1,0:T(8,128)(2,1)S(1)} %get-tuple-element.16, bf16[128,1280]{1,0:T(8,128)(2,1)S(1)} %fusion.22), kind=kOutput, calls=%fused_computation.5 | convolution fusion | flops 252641280 | bytes 2490368 | tf_op jit(solution)/shard_map/dot_general | solution.py:215
  87.2 1.5 %collective-permute-start.12 = (bf16[2,128,96]{1,2,0:T(8,128)(2,1)S(1)}, bf16[2,128,96]{1,2,0:T(8,128)(2,1)S(1)}, u32[]{:S(2)}, u32[]{:S(2)}) collective-permute-start(bf16[2,128,96]{1,2,0:T(8,128)(2,1)S(1)} %add_convert_fusion.5), channel_id=1, source_target_pairs={{0,16},{8,24},{16,0},{24,8},{1,17},{9,25},{17,1},{25,9},{2,18},{10... | collective-permute-start | bytes 147464 | tf_op jit(solution)/shard_map/ppermute | solution.py:67
  89.4 1.5 %collective-permute-start.14 = (bf16[2,128,96]{1,2,0:T(8,128)(2,1)S(1)}, bf16[2,128,96]{1,2,0:T(8,128)(2,1)S(1)}, u32[]{:S(2)}, u32[]{:S(2)}) collective-permute-start(bf16[2,128,96]{1,2,0:T(8,128)(2,1)S(1)} %add_convert_fusion.4), channel_id=1, source_target_pairs={{0,16},{8,24},{16,0},{24,8},{1,17},{9,25},{17,1},{25,9},{2,18},{10... | collective-permute-start | bytes 147464 | tf_op jit(solution)/shard_map/ppermute | solution.py:67
  91.6 1.5 %collective-permute-done.18 = bf16[2,128,96]{1,2,0:T(8,128)(2,1)S(1)} collective-permute-done((bf16[2,128,96]{1,2,0:T(8,128)(2,1)S(1)}, bf16[2,128,96]{1,2,0:T(8,128)(2,1)S(1)}, u32[]{:S(2)}, u32[]{:S(2)}) %collective-permute-start.18) | collective-permute-done | bytes 49184 | tf_op jit(solution)/shard_map/ppermute | solution.py:67
  94.8 3.3 %all-to-all-start.1 = ((f32[8,3,16]{2,1,0:T(4,128)}), f32[8,3,16]{2,1,0:T(4,128)S(1)}, u32[]{:S(2)}, u32[]{:S(2)}) async-start(f32[8,3,16]{2,1,0:T(4,128)} %copy.45), calls=%async_computation.1 | async-start | bytes 32768 | tf_op jit(solution)/shard_map/all_to_all | solution.py:234
  98.2 1.2 %fusion.30 = f32[2,1280,96]{1,2,0:T(8,128)} fusion(bf16[2,128,1280]{2,1,0:T(8,128)(2,1)S(1)} %bitcast.93, bf16[2,128,96]{1,2,0:T(8,128)(2,1)S(1)} %collective-permute-done.10, bf16[2,128,96]{1,2,0:T(8,128)(2,1)S(1)} %add_convert_fusion.6, bf16[2,128,96]{1,2,0:T(8,128)(2,1)S(1)} %collective-permute-done.12, bf16[2,128,96]{1,2,0:T(8,128)(2,1)S(1)} %add_convert_fusion.5, ...), kind=kOutput, calls=%fused_computation.81 | convolution fusion | flops 63381504 | bytes 1933312 | tf_op jit(solution)/shard_map/jrd,jrh->jdh/dot_general | solution.py:220
  99.4 1.2 %fusion.31 = f32[2,1280,96]{1,2,0:T(8,128)} fusion(bf16[2,128,1280]{2,1,0:T(8,128)(2,1)S(1)} %bitcast.94, bf16[2,128,96]{1,2,0:T(8,128)(2,1)S(1)} %collective-permute-done.10, bf16[2,128,96]{1,2,0:T(8,128)(2,1)S(1)} %add_convert_fusion.6, bf16[2,128,96]{1,2,0:T(8,128)(2,1)S(1)} %collective-permute-done.14, bf16[2,128,96]{1,2,0:T(8,128)(2,1)S(1)} %add_convert_fusion.4), kind=kOutput, calls=%fused_computation.82 | convolution fusion | flops 63209472 | bytes 1835008 | tf_op jit(solution)/shard_map/jrd,jrh->jdh/dot_general | solution.py:223
  100.7 2.4 %fusion.23 = f32[2,96,1280]{2,1,0:T(8,128)} fusion(bf16[2,128,96]{1,2,0:T(8,128)(2,1)S(1)} %get-tuple-element.20, bf16[2,128,1280]{2,1,0:T(8,128)(2,1)} %bitcast.101, f32[2,128]{1,0:T(2,128)S(1)} %reshape.137), kind=kOutput, calls=%fused_computation.29 | convolution fusion | flops 63897600 | bytes 1688576 | tf_op jit(solution)/shard_map/jrh,jrd->jhd/dot_general | solution.py:224
  103.0 1.6 %all-to-all-done.1 = f32[8,3,16]{2,1,0:T(4,128)S(1)} async-done(((f32[8,3,16]{2,1,0:T(4,128)}), f32[8,3,16]{2,1,0:T(4,128)S(1)}, u32[]{:S(2)}, u32[]{:S(2)}) %all-to-all-start.1) | async-done | bytes 1568 | tf_op jit(solution)/shard_map/all_to_all | solution.py:234
  (130 shorter events, 17.1 us)
Async XLA Ops:
  7.2 41.0 %copy-start = (bf16[1,768,1280]{2,1,0:T(8,128)(2,1)S(1)}, bf16[1,768,1280]{2,1,0:T(8,128)(2,1)}, u32[]{:S(2)}) copy-start(bf16[1,768,1280]{2,1,0:T(8,128)(2,1)} %param.18) | copy-start | bytes 5898244
  7.2 5.9 %copy-start.7 = (bf16[256,1280]{1,0:T(8,128)(2,1)S(1)}, bf16[256,1280]{1,0:T(8,128)(2,1)}, u32[]{:S(2)}) copy-start(bf16[256,1280]{1,0:T(8,128)(2,1)} %param.11) | copy-start | bytes 1966084
  14.2 8.5 %slice-start = ((bf16[160,1280]{1,0:T(8,128)(2,1)}), bf16[32,1280]{1,0:T(8,128)(2,1)S(1)}, s32[]{:S(2)}) async-start(bf16[160,1280]{1,0:T(8,128)(2,1)} %copy-done.4), calls=%async_computation.3 | async-start | bytes 163840 | tf_op jit(solution)/shard_map/slice | solution.py:128
  15.2 32.8 %all-to-all-start = ((bf16[8,40,1280]{2,1,0:T(8,128)(2,1)}), bf16[8,40,1280]{2,1,0:T(8,128)(2,1)S(1)}, u32[]{:S(2)}, u32[]{:S(2)}) async-start(bf16[8,40,1280]{2,1,0:T(8,128)(2,1)} %pad_maximum_fusion), calls=%async_computation | async-start | bytes 1638400 | tf_op jit(solution)/shard_map/all_to_all | solution.py:159
  22.4 50.1 %all-gather.3.cloned.1.call-start = ((), (), s32[]{:S(2)}) async-start(), calls=%async_computation.2 | async-start | bytes 1658880 | tf_op jit(solution)/shard_map/all_gather | solution.py:144
  48.2 2.2 %copy-start.2 = (bf16[1,1280,768]{2,1,0:T(8,128)(2,1)S(1)}, bf16[1,1280,768]{2,1,0:T(8,128)(2,1)}, u32[]{:S(2)}) copy-start(bf16[1,1280,768]{2,1,0:T(8,128)(2,1)} %param.16) | copy-start | bytes 5898244
  49.0 2.3 %copy-start.3 = (bf16[1,1280,768]{2,1,0:T(8,128)(2,1)S(1)}, bf16[1,1280,768]{2,1,0:T(8,128)(2,1)}, u32[]{:S(2)}) copy-start(bf16[1,1280,768]{2,1,0:T(8,128)(2,1)} %param.17) | copy-start | bytes 5898244
  49.0 3.0 %collective-permute-start = (bf16[64,768]{1,0:T(8,128)(2,1)S(1)}, bf16[64,768]{1,0:T(8,128)(2,1)S(1)}, u32[]{:S(2)}, u32[]{:S(2)}) collective-permute-start(bf16[64,768]{1,0:T(8,128)(2,1)S(1)} %broadcast_select_fusion.8), channel_id=1, source_target_pairs={{0,8},{8,0},{16,24},{24,16},{1,9},{9,1},{17,25},{25,17},{2,10},{10... | collective-permute-start | bytes 294920 | tf_op jit(solution)/shard_map/ppermute | solution.py:86
  50.9 2.7 %collective-permute-start.6 = (bf16[64,768]{1,0:T(8,128)(2,1)S(1)}, bf16[64,768]{1,0:T(8,128)(2,1)S(1)}, u32[]{:S(2)}, u32[]{:S(2)}) collective-permute-start(bf16[64,768]{1,0:T(8,128)(2,1)S(1)} %broadcast_select_fusion.2), channel_id=1, source_target_pairs={{0,8},{8,0},{16,24},{24,16},{1,9},{9,1},{17,25},{25,17},{2,10},{10... | collective-permute-start | bytes 294920 | tf_op jit(solution)/shard_map/ppermute | solution.py:86
  51.8 2.5 %collective-permute-start.3 = (bf16[64,768]{1,0:T(8,128)(2,1)S(1)}, bf16[64,768]{1,0:T(8,128)(2,1)S(1)}, u32[]{:S(2)}, u32[]{:S(2)}) collective-permute-start(bf16[64,768]{1,0:T(8,128)(2,1)S(1)} %broadcast_select_fusion.5), channel_id=1, source_target_pairs={{0,8},{8,0},{16,24},{24,16},{1,9},{9,1},{17,25},{25,17},{2,10},{10... | collective-permute-start | bytes 294920 | tf_op jit(solution)/shard_map/ppermute | solution.py:86
  52.0 5.7 %collective-permute-start.1 = (bf16[64,768]{1,0:T(8,128)(2,1)S(1)}, bf16[64,768]{1,0:T(8,128)(2,1)S(1)}, u32[]{:S(2)}, u32[]{:S(2)}) collective-permute-start(bf16[64,768]{1,0:T(8,128)(2,1)S(1)} %add_convert_fusion.2), channel_id=1, source_target_pairs={{0,16},{8,24},{16,0},{24,8},{1,17},{9,25},{17,1},{25,9},{2,18},{10... | collective-permute-start | bytes 294920 | tf_op jit(solution)/shard_map/ppermute | solution.py:92
  53.6 6.2 %collective-permute-start.7 = (bf16[64,768]{1,0:T(8,128)(2,1)S(1)}, bf16[64,768]{1,0:T(8,128)(2,1)S(1)}, u32[]{:S(2)}, u32[]{:S(2)}) collective-permute-start(bf16[64,768]{1,0:T(8,128)(2,1)S(1)} %add_convert_fusion), channel_id=1, source_target_pairs={{0,16},{8,24},{16,0},{24,8},{1,17},{9,25},{17,1},{25,9},{2,18},{10... | collective-permute-start | bytes 294920 | tf_op jit(solution)/shard_map/ppermute | solution.py:92
  54.3 7.1 %collective-permute-start.4 = (bf16[64,768]{1,0:T(8,128)(2,1)S(1)}, bf16[64,768]{1,0:T(8,128)(2,1)S(1)}, u32[]{:S(2)}, u32[]{:S(2)}) collective-permute-start(bf16[64,768]{1,0:T(8,128)(2,1)S(1)} %add_convert_fusion.1), channel_id=1, source_target_pairs={{0,16},{8,24},{16,0},{24,8},{1,17},{9,25},{17,1},{25,9},{2,18},{10... | collective-permute-start | bytes 294920 | tf_op jit(solution)/shard_map/ppermute | solution.py:92
  57.7 3.7 %collective-permute-start.2 = (f32[64,768]{1,0:T(8,128)S(1)}, f32[64,768]{1,0:T(8,128)S(1)}, u32[]{:S(2)}, u32[]{:S(2)}) collective-permute-start(f32[64,768]{1,0:T(8,128)S(1)} %convert_add_fusion.2), channel_id=1, source_target_pairs={{0,8},{8,0},{16,24},{24,16},{1,9},{9,1},{17,25},{25,17},{2,10},{10... | collective-permute-start | bytes 589832 | tf_op jit(solution)/shard_map/ppermute | solution.py:95
  59.9 1.7 %collective-permute-start.8 = (f32[64,768]{1,0:T(8,128)S(1)}, f32[64,768]{1,0:T(8,128)S(1)}, u32[]{:S(2)}, u32[]{:S(2)}) collective-permute-start(f32[64,768]{1,0:T(8,128)S(1)} %convert_add_fusion), channel_id=1, source_target_pairs={{0,8},{8,0},{16,24},{24,16},{1,9},{9,1},{17,25},{25,17},{2,10},{10... | collective-permute-start | bytes 589832 | tf_op jit(solution)/shard_map/ppermute | solution.py:95
  61.4 1.5 %collective-permute-start.5 = (f32[64,768]{1,0:T(8,128)S(1)}, f32[64,768]{1,0:T(8,128)S(1)}, u32[]{:S(2)}, u32[]{:S(2)}) collective-permute-start(f32[64,768]{1,0:T(8,128)S(1)} %convert_add_fusion.1), channel_id=1, source_target_pairs={{0,8},{8,0},{16,24},{24,16},{1,9},{9,1},{17,25},{25,17},{2,10},{10... | collective-permute-start | bytes 589832 | tf_op jit(solution)/shard_map/ppermute | solution.py:95
  64.5 1.2 %collective-permute-start.15 = (f32[8,1,16]{2,0,1:T(8,128)S(1)}, f32[8,1,16]{2,0,1:T(8,128)S(1)}, u32[]{:S(2)}, u32[]{:S(2)}) collective-permute-start(f32[8,1,16]{2,0,1:T(8,128)S(1)} %reshape.132), channel_id=1, source_target_pairs={{0,8},{8,0},{16,24},{24,16},{1,9},{9,1},{17,25},{25,17},{2,10},{10... | collective-permute-start | bytes 1544 | tf_op jit(solution)/shard_map/ppermute | solution.py:53
  65.7 3.6 %collective-permute-start.16 = (f32[8,1,16]{2,0,1:T(8,128)S(1)}, f32[8,1,16]{2,0,1:T(8,128)S(1)}, u32[]{:S(2)}, u32[]{:S(2)}) collective-permute-start(f32[8,1,16]{2,0,1:T(8,128)S(1)} %add.91), channel_id=1, source_target_pairs={{0,16},{8,24},{16,0},{24,8},{1,17},{9,25},{17,1},{25,9},{2,18},{10... | collective-permute-start | bytes 1544 | tf_op jit(solution)/shard_map/ppermute | solution.py:53
  76.1 3.4 %copy-start.8 = (bf16[2,1280,96]{1,2,0:T(8,128)(2,1)S(1)}, bf16[2,1280,96]{1,2,0:T(8,128)(2,1)}, u32[]{:S(2)}) copy-start(bf16[2,1280,96]{1,2,0:T(8,128)(2,1)} %param.20) | copy-start | bytes 1474564
  76.1 3.7 %copy-start.9 = (bf16[2,1280,96]{1,2,0:T(8,128)(2,1)S(1)}, bf16[2,1280,96]{1,2,0:T(8,128)(2,1)}, u32[]{:S(2)}) copy-start(bf16[2,1280,96]{1,2,0:T(8,128)(2,1)} %param.19) | copy-start | bytes 1474564
  77.8 3.5 %copy-start.6 = (bf16[128,768]{1,0:T(8,128)(2,1)S(1)}, bf16[128,768]{1,0:T(8,128)(2,1)}, u32[]{:S(2)}) copy-start(bf16[128,768]{1,0:T(8,128)(2,1)} %get-tuple-element.14) | copy-start | bytes 589828
  79.8 3.4 %copy-start.5 = (bf16[128,768]{1,0:T(8,128)(2,1)S(1)}, bf16[128,768]{1,0:T(8,128)(2,1)}, u32[]{:S(2)}) copy-start(bf16[128,768]{1,0:T(8,128)(2,1)} %get-tuple-element.15) | copy-start | bytes 589828
  80.2 7.0 %collective-permute-start.11 = (bf16[2,128,96]{1,2,0:T(8,128)(2,1)S(1)}, bf16[2,128,96]{1,2,0:T(8,128)(2,1)S(1)}, u32[]{:S(2)}, u32[]{:S(2)}) collective-permute-start(bf16[2,128,96]{1,2,0:T(8,128)(2,1)S(1)} %convolution_convert_fusion.6), channel_id=1, source_target_pairs={{0,8},{8,0},{16,24},{24,16},{1,9},{9,1},{17,25},{25,17},{2,10},{10... | collective-permute-start | bytes 147464 | tf_op jit(solution)/shard_map/ppermute | solution.py:67
  80.3 8.5 %collective-permute-start.17 = (bf16[2,128,96]{1,2,0:T(8,128)(2,1)S(1)}, bf16[2,128,96]{1,2,0:T(8,128)(2,1)S(1)}, u32[]{:S(2)}, u32[]{:S(2)}) collective-permute-start(bf16[2,128,96]{1,2,0:T(8,128)(2,1)S(1)} %convolution_convert_fusion.5), channel_id=1, source_target_pairs={{0,8},{8,0},{16,24},{24,16},{1,9},{9,1},{17,25},{25,17},{2,10},{10... | collective-permute-start | bytes 147464 | tf_op jit(solution)/shard_map/ppermute | solution.py:67
  80.8 10.2 %collective-permute-start.9 = (bf16[2,128,96]{1,2,0:T(8,128)(2,1)S(1)}, bf16[2,128,96]{1,2,0:T(8,128)(2,1)S(1)}, u32[]{:S(2)}, u32[]{:S(2)}) collective-permute-start(bf16[2,128,96]{1,2,0:T(8,128)(2,1)S(1)} %convolution_convert_fusion.7), channel_id=1, source_target_pairs={{0,8},{8,0},{16,24},{24,16},{1,9},{9,1},{17,25},{25,17},{2,10},{10... | collective-permute-start | bytes 147464 | tf_op jit(solution)/shard_map/ppermute | solution.py:67
  80.9 8.6 %collective-permute-start.13 = (bf16[2,128,96]{1,2,0:T(8,128)(2,1)S(1)}, bf16[2,128,96]{1,2,0:T(8,128)(2,1)S(1)}, u32[]{:S(2)}, u32[]{:S(2)}) collective-permute-start(bf16[2,128,96]{1,2,0:T(8,128)(2,1)S(1)} %fusion.37), channel_id=1, source_target_pairs={{0,8},{8,0},{16,24},{24,16},{1,9},{9,1},{17,25},{25,17},{2,10},{10... | collective-permute-start | bytes 147464 | tf_op jit(solution)/shard_map/ppermute | solution.py:67
  87.2 4.4 %collective-permute-start.12 = (bf16[2,128,96]{1,2,0:T(8,128)(2,1)S(1)}, bf16[2,128,96]{1,2,0:T(8,128)(2,1)S(1)}, u32[]{:S(2)}, u32[]{:S(2)}) collective-permute-start(bf16[2,128,96]{1,2,0:T(8,128)(2,1)S(1)} %add_convert_fusion.5), channel_id=1, source_target_pairs={{0,16},{8,24},{16,0},{24,8},{1,17},{9,25},{17,1},{25,9},{2,18},{10... | collective-permute-start | bytes 147464 | tf_op jit(solution)/shard_map/ppermute | solution.py:67
  88.8 4.3 %collective-permute-start.18 = (bf16[2,128,96]{1,2,0:T(8,128)(2,1)S(1)}, bf16[2,128,96]{1,2,0:T(8,128)(2,1)S(1)}, u32[]{:S(2)}, u32[]{:S(2)}) collective-permute-start(bf16[2,128,96]{1,2,0:T(8,128)(2,1)S(1)} %add_convert_fusion.3), channel_id=1, source_target_pairs={{0,16},{8,24},{16,0},{24,8},{1,17},{9,25},{17,1},{25,9},{2,18},{10... | collective-permute-start | bytes 147464 | tf_op jit(solution)/shard_map/ppermute | solution.py:67
  89.4 4.6 %collective-permute-start.14 = (bf16[2,128,96]{1,2,0:T(8,128)(2,1)S(1)}, bf16[2,128,96]{1,2,0:T(8,128)(2,1)S(1)}, u32[]{:S(2)}, u32[]{:S(2)}) collective-permute-start(bf16[2,128,96]{1,2,0:T(8,128)(2,1)S(1)} %add_convert_fusion.4), channel_id=1, source_target_pairs={{0,16},{8,24},{16,0},{24,8},{1,17},{9,25},{17,1},{25,9},{2,18},{10... | collective-permute-start | bytes 147464 | tf_op jit(solution)/shard_map/ppermute | solution.py:67
  91.0 7.2 %collective-permute-start.10 = (bf16[2,128,96]{1,2,0:T(8,128)(2,1)S(1)}, bf16[2,128,96]{1,2,0:T(8,128)(2,1)S(1)}, u32[]{:S(2)}, u32[]{:S(2)}) collective-permute-start(bf16[2,128,96]{1,2,0:T(8,128)(2,1)S(1)} %add_convert_fusion.6), channel_id=1, source_target_pairs={{0,16},{8,24},{16,0},{24,8},{1,17},{9,25},{17,1},{25,9},{2,18},{10... | collective-permute-start | bytes 147464 | tf_op jit(solution)/shard_map/ppermute | solution.py:67
  94.8 9.9 %all-to-all-start.1 = ((f32[8,3,16]{2,1,0:T(4,128)}), f32[8,3,16]{2,1,0:T(4,128)S(1)}, u32[]{:S(2)}, u32[]{:S(2)}) async-start(f32[8,3,16]{2,1,0:T(4,128)} %copy.45), calls=%async_computation.1 | async-start | bytes 32768 | tf_op jit(solution)/shard_map/all_to_all | solution.py:234
  99.4 5.4 %copy-start.10 = (s32[256,6]{0,1:T(8,128)S(1)}, s32[256,6]{0,1:T(8,128)}, u32[]{:S(2)}) copy-start(s32[256,6]{0,1:T(8,128)} %param.14) | copy-start | bytes 18436
  (2 other events, 1.8 us)
Sparse Core Ops, SparseCore 0:
  26.0 46.4 all-gather.2

commit v15 on v13

--- a/solution.py
+++ b/solution.py
@@ -141,7 +141,7 @@
         scale_lines, slice_width
     )
     hot_outgoing = jnp.concatenate([hot_feats, hot_cotan, scale_block], axis=0)
-    gathered = lax.all_gather(hot_outgoing, "ep", axis=0, tiled=False)
+    gathered = lax.all_gather(hot_outgoing, "ep", axis=1, tiled=False)
     cold_lines = -(-capacity // slice_width)
     cold_lines = -(-cold_lines // 8) * 8
     cold_scale_block = jnp.pad(
@@ -171,13 +171,10 @@
     part_hidden = lax.dot_general(
         weighted, w_down, (((1,), (1,)), ((), ())), preferred_element_type=jnp.float32
     )
-    all_rows = gathered[:, : 2 * hot_rows].reshape(blocks, 2, hot_count, capacity, slice_width)
-    all_rows = jnp.transpose(all_rows, (1, 2, 0, 3, 4)).reshape(
-        2, hot_count, blocks * capacity, slice_width
-    )
-    all_scale = gathered[:, 2 * hot_rows :].reshape(blocks, -1)[:, :hot_rows]
-    all_scale = jnp.transpose(all_scale.reshape(blocks, hot_count, capacity), (1, 0, 2))
-    rows_feat, rows_cot = all_rows[0], all_rows[1]
+    rows_feat = gathered[:hot_rows].reshape(hot_count, capacity * blocks, slice_width)
+    rows_cot = gathered[hot_rows : 2 * hot_rows].reshape(hot_count, capacity * blocks, slice_width)
+    all_scale = jnp.transpose(gathered[2 * hot_rows :], (1, 0, 2)).reshape(blocks, -1)[:, :hot_rows]
+    all_scale = jnp.transpose(all_scale.reshape(blocks, hot_count, capacity), (1, 2, 0))
     rows_wt = (
         all_scale.reshape(hot_count, blocks * capacity, 1).astype(jnp.float32)
         * rows_cot.astype(jnp.float32)
@@ -224,7 +221,7 @@
     route_parts = jnp.concatenate(
         [
             cold_route,
-            jnp.transpose(hot_route_part.reshape(hot_count, blocks, capacity), (1, 0, 2)),
+            jnp.transpose(hot_route_part.reshape(hot_count, capacity, blocks), (2, 0, 1)),
         ],
         axis=1,
     )

time: 110 us -> 122 us (1.11)
  local copies, waits for them, and re-layouts: 7.37 us -> 12.8 us
  matrix products: 18.8 us -> 22.7 us
  other arithmetic: 11 us -> 14.8 us
    reshape x2 -> x4, local copies, waits for them, and re-layouts: 0.86 us -> 5.08 us  [the longest x1 1.98 us: body(): jnp.transpose(gathered[2 * hot_rows:], (1, 0, 2)).reshape(blocks, -1)]
    convert_element_type x4, other arithmetic: 0.07 us -> 2.51 us  [grp_sum_doubling(): mine = [s.astype(jnp.bfloat16) for s in sums]]
    dot_general x1, matrix products: 0.34 us -> 2 us  [body(): jnp.einsum('jrd,jdh->jrh', rows_feat, up_hot, preferred_element_type=jnp....]
    slice x3 -> x5, local copies, waits for them, and re-layouts: 1.68 us -> 3.09 us  [the longest x1 2.21 us: body(): gathered[hot_rows:2 * hot_rows]]
    concatenate x1, other arithmetic: 0.01 us -> 1.33 us  [body(): jnp.concatenate([cold_route, jnp.transpose(hot_route_part.reshape(hot_cou...]
    unnamed x34 -> x22, local copies, waits for them, and re-layouts: 2.8 us -> 1.82 us
  transfers between devices with their start and end apart: 22 -> 22, of which waited for: 9 -> 8; matrix products, arithmetic and copies ran while one was open for 18% -> 29% of each run, Pallas kernels for 0% -> 0%
where the time goes in v15:
time: 122 us; the launch traced here: 121 us
  waiting for transfers between devices  33.3 us (27%)
  starting transfers between devices  22.9 us (19%)
  matrix products  22.7 us (19%)
  other arithmetic  14.8 us (12%)
  between operations  14.5 us (12%)
  local copies, waits for them, and re-layouts  12.8 us (10%)
    all_to_all x1, waiting for transfers between devices, body(): lax.all_to_all(outgoing, 'ep', split_axis=0, concat_axis=0, tiled=True)  24.4 us
    all_to_all x1, starting transfers between devices, body(): lax.all_to_all(outgoing, 'ep', split_axis=0, concat_axis=0, tiled=True)  7.28 us
    ppermute x8, starting transfers between devices, grp_sum_doubling(): got = lax.ppermute(mine, axis_name, partner)  5.4 us
    ppermute x3, waiting for transfers between devices, grp_sum_rounded(): got = lax.ppermute(mine, axis_name, partner)  4.58 us
    ppermute x3, starting transfers between devices, grp_sum_rounded(): got = lax.ppermute(mine, axis_name, partner)  3.94 us
    all_to_all x1, starting transfers between devices, body(): lax.all_to_all(route_parts, 'ep', split_axis=0, concat_axis=0, tiled=True)  3.92 us
    convert_element_type x4, other arithmetic, grp_sum_doubling(): mine = [s.astype(jnp.bfloat16) for s in sums]  2.51 us
    ppermute x8, waiting for transfers between devices, grp_sum_doubling(): got = lax.ppermute(mine, axis_name, partner)  2.44 us
  transfers between devices with their start and end apart: 22, of which 8 were waited for; matrix products, arithmetic and copies ran while one was open for 29% of the time, Pallas kernels for 0%

profile of v15, /device:TPU:0, one launch (start us, length us, event | category | flops | bytes accessed | tf_op | source)
XLA Modules:
  0.0 121.0 jit_solution(3986950246152026121)
XLA Ops:
  11.7 1.4 %convolution_convert_fusion.3 = bf16[160,1280]{1,0:T(8,128)(2,1)S(1)} fusion(pred[160,256]{1,0:T(32,128)(4,1)S(1)} %fusion.27, bf16[256,1280]{1,0:T(8,128)(2,1)} %param.12), kind=kOutput, calls=%fused_computation.7 | convolution fusion | flops 105062400 | bytes 1105920 | tf_op jit(solution)/shard_map/dot_general | solution.py:20
  15.1 7.3 %all-to-all-start = ((bf16[8,40,1280]{2,1,0:T(8,128)(2,1)}), bf16[8,40,1280]{2,1,0:T(8,128)(2,1)S(1)}, u32[]{:S(2)}, u32[]{:S(2)}) async-start(bf16[8,40,1280]{2,1,0:T(8,128)(2,1)} %pad_maximum_fusion), calls=%async_computation | async-start | bytes 1638400 | tf_op jit(solution)/shard_map/all_to_all | solution.py:159
  23.4 24.4 %all-to-all-done = bf16[8,40,1280]{2,1,0:T(8,128)(2,1)S(1)} async-done(((bf16[8,40,1280]{2,1,0:T(8,128)(2,1)}), bf16[8,40,1280]{2,1,0:T(8,128)(2,1)S(1)}, u32[]{:S(2)}, u32[]{:S(2)}) %all-to-all-start) | async-done | bytes 819232 | tf_op jit(solution)/shard_map/all_to_all | solution.py:159
  52.1 1.8 %collective-permute-start.1 = (bf16[64,768]{1,0:T(8,128)(2,1)S(1)}, bf16[64,768]{1,0:T(8,128)(2,1)S(1)}, u32[]{:S(2)}, u32[]{:S(2)}) collective-permute-start(bf16[64,768]{1,0:T(8,128)(2,1)S(1)} %add_convert_fusion.2), channel_id=1, source_target_pairs={{0,16},{8,24},{16,0},{24,8},{1,17},{9,25},{17,1},{25,9},{2,18},{10... | collective-permute-start | bytes 294920 | tf_op jit(solution)/shard_map/ppermute | solution.py:92
  54.3 1.8 %collective-permute-start.4 = (bf16[64,768]{1,0:T(8,128)(2,1)S(1)}, bf16[64,768]{1,0:T(8,128)(2,1)S(1)}, u32[]{:S(2)}, u32[]{:S(2)}) collective-permute-start(bf16[64,768]{1,0:T(8,128)(2,1)S(1)} %add_convert_fusion.1), channel_id=1, source_target_pairs={{0,16},{8,24},{16,0},{24,8},{1,17},{9,25},{17,1},{25,9},{2,18},{10... | collective-permute-start | bytes 294920 | tf_op jit(solution)/shard_map/ppermute | solution.py:92
  56.1 1.6 %collective-permute-done.1 = bf16[64,768]{1,0:T(8,128)(2,1)S(1)} collective-permute-done((bf16[64,768]{1,0:T(8,128)(2,1)S(1)}, bf16[64,768]{1,0:T(8,128)(2,1)S(1)}, u32[]{:S(2)}, u32[]{:S(2)}) %collective-permute-start.1) | collective-permute-done | bytes 98336 | tf_op jit(solution)/shard_map/ppermute | solution.py:92
  58.4 1.4 %collective-permute-done.7 = bf16[64,768]{1,0:T(8,128)(2,1)S(1)} collective-permute-done((bf16[64,768]{1,0:T(8,128)(2,1)S(1)}, bf16[64,768]{1,0:T(8,128)(2,1)S(1)}, u32[]{:S(2)}, u32[]{:S(2)}) %collective-permute-start.7) | collective-permute-done | bytes 98336 | tf_op jit(solution)/shard_map/ppermute | solution.py:92
  59.9 1.6 %collective-permute-done.4 = bf16[64,768]{1,0:T(8,128)(2,1)S(1)} collective-permute-done((bf16[64,768]{1,0:T(8,128)(2,1)S(1)}, bf16[64,768]{1,0:T(8,128)(2,1)S(1)}, u32[]{:S(2)}, u32[]{:S(2)}) %collective-permute-start.4) | collective-permute-done | bytes 98336 | tf_op jit(solution)/shard_map/ppermute | solution.py:92
  61.7 1.4 %collective-permute-done.5 = f32[64,768]{1,0:T(8,128)S(1)} collective-permute-done((f32[64,768]{1,0:T(8,128)S(1)}, f32[64,768]{1,0:T(8,128)S(1)}, u32[]{:S(2)}, u32[]{:S(2)}) %collective-permute-start.5) | collective-permute-done | bytes 196640 | tf_op jit(solution)/shard_map/ppermute | solution.py:95
  63.9 1.0 broadcast_select_fusion.7
  64.9 2.0 %fusion = bf16[1,1280,768]{2,1,0:T(8,128)(2,1)} fusion(bf16[128,1280]{1,0:T(8,128)(2,1)S(1)} %bitcast.86, f32[64,768]{1,0:T(8,128)S(1)} %get-tuple-element.18, f32[64,768]{1,0:T(8,128)S(1)} %get-tuple-element.17, f32[64,768]{1,0:T(8,128)S(1)} %get-tuple-element.16, f32[64,768]{1,0:T(8,128)S(1)} %get-tuple-element.15, f32[64,768]{1,0:T(8,128)S(1)} %get-tuple-element.14, ...), kind=kOutput, calls=%fused_computation.3 | convolution fusion | flops 253919232 | bytes 3473408 | tf_op jit(solution)/shard_map/dot_general | solution.py:203
  66.9 2.0 %fusion.1 = bf16[1,1280,768]{2,1,0:T(8,128)(2,1)} fusion(bf16[128,1280]{1,0:T(8,128)(2,1)S(1)} %bitcast.87, f32[64,768]{1,0:T(8,128)S(1)} %get-tuple-element.14, f32[64,768]{1,0:T(8,128)S(1)} %get-tuple-element.13, f32[64,768]{1,0:T(8,128)S(1)} %get-tuple-element.18, f32[64,768]{1,0:T(8,128)S(1)} %get-tuple-element.17), kind=kOutput, calls=%fused_computation.4 | convolution fusion | flops 253427712 | bytes 3080192 | tf_op jit(solution)/shard_map/dot_general | solution.py:206
  68.9 1.7 %collective-permute-start.16 = (f32[8,1,16]{2,0,1:T(8,128)S(1)}, f32[8,1,16]{2,0,1:T(8,128)S(1)}, u32[]{:S(2)}, u32[]{:S(2)}) collective-permute-start(f32[8,1,16]{2,0,1:T(8,128)S(1)} %add.91), channel_id=1, source_target_pairs={{0,16},{8,24},{16,0},{24,8},{1,17},{9,25},{17,1},{25,9},{2,18},{10... | collective-permute-start | bytes 1544 | tf_op jit(solution)/shard_map/ppermute | solution.py:53
  70.7 2.0 %fusion.2 = bf16[1,768,1280]{2,1,0:T(8,128)(2,1)} fusion(bf16[128,768]{1,0:T(8,128)(2,1)S(1)} %multiply_convert_fusion.4, bf16[128,1280]{1,0:T(8,128)(2,1)S(1)} %copy-done.4), kind=kOutput, calls=%fused_computation.5 | convolution fusion | flops 252641280 | bytes 2490368 | tf_op jit(solution)/shard_map/dot_general | solution.py:209
  72.7 2.2 %fusion.41 = (bf16[32,10240]{1,0:T(8,128)(2,1)S(1)}, bf16[32,10240]{1,0:T(8,128)(2,1)}) fusion(bf16[72,10240]{1,0:T(8,128)(2,1)} %all-gather.3.cloned.1.call-done), kind=kLoop, calls=%fused_computation.98 | loop fusion | bytes 2621440 | tf_op jit(solution)/shard_map/slice | solution.py:175
  75.2 2.0 %convolution_convert_fusion.5 = bf16[2,128,96]{1,2,0:T(8,128)(2,1)} fusion(bf16[2,128,1280]{2,1,0:T(8,128)(2,1)S(1)} %reshape.130, bf16[2,96,1280]{2,1,0:T(8,128)(2,1)} %param.21), kind=kOutput, calls=%fused_computation.21 | convolution fusion | flops 62939136 | bytes 1196032 | tf_op jit(solution)/shard_map/jrd,jhd->jrh/dot_general | solution.py:189
  77.3 1.4 %reshape.128 = bf16[2,128,1280]{2,1,0:T(8,128)(2,1)S(1)} reshape(bf16[32,10240]{1,0:T(8,128)(2,1)} %get-tuple-element.10) | data formatting | bytes 1310720 | tf_op jit(solution)/shard_map/reshape | solution.py:174
  78.7 1.4 %convolution_convert_fusion.6 = bf16[2,128,96]{1,2,0:T(8,128)(2,1)S(1)} fusion(bf16[2,128,1280]{2,1,0:T(8,128)(2,1)S(1)} %reshape.128, bf16[2,1280,96]{1,2,0:T(8,128)(2,1)} %param.19), kind=kOutput, calls=%fused_computation.22 | convolution fusion | flops 62939136 | bytes 1196032 | tf_op jit(solution)/shard_map/jrd,jdh->jrh/dot_general | solution.py:182
  80.1 2.0 %convolution_convert_fusion.7 = bf16[2,128,96]{1,2,0:T(8,128)(2,1)} fusion(bf16[2,128,1280]{2,1,0:T(8,128)(2,1)S(1)} %reshape.128, bf16[2,1280,96]{1,2,0:T(8,128)(2,1)} %param.20), kind=kOutput, calls=%fused_computation.23 | convolution fusion | flops 62939136 | bytes 1196032 | tf_op jit(solution)/shard_map/jrd,jdh->jrh/dot_general | solution.py:185
  82.6 2.0 %copy.40 = bf16[8,8,1280]{0,2,1:T(8,128)(2,1)} copy(bf16[8,8,1280]{2,1,0:T(8,128)(2,1)S(1)} %bitcast.90) | data formatting | bytes 327680 | tf_op jit(solution)/shard_map/reshape | solution.py:176
  85.4 1.4 %convolution_convert_fusion.8 = bf16[2,128,96]{1,2,0:T(8,128)(2,1)S(1)} fusion(bf16[2,96,1280]{2,1,0:T(8,128)(2,1)} %param.21, bf16[2,128,1280]{2,1,0:T(8,128)(2,1)S(1)} %reshape.130, f32[2,128]{1,0:T(2,128)S(1)} %reshape.136), kind=kOutput, calls=%fused_computation.24 | convolution fusion | flops 63922176 | bytes 1197056 | tf_op jit(solution)/shard_map/jrd,jhd->jrh/dot_general | solution.py:186
  88.2 1.7 %collective-permute-start.18 = (bf16[2,128,96]{1,2,0:T(8,128)(2,1)S(1)}, bf16[2,128,96]{1,2,0:T(8,128)(2,1)S(1)}, u32[]{:S(2)}, u32[]{:S(2)}) collective-permute-start(bf16[2,128,96]{1,2,0:T(8,128)(2,1)S(1)} %add_convert_fusion.3), channel_id=1, source_target_pairs={{0,16},{8,24},{16,0},{24,8},{1,17},{9,25},{17,1},{25,9},{2,18},{10... | collective-permute-start | bytes 147464 | tf_op jit(solution)/shard_map/ppermute | solution.py:67
  92.0 1.7 %collective-permute-start.14 = (bf16[2,128,96]{1,2,0:T(8,128)(2,1)S(1)}, bf16[2,128,96]{1,2,0:T(8,128)(2,1)S(1)}, u32[]{:S(2)}, u32[]{:S(2)}) collective-permute-start(bf16[2,128,96]{1,2,0:T(8,128)(2,1)S(1)} %add_convert_fusion.4), channel_id=1, source_target_pairs={{0,16},{8,24},{16,0},{24,8},{1,17},{9,25},{17,1},{25,9},{2,18},{10... | collective-permute-start | bytes 147464 | tf_op jit(solution)/shard_map/ppermute | solution.py:67
  94.2 1.0 collective-permute-done.12
  95.2 1.4 %collective-permute-done.14 = bf16[2,128,96]{1,2,0:T(8,128)(2,1)S(1)} collective-permute-done((bf16[2,128,96]{1,2,0:T(8,128)(2,1)S(1)}, bf16[2,128,96]{1,2,0:T(8,128)(2,1)S(1)}, u32[]{:S(2)}, u32[]{:S(2)}) %collective-permute-start.14) | collective-permute-done | bytes 49184 | tf_op jit(solution)/shard_map/ppermute | solution.py:67
  97.3 1.4 %reshape.132 = f32[2,16,8]{2,1,0:T(8,128)} reshape(f32[2,128]{1,0:T(2,128)} %get-tuple-element.7) | data formatting | bytes 2048 | tf_op jit(solution)/shard_map/reshape | solution.py:224
  98.6 1.3 %pad_maximum_fusion.5 = f32[8,3,16]{0,2,1:T(8,128)} fusion(f32[8,2,16]{0,2,1:T(8,128)} %bitcast.102, f32[8,1,16]{0,2,1:T(8,128)S(1)} %copy.37), kind=kLoop, calls=%fused_computation.84 | loop fusion | flops 384 | bytes 3072 | tf_op jit(solution)/shard_map/concatenate | solution.py:221
  100.0 1.4 %copy.38 = f32[8,3,16]{2,1,0:T(4,128)} copy(f32[8,3,16]{0,2,1:T(8,128)} %pad_maximum_fusion.5) | data formatting | bytes 3072 | tf_op jit(solution)/shard_map/concatenate | solution.py:221
  101.4 3.9 %all-to-all-start.1 = ((f32[8,3,16]{2,1,0:T(4,128)}), f32[8,3,16]{2,1,0:T(4,128)}, u32[]{:S(2)}, u32[]{:S(2)}) async-start(f32[8,3,16]{2,1,0:T(4,128)} %copy.38), calls=%async_computation.1 | async-start | bytes 32768 | tf_op jit(solution)/shard_map/all_to_all | solution.py:228
  105.3 2.1 %fusion.31 = f32[2,1280,96]{1,2,0:T(8,128)} fusion(bf16[2,128,1280]{2,1,0:T(8,128)(2,1)S(1)} %reshape.128, bf16[2,128,96]{1,2,0:T(8,128)(2,1)} %collective-permute-done.10, bf16[2,128,96]{1,2,0:T(8,128)(2,1)S(1)} %add_convert_fusion.6, bf16[2,128,96]{1,2,0:T(8,128)(2,1)} %copy-done.6, bf16[2,128,96]{1,2,0:T(8,128)(2,1)S(1)} %add_convert_fusion.5, ...), kind=kOutput, calls=%fused_computation.81 | convolution fusion | flops 63381504 | bytes 1933312 | tf_op jit(solution)/shard_map/jrd,jrh->jdh/dot_general | solution.py:214
  107.4 2.0 %fusion.32 = f32[2,1280,96]{1,2,0:T(8,128)} fusion(bf16[2,128,1280]{2,1,0:T(8,128)(2,1)S(1)} %reshape.128, bf16[2,128,96]{1,2,0:T(8,128)(2,1)} %collective-permute-done.10, bf16[2,128,96]{1,2,0:T(8,128)(2,1)S(1)} %add_convert_fusion.6, bf16[2,128,96]{1,2,0:T(8,128)(2,1)S(1)} %collective-permute-done.14, bf16[2,128,96]{1,2,0:T(8,128)(2,1)S(1)} %add_convert_fusion.4), kind=kOutput, calls=%fused_computation.82 | convolution fusion | flops 63209472 | bytes 1835008 | tf_op jit(solution)/shard_map/jrd,jrh->jdh/dot_general | solution.py:217
  109.4 2.0 %fusion.23 = f32[2,96,1280]{2,1,0:T(8,128)} fusion(bf16[2,128,96]{1,2,0:T(8,128)(2,1)S(1)} %get-tuple-element.8, bf16[2,128,1280]{2,1,0:T(8,128)(2,1)S(1)} %reshape.130, f32[2,128]{1,0:T(2,128)} %copy-done.8), kind=kOutput, calls=%fused_computation.29 | convolution fusion | flops 63897600 | bytes 1688576 | tf_op jit(solution)/shard_map/jrh,jrd->jhd/dot_general | solution.py:218
  (127 shorter events, 23.0 us)
Async XLA Ops:
  7.2 40.9 %copy-start = (bf16[1,768,1280]{2,1,0:T(8,128)(2,1)S(1)}, bf16[1,768,1280]{2,1,0:T(8,128)(2,1)}, u32[]{:S(2)}) copy-start(bf16[1,768,1280]{2,1,0:T(8,128)(2,1)} %param.18) | copy-start | bytes 5898244
  11.3 1.8 %copy-start.5 = (bf16[256,1280]{1,0:T(8,128)(2,1)S(1)}, bf16[256,1280]{1,0:T(8,128)(2,1)}, u32[]{:S(2)}) copy-start(bf16[256,1280]{1,0:T(8,128)(2,1)} %param.11) | copy-start | bytes 1966084
  14.2 8.5 %slice-start = ((bf16[160,1280]{1,0:T(8,128)(2,1)}), bf16[32,1280]{1,0:T(8,128)(2,1)S(1)}, s32[]{:S(2)}) async-start(bf16[160,1280]{1,0:T(8,128)(2,1)} %copy-done.3), calls=%async_computation.3 | async-start | bytes 163840 | tf_op jit(solution)/shard_map/slice | solution.py:128
  15.1 32.6 %all-to-all-start = ((bf16[8,40,1280]{2,1,0:T(8,128)(2,1)}), bf16[8,40,1280]{2,1,0:T(8,128)(2,1)S(1)}, u32[]{:S(2)}, u32[]{:S(2)}) async-start(bf16[8,40,1280]{2,1,0:T(8,128)(2,1)} %pad_maximum_fusion), calls=%async_computation | async-start | bytes 1638400 | tf_op jit(solution)/shard_map/all_to_all | solution.py:159
  22.4 50.3 %all-gather.3.cloned.1.call-start = ((), (), s32[]{:S(2)}) async-start(), calls=%async_computation.2 | async-start | bytes 1658880 | tf_op jit(solution)/shard_map/all_gather | solution.py:144
  48.1 1.6 %copy-start.1 = (bf16[1,1280,768]{2,1,0:T(8,128)(2,1)S(1)}, bf16[1,1280,768]{2,1,0:T(8,128)(2,1)}, u32[]{:S(2)}) copy-start(bf16[1,1280,768]{2,1,0:T(8,128)(2,1)} %param.16) | copy-start | bytes 5898244
  48.9 1.7 %copy-start.2 = (bf16[1,1280,768]{2,1,0:T(8,128)(2,1)S(1)}, bf16[1,1280,768]{2,1,0:T(8,128)(2,1)}, u32[]{:S(2)}) copy-start(bf16[1,1280,768]{2,1,0:T(8,128)(2,1)} %param.17) | copy-start | bytes 5898244
  48.9 3.1 %collective-permute-start = (bf16[64,768]{1,0:T(8,128)(2,1)S(1)}, bf16[64,768]{1,0:T(8,128)(2,1)S(1)}, u32[]{:S(2)}, u32[]{:S(2)}) collective-permute-start(bf16[64,768]{1,0:T(8,128)(2,1)S(1)} %broadcast_select_fusion.8), channel_id=1, source_target_pairs={{0,8},{8,0},{16,24},{24,16},{1,9},{9,1},{17,25},{25,17},{2,10},{10... | collective-permute-start | bytes 294920 | tf_op jit(solution)/shard_map/ppermute | solution.py:86
  50.1 3.8 %collective-permute-start.6 = (bf16[64,768]{1,0:T(8,128)(2,1)S(1)}, bf16[64,768]{1,0:T(8,128)(2,1)S(1)}, u32[]{:S(2)}, u32[]{:S(2)}) collective-permute-start(bf16[64,768]{1,0:T(8,128)(2,1)S(1)} %broadcast_select_fusion.2), channel_id=1, source_target_pairs={{0,8},{8,0},{16,24},{24,16},{1,9},{9,1},{17,25},{25,17},{2,10},{10... | collective-permute-start | bytes 294920 | tf_op jit(solution)/shard_map/ppermute | solution.py:86
  51.0 3.2 %collective-permute-start.3 = (bf16[64,768]{1,0:T(8,128)(2,1)S(1)}, bf16[64,768]{1,0:T(8,128)(2,1)S(1)}, u32[]{:S(2)}, u32[]{:S(2)}) collective-permute-start(bf16[64,768]{1,0:T(8,128)(2,1)S(1)} %broadcast_select_fusion.5), channel_id=1, source_target_pairs={{0,8},{8,0},{16,24},{24,16},{1,9},{9,1},{17,25},{25,17},{2,10},{10... | collective-permute-start | bytes 294920 | tf_op jit(solution)/shard_map/ppermute | solution.py:86
  52.1 5.7 %collective-permute-start.1 = (bf16[64,768]{1,0:T(8,128)(2,1)S(1)}, bf16[64,768]{1,0:T(8,128)(2,1)S(1)}, u32[]{:S(2)}, u32[]{:S(2)}) collective-permute-start(bf16[64,768]{1,0:T(8,128)(2,1)S(1)} %add_convert_fusion.2), channel_id=1, source_target_pairs={{0,16},{8,24},{16,0},{24,8},{1,17},{9,25},{17,1},{25,9},{2,18},{10... | collective-permute-start | bytes 294920 | tf_op jit(solution)/shard_map/ppermute | solution.py:92
  53.9 5.9 %collective-permute-start.7 = (bf16[64,768]{1,0:T(8,128)(2,1)S(1)}, bf16[64,768]{1,0:T(8,128)(2,1)S(1)}, u32[]{:S(2)}, u32[]{:S(2)}) collective-permute-start(bf16[64,768]{1,0:T(8,128)(2,1)S(1)} %add_convert_fusion), channel_id=1, source_target_pairs={{0,16},{8,24},{16,0},{24,8},{1,17},{9,25},{17,1},{25,9},{2,18},{10... | collective-permute-start | bytes 294920 | tf_op jit(solution)/shard_map/ppermute | solution.py:92
  54.3 7.2 %collective-permute-start.4 = (bf16[64,768]{1,0:T(8,128)(2,1)S(1)}, bf16[64,768]{1,0:T(8,128)(2,1)S(1)}, u32[]{:S(2)}, u32[]{:S(2)}) collective-permute-start(bf16[64,768]{1,0:T(8,128)(2,1)S(1)} %add_convert_fusion.1), channel_id=1, source_target_pairs={{0,16},{8,24},{16,0},{24,8},{1,17},{9,25},{17,1},{25,9},{2,18},{10... | collective-permute-start | bytes 294920 | tf_op jit(solution)/shard_map/ppermute | solution.py:92
  58.4 5.5 %collective-permute-start.2 = (f32[64,768]{1,0:T(8,128)}, f32[64,768]{1,0:T(8,128)}, u32[]{:S(2)}, u32[]{:S(2)}) collective-permute-start(f32[64,768]{1,0:T(8,128)} %convert_add_fusion.2), channel_id=1, source_target_pairs={{0,8},{8,0},{16,24},{24,16},{1,9},{9,1},{17,25},{25,17},{2,10},{10... | collective-permute-start | bytes 589832 | tf_op jit(solution)/shard_map/ppermute | solution.py:95
  59.9 1.7 %collective-permute-start.8 = (f32[64,768]{1,0:T(8,128)S(1)}, f32[64,768]{1,0:T(8,128)S(1)}, u32[]{:S(2)}, u32[]{:S(2)}) collective-permute-start(f32[64,768]{1,0:T(8,128)S(1)} %convert_add_fusion), channel_id=1, source_target_pairs={{0,8},{8,0},{16,24},{24,16},{1,9},{9,1},{17,25},{25,17},{2,10},{10... | collective-permute-start | bytes 589832 | tf_op jit(solution)/shard_map/ppermute | solution.py:95
  61.5 1.5 %collective-permute-start.5 = (f32[64,768]{1,0:T(8,128)S(1)}, f32[64,768]{1,0:T(8,128)S(1)}, u32[]{:S(2)}, u32[]{:S(2)}) collective-permute-start(f32[64,768]{1,0:T(8,128)S(1)} %convert_add_fusion.1), channel_id=1, source_target_pairs={{0,8},{8,0},{16,24},{24,16},{1,9},{9,1},{17,25},{25,17},{2,10},{10... | collective-permute-start | bytes 589832 | tf_op jit(solution)/shard_map/ppermute | solution.py:95
  63.8 5.1 %collective-permute-start.15 = (f32[8,1,16]{2,0,1:T(8,128)S(1)}, f32[8,1,16]{2,0,1:T(8,128)S(1)}, u32[]{:S(2)}, u32[]{:S(2)}) collective-permute-start(f32[8,1,16]{2,0,1:T(8,128)S(1)} %reshape.131), channel_id=1, source_target_pairs={{0,8},{8,0},{16,24},{24,16},{1,9},{9,1},{17,25},{25,17},{2,10},{10... | collective-permute-start | bytes 1544 | tf_op jit(solution)/shard_map/ppermute | solution.py:53
  66.9 3.7 %copy-start.4 = (bf16[128,1280]{1,0:T(8,128)(2,1)S(1)}, bf16[128,1280]{1,0:T(8,128)(2,1)}, u32[]{:S(2)}) copy-start(bf16[128,1280]{1,0:T(8,128)(2,1)} %fusion.22) | copy-start | bytes 983044
  68.9 3.7 %collective-permute-start.16 = (f32[8,1,16]{2,0,1:T(8,128)S(1)}, f32[8,1,16]{2,0,1:T(8,128)S(1)}, u32[]{:S(2)}, u32[]{:S(2)}) collective-permute-start(f32[8,1,16]{2,0,1:T(8,128)S(1)} %add.91), channel_id=1, source_target_pairs={{0,16},{8,24},{16,0},{24,8},{1,17},{9,25},{17,1},{25,9},{2,18},{10... | collective-permute-start | bytes 1544 | tf_op jit(solution)/shard_map/ppermute | solution.py:53
  77.2 10.1 %collective-permute-start.17 = (bf16[2,128,96]{1,2,0:T(8,128)(2,1)}, bf16[2,128,96]{1,2,0:T(8,128)(2,1)}, u32[]{:S(2)}, u32[]{:S(2)}) collective-permute-start(bf16[2,128,96]{1,2,0:T(8,128)(2,1)} %convolution_convert_fusion.5), channel_id=1, source_target_pairs={{0,8},{8,0},{16,24},{24,16},{1,9},{9,1},{17,25},{25,17},{2,10},{10... | collective-permute-start | bytes 147464 | tf_op jit(solution)/shard_map/ppermute | solution.py:67
  77.3 5.3 %slice-start.1 = ((bf16[72,10240]{1,0:T(8,128)(2,1)}), bf16[8,10240]{1,0:T(8,128)(2,1)S(1)}, s32[]{:S(2)}) async-start(bf16[72,10240]{1,0:T(8,128)(2,1)} %all-gather.3.cloned.1.call-done), calls=%async_computation.4 | async-start | bytes 327680 | tf_op jit(solution)/shard_map/slice | solution.py:176
  82.1 7.8 %collective-permute-start.11 = (bf16[2,128,96]{1,2,0:T(8,128)(2,1)}, bf16[2,128,96]{1,2,0:T(8,128)(2,1)}, u32[]{:S(2)}, u32[]{:S(2)}) collective-permute-start(bf16[2,128,96]{1,2,0:T(8,128)(2,1)} %convolution_convert_fusion.7), channel_id=1, source_target_pairs={{0,8},{8,0},{16,24},{24,16},{1,9},{9,1},{17,25},{25,17},{2,10},{10... | collective-permute-start | bytes 147464 | tf_op jit(solution)/shard_map/ppermute | solution.py:67
  82.5 8.7 %collective-permute-start.13 = (bf16[2,128,96]{1,2,0:T(8,128)(2,1)S(1)}, bf16[2,128,96]{1,2,0:T(8,128)(2,1)}, u32[]{:S(2)}, u32[]{:S(2)}) collective-permute-start(bf16[2,128,96]{1,2,0:T(8,128)(2,1)S(1)} %convolution_convert_fusion.6), channel_id=1, source_target_pairs={{0,8},{8,0},{16,24},{24,16},{1,9},{9,1},{17,25},{25,17},{2,10},{10... | collective-permute-start | bytes 147464 | tf_op jit(solution)/shard_map/ppermute | solution.py:67
  85.4 9.9 %copy-start.8 = (f32[2,128]{1,0:T(2,128)}, f32[2,128]{1,0:T(2,128)S(1)}, u32[]{:S(2)}) copy-start(f32[2,128]{1,0:T(2,128)S(1)} %reshape.136) | copy-start | bytes 3076
  86.8 6.9 %collective-permute-start.9 = (bf16[2,128,96]{1,2,0:T(8,128)(2,1)S(1)}, bf16[2,128,96]{1,2,0:T(8,128)(2,1)S(1)}, u32[]{:S(2)}, u32[]{:S(2)}) collective-permute-start(bf16[2,128,96]{1,2,0:T(8,128)(2,1)S(1)} %convolution_convert_fusion.8), channel_id=1, source_target_pairs={{0,8},{8,0},{16,24},{24,16},{1,9},{9,1},{17,25},{25,17},{2,10},{10... | collective-permute-start | bytes 147464 | tf_op jit(solution)/shard_map/ppermute | solution.py:67
  88.2 6.0 %collective-permute-start.18 = (bf16[2,128,96]{1,2,0:T(8,128)(2,1)S(1)}, bf16[2,128,96]{1,2,0:T(8,128)(2,1)S(1)}, u32[]{:S(2)}, u32[]{:S(2)}) collective-permute-start(bf16[2,128,96]{1,2,0:T(8,128)(2,1)S(1)} %add_convert_fusion.3), channel_id=1, source_target_pairs={{0,16},{8,24},{16,0},{24,8},{1,17},{9,25},{17,1},{25,9},{2,18},{10... | collective-permute-start | bytes 147464 | tf_op jit(solution)/shard_map/ppermute | solution.py:67
  90.7 4.5 %collective-permute-start.12 = (bf16[2,128,96]{1,2,0:T(8,128)(2,1)S(1)}, bf16[2,128,96]{1,2,0:T(8,128)(2,1)S(1)}, u32[]{:S(2)}, u32[]{:S(2)}) collective-permute-start(bf16[2,128,96]{1,2,0:T(8,128)(2,1)S(1)} %add_convert_fusion.5), channel_id=1, source_target_pairs={{0,16},{8,24},{16,0},{24,8},{1,17},{9,25},{17,1},{25,9},{2,18},{10... | collective-permute-start | bytes 147464 | tf_op jit(solution)/shard_map/ppermute | solution.py:67
  92.0 4.6 %collective-permute-start.14 = (bf16[2,128,96]{1,2,0:T(8,128)(2,1)S(1)}, bf16[2,128,96]{1,2,0:T(8,128)(2,1)S(1)}, u32[]{:S(2)}, u32[]{:S(2)}) collective-permute-start(bf16[2,128,96]{1,2,0:T(8,128)(2,1)S(1)} %add_convert_fusion.4), channel_id=1, source_target_pairs={{0,16},{8,24},{16,0},{24,8},{1,17},{9,25},{17,1},{25,9},{2,18},{10... | collective-permute-start | bytes 147464 | tf_op jit(solution)/shard_map/ppermute | solution.py:67
  93.7 11.6 %collective-permute-start.10 = (bf16[2,128,96]{1,2,0:T(8,128)(2,1)S(1)}, bf16[2,128,96]{1,2,0:T(8,128)(2,1)}, u32[]{:S(2)}, u32[]{:S(2)}) collective-permute-start(bf16[2,128,96]{1,2,0:T(8,128)(2,1)S(1)} %add_convert_fusion.6), channel_id=1, source_target_pairs={{0,16},{8,24},{16,0},{24,8},{1,17},{9,25},{17,1},{25,9},{2,18},{10... | collective-permute-start | bytes 147464 | tf_op jit(solution)/shard_map/ppermute | solution.py:67
  95.2 2.0 %copy-start.6 = (bf16[2,128,96]{1,2,0:T(8,128)(2,1)}, bf16[2,128,96]{1,2,0:T(8,128)(2,1)S(1)}, u32[]{:S(2)}) copy-start(bf16[2,128,96]{1,2,0:T(8,128)(2,1)S(1)} %collective-permute-done.12) | copy-start | bytes 147460
  101.4 10.5 %all-to-all-start.1 = ((f32[8,3,16]{2,1,0:T(4,128)}), f32[8,3,16]{2,1,0:T(4,128)}, u32[]{:S(2)}, u32[]{:S(2)}) async-start(f32[8,3,16]{2,1,0:T(4,128)} %copy.38), calls=%async_computation.1 | async-start | bytes 32768 | tf_op jit(solution)/shard_map/all_to_all | solution.py:228
  107.4 6.1 %copy-start.7 = (s32[256,6]{0,1:T(8,128)S(1)}, s32[256,6]{0,1:T(8,128)}, u32[]{:S(2)}) copy-start(s32[256,6]{0,1:T(8,128)} %param.14) | copy-start | bytes 18436
  (1 other events, 0.8 us)
Sparse Core Ops, SparseCore 0:
  26.1 46.2 all-gather.2

commit v16 on v13

--- a/solution.py
+++ b/solution.py
@@ -192,9 +192,7 @@
     part_cot_hot = jnp.einsum(
         "jrd,jhd->jrh", rows_cot, down_hot, preferred_element_type=jnp.float32
     )
-    pre_gate, pre_up, grad_hidden = grp_sum_rounded(
-        [part_gate, part_up, part_hidden], [0, 0, 0], "grp"
-    )
+    pre_gate, pre_up, grad_hidden = grp_sum_doubling([part_gate, part_up, part_hidden], "grp")
     pre_gate_hot, pre_up_hot, grad_hidden_hot, cot_down = grp_sum_doubling(
         [part_gate_hot, part_up_hot, part_hidden_hot, part_cot_hot], "grp"
     )

time: 110 us -> 112 us (1.018)
  waiting for transfers between devices: 34.5 us -> 39.4 us
  matrix products: 18.8 us -> 21.4 us
  local copies, waits for them, and re-layouts: 7.37 us -> 4.98 us
  other arithmetic: 11 us -> 8.64 us
    ppermute x8 -> x14, waiting for transfers between devices: 2.41 us -> 13.5 us  [grp_sum_doubling(): got = lax.ppermute(mine, axis_name, partner)]
    ppermute x9 -> x0, waiting for transfers between devices: 6.19 us -> none  [the longest x3 4.8 us: grp_sum_rounded(): got = lax.ppermute(mine, axis_name, partner)]
    ppermute x8 -> x14, starting transfers between devices: 5.45 us -> 9.86 us  [grp_sum_doubling(): got = lax.ppermute(mine, axis_name, partner)]
    ppermute x9 -> x0, starting transfers between devices: 4.14 us -> none  [the longest x3 3.71 us: grp_sum_rounded(): got = lax.ppermute(mine, axis_name, partner)]
    dot_general x1, matrix products: 0.44 us -> 2.12 us  [body(): part_gate = jnp.dot(recv_feats, w_gate, preferred_element_type=jnp.float32)]
    unnamed x34 -> x28, local copies, waits for them, and re-layouts: 2.8 us -> 1.8 us
  transfers between devices with their start and end apart: 22 -> 19, of which waited for: 9 -> 8; matrix products, arithmetic and copies ran while one was open for 18% -> 18% of each run, Pallas kernels for 0% -> 0%
where the time goes in v16:
time: 112 us; the launch traced here: 111 us
  waiting for transfers between devices  39.4 us (35%)
  starting transfers between devices  22.1 us (20%)
  matrix products  21.4 us (19%)
  between operations  14.5 us (13%)
  other arithmetic  8.64 us (8%)
  local copies, waits for them, and re-layouts  4.98 us (4%)
    all_to_all x1, waiting for transfers between devices, body(): lax.all_to_all(outgoing, 'ep', split_axis=0, concat_axis=0, tiled=True)  24.6 us
    ppermute x14, waiting for transfers between devices, grp_sum_doubling(): got = lax.ppermute(mine, axis_name, partner)  13.5 us
    ppermute x14, starting transfers between devices, grp_sum_doubling(): got = lax.ppermute(mine, axis_name, partner)  9.86 us
    all_to_all x1, starting transfers between devices, body(): lax.all_to_all(outgoing, 'ep', split_axis=0, concat_axis=0, tiled=True)  7.28 us
    all_to_all x1, starting transfers between devices, body(): lax.all_to_all(route_parts, 'ep', split_axis=0, concat_axis=0, tiled=True)  3.41 us
    dot_general x1, matrix products, body(): lax.dot_general(recv_feats, back_gate, contract_rows, preferred_element_t...  2.95 us
  transfers between devices with their start and end apart: 19, of which 8 were waited for; matrix products, arithmetic and copies ran while one was open for 18% of the time, Pallas kernels for 0%

profile of v16, /device:TPU:0, one launch (start us, length us, event | category | flops | bytes accessed | tf_op | source)
XLA Modules:
  0.0 111.0 jit_solution(16591121626801151537)
XLA Ops:
  7.2 0.8 convert_bitcast_fusion
  8.8 0.8 compare_reduce_fusion
  9.6 0.8 fusion.29
  11.7 1.4 %convolution_convert_fusion.3 = bf16[160,1280]{1,0:T(8,128)(2,1)S(1)} fusion(pred[160,256]{1,0:T(32,128)(4,1)S(1)} %fusion.27, bf16[256,1280]{1,0:T(8,128)(2,1)} %param.12), kind=kOutput, calls=%fused_computation.7 | convolution fusion | flops 105062400 | bytes 1105920 | tf_op jit(solution)/shard_map/dot_general | solution.py:20
  14.2 0.9 pad_maximum_fusion
  15.2 7.3 %all-to-all-start = ((bf16[8,40,1280]{2,1,0:T(8,128)(2,1)}), bf16[8,40,1280]{2,1,0:T(8,128)(2,1)S(1)}, u32[]{:S(2)}, u32[]{:S(2)}) async-start(bf16[8,40,1280]{2,1,0:T(8,128)(2,1)} %pad_maximum_fusion), calls=%async_computation | async-start | bytes 1638400 | tf_op jit(solution)/shard_map/all_to_all | solution.py:159
  23.4 24.6 %all-to-all-done = bf16[8,40,1280]{2,1,0:T(8,128)(2,1)S(1)} async-done(((bf16[8,40,1280]{2,1,0:T(8,128)(2,1)}), bf16[8,40,1280]{2,1,0:T(8,128)(2,1)S(1)}, u32[]{:S(2)}, u32[]{:S(2)}) %all-to-all-start) | async-done | bytes 819232 | tf_op jit(solution)/shard_map/all_to_all | solution.py:159
  48.2 2.1 %fusion.19 = bf16[128,768]{1,0:T(8,128)(2,1)S(1)} fusion(bf16[128,1280]{1,0:T(8,128)(2,1)S(1)} %bitcast.93, bf16[1,1280,768]{2,1,0:T(8,128)(2,1)} %param.16), kind=kOutput, calls=%fused_computation.21 | convolution fusion | flops 251756544 | bytes 2490368 | tf_op jit(solution)/shard_map/dot_general | solution.py:169
  51.5 0.8 fusion.13
  52.4 0.8 fusion.22
  53.3 1.6 %collective-permute-start.3 = (bf16[128,768]{1,0:T(8,128)(2,1)S(1)}, bf16[128,768]{1,0:T(8,128)(2,1)S(1)}, u32[]{:S(2)}, u32[]{:S(2)}) collective-permute-start(bf16[128,768]{1,0:T(8,128)(2,1)S(1)} %add_convert_fusion.1), channel_id=1, source_target_pairs={{0,16},{8,24},{16,0},{24,8},{1,17},{9,25},{17,1},{25,9},{2,18},{10... | collective-permute-start | bytes 589832 | tf_op jit(solution)/shard_map/ppermute | solution.py:67
  55.6 1.6 %collective-permute-start.1 = (bf16[128,768]{1,0:T(8,128)(2,1)S(1)}, bf16[128,768]{1,0:T(8,128)(2,1)S(1)}, u32[]{:S(2)}, u32[]{:S(2)}) collective-permute-start(bf16[128,768]{1,0:T(8,128)(2,1)S(1)} %add_convert_fusion.2), channel_id=1, source_target_pairs={{0,16},{8,24},{16,0},{24,8},{1,17},{9,25},{17,1},{25,9},{2,18},{10... | collective-permute-start | bytes 589832 | tf_op jit(solution)/shard_map/ppermute | solution.py:67
  57.1 3.9 %collective-permute-done.3 = bf16[128,768]{1,0:T(8,128)(2,1)S(1)} collective-permute-done((bf16[128,768]{1,0:T(8,128)(2,1)S(1)}, bf16[128,768]{1,0:T(8,128)(2,1)S(1)}, u32[]{:S(2)}, u32[]{:S(2)}) %collective-permute-start.3) | collective-permute-done | bytes 196640 | tf_op jit(solution)/shard_map/ppermute | solution.py:67
  61.1 4.2 %collective-permute-done.5 = bf16[128,768]{1,0:T(8,128)(2,1)S(1)} collective-permute-done((bf16[128,768]{1,0:T(8,128)(2,1)S(1)}, bf16[128,768]{1,0:T(8,128)(2,1)S(1)}, u32[]{:S(2)}, u32[]{:S(2)}) %collective-permute-start.5) | collective-permute-done | bytes 196640 | tf_op jit(solution)/shard_map/ppermute | solution.py:67
  66.1 2.9 %collective-permute-done.1 = bf16[128,768]{1,0:T(8,128)(2,1)S(1)} collective-permute-done((bf16[128,768]{1,0:T(8,128)(2,1)S(1)}, bf16[128,768]{1,0:T(8,128)(2,1)S(1)}, u32[]{:S(2)}, u32[]{:S(2)}) %collective-permute-start.1) | collective-permute-done | bytes 196640 | tf_op jit(solution)/shard_map/ppermute | solution.py:67
  69.0 3.0 %fusion = bf16[1,1280,768]{2,1,0:T(8,128)(2,1)} fusion(bf16[128,1280]{1,0:T(8,128)(2,1)S(1)} %bitcast.95, bf16[128,768]{1,0:T(8,128)(2,1)S(1)} %collective-permute-done.1, bf16[128,768]{1,0:T(8,128)(2,1)S(1)} %add_convert_fusion.2, bf16[128,768]{1,0:T(8,128)(2,1)} %copy-done.4, bf16[128,768]{1,0:T(8,128)(2,1)S(1)} %add_convert_fusion.1, ...), kind=kOutput, calls=%fused_computation.3 | convolution fusion | flops 254509056 | bytes 3473408 | tf_op jit(solution)/shard_map/dot_general | solution.py:204
  72.0 2.0 %fusion.1 = bf16[1,1280,768]{2,1,0:T(8,128)(2,1)} fusion(bf16[128,1280]{1,0:T(8,128)(2,1)S(1)} %bitcast.96, bf16[128,768]{1,0:T(8,128)(2,1)S(1)} %collective-permute-done.1, bf16[128,768]{1,0:T(8,128)(2,1)S(1)} %add_convert_fusion.2, bf16[128,768]{1,0:T(8,128)(2,1)S(1)} %collective-permute-done.5, bf16[128,768]{1,0:T(8,128)(2,1)S(1)} %add_convert_fusion), kind=kOutput, calls=%fused_computation.4 | convolution fusion | flops 253820928 | bytes 3080192 | tf_op jit(solution)/shard_map/dot_general | solution.py:207
  74.0 1.5 %collective-permute-start.13 = (f32[8,1,16]{2,0,1:T(8,128)S(1)}, f32[8,1,16]{2,0,1:T(8,128)S(1)}, u32[]{:S(2)}, u32[]{:S(2)}) collective-permute-start(f32[8,1,16]{2,0,1:T(8,128)S(1)} %add.86), channel_id=1, source_target_pairs={{0,16},{8,24},{16,0},{24,8},{1,17},{9,25},{17,1},{25,9},{2,18},{10... | collective-permute-start | bytes 1544 | tf_op jit(solution)/shard_map/ppermute | solution.py:53
  75.5 2.0 %fusion.2 = bf16[1,768,1280]{2,1,0:T(8,128)(2,1)} fusion(bf16[128,768]{1,0:T(8,128)(2,1)S(1)} %multiply_convert_fusion.4, bf16[128,1280]{1,0:T(8,128)(2,1)S(1)} %copy-done.3), kind=kOutput, calls=%fused_computation.5 | convolution fusion | flops 252641280 | bytes 2490368 | tf_op jit(solution)/shard_map/dot_general | solution.py:210
  77.6 0.9 slice_bitcast_fusion
  78.6 1.4 %slice.96 = bf16[8,64,1280]{2,1,0:T(8,128)(2,1)S(1)} slice(bf16[8,72,1280]{2,1,0:T(8,128)(2,1)} %bitcast.104), slice={[0:8], [0:64], [0:1280]} | slice | bytes 2621440 | tf_op jit(solution)/shard_map/slice | solution.py:174
  80.4 1.5 %convolution_convert_fusion.5 = bf16[2,128,96]{1,2,0:T(8,128)(2,1)S(1)} fusion(bf16[2,128,1280]{2,1,0:T(8,128)(2,1)S(1)} %bitcast.97, bf16[2,96,1280]{2,1,0:T(8,128)(2,1)} %param.21), kind=kOutput, calls=%fused_computation.22 | convolution fusion | flops 62939136 | bytes 1196032 | tf_op jit(solution)/shard_map/jrd,jhd->jrh/dot_general | solution.py:192
  81.9 1.4 %convolution_convert_fusion.8 = bf16[2,128,96]{1,2,0:T(8,128)(2,1)S(1)} fusion(bf16[2,96,1280]{2,1,0:T(8,128)(2,1)} %param.21, bf16[2,128,1280]{2,1,0:T(8,128)(2,1)S(1)} %bitcast.98, f32[2,128]{1,0:T(2,128)S(1)} %reshape.137), kind=kOutput, calls=%fused_computation.25 | convolution fusion | flops 63922176 | bytes 1197056 | tf_op jit(solution)/shard_map/jrd,jhd->jrh/dot_general | solution.py:189
  85.2 1.6 %collective-permute-start.9 = (bf16[2,128,96]{1,2,0:T(8,128)(2,1)S(1)}, bf16[2,128,96]{1,2,0:T(8,128)(2,1)S(1)}, u32[]{:S(2)}, u32[]{:S(2)}) collective-permute-start(bf16[2,128,96]{1,2,0:T(8,128)(2,1)S(1)} %add_convert_fusion.5), channel_id=1, source_target_pairs={{0,16},{8,24},{16,0},{24,8},{1,17},{9,25},{17,1},{25,9},{2,18},{10... | collective-permute-start | bytes 147464 | tf_op jit(solution)/shard_map/ppermute | solution.py:67
  87.4 1.6 %collective-permute-start.15 = (bf16[2,128,96]{1,2,0:T(8,128)(2,1)S(1)}, bf16[2,128,96]{1,2,0:T(8,128)(2,1)S(1)}, u32[]{:S(2)}, u32[]{:S(2)}) collective-permute-start(bf16[2,128,96]{1,2,0:T(8,128)(2,1)S(1)} %add_convert_fusion.3), channel_id=1, source_target_pairs={{0,16},{8,24},{16,0},{24,8},{1,17},{9,25},{17,1},{25,9},{2,18},{10... | collective-permute-start | bytes 147464 | tf_op jit(solution)/shard_map/ppermute | solution.py:67
  89.6 1.5 %collective-permute-done.11 = bf16[2,128,96]{1,2,0:T(8,128)(2,1)S(1)} collective-permute-done((bf16[2,128,96]{1,2,0:T(8,128)(2,1)S(1)}, bf16[2,128,96]{1,2,0:T(8,128)(2,1)S(1)}, u32[]{:S(2)}, u32[]{:S(2)}) %collective-permute-start.11) | collective-permute-done | bytes 49184 | tf_op jit(solution)/shard_map/ppermute | solution.py:67
  91.1 0.9 collective-permute-done.15
  93.4 3.4 %all-to-all-start.1 = ((f32[8,3,16]{2,1,0:T(4,128)}), f32[8,3,16]{2,1,0:T(4,128)S(1)}, u32[]{:S(2)}, u32[]{:S(2)}) async-start(f32[8,3,16]{2,1,0:T(4,128)} %copy.45), calls=%async_computation.1 | async-start | bytes 32768 | tf_op jit(solution)/shard_map/all_to_all | solution.py:229
  96.8 2.1 %fusion.31 = f32[2,1280,96]{1,2,0:T(8,128)} fusion(bf16[2,128,1280]{2,1,0:T(8,128)(2,1)S(1)} %bitcast.91, bf16[2,128,96]{1,2,0:T(8,128)(2,1)} %collective-permute-done.7, bf16[2,128,96]{1,2,0:T(8,128)(2,1)S(1)} %add_convert_fusion.6, bf16[2,128,96]{1,2,0:T(8,128)(2,1)} %copy-done.9, bf16[2,128,96]{1,2,0:T(8,128)(2,1)S(1)} %add_convert_fusion.5, ...), kind=kOutput, calls=%fused_computation.71 | convolution fusion | flops 63381504 | bytes 1933312 | tf_op jit(solution)/shard_map/jrd,jrh->jdh/dot_general | solution.py:215
  98.9 2.1 %fusion.32 = f32[2,1280,96]{1,2,0:T(8,128)} fusion(bf16[2,128,1280]{2,1,0:T(8,128)(2,1)S(1)} %bitcast.92, bf16[2,128,96]{1,2,0:T(8,128)(2,1)} %collective-permute-done.7, bf16[2,128,96]{1,2,0:T(8,128)(2,1)S(1)} %add_convert_fusion.6, bf16[2,128,96]{1,2,0:T(8,128)(2,1)S(1)} %collective-permute-done.11, bf16[2,128,96]{1,2,0:T(8,128)(2,1)S(1)} %add_convert_fusion.4), kind=kOutput, calls=%fused_computation.72 | convolution fusion | flops 63209472 | bytes 1835008 | tf_op jit(solution)/shard_map/jrd,jrh->jdh/dot_general | solution.py:218
  100.9 1.3 %fusion.23 = f32[2,96,1280]{2,1,0:T(8,128)} fusion(bf16[2,128,96]{1,2,0:T(8,128)(2,1)S(1)} %copy-done.8, bf16[2,128,1280]{2,1,0:T(8,128)(2,1)S(1)} %bitcast.99, f32[2,128]{1,0:T(2,128)S(1)} %reshape.137), kind=kOutput, calls=%fused_computation.30 | convolution fusion | flops 63897600 | bytes 1688576 | tf_op jit(solution)/shard_map/jrh,jrd->jhd/dot_general | solution.py:219
  102.2 1.1 %all-to-all-done.1 = f32[8,3,16]{2,1,0:T(4,128)S(1)} async-done(((f32[8,3,16]{2,1,0:T(4,128)}), f32[8,3,16]{2,1,0:T(4,128)S(1)}, u32[]{:S(2)}, u32[]{:S(2)}) %all-to-all-start.1) | async-done | bytes 1568 | tf_op jit(solution)/shard_map/all_to_all | solution.py:229
  (115 shorter events, 12.9 us)
Async XLA Ops:
  7.2 44.3 %copy-start = (bf16[1,768,1280]{2,1,0:T(8,128)(2,1)S(1)}, bf16[1,768,1280]{2,1,0:T(8,128)(2,1)}, u32[]{:S(2)}) copy-start(bf16[1,768,1280]{2,1,0:T(8,128)(2,1)} %param.18) | copy-start | bytes 5898244
  7.2 5.9 %copy-start.5 = (bf16[256,1280]{1,0:T(8,128)(2,1)S(1)}, bf16[256,1280]{1,0:T(8,128)(2,1)}, u32[]{:S(2)}) copy-start(bf16[256,1280]{1,0:T(8,128)(2,1)} %param.11) | copy-start | bytes 1966084
  13.4 0.8 copy-start.2
  14.2 8.5 %slice-start = ((bf16[160,1280]{1,0:T(8,128)(2,1)}), bf16[32,1280]{1,0:T(8,128)(2,1)S(1)}, s32[]{:S(2)}) async-start(bf16[160,1280]{1,0:T(8,128)(2,1)} %copy-done.2), calls=%async_computation.3 | async-start | bytes 163840 | tf_op jit(solution)/shard_map/slice | solution.py:128
  15.2 32.8 %all-to-all-start = ((bf16[8,40,1280]{2,1,0:T(8,128)(2,1)}), bf16[8,40,1280]{2,1,0:T(8,128)(2,1)S(1)}, u32[]{:S(2)}, u32[]{:S(2)}) async-start(bf16[8,40,1280]{2,1,0:T(8,128)(2,1)} %pad_maximum_fusion), calls=%async_computation | async-start | bytes 1638400 | tf_op jit(solution)/shard_map/all_to_all | solution.py:159
  22.4 55.2 %all-gather.3.cloned.1.call-start = ((), (), s32[]{:S(2)}) async-start(), calls=%async_computation.2 | async-start | bytes 1658880 | tf_op jit(solution)/shard_map/all_gather | solution.py:144
  48.1 2.2 %copy-start.1 = (bf16[1,1280,768]{2,1,0:T(8,128)(2,1)S(1)}, bf16[1,1280,768]{2,1,0:T(8,128)(2,1)}, u32[]{:S(2)}) copy-start(bf16[1,1280,768]{2,1,0:T(8,128)(2,1)} %param.17) | copy-start | bytes 5898244
  50.8 2.5 %collective-permute-start.2 = (bf16[128,768]{1,0:T(8,128)(2,1)S(1)}, bf16[128,768]{1,0:T(8,128)(2,1)S(1)}, u32[]{:S(2)}, u32[]{:S(2)}) collective-permute-start(bf16[128,768]{1,0:T(8,128)(2,1)S(1)} %fusion.16), channel_id=1, source_target_pairs={{0,8},{8,0},{16,24},{24,16},{1,9},{9,1},{17,25},{25,17},{2,10},{10... | collective-permute-start | bytes 589832 | tf_op jit(solution)/shard_map/ppermute | solution.py:67
  50.9 4.0 %collective-permute-start.4 = (bf16[128,768]{1,0:T(8,128)(2,1)S(1)}, bf16[128,768]{1,0:T(8,128)(2,1)S(1)}, u32[]{:S(2)}, u32[]{:S(2)}) collective-permute-start(bf16[128,768]{1,0:T(8,128)(2,1)S(1)} %fusion.19), channel_id=1, source_target_pairs={{0,8},{8,0},{16,24},{24,16},{1,9},{9,1},{17,25},{25,17},{2,10},{10... | collective-permute-start | bytes 589832 | tf_op jit(solution)/shard_map/ppermute | solution.py:67
  52.3 3.2 %collective-permute-start = (bf16[128,768]{1,0:T(8,128)(2,1)S(1)}, bf16[128,768]{1,0:T(8,128)(2,1)S(1)}, u32[]{:S(2)}, u32[]{:S(2)}) collective-permute-start(bf16[128,768]{1,0:T(8,128)(2,1)S(1)} %fusion.13), channel_id=1, source_target_pairs={{0,8},{8,0},{16,24},{24,16},{1,9},{9,1},{17,25},{25,17},{2,10},{10... | collective-permute-start | bytes 589832 | tf_op jit(solution)/shard_map/ppermute | solution.py:67
  53.3 7.8 %collective-permute-start.3 = (bf16[128,768]{1,0:T(8,128)(2,1)S(1)}, bf16[128,768]{1,0:T(8,128)(2,1)S(1)}, u32[]{:S(2)}, u32[]{:S(2)}) collective-permute-start(bf16[128,768]{1,0:T(8,128)(2,1)S(1)} %add_convert_fusion.1), channel_id=1, source_target_pairs={{0,16},{8,24},{16,0},{24,8},{1,17},{9,25},{17,1},{25,9},{2,18},{10... | collective-permute-start | bytes 589832 | tf_op jit(solution)/shard_map/ppermute | solution.py:67
  54.9 10.4 %collective-permute-start.5 = (bf16[128,768]{1,0:T(8,128)(2,1)S(1)}, bf16[128,768]{1,0:T(8,128)(2,1)S(1)}, u32[]{:S(2)}, u32[]{:S(2)}) collective-permute-start(bf16[128,768]{1,0:T(8,128)(2,1)S(1)} %add_convert_fusion), channel_id=1, source_target_pairs={{0,16},{8,24},{16,0},{24,8},{1,17},{9,25},{17,1},{25,9},{2,18},{10... | collective-permute-start | bytes 589832 | tf_op jit(solution)/shard_map/ppermute | solution.py:67
  55.6 13.5 %collective-permute-start.1 = (bf16[128,768]{1,0:T(8,128)(2,1)S(1)}, bf16[128,768]{1,0:T(8,128)(2,1)S(1)}, u32[]{:S(2)}, u32[]{:S(2)}) collective-permute-start(bf16[128,768]{1,0:T(8,128)(2,1)S(1)} %add_convert_fusion.2), channel_id=1, source_target_pairs={{0,16},{8,24},{16,0},{24,8},{1,17},{9,25},{17,1},{25,9},{2,18},{10... | collective-permute-start | bytes 589832 | tf_op jit(solution)/shard_map/ppermute | solution.py:67
  61.1 4.2 %copy-start.4 = (bf16[128,768]{1,0:T(8,128)(2,1)}, bf16[128,768]{1,0:T(8,128)(2,1)S(1)}, u32[]{:S(2)}) copy-start(bf16[128,768]{1,0:T(8,128)(2,1)S(1)} %collective-permute-done.3) | copy-start | bytes 589828
  66.1 7.9 %collective-permute-start.12 = (f32[8,1,16]{2,0,1:T(8,128)S(1)}, f32[8,1,16]{2,0,1:T(8,128)S(1)}, u32[]{:S(2)}, u32[]{:S(2)}) collective-permute-start(f32[8,1,16]{2,0,1:T(8,128)S(1)} %reshape.132), channel_id=1, source_target_pairs={{0,8},{8,0},{16,24},{24,16},{1,9},{9,1},{17,25},{25,17},{2,10},{10... | collective-permute-start | bytes 1544 | tf_op jit(solution)/shard_map/ppermute | solution.py:53
  72.0 3.5 %copy-start.3 = (bf16[128,1280]{1,0:T(8,128)(2,1)S(1)}, bf16[128,1280]{1,0:T(8,128)(2,1)}, u32[]{:S(2)}) copy-start(bf16[128,1280]{1,0:T(8,128)(2,1)} %fusion.22) | copy-start | bytes 983044
  74.0 3.6 %collective-permute-start.13 = (f32[8,1,16]{2,0,1:T(8,128)S(1)}, f32[8,1,16]{2,0,1:T(8,128)S(1)}, u32[]{:S(2)}, u32[]{:S(2)}) collective-permute-start(f32[8,1,16]{2,0,1:T(8,128)S(1)} %add.86), channel_id=1, source_target_pairs={{0,16},{8,24},{16,0},{24,8},{1,17},{9,25},{17,1},{25,9},{2,18},{10... | collective-permute-start | bytes 1544 | tf_op jit(solution)/shard_map/ppermute | solution.py:53
  80.4 2.9 %copy-start.6 = (bf16[2,1280,96]{1,2,0:T(8,128)(2,1)S(1)}, bf16[2,1280,96]{1,2,0:T(8,128)(2,1)}, u32[]{:S(2)}) copy-start(bf16[2,1280,96]{1,2,0:T(8,128)(2,1)} %param.20) | copy-start | bytes 1474564
  80.4 3.3 %copy-start.7 = (bf16[2,1280,96]{1,2,0:T(8,128)(2,1)S(1)}, bf16[2,1280,96]{1,2,0:T(8,128)(2,1)}, u32[]{:S(2)}) copy-start(bf16[2,1280,96]{1,2,0:T(8,128)(2,1)} %param.19) | copy-start | bytes 1474564
  83.7 1.5 %collective-permute-start.8 = (bf16[2,128,96]{1,2,0:T(8,128)(2,1)S(1)}, bf16[2,128,96]{1,2,0:T(8,128)(2,1)S(1)}, u32[]{:S(2)}, u32[]{:S(2)}) collective-permute-start(bf16[2,128,96]{1,2,0:T(8,128)(2,1)S(1)} %convolution_convert_fusion.7), channel_id=1, source_target_pairs={{0,8},{8,0},{16,24},{24,16},{1,9},{9,1},{17,25},{25,17},{2,10},{10... | collective-permute-start | bytes 147464 | tf_op jit(solution)/shard_map/ppermute | solution.py:67
  84.1 2.6 %collective-permute-start.10 = (bf16[2,128,96]{1,2,0:T(8,128)(2,1)S(1)}, bf16[2,128,96]{1,2,0:T(8,128)(2,1)S(1)}, u32[]{:S(2)}, u32[]{:S(2)}) collective-permute-start(bf16[2,128,96]{1,2,0:T(8,128)(2,1)S(1)} %convolution_convert_fusion.6), channel_id=1, source_target_pairs={{0,8},{8,0},{16,24},{24,16},{1,9},{9,1},{17,25},{25,17},{2,10},{10... | collective-permute-start | bytes 147464 | tf_op jit(solution)/shard_map/ppermute | solution.py:67
  84.7 2.7 %collective-permute-start.14 = (bf16[2,128,96]{1,2,0:T(8,128)(2,1)S(1)}, bf16[2,128,96]{1,2,0:T(8,128)(2,1)S(1)}, u32[]{:S(2)}, u32[]{:S(2)}) collective-permute-start(bf16[2,128,96]{1,2,0:T(8,128)(2,1)S(1)} %convolution_convert_fusion.5), channel_id=1, source_target_pairs={{0,8},{8,0},{16,24},{24,16},{1,9},{9,1},{17,25},{25,17},{2,10},{10... | collective-permute-start | bytes 147464 | tf_op jit(solution)/shard_map/ppermute | solution.py:67
  84.7 4.2 %collective-permute-start.6 = (bf16[2,128,96]{1,2,0:T(8,128)(2,1)S(1)}, bf16[2,128,96]{1,2,0:T(8,128)(2,1)S(1)}, u32[]{:S(2)}, u32[]{:S(2)}) collective-permute-start(bf16[2,128,96]{1,2,0:T(8,128)(2,1)S(1)} %convolution_convert_fusion.8), channel_id=1, source_target_pairs={{0,8},{8,0},{16,24},{24,16},{1,9},{9,1},{17,25},{25,17},{2,10},{10... | collective-permute-start | bytes 147464 | tf_op jit(solution)/shard_map/ppermute | solution.py:67
  85.2 4.4 %collective-permute-start.9 = (bf16[2,128,96]{1,2,0:T(8,128)(2,1)S(1)}, bf16[2,128,96]{1,2,0:T(8,128)(2,1)S(1)}, u32[]{:S(2)}, u32[]{:S(2)}) collective-permute-start(bf16[2,128,96]{1,2,0:T(8,128)(2,1)S(1)} %add_convert_fusion.5), channel_id=1, source_target_pairs={{0,16},{8,24},{16,0},{24,8},{1,17},{9,25},{17,1},{25,9},{2,18},{10... | collective-permute-start | bytes 147464 | tf_op jit(solution)/shard_map/ppermute | solution.py:67
  86.8 4.3 %collective-permute-start.11 = (bf16[2,128,96]{1,2,0:T(8,128)(2,1)S(1)}, bf16[2,128,96]{1,2,0:T(8,128)(2,1)S(1)}, u32[]{:S(2)}, u32[]{:S(2)}) collective-permute-start(bf16[2,128,96]{1,2,0:T(8,128)(2,1)S(1)} %add_convert_fusion.4), channel_id=1, source_target_pairs={{0,16},{8,24},{16,0},{24,8},{1,17},{9,25},{17,1},{25,9},{2,18},{10... | collective-permute-start | bytes 147464 | tf_op jit(solution)/shard_map/ppermute | solution.py:67
  87.4 4.6 %collective-permute-start.15 = (bf16[2,128,96]{1,2,0:T(8,128)(2,1)S(1)}, bf16[2,128,96]{1,2,0:T(8,128)(2,1)S(1)}, u32[]{:S(2)}, u32[]{:S(2)}) collective-permute-start(bf16[2,128,96]{1,2,0:T(8,128)(2,1)S(1)} %add_convert_fusion.3), channel_id=1, source_target_pairs={{0,16},{8,24},{16,0},{24,8},{1,17},{9,25},{17,1},{25,9},{2,18},{10... | collective-permute-start | bytes 147464 | tf_op jit(solution)/shard_map/ppermute | solution.py:67
  89.0 7.8 %collective-permute-start.7 = (bf16[2,128,96]{1,2,0:T(8,128)(2,1)S(1)}, bf16[2,128,96]{1,2,0:T(8,128)(2,1)}, u32[]{:S(2)}, u32[]{:S(2)}) collective-permute-start(bf16[2,128,96]{1,2,0:T(8,128)(2,1)S(1)} %add_convert_fusion.6), channel_id=1, source_target_pairs={{0,16},{8,24},{16,0},{24,8},{1,17},{9,25},{17,1},{25,9},{2,18},{10... | collective-permute-start | bytes 147464 | tf_op jit(solution)/shard_map/ppermute | solution.py:67
  89.6 3.1 %copy-start.9 = (bf16[2,128,96]{1,2,0:T(8,128)(2,1)}, bf16[2,128,96]{1,2,0:T(8,128)(2,1)S(1)}, u32[]{:S(2)}) copy-start(bf16[2,128,96]{1,2,0:T(8,128)(2,1)S(1)} %collective-permute-done.9) | copy-start | bytes 147460
  93.4 10.0 %all-to-all-start.1 = ((f32[8,3,16]{2,1,0:T(4,128)}), f32[8,3,16]{2,1,0:T(4,128)S(1)}, u32[]{:S(2)}, u32[]{:S(2)}) async-start(f32[8,3,16]{2,1,0:T(4,128)} %copy.45), calls=%async_computation.1 | async-start | bytes 32768 | tf_op jit(solution)/shard_map/all_to_all | solution.py:229
  96.8 4.1 %copy-start.8 = (bf16[2,128,96]{1,2,0:T(8,128)(2,1)S(1)}, bf16[2,128,96]{1,2,0:T(8,128)(2,1)}, u32[]{:S(2)}) copy-start(bf16[2,128,96]{1,2,0:T(8,128)(2,1)} %get-tuple-element.8) | copy-start | bytes 147460
  98.9 4.6 %copy-start.10 = (s32[256,6]{0,1:T(8,128)S(1)}, s32[256,6]{0,1:T(8,128)}, u32[]{:S(2)}) copy-start(s32[256,6]{0,1:T(8,128)} %param.14) | copy-start | bytes 18436
Sparse Core Ops, SparseCore 0:
  26.0 46.5 all-gather.2

commit v17 on v13

--- a/solution.py
+++ b/solution.py
@@ -135,18 +135,20 @@
         scale_all[:cold_total],
     )
     hot_rows = hot_count * capacity
-    scale_lines = -(-hot_rows // slice_width)
-    scale_lines = -(-scale_lines // 8) * 8
-    scale_block = jnp.pad(hot_scale, (0, scale_lines * slice_width - hot_rows)).reshape(
-        scale_lines, slice_width
-    )
-    hot_outgoing = jnp.concatenate([hot_feats, hot_cotan, scale_block], axis=0)
+    hot_outgoing = jnp.concatenate([hot_feats, hot_cotan], axis=0)
     gathered = lax.all_gather(hot_outgoing, "ep", axis=0, tiled=False)
-    cold_lines = -(-capacity // slice_width)
+    scale_width = capacity + hot_rows
+    cold_lines = -(-scale_width // slice_width)
     cold_lines = -(-cold_lines // 8) * 8
+    both_scales = jnp.concatenate(
+        [
+            cold_scale.reshape(cold_count, capacity),
+            jnp.broadcast_to(hot_scale[None, :], (cold_count, hot_rows)),
+        ],
+        axis=1,
+    )
     cold_scale_block = jnp.pad(
-        cold_scale.reshape(cold_count, capacity),
-        ((0, 0), (0, cold_lines * slice_width - capacity)),
+        both_scales, ((0, 0), (0, cold_lines * slice_width - scale_width))
     ).reshape(cold_count, cold_lines, slice_width)
     outgoing = jnp.concatenate(
         [
@@ -159,7 +161,8 @@
     received = lax.all_to_all(outgoing, "ep", split_axis=0, concat_axis=0, tiled=True)
     recv_feats = received[:, :capacity].reshape(-1, slice_width)
     recv_cotan = received[:, capacity : 2 * capacity].reshape(-1, slice_width)
-    recv_scale = received[:, 2 * capacity :].reshape(cold_count, -1)[:, :capacity]
+    recv_scales = received[:, 2 * capacity :].reshape(cold_count, -1)
+    recv_scale = recv_scales[:, :capacity]
     weighted = (
         recv_scale.reshape(-1, 1).astype(jnp.float32) * recv_cotan.astype(jnp.float32)
     ).astype(jnp.bfloat16)
@@ -175,7 +178,7 @@
     all_rows = jnp.transpose(all_rows, (1, 2, 0, 3, 4)).reshape(
         2, hot_count, blocks * capacity, slice_width
     )
-    all_scale = gathered[:, 2 * hot_rows :].reshape(blocks, -1)[:, :hot_rows]
+    all_scale = recv_scales[:, capacity:scale_width]
     all_scale = jnp.transpose(all_scale.reshape(blocks, hot_count, capacity), (1, 0, 2))
     rows_feat, rows_cot = all_rows[0], all_rows[1]
     rows_wt = (

time: 110 us -> 106 us (0.964)
  matrix products: 18.8 us -> 16.7 us
    slice x1 -> x3, local copies, waits for them, and re-layouts: 0.09 us -> 1.52 us  [body(): rows_feat, rows_cot = (all_rows[0], all_rows[1])]
    slice x2 -> x1, local copies, waits for them, and re-layouts: 1.59 us -> 0.18 us  [the longest x1 1.41 us: body(): gathered[:, :2 * hot_rows]]
    dot_general x1, matrix products: 1.46 us -> 0.34 us  [body(): jnp.einsum('jrd,jhd->jrh', rows_cot, down_hot, preferred_element_type=jnp...]
    unnamed x34 -> x35, local copies, waits for them, and re-layouts: 2.8 us -> 1.88 us
  transfers between devices with their start and end apart: 22 -> 22, of which waited for: 9 -> 8; matrix products, arithmetic and copies ran while one was open for 18% -> 20% of each run, Pallas kernels for 0% -> 0%
where the time goes in v17:
time: 106 us; the launch traced here: 105 us
  waiting for transfers between devices  33.5 us (32%)
  starting transfers between devices  23.3 us (22%)
  matrix products  16.7 us (16%)
  between operations  14.6 us (14%)
  other arithmetic  11.1 us (10%)
  local copies, waits for them, and re-layouts  6.34 us (6%)
    all_to_all x1, waiting for transfers between devices, body(): lax.all_to_all(outgoing, 'ep', split_axis=0, concat_axis=0, tiled=True)  23.9 us
    all_to_all x1, starting transfers between devices, body(): lax.all_to_all(outgoing, 'ep', split_axis=0, concat_axis=0, tiled=True)  7.28 us
    ppermute x8, starting transfers between devices, grp_sum_doubling(): got = lax.ppermute(mine, axis_name, partner)  5.75 us
    ppermute x3, waiting for transfers between devices, grp_sum_rounded(): got = lax.ppermute(mine, axis_name, partner)  4.56 us
    ppermute x3, starting transfers between devices, grp_sum_rounded(): got = lax.ppermute(mine, axis_name, partner)  3.96 us
    all_to_all x1, starting transfers between devices, body(): lax.all_to_all(route_parts, 'ep', split_axis=0, concat_axis=0, tiled=True)  3.95 us
    ppermute x8, waiting for transfers between devices, grp_sum_doubling(): got = lax.ppermute(mine, axis_name, partner)  2.47 us
  transfers between devices with their start and end apart: 22, of which 8 were waited for; matrix products, arithmetic and copies ran while one was open for 20% of the time, Pallas kernels for 0%

profile of v17, /device:TPU:0, one launch (start us, length us, event | category | flops | bytes accessed | tf_op | source)
XLA Modules:
  0.0 105.5 jit_solution(7305889444607273234)
XLA Ops:
  7.2 0.8 convert_bitcast_fusion
  8.7 0.8 compare_reduce_fusion
  9.6 0.8 fusion.29
  11.9 1.4 %convolution_convert_fusion.3 = bf16[160,1280]{1,0:T(8,128)(2,1)S(1)} fusion(pred[160,256]{1,0:T(32,128)(4,1)S(1)} %fusion.27, bf16[256,1280]{1,0:T(8,128)(2,1)} %param.12), kind=kOutput, calls=%fused_computation.7 | convolution fusion | flops 105062400 | bytes 1105920 | tf_op jit(solution)/shard_map/dot_general | solution.py:20
  13.6 0.7 copy-done.3
  14.4 0.9 pad_maximum_fusion
  15.3 7.3 %all-to-all-start = ((bf16[8,40,1280]{2,1,0:T(8,128)(2,1)}), bf16[8,40,1280]{2,1,0:T(8,128)(2,1)S(1)}, u32[]{:S(2)}, u32[]{:S(2)}) async-start(bf16[8,40,1280]{2,1,0:T(8,128)(2,1)} %pad_maximum_fusion), calls=%async_computation | async-start | bytes 1638400 | tf_op jit(solution)/shard_map/all_to_all | solution.py:161
  23.4 23.9 %all-to-all-done = bf16[8,40,1280]{2,1,0:T(8,128)(2,1)S(1)} async-done(((bf16[8,40,1280]{2,1,0:T(8,128)(2,1)}), bf16[8,40,1280]{2,1,0:T(8,128)(2,1)S(1)}, u32[]{:S(2)}, u32[]{:S(2)}) %all-to-all-start) | async-done | bytes 819232 | tf_op jit(solution)/shard_map/all_to_all | solution.py:161
  47.9 0.8 fusion.13
  51.0 0.8 fusion.22
  51.9 1.8 %collective-permute-start.1 = (bf16[64,768]{1,0:T(8,128)(2,1)S(1)}, bf16[64,768]{1,0:T(8,128)(2,1)S(1)}, u32[]{:S(2)}, u32[]{:S(2)}) collective-permute-start(bf16[64,768]{1,0:T(8,128)(2,1)S(1)} %add_convert_fusion.2), channel_id=1, source_target_pairs={{0,16},{8,24},{16,0},{24,8},{1,17},{9,25},{17,1},{25,9},{2,18},{10... | collective-permute-start | bytes 294920 | tf_op jit(solution)/shard_map/ppermute | solution.py:92
  54.1 1.8 %collective-permute-start.4 = (bf16[64,768]{1,0:T(8,128)(2,1)S(1)}, bf16[64,768]{1,0:T(8,128)(2,1)S(1)}, u32[]{:S(2)}, u32[]{:S(2)}) collective-permute-start(bf16[64,768]{1,0:T(8,128)(2,1)S(1)} %add_convert_fusion.1), channel_id=1, source_target_pairs={{0,16},{8,24},{16,0},{24,8},{1,17},{9,25},{17,1},{25,9},{2,18},{10... | collective-permute-start | bytes 294920 | tf_op jit(solution)/shard_map/ppermute | solution.py:92
  55.9 1.6 %collective-permute-done.1 = bf16[64,768]{1,0:T(8,128)(2,1)S(1)} collective-permute-done((bf16[64,768]{1,0:T(8,128)(2,1)S(1)}, bf16[64,768]{1,0:T(8,128)(2,1)S(1)}, u32[]{:S(2)}, u32[]{:S(2)}) %collective-permute-start.1) | collective-permute-done | bytes 98336 | tf_op jit(solution)/shard_map/ppermute | solution.py:92
  58.2 1.4 %collective-permute-done.7 = bf16[64,768]{1,0:T(8,128)(2,1)S(1)} collective-permute-done((bf16[64,768]{1,0:T(8,128)(2,1)S(1)}, bf16[64,768]{1,0:T(8,128)(2,1)S(1)}, u32[]{:S(2)}, u32[]{:S(2)}) %collective-permute-start.7) | collective-permute-done | bytes 98336 | tf_op jit(solution)/shard_map/ppermute | solution.py:92
  59.7 1.6 %collective-permute-done.4 = bf16[64,768]{1,0:T(8,128)(2,1)S(1)} collective-permute-done((bf16[64,768]{1,0:T(8,128)(2,1)S(1)}, bf16[64,768]{1,0:T(8,128)(2,1)S(1)}, u32[]{:S(2)}, u32[]{:S(2)}) %collective-permute-start.4) | collective-permute-done | bytes 98336 | tf_op jit(solution)/shard_map/ppermute | solution.py:92
  61.4 1.4 %collective-permute-done.5 = f32[64,768]{1,0:T(8,128)S(1)} collective-permute-done((f32[64,768]{1,0:T(8,128)S(1)}, f32[64,768]{1,0:T(8,128)S(1)}, u32[]{:S(2)}, u32[]{:S(2)}) %collective-permute-start.5) | collective-permute-done | bytes 196640 | tf_op jit(solution)/shard_map/ppermute | solution.py:95
  63.7 1.0 broadcast_select_fusion.7
  64.7 2.0 %fusion = bf16[1,1280,768]{2,1,0:T(8,128)(2,1)} fusion(bf16[128,1280]{1,0:T(8,128)(2,1)S(1)} %bitcast.91, f32[64,768]{1,0:T(8,128)S(1)} %get-tuple-element.18, f32[64,768]{1,0:T(8,128)S(1)} %get-tuple-element.17, f32[64,768]{1,0:T(8,128)S(1)} %get-tuple-element.16, f32[64,768]{1,0:T(8,128)S(1)} %get-tuple-element.15, f32[64,768]{1,0:T(8,128)S(1)} %get-tuple-element.14, ...), kind=kOutput, calls=%fused_computation.3 | convolution fusion | flops 253919232 | bytes 3473408 | tf_op jit(solution)/shard_map/dot_general | solution.py:209
  66.7 2.0 %fusion.1 = bf16[1,1280,768]{2,1,0:T(8,128)(2,1)} fusion(bf16[128,1280]{1,0:T(8,128)(2,1)S(1)} %bitcast.92, f32[64,768]{1,0:T(8,128)S(1)} %get-tuple-element.14, f32[64,768]{1,0:T(8,128)S(1)} %get-tuple-element.13, f32[64,768]{1,0:T(8,128)S(1)} %get-tuple-element.18, f32[64,768]{1,0:T(8,128)S(1)} %get-tuple-element.17), kind=kOutput, calls=%fused_computation.4 | convolution fusion | flops 253427712 | bytes 3080192 | tf_op jit(solution)/shard_map/dot_general | solution.py:212
  68.7 1.7 %collective-permute-start.16 = (f32[8,1,16]{2,0,1:T(8,128)S(1)}, f32[8,1,16]{2,0,1:T(8,128)S(1)}, u32[]{:S(2)}, u32[]{:S(2)}) collective-permute-start(f32[8,1,16]{2,0,1:T(8,128)S(1)} %add.89), channel_id=1, source_target_pairs={{0,16},{8,24},{16,0},{24,8},{1,17},{9,25},{17,1},{25,9},{2,18},{10... | collective-permute-start | bytes 1544 | tf_op jit(solution)/shard_map/ppermute | solution.py:53
  70.4 2.0 %fusion.2 = bf16[1,768,1280]{2,1,0:T(8,128)(2,1)} fusion(bf16[128,768]{1,0:T(8,128)(2,1)S(1)} %multiply_convert_fusion.4, bf16[128,1280]{1,0:T(8,128)(2,1)S(1)} %copy-done.4), kind=kOutput, calls=%fused_computation.5 | convolution fusion | flops 252641280 | bytes 2490368 | tf_op jit(solution)/shard_map/dot_general | solution.py:215
  72.4 1.4 %fusion.41 = (bf16[1,2,8,16,1280]{4,3,1,0,2:T(8,128)(2,1)S(1)}, bf16[1,2,8,16,1280]{4,3,1,0,2:T(8,128)(2,1)S(1)}) fusion(bf16[2,2,8,16,1280]{4,3,1,0,2:T(8,128)(2,1)} %bitcast.98), kind=kLoop, calls=%fused_computation.100 | loop fusion | bytes 2621440 | tf_op jit(solution)/shard_map/slice | solution.py:183
  76.7 1.7 %collective-permute-start.18 = (bf16[2,128,96]{1,2,0:T(8,128)(2,1)S(1)}, bf16[2,128,96]{1,2,0:T(8,128)(2,1)S(1)}, u32[]{:S(2)}, u32[]{:S(2)}) collective-permute-start(bf16[2,128,96]{1,2,0:T(8,128)(2,1)S(1)} %add_convert_fusion.3), channel_id=1, source_target_pairs={{0,16},{8,24},{16,0},{24,8},{1,17},{9,25},{17,1},{25,9},{2,18},{10... | collective-permute-start | bytes 147464 | tf_op jit(solution)/shard_map/ppermute | solution.py:67
  79.1 1.5 %collective-permute-start.14 = (bf16[2,128,96]{1,2,0:T(8,128)(2,1)S(1)}, bf16[2,128,96]{1,2,0:T(8,128)(2,1)S(1)}, u32[]{:S(2)}, u32[]{:S(2)}) collective-permute-start(bf16[2,128,96]{1,2,0:T(8,128)(2,1)S(1)} %add_convert_fusion.4), channel_id=1, source_target_pairs={{0,16},{8,24},{16,0},{24,8},{1,17},{9,25},{17,1},{25,9},{2,18},{10... | collective-permute-start | bytes 147464 | tf_op jit(solution)/shard_map/ppermute | solution.py:67
  81.3 1.6 %collective-permute-done.12 = bf16[2,128,96]{1,2,0:T(8,128)(2,1)S(1)} collective-permute-done((bf16[2,128,96]{1,2,0:T(8,128)(2,1)S(1)}, bf16[2,128,96]{1,2,0:T(8,128)(2,1)S(1)}, u32[]{:S(2)}, u32[]{:S(2)}) %collective-permute-start.12) | collective-permute-done | bytes 49184 | tf_op jit(solution)/shard_map/ppermute | solution.py:67
  82.9 0.8 collective-permute-done.14
  84.4 0.8 reshape.126
  85.8 3.9 %all-to-all-start.1 = ((f32[8,3,16]{2,1,0:T(4,128)}), f32[8,3,16]{2,1,0:T(4,128)}, u32[]{:S(2)}, u32[]{:S(2)}) async-start(f32[8,3,16]{2,1,0:T(4,128)} %copy.45), calls=%async_computation.1 | async-start | bytes 32768 | tf_op jit(solution)/shard_map/all_to_all | solution.py:234
  89.8 2.1 %fusion.31 = f32[2,1280,96]{1,2,0:T(8,128)} fusion(bf16[2,128,1280]{2,1,0:T(8,128)(2,1)S(1)} %bitcast.87, bf16[2,128,96]{1,2,0:T(8,128)(2,1)} %collective-permute-done.10, bf16[2,128,96]{1,2,0:T(8,128)(2,1)S(1)} %add_convert_fusion.6, bf16[2,128,96]{1,2,0:T(8,128)(2,1)} %copy-done.9, bf16[2,128,96]{1,2,0:T(8,128)(2,1)S(1)} %add_convert_fusion.5, ...), kind=kOutput, calls=%fused_computation.82 | convolution fusion | flops 63381504 | bytes 1933312 | tf_op jit(solution)/shard_map/jrd,jrh->jdh/dot_general | solution.py:220
  91.8 2.1 %fusion.32 = f32[2,1280,96]{1,2,0:T(8,128)} fusion(bf16[2,128,1280]{2,1,0:T(8,128)(2,1)S(1)} %bitcast.88, bf16[2,128,96]{1,2,0:T(8,128)(2,1)} %collective-permute-done.10, bf16[2,128,96]{1,2,0:T(8,128)(2,1)S(1)} %add_convert_fusion.6, bf16[2,128,96]{1,2,0:T(8,128)(2,1)S(1)} %collective-permute-done.14, bf16[2,128,96]{1,2,0:T(8,128)(2,1)S(1)} %add_convert_fusion.4), kind=kOutput, calls=%fused_computation.83 | convolution fusion | flops 63209472 | bytes 1835008 | tf_op jit(solution)/shard_map/jrd,jrh->jdh/dot_general | solution.py:223
  93.9 1.3 %fusion.23 = f32[2,96,1280]{2,1,0:T(8,128)} fusion(bf16[2,128,96]{1,2,0:T(8,128)(2,1)S(1)} %get-tuple-element.8, bf16[2,128,1280]{2,1,0:T(8,128)(2,1)S(1)} %bitcast.95, f32[2,128]{1,0:T(2,128)S(1)} %copy-done.14), kind=kOutput, calls=%fused_computation.29 | convolution fusion | flops 63897600 | bytes 1688576 | tf_op jit(solution)/shard_map/jrh,jrd->jhd/dot_general | solution.py:224
  95.2 1.2 %all-to-all-done.1 = f32[8,3,16]{2,1,0:T(4,128)} async-done(((f32[8,3,16]{2,1,0:T(4,128)}), f32[8,3,16]{2,1,0:T(4,128)}, u32[]{:S(2)}, u32[]{:S(2)}) %all-to-all-start.1) | async-done | bytes 1568 | tf_op jit(solution)/shard_map/all_to_all | solution.py:234
  (136 shorter events, 16.2 us)
Async XLA Ops:
  7.2 40.7 %copy-start = (bf16[1,768,1280]{2,1,0:T(8,128)(2,1)S(1)}, bf16[1,768,1280]{2,1,0:T(8,128)(2,1)}, u32[]{:S(2)}) copy-start(bf16[1,768,1280]{2,1,0:T(8,128)(2,1)} %param.18) | copy-start | bytes 5898244
  8.7 1.6 %copy-start.11 = (s32[10]{0:T(128)}, s32[10]{0:T(128)S(1)}, u32[]{:S(2)}) copy-start(s32[10]{0:T(128)S(1)} %pad_add_fusion) | copy-start | bytes 124
  11.7 1.7 %copy-start.5 = (bf16[256,1280]{1,0:T(8,128)(2,1)S(1)}, bf16[256,1280]{1,0:T(8,128)(2,1)}, u32[]{:S(2)}) copy-start(bf16[256,1280]{1,0:T(8,128)(2,1)} %param.11) | copy-start | bytes 1966084
  14.4 8.3 %slice-start = ((bf16[160,1280]{1,0:T(8,128)(2,1)}), bf16[32,1280]{1,0:T(8,128)(2,1)S(1)}, s32[]{:S(2)}) async-start(bf16[160,1280]{1,0:T(8,128)(2,1)} %copy-done.3), calls=%async_computation.3 | async-start | bytes 163840 | tf_op jit(solution)/shard_map/slice | solution.py:128
  15.3 32.0 %all-to-all-start = ((bf16[8,40,1280]{2,1,0:T(8,128)(2,1)}), bf16[8,40,1280]{2,1,0:T(8,128)(2,1)S(1)}, u32[]{:S(2)}, u32[]{:S(2)}) async-start(bf16[8,40,1280]{2,1,0:T(8,128)(2,1)} %pad_maximum_fusion), calls=%async_computation | async-start | bytes 1638400 | tf_op jit(solution)/shard_map/all_to_all | solution.py:161
  22.6 49.8 %all-gather.3.cloned.1.call-start = ((), (), s32[]{:S(2)}) async-start(), calls=%async_computation.2 | async-start | bytes 1474560 | tf_op jit(solution)/shard_map/all_gather | solution.py:139
  47.7 26.7 %copy-start.13 = (f32[2,128]{1,0:T(2,128)}, f32[2,128]{1,0:T(2,128)S(1)}, u32[]{:S(2)}) copy-start(f32[2,128]{1,0:T(2,128)S(1)} %reshape.130) | copy-start | bytes 3076
  48.7 1.7 %copy-start.2 = (bf16[1,1280,768]{2,1,0:T(8,128)(2,1)S(1)}, bf16[1,1280,768]{2,1,0:T(8,128)(2,1)}, u32[]{:S(2)}) copy-start(bf16[1,1280,768]{2,1,0:T(8,128)(2,1)} %param.17) | copy-start | bytes 5898244
  48.7 3.1 %collective-permute-start = (bf16[64,768]{1,0:T(8,128)(2,1)S(1)}, bf16[64,768]{1,0:T(8,128)(2,1)S(1)}, u32[]{:S(2)}, u32[]{:S(2)}) collective-permute-start(bf16[64,768]{1,0:T(8,128)(2,1)S(1)} %broadcast_select_fusion.8), channel_id=1, source_target_pairs={{0,8},{8,0},{16,24},{24,16},{1,9},{9,1},{17,25},{25,17},{2,10},{10... | collective-permute-start | bytes 294920 | tf_op jit(solution)/shard_map/ppermute | solution.py:86
  49.9 3.8 %collective-permute-start.6 = (bf16[64,768]{1,0:T(8,128)(2,1)S(1)}, bf16[64,768]{1,0:T(8,128)(2,1)S(1)}, u32[]{:S(2)}, u32[]{:S(2)}) collective-permute-start(bf16[64,768]{1,0:T(8,128)(2,1)S(1)} %broadcast_select_fusion.2), channel_id=1, source_target_pairs={{0,8},{8,0},{16,24},{24,16},{1,9},{9,1},{17,25},{25,17},{2,10},{10... | collective-permute-start | bytes 294920 | tf_op jit(solution)/shard_map/ppermute | solution.py:86
  50.8 3.2 %collective-permute-start.3 = (bf16[64,768]{1,0:T(8,128)(2,1)S(1)}, bf16[64,768]{1,0:T(8,128)(2,1)S(1)}, u32[]{:S(2)}, u32[]{:S(2)}) collective-permute-start(bf16[64,768]{1,0:T(8,128)(2,1)S(1)} %broadcast_select_fusion.5), channel_id=1, source_target_pairs={{0,8},{8,0},{16,24},{24,16},{1,9},{9,1},{17,25},{25,17},{2,10},{10... | collective-permute-start | bytes 294920 | tf_op jit(solution)/shard_map/ppermute | solution.py:86
  51.9 5.7 %collective-permute-start.1 = (bf16[64,768]{1,0:T(8,128)(2,1)S(1)}, bf16[64,768]{1,0:T(8,128)(2,1)S(1)}, u32[]{:S(2)}, u32[]{:S(2)}) collective-permute-start(bf16[64,768]{1,0:T(8,128)(2,1)S(1)} %add_convert_fusion.2), channel_id=1, source_target_pairs={{0,16},{8,24},{16,0},{24,8},{1,17},{9,25},{17,1},{25,9},{2,18},{10... | collective-permute-start | bytes 294920 | tf_op jit(solution)/shard_map/ppermute | solution.py:92
  53.7 5.9 %collective-permute-start.7 = (bf16[64,768]{1,0:T(8,128)(2,1)S(1)}, bf16[64,768]{1,0:T(8,128)(2,1)S(1)}, u32[]{:S(2)}, u32[]{:S(2)}) collective-permute-start(bf16[64,768]{1,0:T(8,128)(2,1)S(1)} %add_convert_fusion), channel_id=1, source_target_pairs={{0,16},{8,24},{16,0},{24,8},{1,17},{9,25},{17,1},{25,9},{2,18},{10... | collective-permute-start | bytes 294920 | tf_op jit(solution)/shard_map/ppermute | solution.py:92
  54.1 7.2 %collective-permute-start.4 = (bf16[64,768]{1,0:T(8,128)(2,1)S(1)}, bf16[64,768]{1,0:T(8,128)(2,1)S(1)}, u32[]{:S(2)}, u32[]{:S(2)}) collective-permute-start(bf16[64,768]{1,0:T(8,128)(2,1)S(1)} %add_convert_fusion.1), channel_id=1, source_target_pairs={{0,16},{8,24},{16,0},{24,8},{1,17},{9,25},{17,1},{25,9},{2,18},{10... | collective-permute-start | bytes 294920 | tf_op jit(solution)/shard_map/ppermute | solution.py:92
  58.2 5.5 %collective-permute-start.2 = (f32[64,768]{1,0:T(8,128)}, f32[64,768]{1,0:T(8,128)}, u32[]{:S(2)}, u32[]{:S(2)}) collective-permute-start(f32[64,768]{1,0:T(8,128)} %convert_add_fusion.2), channel_id=1, source_target_pairs={{0,8},{8,0},{16,24},{24,16},{1,9},{9,1},{17,25},{25,17},{2,10},{10... | collective-permute-start | bytes 589832 | tf_op jit(solution)/shard_map/ppermute | solution.py:95
  59.6 1.7 %collective-permute-start.8 = (f32[64,768]{1,0:T(8,128)S(1)}, f32[64,768]{1,0:T(8,128)S(1)}, u32[]{:S(2)}, u32[]{:S(2)}) collective-permute-start(f32[64,768]{1,0:T(8,128)S(1)} %convert_add_fusion), channel_id=1, source_target_pairs={{0,8},{8,0},{16,24},{24,16},{1,9},{9,1},{17,25},{25,17},{2,10},{10... | collective-permute-start | bytes 589832 | tf_op jit(solution)/shard_map/ppermute | solution.py:95
  61.3 1.5 %collective-permute-start.5 = (f32[64,768]{1,0:T(8,128)S(1)}, f32[64,768]{1,0:T(8,128)S(1)}, u32[]{:S(2)}, u32[]{:S(2)}) collective-permute-start(f32[64,768]{1,0:T(8,128)S(1)} %convert_add_fusion.1), channel_id=1, source_target_pairs={{0,8},{8,0},{16,24},{24,16},{1,9},{9,1},{17,25},{25,17},{2,10},{10... | collective-permute-start | bytes 589832 | tf_op jit(solution)/shard_map/ppermute | solution.py:95
  63.6 5.1 %collective-permute-start.15 = (f32[8,1,16]{2,0,1:T(8,128)S(1)}, f32[8,1,16]{2,0,1:T(8,128)S(1)}, u32[]{:S(2)}, u32[]{:S(2)}) collective-permute-start(f32[8,1,16]{2,0,1:T(8,128)S(1)} %reshape.125), channel_id=1, source_target_pairs={{0,8},{8,0},{16,24},{24,16},{1,9},{9,1},{17,25},{25,17},{2,10},{10... | collective-permute-start | bytes 1544 | tf_op jit(solution)/shard_map/ppermute | solution.py:53
  66.7 3.7 %copy-start.4 = (bf16[128,1280]{1,0:T(8,128)(2,1)S(1)}, bf16[128,1280]{1,0:T(8,128)(2,1)}, u32[]{:S(2)}) copy-start(bf16[128,1280]{1,0:T(8,128)(2,1)} %fusion.22) | copy-start | bytes 983044
  68.7 3.7 %collective-permute-start.16 = (f32[8,1,16]{2,0,1:T(8,128)S(1)}, f32[8,1,16]{2,0,1:T(8,128)S(1)}, u32[]{:S(2)}, u32[]{:S(2)}) collective-permute-start(f32[8,1,16]{2,0,1:T(8,128)S(1)} %add.89), channel_id=1, source_target_pairs={{0,16},{8,24},{16,0},{24,8},{1,17},{9,25},{17,1},{25,9},{2,18},{10... | collective-permute-start | bytes 1544 | tf_op jit(solution)/shard_map/ppermute | solution.py:53
  74.3 2.4 %collective-permute-start.17 = (bf16[2,128,96]{1,2,0:T(8,128)(2,1)S(1)}, bf16[2,128,96]{1,2,0:T(8,128)(2,1)S(1)}, u32[]{:S(2)}, u32[]{:S(2)}) collective-permute-start(bf16[2,128,96]{1,2,0:T(8,128)(2,1)S(1)} %convolution_convert_fusion.5), channel_id=1, source_target_pairs={{0,8},{8,0},{16,24},{24,16},{1,9},{9,1},{17,25},{25,17},{2,10},{10... | collective-permute-start | bytes 147464 | tf_op jit(solution)/shard_map/ppermute | solution.py:67
  74.8 5.7 %collective-permute-start.9 = (bf16[2,128,96]{1,2,0:T(8,128)(2,1)S(1)}, bf16[2,128,96]{1,2,0:T(8,128)(2,1)S(1)}, u32[]{:S(2)}, u32[]{:S(2)}) collective-permute-start(bf16[2,128,96]{1,2,0:T(8,128)(2,1)S(1)} %convolution_convert_fusion.8), channel_id=1, source_target_pairs={{0,8},{8,0},{16,24},{24,16},{1,9},{9,1},{17,25},{25,17},{2,10},{10... | collective-permute-start | bytes 147464 | tf_op jit(solution)/shard_map/ppermute | solution.py:67
  76.1 2.3 %collective-permute-start.11 = (bf16[2,128,96]{1,2,0:T(8,128)(2,1)S(1)}, bf16[2,128,96]{1,2,0:T(8,128)(2,1)S(1)}, u32[]{:S(2)}, u32[]{:S(2)}) collective-permute-start(bf16[2,128,96]{1,2,0:T(8,128)(2,1)S(1)} %convolution_convert_fusion.7), channel_id=1, source_target_pairs={{0,8},{8,0},{16,24},{24,16},{1,9},{9,1},{17,25},{25,17},{2,10},{10... | collective-permute-start | bytes 147464 | tf_op jit(solution)/shard_map/ppermute | solution.py:67
  76.2 2.9 %collective-permute-start.13 = (bf16[2,128,96]{1,2,0:T(8,128)(2,1)S(1)}, bf16[2,128,96]{1,2,0:T(8,128)(2,1)S(1)}, u32[]{:S(2)}, u32[]{:S(2)}) collective-permute-start(bf16[2,128,96]{1,2,0:T(8,128)(2,1)S(1)} %convolution_convert_fusion.6), channel_id=1, source_target_pairs={{0,8},{8,0},{16,24},{24,16},{1,9},{9,1},{17,25},{25,17},{2,10},{10... | collective-permute-start | bytes 147464 | tf_op jit(solution)/shard_map/ppermute | solution.py:67
  76.7 4.6 %collective-permute-start.18 = (bf16[2,128,96]{1,2,0:T(8,128)(2,1)S(1)}, bf16[2,128,96]{1,2,0:T(8,128)(2,1)S(1)}, u32[]{:S(2)}, u32[]{:S(2)}) collective-permute-start(bf16[2,128,96]{1,2,0:T(8,128)(2,1)S(1)} %add_convert_fusion.3), channel_id=1, source_target_pairs={{0,16},{8,24},{16,0},{24,8},{1,17},{9,25},{17,1},{25,9},{2,18},{10... | collective-permute-start | bytes 147464 | tf_op jit(solution)/shard_map/ppermute | solution.py:67
  78.4 4.5 %collective-permute-start.12 = (bf16[2,128,96]{1,2,0:T(8,128)(2,1)S(1)}, bf16[2,128,96]{1,2,0:T(8,128)(2,1)S(1)}, u32[]{:S(2)}, u32[]{:S(2)}) collective-permute-start(bf16[2,128,96]{1,2,0:T(8,128)(2,1)S(1)} %add_convert_fusion.5), channel_id=1, source_target_pairs={{0,16},{8,24},{16,0},{24,8},{1,17},{9,25},{17,1},{25,9},{2,18},{10... | collective-permute-start | bytes 147464 | tf_op jit(solution)/shard_map/ppermute | solution.py:67
  79.1 4.6 %collective-permute-start.14 = (bf16[2,128,96]{1,2,0:T(8,128)(2,1)S(1)}, bf16[2,128,96]{1,2,0:T(8,128)(2,1)S(1)}, u32[]{:S(2)}, u32[]{:S(2)}) collective-permute-start(bf16[2,128,96]{1,2,0:T(8,128)(2,1)S(1)} %add_convert_fusion.4), channel_id=1, source_target_pairs={{0,16},{8,24},{16,0},{24,8},{1,17},{9,25},{17,1},{25,9},{2,18},{10... | collective-permute-start | bytes 147464 | tf_op jit(solution)/shard_map/ppermute | solution.py:67
  80.6 9.1 %collective-permute-start.10 = (bf16[2,128,96]{1,2,0:T(8,128)(2,1)S(1)}, bf16[2,128,96]{1,2,0:T(8,128)(2,1)}, u32[]{:S(2)}, u32[]{:S(2)}) collective-permute-start(bf16[2,128,96]{1,2,0:T(8,128)(2,1)S(1)} %add_convert_fusion.6), channel_id=1, source_target_pairs={{0,16},{8,24},{16,0},{24,8},{1,17},{9,25},{17,1},{25,9},{2,18},{10... | collective-permute-start | bytes 147464 | tf_op jit(solution)/shard_map/ppermute | solution.py:67
  85.2 8.7 %copy-start.14 = (f32[2,128]{1,0:T(2,128)S(1)}, f32[2,128]{1,0:T(2,128)}, u32[]{:S(2)}) copy-start(f32[2,128]{1,0:T(2,128)} %copy-done.13) | copy-start | bytes 3076
  85.8 10.5 %all-to-all-start.1 = ((f32[8,3,16]{2,1,0:T(4,128)}), f32[8,3,16]{2,1,0:T(4,128)}, u32[]{:S(2)}, u32[]{:S(2)}) async-start(f32[8,3,16]{2,1,0:T(4,128)} %copy.45), calls=%async_computation.1 | async-start | bytes 32768 | tf_op jit(solution)/shard_map/all_to_all | solution.py:234
  91.8 6.1 %copy-start.10 = (s32[256,6]{0,1:T(8,128)S(1)}, s32[256,6]{0,1:T(8,128)}, u32[]{:S(2)}) copy-start(s32[256,6]{0,1:T(8,128)} %param.14) | copy-start | bytes 18436
  91.8 6.1 %copy-start.12 = (s32[10]{0:T(128)S(1)}, s32[10]{0:T(128)}, u32[]{:S(2)}) copy-start(s32[10]{0:T(128)} %copy-done.11) | copy-start | bytes 124
  (6 other events, 8.3 us)
Sparse Core Ops, SparseCore 0:
  26.2 45.3 all-gather.2

commit v18 on v17

--- a/solution.py
+++ b/solution.py
@@ -92,7 +92,10 @@
         got = lax.ppermute(mine, axis_name, partner)
         sums = [m.astype(jnp.float32) + g.astype(jnp.float32) for m, g in zip(mine, got)]
         bit *= 2
+    sums = [s.astype(jnp.bfloat16) for s in sums]
     other = lax.ppermute(sums, axis_name, swap)
+    sums = [s.astype(jnp.float32) for s in sums]
+    other = [o.astype(jnp.float32) for o in other]
     full = []
     for s, o, a in zip(sums, other, axes):
         first = jnp.where(first_core, s, o)

time: 106 us -> 106 us (level)
  other arithmetic: 11.1 us -> 9.5 us
  transfers between devices with their start and end apart: 22 -> 22, of which waited for: 8 -> 8; matrix products, arithmetic and copies ran while one was open for 20% -> 18% of each run, Pallas kernels for 0% -> 0%
where the time goes in v18:
time: 106 us; the launch traced here: 105 us
  waiting for transfers between devices  33.8 us (32%)
  starting transfers between devices  24 us (23%)
  matrix products  16.6 us (16%)
  between operations  14.6 us (14%)
  other arithmetic  9.5 us (9%)
  local copies, waits for them, and re-layouts  6.34 us (6%)
    all_to_all x1, waiting for transfers between devices, body(): lax.all_to_all(outgoing, 'ep', split_axis=0, concat_axis=0, tiled=True)  23.9 us
    all_to_all x1, starting transfers between devices, body(): lax.all_to_all(outgoing, 'ep', split_axis=0, concat_axis=0, tiled=True)  7.28 us
    ppermute x8, starting transfers between devices, grp_sum_doubling(): got = lax.ppermute(mine, axis_name, partner)  5.73 us
    ppermute x3, waiting for transfers between devices, grp_sum_rounded(): got = lax.ppermute(mine, axis_name, partner)  5.26 us
    ppermute x3, starting transfers between devices, grp_sum_rounded(): got = lax.ppermute(mine, axis_name, partner)  3.96 us
    all_to_all x1, starting transfers between devices, body(): lax.all_to_all(route_parts, 'ep', split_axis=0, concat_axis=0, tiled=True)  3.95 us
    ppermute x8, waiting for transfers between devices, grp_sum_doubling(): got = lax.ppermute(mine, axis_name, partner)  2.47 us
  transfers between devices with their start and end apart: 22, of which 8 were waited for; matrix products, arithmetic and copies ran while one was open for 18% of the time, Pallas kernels for 0%

profile of v18, /device:TPU:0, one launch (start us, length us, event | category | flops | bytes accessed | tf_op | source)
XLA Modules:
  0.0 104.8 jit_solution(10262866289397380139)
XLA Ops:
  7.2 0.8 convert_bitcast_fusion
  8.0 0.7 pad_add_fusion
  8.7 0.8 compare_reduce_fusion
  9.6 0.8 fusion.29
  11.9 1.4 %convolution_convert_fusion.3 = bf16[160,1280]{1,0:T(8,128)(2,1)S(1)} fusion(pred[160,256]{1,0:T(32,128)(4,1)S(1)} %fusion.27, bf16[256,1280]{1,0:T(8,128)(2,1)} %param.12), kind=kOutput, calls=%fused_computation.7 | convolution fusion | flops 105062400 | bytes 1105920 | tf_op jit(solution)/shard_map/dot_general | solution.py:20
  13.6 0.7 copy-done.3
  14.4 0.9 pad_maximum_fusion
  15.3 7.3 %all-to-all-start = ((bf16[8,40,1280]{2,1,0:T(8,128)(2,1)}), bf16[8,40,1280]{2,1,0:T(8,128)(2,1)S(1)}, u32[]{:S(2)}, u32[]{:S(2)}) async-start(bf16[8,40,1280]{2,1,0:T(8,128)(2,1)} %pad_maximum_fusion), calls=%async_computation | async-start | bytes 1638400 | tf_op jit(solution)/shard_map/all_to_all | solution.py:164
  23.4 23.9 %all-to-all-done = bf16[8,40,1280]{2,1,0:T(8,128)(2,1)S(1)} async-done(((bf16[8,40,1280]{2,1,0:T(8,128)(2,1)}), bf16[8,40,1280]{2,1,0:T(8,128)(2,1)S(1)}, u32[]{:S(2)}, u32[]{:S(2)}) %all-to-all-start) | async-done | bytes 819232 | tf_op jit(solution)/shard_map/all_to_all | solution.py:164
  47.9 0.8 fusion.13
  51.0 0.8 fusion.22
  51.9 1.8 %collective-permute-start.1 = (bf16[64,768]{1,0:T(8,128)(2,1)S(1)}, bf16[64,768]{1,0:T(8,128)(2,1)S(1)}, u32[]{:S(2)}, u32[]{:S(2)}) collective-permute-start(bf16[64,768]{1,0:T(8,128)(2,1)S(1)} %add_convert_fusion.5), channel_id=1, source_target_pairs={{0,16},{8,24},{16,0},{24,8},{1,17},{9,25},{17,1},{25,9},{2,18},{10... | collective-permute-start | bytes 294920 | tf_op jit(solution)/shard_map/ppermute | solution.py:92
  54.1 1.8 %collective-permute-start.4 = (bf16[64,768]{1,0:T(8,128)(2,1)S(1)}, bf16[64,768]{1,0:T(8,128)(2,1)S(1)}, u32[]{:S(2)}, u32[]{:S(2)}) collective-permute-start(bf16[64,768]{1,0:T(8,128)(2,1)S(1)} %add_convert_fusion.3), channel_id=1, source_target_pairs={{0,16},{8,24},{16,0},{24,8},{1,17},{9,25},{17,1},{25,9},{2,18},{10... | collective-permute-start | bytes 294920 | tf_op jit(solution)/shard_map/ppermute | solution.py:92
  55.9 1.6 %collective-permute-done.1 = bf16[64,768]{1,0:T(8,128)(2,1)S(1)} collective-permute-done((bf16[64,768]{1,0:T(8,128)(2,1)S(1)}, bf16[64,768]{1,0:T(8,128)(2,1)S(1)}, u32[]{:S(2)}, u32[]{:S(2)}) %collective-permute-start.1) | collective-permute-done | bytes 98336 | tf_op jit(solution)/shard_map/ppermute | solution.py:92
  57.6 3.7 %collective-permute-done.4 = bf16[64,768]{1,0:T(8,128)(2,1)S(1)} collective-permute-done((bf16[64,768]{1,0:T(8,128)(2,1)S(1)}, bf16[64,768]{1,0:T(8,128)(2,1)S(1)}, u32[]{:S(2)}, u32[]{:S(2)}) %collective-permute-start.4) | collective-permute-done | bytes 98336 | tf_op jit(solution)/shard_map/ppermute | solution.py:92
  64.1 2.0 %fusion = bf16[1,1280,768]{2,1,0:T(8,128)(2,1)} fusion(bf16[128,1280]{1,0:T(8,128)(2,1)S(1)} %bitcast.91, f32[64,768]{1,0:T(8,128)S(1)} %get-tuple-element.18, f32[64,768]{1,0:T(8,128)S(1)} %get-tuple-element.17, f32[64,768]{1,0:T(8,128)S(1)} %get-tuple-element.16, f32[64,768]{1,0:T(8,128)S(1)} %get-tuple-element.15, f32[64,768]{1,0:T(8,128)S(1)} %get-tuple-element.14, ...), kind=kOutput, calls=%fused_computation.3 | convolution fusion | flops 253919232 | bytes 3473408 | tf_op jit(solution)/shard_map/dot_general | solution.py:212
  66.1 2.0 %fusion.1 = bf16[1,1280,768]{2,1,0:T(8,128)(2,1)} fusion(bf16[128,1280]{1,0:T(8,128)(2,1)S(1)} %bitcast.92, f32[64,768]{1,0:T(8,128)S(1)} %get-tuple-element.14, f32[64,768]{1,0:T(8,128)S(1)} %get-tuple-element.13, f32[64,768]{1,0:T(8,128)S(1)} %get-tuple-element.18, f32[64,768]{1,0:T(8,128)S(1)} %get-tuple-element.17), kind=kOutput, calls=%fused_computation.4 | convolution fusion | flops 253427712 | bytes 3080192 | tf_op jit(solution)/shard_map/dot_general | solution.py:215
  68.1 1.7 %collective-permute-start.16 = (f32[8,1,16]{2,0,1:T(8,128)S(1)}, f32[8,1,16]{2,0,1:T(8,128)S(1)}, u32[]{:S(2)}, u32[]{:S(2)}) collective-permute-start(f32[8,1,16]{2,0,1:T(8,128)S(1)} %add.89), channel_id=1, source_target_pairs={{0,16},{8,24},{16,0},{24,8},{1,17},{9,25},{17,1},{25,9},{2,18},{10... | collective-permute-start | bytes 1544 | tf_op jit(solution)/shard_map/ppermute | solution.py:53
  69.8 2.0 %fusion.2 = bf16[1,768,1280]{2,1,0:T(8,128)(2,1)} fusion(bf16[128,768]{1,0:T(8,128)(2,1)S(1)} %multiply_convert_fusion.4, bf16[128,1280]{1,0:T(8,128)(2,1)S(1)} %copy-done.4), kind=kOutput, calls=%fused_computation.5 | convolution fusion | flops 252641280 | bytes 2490368 | tf_op jit(solution)/shard_map/dot_general | solution.py:218
  71.8 1.4 %fusion.41 = (bf16[1,2,8,16,1280]{4,3,1,0,2:T(8,128)(2,1)S(1)}, bf16[1,2,8,16,1280]{4,3,1,0,2:T(8,128)(2,1)S(1)}) fusion(bf16[2,2,8,16,1280]{4,3,1,0,2:T(8,128)(2,1)} %bitcast.98), kind=kLoop, calls=%fused_computation.100 | loop fusion | bytes 2621440 | tf_op jit(solution)/shard_map/slice | solution.py:186
  76.1 1.7 %collective-permute-start.18 = (bf16[2,128,96]{1,2,0:T(8,128)(2,1)S(1)}, bf16[2,128,96]{1,2,0:T(8,128)(2,1)S(1)}, u32[]{:S(2)}, u32[]{:S(2)}) collective-permute-start(bf16[2,128,96]{1,2,0:T(8,128)(2,1)S(1)} %add_convert_fusion.6), channel_id=1, source_target_pairs={{0,16},{8,24},{16,0},{24,8},{1,17},{9,25},{17,1},{25,9},{2,18},{10... | collective-permute-start | bytes 147464 | tf_op jit(solution)/shard_map/ppermute | solution.py:67
  78.5 1.5 %collective-permute-start.14 = (bf16[2,128,96]{1,2,0:T(8,128)(2,1)S(1)}, bf16[2,128,96]{1,2,0:T(8,128)(2,1)S(1)}, u32[]{:S(2)}, u32[]{:S(2)}) collective-permute-start(bf16[2,128,96]{1,2,0:T(8,128)(2,1)S(1)} %add_convert_fusion.7), channel_id=1, source_target_pairs={{0,16},{8,24},{16,0},{24,8},{1,17},{9,25},{17,1},{25,9},{2,18},{10... | collective-permute-start | bytes 147464 | tf_op jit(solution)/shard_map/ppermute | solution.py:67
  80.7 1.6 %collective-permute-done.12 = bf16[2,128,96]{1,2,0:T(8,128)(2,1)S(1)} collective-permute-done((bf16[2,128,96]{1,2,0:T(8,128)(2,1)S(1)}, bf16[2,128,96]{1,2,0:T(8,128)(2,1)S(1)}, u32[]{:S(2)}, u32[]{:S(2)}) %collective-permute-start.12) | collective-permute-done | bytes 49184 | tf_op jit(solution)/shard_map/ppermute | solution.py:67
  82.3 0.8 collective-permute-done.14
  83.8 0.8 reshape.126
  85.2 3.9 %all-to-all-start.1 = ((f32[8,3,16]{2,1,0:T(4,128)}), f32[8,3,16]{2,1,0:T(4,128)}, u32[]{:S(2)}, u32[]{:S(2)}) async-start(f32[8,3,16]{2,1,0:T(4,128)} %copy.45), calls=%async_computation.1 | async-start | bytes 32768 | tf_op jit(solution)/shard_map/all_to_all | solution.py:237
  89.1 2.1 %fusion.31 = f32[2,1280,96]{1,2,0:T(8,128)} fusion(bf16[2,128,1280]{2,1,0:T(8,128)(2,1)S(1)} %bitcast.87, bf16[2,128,96]{1,2,0:T(8,128)(2,1)} %collective-permute-done.10, bf16[2,128,96]{1,2,0:T(8,128)(2,1)S(1)} %add_convert_fusion.9, bf16[2,128,96]{1,2,0:T(8,128)(2,1)} %copy-done.9, bf16[2,128,96]{1,2,0:T(8,128)(2,1)S(1)} %add_convert_fusion.8, ...), kind=kOutput, calls=%fused_computation.82 | convolution fusion | flops 63381504 | bytes 1933312 | tf_op jit(solution)/shard_map/jrd,jrh->jdh/dot_general | solution.py:223
  91.2 2.1 %fusion.32 = f32[2,1280,96]{1,2,0:T(8,128)} fusion(bf16[2,128,1280]{2,1,0:T(8,128)(2,1)S(1)} %bitcast.88, bf16[2,128,96]{1,2,0:T(8,128)(2,1)} %collective-permute-done.10, bf16[2,128,96]{1,2,0:T(8,128)(2,1)S(1)} %add_convert_fusion.9, bf16[2,128,96]{1,2,0:T(8,128)(2,1)S(1)} %collective-permute-done.14, bf16[2,128,96]{1,2,0:T(8,128)(2,1)S(1)} %add_convert_fusion.7), kind=kOutput, calls=%fused_computation.83 | convolution fusion | flops 63209472 | bytes 1835008 | tf_op jit(solution)/shard_map/jrd,jrh->jdh/dot_general | solution.py:226
  93.2 1.3 %fusion.23 = f32[2,96,1280]{2,1,0:T(8,128)} fusion(bf16[2,128,96]{1,2,0:T(8,128)(2,1)S(1)} %get-tuple-element.8, bf16[2,128,1280]{2,1,0:T(8,128)(2,1)S(1)} %bitcast.95, f32[2,128]{1,0:T(2,128)S(1)} %copy-done.14), kind=kOutput, calls=%fused_computation.29 | convolution fusion | flops 63897600 | bytes 1688576 | tf_op jit(solution)/shard_map/jrh,jrd->jhd/dot_general | solution.py:227
  94.5 1.2 %all-to-all-done.1 = f32[8,3,16]{2,1,0:T(4,128)} async-done(((f32[8,3,16]{2,1,0:T(4,128)}), f32[8,3,16]{2,1,0:T(4,128)}, u32[]{:S(2)}, u32[]{:S(2)}) %all-to-all-start.1) | async-done | bytes 1568 | tf_op jit(solution)/shard_map/all_to_all | solution.py:237
  95.7 0.7 slice_reduce_fusion.1
  96.4 0.7 slice.89
  (136 shorter events, 15.0 us)
Async XLA Ops:
  7.2 40.7 %copy-start = (bf16[1,768,1280]{2,1,0:T(8,128)(2,1)S(1)}, bf16[1,768,1280]{2,1,0:T(8,128)(2,1)}, u32[]{:S(2)}) copy-start(bf16[1,768,1280]{2,1,0:T(8,128)(2,1)} %param.18) | copy-start | bytes 5898244
  8.7 1.6 %copy-start.11 = (s32[10]{0:T(128)}, s32[10]{0:T(128)S(1)}, u32[]{:S(2)}) copy-start(s32[10]{0:T(128)S(1)} %pad_add_fusion) | copy-start | bytes 124
  11.7 1.7 %copy-start.5 = (bf16[256,1280]{1,0:T(8,128)(2,1)S(1)}, bf16[256,1280]{1,0:T(8,128)(2,1)}, u32[]{:S(2)}) copy-start(bf16[256,1280]{1,0:T(8,128)(2,1)} %param.11) | copy-start | bytes 1966084
  14.4 8.3 %slice-start = ((bf16[160,1280]{1,0:T(8,128)(2,1)}), bf16[32,1280]{1,0:T(8,128)(2,1)S(1)}, s32[]{:S(2)}) async-start(bf16[160,1280]{1,0:T(8,128)(2,1)} %copy-done.3), calls=%async_computation.3 | async-start | bytes 163840 | tf_op jit(solution)/shard_map/slice | solution.py:131
  15.3 32.0 %all-to-all-start = ((bf16[8,40,1280]{2,1,0:T(8,128)(2,1)}), bf16[8,40,1280]{2,1,0:T(8,128)(2,1)S(1)}, u32[]{:S(2)}, u32[]{:S(2)}) async-start(bf16[8,40,1280]{2,1,0:T(8,128)(2,1)} %pad_maximum_fusion), calls=%async_computation | async-start | bytes 1638400 | tf_op jit(solution)/shard_map/all_to_all | solution.py:164
  22.6 49.2 %all-gather.3.cloned.1.call-start = ((), (), s32[]{:S(2)}) async-start(), calls=%async_computation.2 | async-start | bytes 1474560 | tf_op jit(solution)/shard_map/all_gather | solution.py:142
  47.7 26.0 %copy-start.13 = (f32[2,128]{1,0:T(2,128)}, f32[2,128]{1,0:T(2,128)S(1)}, u32[]{:S(2)}) copy-start(f32[2,128]{1,0:T(2,128)S(1)} %reshape.130) | copy-start | bytes 3076
  48.7 1.7 %copy-start.2 = (bf16[1,1280,768]{2,1,0:T(8,128)(2,1)S(1)}, bf16[1,1280,768]{2,1,0:T(8,128)(2,1)}, u32[]{:S(2)}) copy-start(bf16[1,1280,768]{2,1,0:T(8,128)(2,1)} %param.17) | copy-start | bytes 5898244
  48.7 3.1 %collective-permute-start = (bf16[64,768]{1,0:T(8,128)(2,1)S(1)}, bf16[64,768]{1,0:T(8,128)(2,1)S(1)}, u32[]{:S(2)}, u32[]{:S(2)}) collective-permute-start(bf16[64,768]{1,0:T(8,128)(2,1)S(1)} %broadcast_select_fusion.2), channel_id=1, source_target_pairs={{0,8},{8,0},{16,24},{24,16},{1,9},{9,1},{17,25},{25,17},{2,10},{10... | collective-permute-start | bytes 294920 | tf_op jit(solution)/shard_map/ppermute | solution.py:86
  49.9 3.8 %collective-permute-start.6 = (bf16[64,768]{1,0:T(8,128)(2,1)S(1)}, bf16[64,768]{1,0:T(8,128)(2,1)S(1)}, u32[]{:S(2)}, u32[]{:S(2)}) collective-permute-start(bf16[64,768]{1,0:T(8,128)(2,1)S(1)} %broadcast_select_fusion), channel_id=1, source_target_pairs={{0,8},{8,0},{16,24},{24,16},{1,9},{9,1},{17,25},{25,17},{2,10},{10... | collective-permute-start | bytes 294920 | tf_op jit(solution)/shard_map/ppermute | solution.py:86
  50.8 3.2 %collective-permute-start.3 = (bf16[64,768]{1,0:T(8,128)(2,1)S(1)}, bf16[64,768]{1,0:T(8,128)(2,1)S(1)}, u32[]{:S(2)}, u32[]{:S(2)}) collective-permute-start(bf16[64,768]{1,0:T(8,128)(2,1)S(1)} %broadcast_select_fusion.1), channel_id=1, source_target_pairs={{0,8},{8,0},{16,24},{24,16},{1,9},{9,1},{17,25},{25,17},{2,10},{10... | collective-permute-start | bytes 294920 | tf_op jit(solution)/shard_map/ppermute | solution.py:86
  51.9 5.7 %collective-permute-start.1 = (bf16[64,768]{1,0:T(8,128)(2,1)S(1)}, bf16[64,768]{1,0:T(8,128)(2,1)S(1)}, u32[]{:S(2)}, u32[]{:S(2)}) collective-permute-start(bf16[64,768]{1,0:T(8,128)(2,1)S(1)} %add_convert_fusion.5), channel_id=1, source_target_pairs={{0,16},{8,24},{16,0},{24,8},{1,17},{9,25},{17,1},{25,9},{2,18},{10... | collective-permute-start | bytes 294920 | tf_op jit(solution)/shard_map/ppermute | solution.py:92
  53.7 7.7 %collective-permute-start.7 = (bf16[64,768]{1,0:T(8,128)(2,1)S(1)}, bf16[64,768]{1,0:T(8,128)(2,1)S(1)}, u32[]{:S(2)}, u32[]{:S(2)}) collective-permute-start(bf16[64,768]{1,0:T(8,128)(2,1)S(1)} %add_convert_fusion.1), channel_id=1, source_target_pairs={{0,16},{8,24},{16,0},{24,8},{1,17},{9,25},{17,1},{25,9},{2,18},{10... | collective-permute-start | bytes 294920 | tf_op jit(solution)/shard_map/ppermute | solution.py:92
  54.1 7.2 %collective-permute-start.4 = (bf16[64,768]{1,0:T(8,128)(2,1)S(1)}, bf16[64,768]{1,0:T(8,128)(2,1)S(1)}, u32[]{:S(2)}, u32[]{:S(2)}) collective-permute-start(bf16[64,768]{1,0:T(8,128)(2,1)S(1)} %add_convert_fusion.3), channel_id=1, source_target_pairs={{0,16},{8,24},{16,0},{24,8},{1,17},{9,25},{17,1},{25,9},{2,18},{10... | collective-permute-start | bytes 294920 | tf_op jit(solution)/shard_map/ppermute | solution.py:92
  57.5 6.5 %collective-permute-start.2 = (bf16[64,768]{1,0:T(8,128)(2,1)S(1)}, bf16[64,768]{1,0:T(8,128)(2,1)S(1)}, u32[]{:S(2)}, u32[]{:S(2)}) collective-permute-start(bf16[64,768]{1,0:T(8,128)(2,1)S(1)} %add_convert_fusion.4), channel_id=1, source_target_pairs={{0,8},{8,0},{16,24},{24,16},{1,9},{9,1},{17,25},{25,17},{2,10},{10... | collective-permute-start | bytes 294920 | tf_op jit(solution)/shard_map/ppermute | solution.py:96
  61.3 1.4 %collective-permute-start.5 = (bf16[64,768]{1,0:T(8,128)(2,1)S(1)}, bf16[64,768]{1,0:T(8,128)(2,1)S(1)}, u32[]{:S(2)}, u32[]{:S(2)}) collective-permute-start(bf16[64,768]{1,0:T(8,128)(2,1)S(1)} %add_convert_fusion.2), channel_id=1, source_target_pairs={{0,8},{8,0},{16,24},{24,16},{1,9},{9,1},{17,25},{25,17},{2,10},{10... | collective-permute-start | bytes 294920 | tf_op jit(solution)/shard_map/ppermute | solution.py:96
  61.4 1.5 %collective-permute-start.8 = (bf16[64,768]{1,0:T(8,128)(2,1)S(1)}, bf16[64,768]{1,0:T(8,128)(2,1)S(1)}, u32[]{:S(2)}, u32[]{:S(2)}) collective-permute-start(bf16[64,768]{1,0:T(8,128)(2,1)S(1)} %add_convert_fusion), channel_id=1, source_target_pairs={{0,8},{8,0},{16,24},{24,16},{1,9},{9,1},{17,25},{25,17},{2,10},{10... | collective-permute-start | bytes 294920 | tf_op jit(solution)/shard_map/ppermute | solution.py:96
  63.7 4.4 %collective-permute-start.15 = (f32[8,1,16]{2,0,1:T(8,128)S(1)}, f32[8,1,16]{2,0,1:T(8,128)S(1)}, u32[]{:S(2)}, u32[]{:S(2)}) collective-permute-start(f32[8,1,16]{2,0,1:T(8,128)S(1)} %reshape.125), channel_id=1, source_target_pairs={{0,8},{8,0},{16,24},{24,16},{1,9},{9,1},{17,25},{25,17},{2,10},{10... | collective-permute-start | bytes 1544 | tf_op jit(solution)/shard_map/ppermute | solution.py:53
  66.1 3.7 %copy-start.4 = (bf16[128,1280]{1,0:T(8,128)(2,1)S(1)}, bf16[128,1280]{1,0:T(8,128)(2,1)}, u32[]{:S(2)}) copy-start(bf16[128,1280]{1,0:T(8,128)(2,1)} %fusion.22) | copy-start | bytes 983044
  68.1 3.7 %collective-permute-start.16 = (f32[8,1,16]{2,0,1:T(8,128)S(1)}, f32[8,1,16]{2,0,1:T(8,128)S(1)}, u32[]{:S(2)}, u32[]{:S(2)}) collective-permute-start(f32[8,1,16]{2,0,1:T(8,128)S(1)} %add.89), channel_id=1, source_target_pairs={{0,16},{8,24},{16,0},{24,8},{1,17},{9,25},{17,1},{25,9},{2,18},{10... | collective-permute-start | bytes 1544 | tf_op jit(solution)/shard_map/ppermute | solution.py:53
  73.7 2.4 %collective-permute-start.17 = (bf16[2,128,96]{1,2,0:T(8,128)(2,1)S(1)}, bf16[2,128,96]{1,2,0:T(8,128)(2,1)S(1)}, u32[]{:S(2)}, u32[]{:S(2)}) collective-permute-start(bf16[2,128,96]{1,2,0:T(8,128)(2,1)S(1)} %convolution_convert_fusion.5), channel_id=1, source_target_pairs={{0,8},{8,0},{16,24},{24,16},{1,9},{9,1},{17,25},{25,17},{2,10},{10... | collective-permute-start | bytes 147464 | tf_op jit(solution)/shard_map/ppermute | solution.py:67
  74.2 5.8 %collective-permute-start.9 = (bf16[2,128,96]{1,2,0:T(8,128)(2,1)S(1)}, bf16[2,128,96]{1,2,0:T(8,128)(2,1)S(1)}, u32[]{:S(2)}, u32[]{:S(2)}) collective-permute-start(bf16[2,128,96]{1,2,0:T(8,128)(2,1)S(1)} %convolution_convert_fusion.8), channel_id=1, source_target_pairs={{0,8},{8,0},{16,24},{24,16},{1,9},{9,1},{17,25},{25,17},{2,10},{10... | collective-permute-start | bytes 147464 | tf_op jit(solution)/shard_map/ppermute | solution.py:67
  75.5 2.3 %collective-permute-start.11 = (bf16[2,128,96]{1,2,0:T(8,128)(2,1)S(1)}, bf16[2,128,96]{1,2,0:T(8,128)(2,1)S(1)}, u32[]{:S(2)}, u32[]{:S(2)}) collective-permute-start(bf16[2,128,96]{1,2,0:T(8,128)(2,1)S(1)} %convolution_convert_fusion.7), channel_id=1, source_target_pairs={{0,8},{8,0},{16,24},{24,16},{1,9},{9,1},{17,25},{25,17},{2,10},{10... | collective-permute-start | bytes 147464 | tf_op jit(solution)/shard_map/ppermute | solution.py:67
  75.6 2.9 %collective-permute-start.13 = (bf16[2,128,96]{1,2,0:T(8,128)(2,1)S(1)}, bf16[2,128,96]{1,2,0:T(8,128)(2,1)S(1)}, u32[]{:S(2)}, u32[]{:S(2)}) collective-permute-start(bf16[2,128,96]{1,2,0:T(8,128)(2,1)S(1)} %convolution_convert_fusion.6), channel_id=1, source_target_pairs={{0,8},{8,0},{16,24},{24,16},{1,9},{9,1},{17,25},{25,17},{2,10},{10... | collective-permute-start | bytes 147464 | tf_op jit(solution)/shard_map/ppermute | solution.py:67
  76.1 4.6 %collective-permute-start.18 = (bf16[2,128,96]{1,2,0:T(8,128)(2,1)S(1)}, bf16[2,128,96]{1,2,0:T(8,128)(2,1)S(1)}, u32[]{:S(2)}, u32[]{:S(2)}) collective-permute-start(bf16[2,128,96]{1,2,0:T(8,128)(2,1)S(1)} %add_convert_fusion.6), channel_id=1, source_target_pairs={{0,16},{8,24},{16,0},{24,8},{1,17},{9,25},{17,1},{25,9},{2,18},{10... | collective-permute-start | bytes 147464 | tf_op jit(solution)/shard_map/ppermute | solution.py:67
  77.8 4.5 %collective-permute-start.12 = (bf16[2,128,96]{1,2,0:T(8,128)(2,1)S(1)}, bf16[2,128,96]{1,2,0:T(8,128)(2,1)S(1)}, u32[]{:S(2)}, u32[]{:S(2)}) collective-permute-start(bf16[2,128,96]{1,2,0:T(8,128)(2,1)S(1)} %add_convert_fusion.8), channel_id=1, source_target_pairs={{0,16},{8,24},{16,0},{24,8},{1,17},{9,25},{17,1},{25,9},{2,18},{10... | collective-permute-start | bytes 147464 | tf_op jit(solution)/shard_map/ppermute | solution.py:67
  78.5 4.6 %collective-permute-start.14 = (bf16[2,128,96]{1,2,0:T(8,128)(2,1)S(1)}, bf16[2,128,96]{1,2,0:T(8,128)(2,1)S(1)}, u32[]{:S(2)}, u32[]{:S(2)}) collective-permute-start(bf16[2,128,96]{1,2,0:T(8,128)(2,1)S(1)} %add_convert_fusion.7), channel_id=1, source_target_pairs={{0,16},{8,24},{16,0},{24,8},{1,17},{9,25},{17,1},{25,9},{2,18},{10... | collective-permute-start | bytes 147464 | tf_op jit(solution)/shard_map/ppermute | solution.py:67
  80.0 9.1 %collective-permute-start.10 = (bf16[2,128,96]{1,2,0:T(8,128)(2,1)S(1)}, bf16[2,128,96]{1,2,0:T(8,128)(2,1)}, u32[]{:S(2)}, u32[]{:S(2)}) collective-permute-start(bf16[2,128,96]{1,2,0:T(8,128)(2,1)S(1)} %add_convert_fusion.9), channel_id=1, source_target_pairs={{0,16},{8,24},{16,0},{24,8},{1,17},{9,25},{17,1},{25,9},{2,18},{10... | collective-permute-start | bytes 147464 | tf_op jit(solution)/shard_map/ppermute | solution.py:67
  84.5 8.7 %copy-start.14 = (f32[2,128]{1,0:T(2,128)S(1)}, f32[2,128]{1,0:T(2,128)}, u32[]{:S(2)}) copy-start(f32[2,128]{1,0:T(2,128)} %copy-done.13) | copy-start | bytes 3076
  85.2 10.5 %all-to-all-start.1 = ((f32[8,3,16]{2,1,0:T(4,128)}), f32[8,3,16]{2,1,0:T(4,128)}, u32[]{:S(2)}, u32[]{:S(2)}) async-start(f32[8,3,16]{2,1,0:T(4,128)} %copy.45), calls=%async_computation.1 | async-start | bytes 32768 | tf_op jit(solution)/shard_map/all_to_all | solution.py:237
  91.2 6.1 %copy-start.10 = (s32[256,6]{0,1:T(8,128)S(1)}, s32[256,6]{0,1:T(8,128)}, u32[]{:S(2)}) copy-start(s32[256,6]{0,1:T(8,128)} %param.14) | copy-start | bytes 18436
  91.2 6.1 %copy-start.12 = (s32[10]{0:T(128)S(1)}, s32[10]{0:T(128)}, u32[]{:S(2)}) copy-start(s32[10]{0:T(128)} %copy-done.11) | copy-start | bytes 124
  (6 other events, 8.3 us)
Sparse Core Ops, SparseCore 0:
  26.2 45.3 all-gather.2

commit v19 on v17

--- a/solution.py
+++ b/solution.py
@@ -139,7 +139,6 @@
     gathered = lax.all_gather(hot_outgoing, "ep", axis=0, tiled=False)
     scale_width = capacity + hot_rows
     cold_lines = -(-scale_width // slice_width)
-    cold_lines = -(-cold_lines // 8) * 8
     both_scales = jnp.concatenate(
         [
             cold_scale.reshape(cold_count, capacity),

time: 106 us -> 106 us (level)
  no operation moved by 1% of the time
where the time goes in v19:
time: 106 us; the launch traced here: 105 us
  waiting for transfers between devices  33.8 us (32%)
  starting transfers between devices  23 us (22%)
  matrix products  16.6 us (16%)
  between operations  14.5 us (14%)
  other arithmetic  11.2 us (11%)
  local copies, waits for them, and re-layouts  6.32 us (6%)
    all_to_all x1, waiting for transfers between devices, body(): lax.all_to_all(outgoing, 'ep', split_axis=0, concat_axis=0, tiled=True)  24 us
    all_to_all x1, starting transfers between devices, body(): lax.all_to_all(outgoing, 'ep', split_axis=0, concat_axis=0, tiled=True)  7.28 us
    ppermute x8, starting transfers between devices, grp_sum_doubling(): got = lax.ppermute(mine, axis_name, partner)  5.74 us
    ppermute x3, waiting for transfers between devices, grp_sum_rounded(): got = lax.ppermute(mine, axis_name, partner)  4.69 us
    all_to_all x1, starting transfers between devices, body(): lax.all_to_all(route_parts, 'ep', split_axis=0, concat_axis=0, tiled=True)  3.95 us
    ppermute x3, starting transfers between devices, grp_sum_rounded(): got = lax.ppermute(mine, axis_name, partner)  3.82 us
    ppermute x8, waiting for transfers between devices, grp_sum_doubling(): got = lax.ppermute(mine, axis_name, partner)  2.47 us
  transfers between devices with their start and end apart: 22, of which 8 were waited for; matrix products, arithmetic and copies ran while one was open for 20% of the time, Pallas kernels for 0%

profile of v19, /device:TPU:0, one launch (start us, length us, event | category | flops | bytes accessed | tf_op | source)
XLA Modules:
  0.0 105.5 jit_solution(12798226910506745463)
XLA Ops:
  7.2 0.8 convert_bitcast_fusion
  8.8 0.8 compare_reduce_fusion
  9.6 0.8 fusion.29
  11.9 1.4 %convolution_convert_fusion.3 = bf16[160,1280]{1,0:T(8,128)(2,1)S(1)} fusion(pred[160,256]{1,0:T(32,128)(4,1)S(1)} %fusion.27, bf16[256,1280]{1,0:T(8,128)(2,1)} %param.12), kind=kOutput, calls=%fused_computation.7 | convolution fusion | flops 105062400 | bytes 1105920 | tf_op jit(solution)/shard_map/dot_general | solution.py:20
  13.6 0.7 copy-done.3
  14.4 1.0 pad_maximum_fusion
  15.4 7.3 %all-to-all-start = ((bf16[8,33,1280]{2,1,0:T(8,128)(2,1)}), bf16[8,33,1280]{2,1,0:T(8,128)(2,1)S(1)}, u32[]{:S(2)}, u32[]{:S(2)}) async-start(bf16[8,33,1280]{2,1,0:T(8,128)(2,1)} %pad_maximum_fusion), calls=%async_computation | async-start | bytes 1638400 | tf_op jit(solution)/shard_map/all_to_all | solution.py:160
  23.4 24.0 %all-to-all-done = bf16[8,33,1280]{2,1,0:T(8,128)(2,1)S(1)} async-done(((bf16[8,33,1280]{2,1,0:T(8,128)(2,1)}), bf16[8,33,1280]{2,1,0:T(8,128)(2,1)S(1)}, u32[]{:S(2)}, u32[]{:S(2)}) %all-to-all-start) | async-done | bytes 675872 | tf_op jit(solution)/shard_map/all_to_all | solution.py:160
  48.0 0.8 fusion.13
  51.1 0.8 fusion.22
  52.0 1.7 %collective-permute-start.1 = (bf16[64,768]{1,0:T(8,128)(2,1)S(1)}, bf16[64,768]{1,0:T(8,128)(2,1)S(1)}, u32[]{:S(2)}, u32[]{:S(2)}) collective-permute-start(bf16[64,768]{1,0:T(8,128)(2,1)S(1)} %add_convert_fusion.2), channel_id=1, source_target_pairs={{0,16},{8,24},{16,0},{24,8},{1,17},{9,25},{17,1},{25,9},{2,18},{10... | collective-permute-start | bytes 294920 | tf_op jit(solution)/shard_map/ppermute | solution.py:92
  54.2 1.7 %collective-permute-start.4 = (bf16[64,768]{1,0:T(8,128)(2,1)S(1)}, bf16[64,768]{1,0:T(8,128)(2,1)S(1)}, u32[]{:S(2)}, u32[]{:S(2)}) collective-permute-start(bf16[64,768]{1,0:T(8,128)(2,1)S(1)} %add_convert_fusion.1), channel_id=1, source_target_pairs={{0,16},{8,24},{16,0},{24,8},{1,17},{9,25},{17,1},{25,9},{2,18},{10... | collective-permute-start | bytes 294920 | tf_op jit(solution)/shard_map/ppermute | solution.py:92
  55.9 1.8 %collective-permute-done.1 = bf16[64,768]{1,0:T(8,128)(2,1)S(1)} collective-permute-done((bf16[64,768]{1,0:T(8,128)(2,1)S(1)}, bf16[64,768]{1,0:T(8,128)(2,1)S(1)}, u32[]{:S(2)}, u32[]{:S(2)}) %collective-permute-start.1) | collective-permute-done | bytes 98336 | tf_op jit(solution)/shard_map/ppermute | solution.py:92
  58.3 1.4 %collective-permute-done.7 = bf16[64,768]{1,0:T(8,128)(2,1)S(1)} collective-permute-done((bf16[64,768]{1,0:T(8,128)(2,1)S(1)}, bf16[64,768]{1,0:T(8,128)(2,1)S(1)}, u32[]{:S(2)}, u32[]{:S(2)}) %collective-permute-start.7) | collective-permute-done | bytes 98336 | tf_op jit(solution)/shard_map/ppermute | solution.py:92
  59.9 1.5 %collective-permute-done.4 = bf16[64,768]{1,0:T(8,128)(2,1)S(1)} collective-permute-done((bf16[64,768]{1,0:T(8,128)(2,1)S(1)}, bf16[64,768]{1,0:T(8,128)(2,1)S(1)}, u32[]{:S(2)}, u32[]{:S(2)}) %collective-permute-start.4) | collective-permute-done | bytes 98336 | tf_op jit(solution)/shard_map/ppermute | solution.py:92
  61.6 1.4 %collective-permute-done.5 = f32[64,768]{1,0:T(8,128)S(1)} collective-permute-done((f32[64,768]{1,0:T(8,128)S(1)}, f32[64,768]{1,0:T(8,128)S(1)}, u32[]{:S(2)}, u32[]{:S(2)}) %collective-permute-start.5) | collective-permute-done | bytes 196640 | tf_op jit(solution)/shard_map/ppermute | solution.py:95
  63.9 1.0 broadcast_select_fusion.7
  64.8 2.0 %fusion = bf16[1,1280,768]{2,1,0:T(8,128)(2,1)} fusion(bf16[128,1280]{1,0:T(8,128)(2,1)S(1)} %bitcast.89, f32[64,768]{1,0:T(8,128)S(1)} %get-tuple-element.18, f32[64,768]{1,0:T(8,128)S(1)} %get-tuple-element.17, f32[64,768]{1,0:T(8,128)S(1)} %get-tuple-element.16, f32[64,768]{1,0:T(8,128)S(1)} %get-tuple-element.15, f32[64,768]{1,0:T(8,128)S(1)} %get-tuple-element.14, ...), kind=kOutput, calls=%fused_computation.3 | convolution fusion | flops 253919232 | bytes 3473408 | tf_op jit(solution)/shard_map/dot_general | solution.py:208
  66.8 2.0 %fusion.1 = bf16[1,1280,768]{2,1,0:T(8,128)(2,1)} fusion(bf16[128,1280]{1,0:T(8,128)(2,1)S(1)} %bitcast.90, f32[64,768]{1,0:T(8,128)S(1)} %get-tuple-element.14, f32[64,768]{1,0:T(8,128)S(1)} %get-tuple-element.13, f32[64,768]{1,0:T(8,128)S(1)} %get-tuple-element.18, f32[64,768]{1,0:T(8,128)S(1)} %get-tuple-element.17), kind=kOutput, calls=%fused_computation.4 | convolution fusion | flops 253427712 | bytes 3080192 | tf_op jit(solution)/shard_map/dot_general | solution.py:211
  68.8 1.6 %collective-permute-start.16 = (f32[8,1,16]{2,0,1:T(8,128)S(1)}, f32[8,1,16]{2,0,1:T(8,128)S(1)}, u32[]{:S(2)}, u32[]{:S(2)}) collective-permute-start(f32[8,1,16]{2,0,1:T(8,128)S(1)} %add.89), channel_id=1, source_target_pairs={{0,16},{8,24},{16,0},{24,8},{1,17},{9,25},{17,1},{25,9},{2,18},{10... | collective-permute-start | bytes 1544 | tf_op jit(solution)/shard_map/ppermute | solution.py:53
  70.4 2.0 %fusion.2 = bf16[1,768,1280]{2,1,0:T(8,128)(2,1)} fusion(bf16[128,768]{1,0:T(8,128)(2,1)S(1)} %multiply_convert_fusion.4, bf16[128,1280]{1,0:T(8,128)(2,1)S(1)} %copy-done.4), kind=kOutput, calls=%fused_computation.5 | convolution fusion | flops 252641280 | bytes 2490368 | tf_op jit(solution)/shard_map/dot_general | solution.py:214
  72.4 1.4 %fusion.41 = (bf16[1,2,8,16,1280]{4,3,1,0,2:T(8,128)(2,1)S(1)}, bf16[1,2,8,16,1280]{4,3,1,0,2:T(8,128)(2,1)S(1)}) fusion(bf16[2,2,8,16,1280]{4,3,1,0,2:T(8,128)(2,1)} %bitcast.96), kind=kLoop, calls=%fused_computation.100 | loop fusion | bytes 2621440 | tf_op jit(solution)/shard_map/slice | solution.py:182
  76.7 1.7 %collective-permute-start.18 = (bf16[2,128,96]{1,2,0:T(8,128)(2,1)S(1)}, bf16[2,128,96]{1,2,0:T(8,128)(2,1)S(1)}, u32[]{:S(2)}, u32[]{:S(2)}) collective-permute-start(bf16[2,128,96]{1,2,0:T(8,128)(2,1)S(1)} %add_convert_fusion.3), channel_id=1, source_target_pairs={{0,16},{8,24},{16,0},{24,8},{1,17},{9,25},{17,1},{25,9},{2,18},{10... | collective-permute-start | bytes 147464 | tf_op jit(solution)/shard_map/ppermute | solution.py:67
  79.1 1.5 %collective-permute-start.14 = (bf16[2,128,96]{1,2,0:T(8,128)(2,1)S(1)}, bf16[2,128,96]{1,2,0:T(8,128)(2,1)S(1)}, u32[]{:S(2)}, u32[]{:S(2)}) collective-permute-start(bf16[2,128,96]{1,2,0:T(8,128)(2,1)S(1)} %add_convert_fusion.4), channel_id=1, source_target_pairs={{0,16},{8,24},{16,0},{24,8},{1,17},{9,25},{17,1},{25,9},{2,18},{10... | collective-permute-start | bytes 147464 | tf_op jit(solution)/shard_map/ppermute | solution.py:67
  81.3 1.6 %collective-permute-done.12 = bf16[2,128,96]{1,2,0:T(8,128)(2,1)S(1)} collective-permute-done((bf16[2,128,96]{1,2,0:T(8,128)(2,1)S(1)}, bf16[2,128,96]{1,2,0:T(8,128)(2,1)S(1)}, u32[]{:S(2)}, u32[]{:S(2)}) %collective-permute-start.12) | collective-permute-done | bytes 49184 | tf_op jit(solution)/shard_map/ppermute | solution.py:67
  82.9 0.8 collective-permute-done.14
  84.4 0.8 reshape.126
  85.8 3.9 %all-to-all-start.1 = ((f32[8,3,16]{2,1,0:T(4,128)}), f32[8,3,16]{2,1,0:T(4,128)}, u32[]{:S(2)}, u32[]{:S(2)}) async-start(f32[8,3,16]{2,1,0:T(4,128)} %copy.58), calls=%async_computation.1 | async-start | bytes 32768 | tf_op jit(solution)/shard_map/all_to_all | solution.py:233
  89.8 2.1 %fusion.31 = f32[2,1280,96]{1,2,0:T(8,128)} fusion(bf16[2,128,1280]{2,1,0:T(8,128)(2,1)S(1)} %bitcast.85, bf16[2,128,96]{1,2,0:T(8,128)(2,1)} %collective-permute-done.10, bf16[2,128,96]{1,2,0:T(8,128)(2,1)S(1)} %add_convert_fusion.6, bf16[2,128,96]{1,2,0:T(8,128)(2,1)} %copy-done.9, bf16[2,128,96]{1,2,0:T(8,128)(2,1)S(1)} %add_convert_fusion.5, ...), kind=kOutput, calls=%fused_computation.80 | convolution fusion | flops 63381504 | bytes 1933312 | tf_op jit(solution)/shard_map/jrd,jrh->jdh/dot_general | solution.py:219
  91.8 2.1 %fusion.32 = f32[2,1280,96]{1,2,0:T(8,128)} fusion(bf16[2,128,1280]{2,1,0:T(8,128)(2,1)S(1)} %bitcast.86, bf16[2,128,96]{1,2,0:T(8,128)(2,1)} %collective-permute-done.10, bf16[2,128,96]{1,2,0:T(8,128)(2,1)S(1)} %add_convert_fusion.6, bf16[2,128,96]{1,2,0:T(8,128)(2,1)S(1)} %collective-permute-done.14, bf16[2,128,96]{1,2,0:T(8,128)(2,1)S(1)} %add_convert_fusion.4), kind=kOutput, calls=%fused_computation.81 | convolution fusion | flops 63209472 | bytes 1835008 | tf_op jit(solution)/shard_map/jrd,jrh->jdh/dot_general | solution.py:222
  93.9 1.3 %fusion.23 = f32[2,96,1280]{2,1,0:T(8,128)} fusion(bf16[2,128,96]{1,2,0:T(8,128)(2,1)S(1)} %get-tuple-element.8, bf16[2,128,1280]{2,1,0:T(8,128)(2,1)S(1)} %bitcast.93, f32[2,128]{1,0:T(2,128)S(1)} %copy-done.14), kind=kOutput, calls=%fused_computation.29 | convolution fusion | flops 63897600 | bytes 1688576 | tf_op jit(solution)/shard_map/jrh,jrd->jhd/dot_general | solution.py:223
  95.2 1.2 %all-to-all-done.1 = f32[8,3,16]{2,1,0:T(4,128)} async-done(((f32[8,3,16]{2,1,0:T(4,128)}), f32[8,3,16]{2,1,0:T(4,128)}, u32[]{:S(2)}, u32[]{:S(2)}) %all-to-all-start.1) | async-done | bytes 1568 | tf_op jit(solution)/shard_map/all_to_all | solution.py:233
  (136 shorter events, 16.3 us)
Async XLA Ops:
  7.2 40.8 %copy-start = (bf16[1,768,1280]{2,1,0:T(8,128)(2,1)S(1)}, bf16[1,768,1280]{2,1,0:T(8,128)(2,1)}, u32[]{:S(2)}) copy-start(bf16[1,768,1280]{2,1,0:T(8,128)(2,1)} %param.18) | copy-start | bytes 5898244
  7.2 6.1 %copy-start.5 = (bf16[256,1280]{1,0:T(8,128)(2,1)S(1)}, bf16[256,1280]{1,0:T(8,128)(2,1)}, u32[]{:S(2)}) copy-start(bf16[256,1280]{1,0:T(8,128)(2,1)} %param.11) | copy-start | bytes 1966084
  8.8 1.6 %copy-start.11 = (s32[10]{0:T(128)}, s32[10]{0:T(128)S(1)}, u32[]{:S(2)}) copy-start(s32[10]{0:T(128)S(1)} %pad_add_fusion) | copy-start | bytes 124
  14.4 8.3 %slice-start = ((bf16[160,1280]{1,0:T(8,128)(2,1)}), bf16[32,1280]{1,0:T(8,128)(2,1)S(1)}, s32[]{:S(2)}) async-start(bf16[160,1280]{1,0:T(8,128)(2,1)} %copy-done.3), calls=%async_computation.3 | async-start | bytes 163840 | tf_op jit(solution)/shard_map/slice | solution.py:128
  15.4 32.1 %all-to-all-start = ((bf16[8,33,1280]{2,1,0:T(8,128)(2,1)}), bf16[8,33,1280]{2,1,0:T(8,128)(2,1)S(1)}, u32[]{:S(2)}, u32[]{:S(2)}) async-start(bf16[8,33,1280]{2,1,0:T(8,128)(2,1)} %pad_maximum_fusion), calls=%async_computation | async-start | bytes 1638400 | tf_op jit(solution)/shard_map/all_to_all | solution.py:160
  22.7 49.8 %all-gather.3.cloned.1.call-start = ((), (), s32[]{:S(2)}) async-start(), calls=%async_computation.2 | async-start | bytes 1474560 | tf_op jit(solution)/shard_map/all_gather | solution.py:139
  47.8 26.6 %copy-start.13 = (f32[2,128]{1,0:T(2,128)}, f32[2,128]{1,0:T(2,128)S(1)}, u32[]{:S(2)}) copy-start(f32[2,128]{1,0:T(2,128)S(1)} %reshape.130) | copy-start | bytes 3076
  48.8 1.7 %copy-start.2 = (bf16[1,1280,768]{2,1,0:T(8,128)(2,1)S(1)}, bf16[1,1280,768]{2,1,0:T(8,128)(2,1)}, u32[]{:S(2)}) copy-start(bf16[1,1280,768]{2,1,0:T(8,128)(2,1)} %param.17) | copy-start | bytes 5898244
  48.8 3.1 %collective-permute-start = (bf16[64,768]{1,0:T(8,128)(2,1)S(1)}, bf16[64,768]{1,0:T(8,128)(2,1)S(1)}, u32[]{:S(2)}, u32[]{:S(2)}) collective-permute-start(bf16[64,768]{1,0:T(8,128)(2,1)S(1)} %broadcast_select_fusion.8), channel_id=1, source_target_pairs={{0,8},{8,0},{16,24},{24,16},{1,9},{9,1},{17,25},{25,17},{2,10},{10... | collective-permute-start | bytes 294920 | tf_op jit(solution)/shard_map/ppermute | solution.py:86
  50.0 3.7 %collective-permute-start.6 = (bf16[64,768]{1,0:T(8,128)(2,1)S(1)}, bf16[64,768]{1,0:T(8,128)(2,1)S(1)}, u32[]{:S(2)}, u32[]{:S(2)}) collective-permute-start(bf16[64,768]{1,0:T(8,128)(2,1)S(1)} %broadcast_select_fusion.2), channel_id=1, source_target_pairs={{0,8},{8,0},{16,24},{24,16},{1,9},{9,1},{17,25},{25,17},{2,10},{10... | collective-permute-start | bytes 294920 | tf_op jit(solution)/shard_map/ppermute | solution.py:86
  51.0 3.2 %collective-permute-start.3 = (bf16[64,768]{1,0:T(8,128)(2,1)S(1)}, bf16[64,768]{1,0:T(8,128)(2,1)S(1)}, u32[]{:S(2)}, u32[]{:S(2)}) collective-permute-start(bf16[64,768]{1,0:T(8,128)(2,1)S(1)} %broadcast_select_fusion.5), channel_id=1, source_target_pairs={{0,8},{8,0},{16,24},{24,16},{1,9},{9,1},{17,25},{25,17},{2,10},{10... | collective-permute-start | bytes 294920 | tf_op jit(solution)/shard_map/ppermute | solution.py:86
  52.0 5.7 %collective-permute-start.1 = (bf16[64,768]{1,0:T(8,128)(2,1)S(1)}, bf16[64,768]{1,0:T(8,128)(2,1)S(1)}, u32[]{:S(2)}, u32[]{:S(2)}) collective-permute-start(bf16[64,768]{1,0:T(8,128)(2,1)S(1)} %add_convert_fusion.2), channel_id=1, source_target_pairs={{0,16},{8,24},{16,0},{24,8},{1,17},{9,25},{17,1},{25,9},{2,18},{10... | collective-permute-start | bytes 294920 | tf_op jit(solution)/shard_map/ppermute | solution.py:92
  53.7 6.1 %collective-permute-start.7 = (bf16[64,768]{1,0:T(8,128)(2,1)S(1)}, bf16[64,768]{1,0:T(8,128)(2,1)S(1)}, u32[]{:S(2)}, u32[]{:S(2)}) collective-permute-start(bf16[64,768]{1,0:T(8,128)(2,1)S(1)} %add_convert_fusion), channel_id=1, source_target_pairs={{0,16},{8,24},{16,0},{24,8},{1,17},{9,25},{17,1},{25,9},{2,18},{10... | collective-permute-start | bytes 294920 | tf_op jit(solution)/shard_map/ppermute | solution.py:92
  54.2 7.2 %collective-permute-start.4 = (bf16[64,768]{1,0:T(8,128)(2,1)S(1)}, bf16[64,768]{1,0:T(8,128)(2,1)S(1)}, u32[]{:S(2)}, u32[]{:S(2)}) collective-permute-start(bf16[64,768]{1,0:T(8,128)(2,1)S(1)} %add_convert_fusion.1), channel_id=1, source_target_pairs={{0,16},{8,24},{16,0},{24,8},{1,17},{9,25},{17,1},{25,9},{2,18},{10... | collective-permute-start | bytes 294920 | tf_op jit(solution)/shard_map/ppermute | solution.py:92
  58.3 5.5 %collective-permute-start.2 = (f32[64,768]{1,0:T(8,128)}, f32[64,768]{1,0:T(8,128)}, u32[]{:S(2)}, u32[]{:S(2)}) collective-permute-start(f32[64,768]{1,0:T(8,128)} %convert_add_fusion.2), channel_id=1, source_target_pairs={{0,8},{8,0},{16,24},{24,16},{1,9},{9,1},{17,25},{25,17},{2,10},{10... | collective-permute-start | bytes 589832 | tf_op jit(solution)/shard_map/ppermute | solution.py:95
  59.8 1.7 %collective-permute-start.8 = (f32[64,768]{1,0:T(8,128)S(1)}, f32[64,768]{1,0:T(8,128)S(1)}, u32[]{:S(2)}, u32[]{:S(2)}) collective-permute-start(f32[64,768]{1,0:T(8,128)S(1)} %convert_add_fusion), channel_id=1, source_target_pairs={{0,8},{8,0},{16,24},{24,16},{1,9},{9,1},{17,25},{25,17},{2,10},{10... | collective-permute-start | bytes 589832 | tf_op jit(solution)/shard_map/ppermute | solution.py:95
  61.4 1.5 %collective-permute-start.5 = (f32[64,768]{1,0:T(8,128)S(1)}, f32[64,768]{1,0:T(8,128)S(1)}, u32[]{:S(2)}, u32[]{:S(2)}) collective-permute-start(f32[64,768]{1,0:T(8,128)S(1)} %convert_add_fusion.1), channel_id=1, source_target_pairs={{0,8},{8,0},{16,24},{24,16},{1,9},{9,1},{17,25},{25,17},{2,10},{10... | collective-permute-start | bytes 589832 | tf_op jit(solution)/shard_map/ppermute | solution.py:95
  63.7 5.1 %collective-permute-start.15 = (f32[8,1,16]{2,0,1:T(8,128)S(1)}, f32[8,1,16]{2,0,1:T(8,128)S(1)}, u32[]{:S(2)}, u32[]{:S(2)}) collective-permute-start(f32[8,1,16]{2,0,1:T(8,128)S(1)} %reshape.125), channel_id=1, source_target_pairs={{0,8},{8,0},{16,24},{24,16},{1,9},{9,1},{17,25},{25,17},{2,10},{10... | collective-permute-start | bytes 1544 | tf_op jit(solution)/shard_map/ppermute | solution.py:53
  66.8 3.6 %copy-start.4 = (bf16[128,1280]{1,0:T(8,128)(2,1)S(1)}, bf16[128,1280]{1,0:T(8,128)(2,1)}, u32[]{:S(2)}) copy-start(bf16[128,1280]{1,0:T(8,128)(2,1)} %fusion.22) | copy-start | bytes 983044
  68.8 3.6 %collective-permute-start.16 = (f32[8,1,16]{2,0,1:T(8,128)S(1)}, f32[8,1,16]{2,0,1:T(8,128)S(1)}, u32[]{:S(2)}, u32[]{:S(2)}) collective-permute-start(f32[8,1,16]{2,0,1:T(8,128)S(1)} %add.89), channel_id=1, source_target_pairs={{0,16},{8,24},{16,0},{24,8},{1,17},{9,25},{17,1},{25,9},{2,18},{10... | collective-permute-start | bytes 1544 | tf_op jit(solution)/shard_map/ppermute | solution.py:53
  74.3 2.4 %collective-permute-start.17 = (bf16[2,128,96]{1,2,0:T(8,128)(2,1)S(1)}, bf16[2,128,96]{1,2,0:T(8,128)(2,1)S(1)}, u32[]{:S(2)}, u32[]{:S(2)}) collective-permute-start(bf16[2,128,96]{1,2,0:T(8,128)(2,1)S(1)} %convolution_convert_fusion.5), channel_id=1, source_target_pairs={{0,8},{8,0},{16,24},{24,16},{1,9},{9,1},{17,25},{25,17},{2,10},{10... | collective-permute-start | bytes 147464 | tf_op jit(solution)/shard_map/ppermute | solution.py:67
  74.9 5.8 %collective-permute-start.9 = (bf16[2,128,96]{1,2,0:T(8,128)(2,1)S(1)}, bf16[2,128,96]{1,2,0:T(8,128)(2,1)S(1)}, u32[]{:S(2)}, u32[]{:S(2)}) collective-permute-start(bf16[2,128,96]{1,2,0:T(8,128)(2,1)S(1)} %convolution_convert_fusion.8), channel_id=1, source_target_pairs={{0,8},{8,0},{16,24},{24,16},{1,9},{9,1},{17,25},{25,17},{2,10},{10... | collective-permute-start | bytes 147464 | tf_op jit(solution)/shard_map/ppermute | solution.py:67
  76.1 2.3 %collective-permute-start.11 = (bf16[2,128,96]{1,2,0:T(8,128)(2,1)S(1)}, bf16[2,128,96]{1,2,0:T(8,128)(2,1)S(1)}, u32[]{:S(2)}, u32[]{:S(2)}) collective-permute-start(bf16[2,128,96]{1,2,0:T(8,128)(2,1)S(1)} %convolution_convert_fusion.7), channel_id=1, source_target_pairs={{0,8},{8,0},{16,24},{24,16},{1,9},{9,1},{17,25},{25,17},{2,10},{10... | collective-permute-start | bytes 147464 | tf_op jit(solution)/shard_map/ppermute | solution.py:67
  76.3 2.9 %collective-permute-start.13 = (bf16[2,128,96]{1,2,0:T(8,128)(2,1)S(1)}, bf16[2,128,96]{1,2,0:T(8,128)(2,1)S(1)}, u32[]{:S(2)}, u32[]{:S(2)}) collective-permute-start(bf16[2,128,96]{1,2,0:T(8,128)(2,1)S(1)} %convolution_convert_fusion.6), channel_id=1, source_target_pairs={{0,8},{8,0},{16,24},{24,16},{1,9},{9,1},{17,25},{25,17},{2,10},{10... | collective-permute-start | bytes 147464 | tf_op jit(solution)/shard_map/ppermute | solution.py:67
  76.7 4.6 %collective-permute-start.18 = (bf16[2,128,96]{1,2,0:T(8,128)(2,1)S(1)}, bf16[2,128,96]{1,2,0:T(8,128)(2,1)S(1)}, u32[]{:S(2)}, u32[]{:S(2)}) collective-permute-start(bf16[2,128,96]{1,2,0:T(8,128)(2,1)S(1)} %add_convert_fusion.3), channel_id=1, source_target_pairs={{0,16},{8,24},{16,0},{24,8},{1,17},{9,25},{17,1},{25,9},{2,18},{10... | collective-permute-start | bytes 147464 | tf_op jit(solution)/shard_map/ppermute | solution.py:67
  78.4 4.5 %collective-permute-start.12 = (bf16[2,128,96]{1,2,0:T(8,128)(2,1)S(1)}, bf16[2,128,96]{1,2,0:T(8,128)(2,1)S(1)}, u32[]{:S(2)}, u32[]{:S(2)}) collective-permute-start(bf16[2,128,96]{1,2,0:T(8,128)(2,1)S(1)} %add_convert_fusion.5), channel_id=1, source_target_pairs={{0,16},{8,24},{16,0},{24,8},{1,17},{9,25},{17,1},{25,9},{2,18},{10... | collective-permute-start | bytes 147464 | tf_op jit(solution)/shard_map/ppermute | solution.py:67
  79.1 4.6 %collective-permute-start.14 = (bf16[2,128,96]{1,2,0:T(8,128)(2,1)S(1)}, bf16[2,128,96]{1,2,0:T(8,128)(2,1)S(1)}, u32[]{:S(2)}, u32[]{:S(2)}) collective-permute-start(bf16[2,128,96]{1,2,0:T(8,128)(2,1)S(1)} %add_convert_fusion.4), channel_id=1, source_target_pairs={{0,16},{8,24},{16,0},{24,8},{1,17},{9,25},{17,1},{25,9},{2,18},{10... | collective-permute-start | bytes 147464 | tf_op jit(solution)/shard_map/ppermute | solution.py:67
  80.6 9.1 %collective-permute-start.10 = (bf16[2,128,96]{1,2,0:T(8,128)(2,1)S(1)}, bf16[2,128,96]{1,2,0:T(8,128)(2,1)}, u32[]{:S(2)}, u32[]{:S(2)}) collective-permute-start(bf16[2,128,96]{1,2,0:T(8,128)(2,1)S(1)} %add_convert_fusion.6), channel_id=1, source_target_pairs={{0,16},{8,24},{16,0},{24,8},{1,17},{9,25},{17,1},{25,9},{2,18},{10... | collective-permute-start | bytes 147464 | tf_op jit(solution)/shard_map/ppermute | solution.py:67
  85.2 8.7 %copy-start.14 = (f32[2,128]{1,0:T(2,128)S(1)}, f32[2,128]{1,0:T(2,128)}, u32[]{:S(2)}) copy-start(f32[2,128]{1,0:T(2,128)} %copy-done.13) | copy-start | bytes 3076
  85.8 10.5 %all-to-all-start.1 = ((f32[8,3,16]{2,1,0:T(4,128)}), f32[8,3,16]{2,1,0:T(4,128)}, u32[]{:S(2)}, u32[]{:S(2)}) async-start(f32[8,3,16]{2,1,0:T(4,128)} %copy.58), calls=%async_computation.1 | async-start | bytes 32768 | tf_op jit(solution)/shard_map/all_to_all | solution.py:233
  91.8 6.1 %copy-start.10 = (s32[256,6]{0,1:T(8,128)S(1)}, s32[256,6]{0,1:T(8,128)}, u32[]{:S(2)}) copy-start(s32[256,6]{0,1:T(8,128)} %param.14) | copy-start | bytes 18436
  91.8 6.1 %copy-start.12 = (s32[10]{0:T(128)S(1)}, s32[10]{0:T(128)}, u32[]{:S(2)}) copy-start(s32[10]{0:T(128)} %copy-done.11) | copy-start | bytes 124
  (6 other events, 8.3 us)
Sparse Core Ops, SparseCore 0:
  26.2 45.5 all-gather.2

commit v20 on v18

--- a/solution.py
+++ b/solution.py
@@ -142,7 +142,6 @@
     gathered = lax.all_gather(hot_outgoing, "ep", axis=0, tiled=False)
     scale_width = capacity + hot_rows
     cold_lines = -(-scale_width // slice_width)
-    cold_lines = -(-cold_lines // 8) * 8
     both_scales = jnp.concatenate(
         [
             cold_scale.reshape(cold_count, capacity),

time: 106 us -> 106 us (level)
  no operation moved by 1% of the time
where the time goes in v20:
time: 106 us; the launch traced here: 105 us
  waiting for transfers between devices  34 us (32%)
  starting transfers between devices  23.8 us (22%)
  matrix products  16.7 us (16%)
  between operations  14.6 us (14%)
  other arithmetic  9.53 us (9%)
  local copies, waits for them, and re-layouts  6.32 us (6%)
    all_to_all x1, waiting for transfers between devices, body(): lax.all_to_all(outgoing, 'ep', split_axis=0, concat_axis=0, tiled=True)  24 us
    all_to_all x1, starting transfers between devices, body(): lax.all_to_all(outgoing, 'ep', split_axis=0, concat_axis=0, tiled=True)  7.28 us
    ppermute x8, starting transfers between devices, grp_sum_doubling(): got = lax.ppermute(mine, axis_name, partner)  5.73 us
    ppermute x3, waiting for transfers between devices, grp_sum_rounded(): got = lax.ppermute(mine, axis_name, partner)  5.39 us
    all_to_all x1, starting transfers between devices, body(): lax.all_to_all(route_parts, 'ep', split_axis=0, concat_axis=0, tiled=True)  3.95 us
    ppermute x3, starting transfers between devices, grp_sum_rounded(): got = lax.ppermute(mine, axis_name, partner)  3.82 us
    ppermute x8, waiting for transfers between devices, grp_sum_doubling(): got = lax.ppermute(mine, axis_name, partner)  2.47 us
  transfers between devices with their start and end apart: 22, of which 8 were waited for; matrix products, arithmetic and copies ran while one was open for 18% of the time, Pallas kernels for 0%

profile of v20, /device:TPU:0, one launch (start us, length us, event | category | flops | bytes accessed | tf_op | source)
XLA Modules:
  0.0 104.9 jit_solution(15397376212951195937)
XLA Ops:
  7.2 0.8 convert_bitcast_fusion
  8.0 0.7 pad_add_fusion
  8.8 0.8 compare_reduce_fusion
  9.6 0.8 fusion.29
  11.9 1.4 %convolution_convert_fusion.3 = bf16[160,1280]{1,0:T(8,128)(2,1)S(1)} fusion(pred[160,256]{1,0:T(32,128)(4,1)S(1)} %fusion.27, bf16[256,1280]{1,0:T(8,128)(2,1)} %param.12), kind=kOutput, calls=%fused_computation.7 | convolution fusion | flops 105062400 | bytes 1105920 | tf_op jit(solution)/shard_map/dot_general | solution.py:20
  13.6 0.7 copy-done.3
  14.4 1.0 pad_maximum_fusion
  15.4 7.3 %all-to-all-start = ((bf16[8,33,1280]{2,1,0:T(8,128)(2,1)}), bf16[8,33,1280]{2,1,0:T(8,128)(2,1)S(1)}, u32[]{:S(2)}, u32[]{:S(2)}) async-start(bf16[8,33,1280]{2,1,0:T(8,128)(2,1)} %pad_maximum_fusion), calls=%async_computation | async-start | bytes 1638400 | tf_op jit(solution)/shard_map/all_to_all | solution.py:163
  23.4 24.0 %all-to-all-done = bf16[8,33,1280]{2,1,0:T(8,128)(2,1)S(1)} async-done(((bf16[8,33,1280]{2,1,0:T(8,128)(2,1)}), bf16[8,33,1280]{2,1,0:T(8,128)(2,1)S(1)}, u32[]{:S(2)}, u32[]{:S(2)}) %all-to-all-start) | async-done | bytes 675872 | tf_op jit(solution)/shard_map/all_to_all | solution.py:163
  48.0 0.8 fusion.13
  51.1 0.8 fusion.22
  52.0 1.7 %collective-permute-start.1 = (bf16[64,768]{1,0:T(8,128)(2,1)S(1)}, bf16[64,768]{1,0:T(8,128)(2,1)S(1)}, u32[]{:S(2)}, u32[]{:S(2)}) collective-permute-start(bf16[64,768]{1,0:T(8,128)(2,1)S(1)} %add_convert_fusion.5), channel_id=1, source_target_pairs={{0,16},{8,24},{16,0},{24,8},{1,17},{9,25},{17,1},{25,9},{2,18},{10... | collective-permute-start | bytes 294920 | tf_op jit(solution)/shard_map/ppermute | solution.py:92
  54.2 1.7 %collective-permute-start.4 = (bf16[64,768]{1,0:T(8,128)(2,1)S(1)}, bf16[64,768]{1,0:T(8,128)(2,1)S(1)}, u32[]{:S(2)}, u32[]{:S(2)}) collective-permute-start(bf16[64,768]{1,0:T(8,128)(2,1)S(1)} %add_convert_fusion.3), channel_id=1, source_target_pairs={{0,16},{8,24},{16,0},{24,8},{1,17},{9,25},{17,1},{25,9},{2,18},{10... | collective-permute-start | bytes 294920 | tf_op jit(solution)/shard_map/ppermute | solution.py:92
  55.9 1.8 %collective-permute-done.1 = bf16[64,768]{1,0:T(8,128)(2,1)S(1)} collective-permute-done((bf16[64,768]{1,0:T(8,128)(2,1)S(1)}, bf16[64,768]{1,0:T(8,128)(2,1)S(1)}, u32[]{:S(2)}, u32[]{:S(2)}) %collective-permute-start.1) | collective-permute-done | bytes 98336 | tf_op jit(solution)/shard_map/ppermute | solution.py:92
  57.8 3.6 %collective-permute-done.4 = bf16[64,768]{1,0:T(8,128)(2,1)S(1)} collective-permute-done((bf16[64,768]{1,0:T(8,128)(2,1)S(1)}, bf16[64,768]{1,0:T(8,128)(2,1)S(1)}, u32[]{:S(2)}, u32[]{:S(2)}) %collective-permute-start.4) | collective-permute-done | bytes 98336 | tf_op jit(solution)/shard_map/ppermute | solution.py:92
  64.2 2.0 %fusion = bf16[1,1280,768]{2,1,0:T(8,128)(2,1)} fusion(bf16[128,1280]{1,0:T(8,128)(2,1)S(1)} %bitcast.89, f32[64,768]{1,0:T(8,128)S(1)} %get-tuple-element.18, f32[64,768]{1,0:T(8,128)S(1)} %get-tuple-element.17, f32[64,768]{1,0:T(8,128)S(1)} %get-tuple-element.16, f32[64,768]{1,0:T(8,128)S(1)} %get-tuple-element.15, f32[64,768]{1,0:T(8,128)S(1)} %get-tuple-element.14, ...), kind=kOutput, calls=%fused_computation.3 | convolution fusion | flops 253919232 | bytes 3473408 | tf_op jit(solution)/shard_map/dot_general | solution.py:211
  66.2 2.0 %fusion.1 = bf16[1,1280,768]{2,1,0:T(8,128)(2,1)} fusion(bf16[128,1280]{1,0:T(8,128)(2,1)S(1)} %bitcast.90, f32[64,768]{1,0:T(8,128)S(1)} %get-tuple-element.14, f32[64,768]{1,0:T(8,128)S(1)} %get-tuple-element.13, f32[64,768]{1,0:T(8,128)S(1)} %get-tuple-element.18, f32[64,768]{1,0:T(8,128)S(1)} %get-tuple-element.17), kind=kOutput, calls=%fused_computation.4 | convolution fusion | flops 253427712 | bytes 3080192 | tf_op jit(solution)/shard_map/dot_general | solution.py:214
  68.2 1.6 %collective-permute-start.16 = (f32[8,1,16]{2,0,1:T(8,128)S(1)}, f32[8,1,16]{2,0,1:T(8,128)S(1)}, u32[]{:S(2)}, u32[]{:S(2)}) collective-permute-start(f32[8,1,16]{2,0,1:T(8,128)S(1)} %add.89), channel_id=1, source_target_pairs={{0,16},{8,24},{16,0},{24,8},{1,17},{9,25},{17,1},{25,9},{2,18},{10... | collective-permute-start | bytes 1544 | tf_op jit(solution)/shard_map/ppermute | solution.py:53
  69.8 2.0 %fusion.2 = bf16[1,768,1280]{2,1,0:T(8,128)(2,1)} fusion(bf16[128,768]{1,0:T(8,128)(2,1)S(1)} %multiply_convert_fusion.4, bf16[128,1280]{1,0:T(8,128)(2,1)S(1)} %copy-done.4), kind=kOutput, calls=%fused_computation.5 | convolution fusion | flops 252641280 | bytes 2490368 | tf_op jit(solution)/shard_map/dot_general | solution.py:217
  71.8 1.4 %fusion.41 = (bf16[1,2,8,16,1280]{4,3,1,0,2:T(8,128)(2,1)S(1)}, bf16[1,2,8,16,1280]{4,3,1,0,2:T(8,128)(2,1)S(1)}) fusion(bf16[2,2,8,16,1280]{4,3,1,0,2:T(8,128)(2,1)} %bitcast.96), kind=kLoop, calls=%fused_computation.100 | loop fusion | bytes 2621440 | tf_op jit(solution)/shard_map/slice | solution.py:185
  76.1 1.7 %collective-permute-start.18 = (bf16[2,128,96]{1,2,0:T(8,128)(2,1)S(1)}, bf16[2,128,96]{1,2,0:T(8,128)(2,1)S(1)}, u32[]{:S(2)}, u32[]{:S(2)}) collective-permute-start(bf16[2,128,96]{1,2,0:T(8,128)(2,1)S(1)} %add_convert_fusion.6), channel_id=1, source_target_pairs={{0,16},{8,24},{16,0},{24,8},{1,17},{9,25},{17,1},{25,9},{2,18},{10... | collective-permute-start | bytes 147464 | tf_op jit(solution)/shard_map/ppermute | solution.py:67
  78.5 1.5 %collective-permute-start.14 = (bf16[2,128,96]{1,2,0:T(8,128)(2,1)S(1)}, bf16[2,128,96]{1,2,0:T(8,128)(2,1)S(1)}, u32[]{:S(2)}, u32[]{:S(2)}) collective-permute-start(bf16[2,128,96]{1,2,0:T(8,128)(2,1)S(1)} %add_convert_fusion.7), channel_id=1, source_target_pairs={{0,16},{8,24},{16,0},{24,8},{1,17},{9,25},{17,1},{25,9},{2,18},{10... | collective-permute-start | bytes 147464 | tf_op jit(solution)/shard_map/ppermute | solution.py:67
  80.7 1.6 %collective-permute-done.12 = bf16[2,128,96]{1,2,0:T(8,128)(2,1)S(1)} collective-permute-done((bf16[2,128,96]{1,2,0:T(8,128)(2,1)S(1)}, bf16[2,128,96]{1,2,0:T(8,128)(2,1)S(1)}, u32[]{:S(2)}, u32[]{:S(2)}) %collective-permute-start.12) | collective-permute-done | bytes 49184 | tf_op jit(solution)/shard_map/ppermute | solution.py:67
  82.3 0.8 collective-permute-done.14
  83.8 0.8 reshape.126
  85.2 3.9 %all-to-all-start.1 = ((f32[8,3,16]{2,1,0:T(4,128)}), f32[8,3,16]{2,1,0:T(4,128)}, u32[]{:S(2)}, u32[]{:S(2)}) async-start(f32[8,3,16]{2,1,0:T(4,128)} %copy.58), calls=%async_computation.1 | async-start | bytes 32768 | tf_op jit(solution)/shard_map/all_to_all | solution.py:236
  89.2 2.1 %fusion.31 = f32[2,1280,96]{1,2,0:T(8,128)} fusion(bf16[2,128,1280]{2,1,0:T(8,128)(2,1)S(1)} %bitcast.85, bf16[2,128,96]{1,2,0:T(8,128)(2,1)} %collective-permute-done.10, bf16[2,128,96]{1,2,0:T(8,128)(2,1)S(1)} %add_convert_fusion.9, bf16[2,128,96]{1,2,0:T(8,128)(2,1)} %copy-done.9, bf16[2,128,96]{1,2,0:T(8,128)(2,1)S(1)} %add_convert_fusion.8, ...), kind=kOutput, calls=%fused_computation.80 | convolution fusion | flops 63381504 | bytes 1933312 | tf_op jit(solution)/shard_map/jrd,jrh->jdh/dot_general | solution.py:222
  91.2 2.1 %fusion.32 = f32[2,1280,96]{1,2,0:T(8,128)} fusion(bf16[2,128,1280]{2,1,0:T(8,128)(2,1)S(1)} %bitcast.86, bf16[2,128,96]{1,2,0:T(8,128)(2,1)} %collective-permute-done.10, bf16[2,128,96]{1,2,0:T(8,128)(2,1)S(1)} %add_convert_fusion.9, bf16[2,128,96]{1,2,0:T(8,128)(2,1)S(1)} %collective-permute-done.14, bf16[2,128,96]{1,2,0:T(8,128)(2,1)S(1)} %add_convert_fusion.7), kind=kOutput, calls=%fused_computation.81 | convolution fusion | flops 63209472 | bytes 1835008 | tf_op jit(solution)/shard_map/jrd,jrh->jdh/dot_general | solution.py:225
  93.3 1.3 %fusion.23 = f32[2,96,1280]{2,1,0:T(8,128)} fusion(bf16[2,128,96]{1,2,0:T(8,128)(2,1)S(1)} %get-tuple-element.8, bf16[2,128,1280]{2,1,0:T(8,128)(2,1)S(1)} %bitcast.93, f32[2,128]{1,0:T(2,128)S(1)} %copy-done.14), kind=kOutput, calls=%fused_computation.29 | convolution fusion | flops 63897600 | bytes 1688576 | tf_op jit(solution)/shard_map/jrh,jrd->jhd/dot_general | solution.py:226
  94.6 1.2 %all-to-all-done.1 = f32[8,3,16]{2,1,0:T(4,128)} async-done(((f32[8,3,16]{2,1,0:T(4,128)}), f32[8,3,16]{2,1,0:T(4,128)}, u32[]{:S(2)}, u32[]{:S(2)}) %all-to-all-start.1) | async-done | bytes 1568 | tf_op jit(solution)/shard_map/all_to_all | solution.py:236
  95.7 0.7 slice_reduce_fusion.1
  96.5 0.7 slice.89
  (136 shorter events, 15.1 us)
Async XLA Ops:
  7.2 40.8 %copy-start = (bf16[1,768,1280]{2,1,0:T(8,128)(2,1)S(1)}, bf16[1,768,1280]{2,1,0:T(8,128)(2,1)}, u32[]{:S(2)}) copy-start(bf16[1,768,1280]{2,1,0:T(8,128)(2,1)} %param.18) | copy-start | bytes 5898244
  7.2 6.1 %copy-start.5 = (bf16[256,1280]{1,0:T(8,128)(2,1)S(1)}, bf16[256,1280]{1,0:T(8,128)(2,1)}, u32[]{:S(2)}) copy-start(bf16[256,1280]{1,0:T(8,128)(2,1)} %param.11) | copy-start | bytes 1966084
  8.8 1.6 %copy-start.11 = (s32[10]{0:T(128)}, s32[10]{0:T(128)S(1)}, u32[]{:S(2)}) copy-start(s32[10]{0:T(128)S(1)} %pad_add_fusion) | copy-start | bytes 124
  14.4 8.3 %slice-start = ((bf16[160,1280]{1,0:T(8,128)(2,1)}), bf16[32,1280]{1,0:T(8,128)(2,1)S(1)}, s32[]{:S(2)}) async-start(bf16[160,1280]{1,0:T(8,128)(2,1)} %copy-done.3), calls=%async_computation.3 | async-start | bytes 163840 | tf_op jit(solution)/shard_map/slice | solution.py:131
  15.4 32.1 %all-to-all-start = ((bf16[8,33,1280]{2,1,0:T(8,128)(2,1)}), bf16[8,33,1280]{2,1,0:T(8,128)(2,1)S(1)}, u32[]{:S(2)}, u32[]{:S(2)}) async-start(bf16[8,33,1280]{2,1,0:T(8,128)(2,1)} %pad_maximum_fusion), calls=%async_computation | async-start | bytes 1638400 | tf_op jit(solution)/shard_map/all_to_all | solution.py:163
  22.7 49.2 %all-gather.3.cloned.1.call-start = ((), (), s32[]{:S(2)}) async-start(), calls=%async_computation.2 | async-start | bytes 1474560 | tf_op jit(solution)/shard_map/all_gather | solution.py:142
  47.8 25.9 %copy-start.13 = (f32[2,128]{1,0:T(2,128)}, f32[2,128]{1,0:T(2,128)S(1)}, u32[]{:S(2)}) copy-start(f32[2,128]{1,0:T(2,128)S(1)} %reshape.130) | copy-start | bytes 3076
  48.8 1.7 %copy-start.2 = (bf16[1,1280,768]{2,1,0:T(8,128)(2,1)S(1)}, bf16[1,1280,768]{2,1,0:T(8,128)(2,1)}, u32[]{:S(2)}) copy-start(bf16[1,1280,768]{2,1,0:T(8,128)(2,1)} %param.17) | copy-start | bytes 5898244
  48.8 3.1 %collective-permute-start = (bf16[64,768]{1,0:T(8,128)(2,1)S(1)}, bf16[64,768]{1,0:T(8,128)(2,1)S(1)}, u32[]{:S(2)}, u32[]{:S(2)}) collective-permute-start(bf16[64,768]{1,0:T(8,128)(2,1)S(1)} %broadcast_select_fusion.2), channel_id=1, source_target_pairs={{0,8},{8,0},{16,24},{24,16},{1,9},{9,1},{17,25},{25,17},{2,10},{10... | collective-permute-start | bytes 294920 | tf_op jit(solution)/shard_map/ppermute | solution.py:86
  50.0 3.7 %collective-permute-start.6 = (bf16[64,768]{1,0:T(8,128)(2,1)S(1)}, bf16[64,768]{1,0:T(8,128)(2,1)S(1)}, u32[]{:S(2)}, u32[]{:S(2)}) collective-permute-start(bf16[64,768]{1,0:T(8,128)(2,1)S(1)} %broadcast_select_fusion), channel_id=1, source_target_pairs={{0,8},{8,0},{16,24},{24,16},{1,9},{9,1},{17,25},{25,17},{2,10},{10... | collective-permute-start | bytes 294920 | tf_op jit(solution)/shard_map/ppermute | solution.py:86
  51.0 3.2 %collective-permute-start.3 = (bf16[64,768]{1,0:T(8,128)(2,1)S(1)}, bf16[64,768]{1,0:T(8,128)(2,1)S(1)}, u32[]{:S(2)}, u32[]{:S(2)}) collective-permute-start(bf16[64,768]{1,0:T(8,128)(2,1)S(1)} %broadcast_select_fusion.1), channel_id=1, source_target_pairs={{0,8},{8,0},{16,24},{24,16},{1,9},{9,1},{17,25},{25,17},{2,10},{10... | collective-permute-start | bytes 294920 | tf_op jit(solution)/shard_map/ppermute | solution.py:86
  52.0 5.7 %collective-permute-start.1 = (bf16[64,768]{1,0:T(8,128)(2,1)S(1)}, bf16[64,768]{1,0:T(8,128)(2,1)S(1)}, u32[]{:S(2)}, u32[]{:S(2)}) collective-permute-start(bf16[64,768]{1,0:T(8,128)(2,1)S(1)} %add_convert_fusion.5), channel_id=1, source_target_pairs={{0,16},{8,24},{16,0},{24,8},{1,17},{9,25},{17,1},{25,9},{2,18},{10... | collective-permute-start | bytes 294920 | tf_op jit(solution)/shard_map/ppermute | solution.py:92
  53.7 7.8 %collective-permute-start.7 = (bf16[64,768]{1,0:T(8,128)(2,1)S(1)}, bf16[64,768]{1,0:T(8,128)(2,1)S(1)}, u32[]{:S(2)}, u32[]{:S(2)}) collective-permute-start(bf16[64,768]{1,0:T(8,128)(2,1)S(1)} %add_convert_fusion.1), channel_id=1, source_target_pairs={{0,16},{8,24},{16,0},{24,8},{1,17},{9,25},{17,1},{25,9},{2,18},{10... | collective-permute-start | bytes 294920 | tf_op jit(solution)/shard_map/ppermute | solution.py:92
  54.2 7.2 %collective-permute-start.4 = (bf16[64,768]{1,0:T(8,128)(2,1)S(1)}, bf16[64,768]{1,0:T(8,128)(2,1)S(1)}, u32[]{:S(2)}, u32[]{:S(2)}) collective-permute-start(bf16[64,768]{1,0:T(8,128)(2,1)S(1)} %add_convert_fusion.3), channel_id=1, source_target_pairs={{0,16},{8,24},{16,0},{24,8},{1,17},{9,25},{17,1},{25,9},{2,18},{10... | collective-permute-start | bytes 294920 | tf_op jit(solution)/shard_map/ppermute | solution.py:92
  57.7 6.5 %collective-permute-start.2 = (bf16[64,768]{1,0:T(8,128)(2,1)S(1)}, bf16[64,768]{1,0:T(8,128)(2,1)S(1)}, u32[]{:S(2)}, u32[]{:S(2)}) collective-permute-start(bf16[64,768]{1,0:T(8,128)(2,1)S(1)} %add_convert_fusion.4), channel_id=1, source_target_pairs={{0,8},{8,0},{16,24},{24,16},{1,9},{9,1},{17,25},{25,17},{2,10},{10... | collective-permute-start | bytes 294920 | tf_op jit(solution)/shard_map/ppermute | solution.py:96
  61.4 1.4 %collective-permute-start.5 = (bf16[64,768]{1,0:T(8,128)(2,1)S(1)}, bf16[64,768]{1,0:T(8,128)(2,1)S(1)}, u32[]{:S(2)}, u32[]{:S(2)}) collective-permute-start(bf16[64,768]{1,0:T(8,128)(2,1)S(1)} %add_convert_fusion.2), channel_id=1, source_target_pairs={{0,8},{8,0},{16,24},{24,16},{1,9},{9,1},{17,25},{25,17},{2,10},{10... | collective-permute-start | bytes 294920 | tf_op jit(solution)/shard_map/ppermute | solution.py:96
  61.5 1.5 %collective-permute-start.8 = (bf16[64,768]{1,0:T(8,128)(2,1)S(1)}, bf16[64,768]{1,0:T(8,128)(2,1)S(1)}, u32[]{:S(2)}, u32[]{:S(2)}) collective-permute-start(bf16[64,768]{1,0:T(8,128)(2,1)S(1)} %add_convert_fusion), channel_id=1, source_target_pairs={{0,8},{8,0},{16,24},{24,16},{1,9},{9,1},{17,25},{25,17},{2,10},{10... | collective-permute-start | bytes 294920 | tf_op jit(solution)/shard_map/ppermute | solution.py:96
  63.8 4.4 %collective-permute-start.15 = (f32[8,1,16]{2,0,1:T(8,128)S(1)}, f32[8,1,16]{2,0,1:T(8,128)S(1)}, u32[]{:S(2)}, u32[]{:S(2)}) collective-permute-start(f32[8,1,16]{2,0,1:T(8,128)S(1)} %reshape.125), channel_id=1, source_target_pairs={{0,8},{8,0},{16,24},{24,16},{1,9},{9,1},{17,25},{25,17},{2,10},{10... | collective-permute-start | bytes 1544 | tf_op jit(solution)/shard_map/ppermute | solution.py:53
  66.2 3.6 %copy-start.4 = (bf16[128,1280]{1,0:T(8,128)(2,1)S(1)}, bf16[128,1280]{1,0:T(8,128)(2,1)}, u32[]{:S(2)}) copy-start(bf16[128,1280]{1,0:T(8,128)(2,1)} %fusion.22) | copy-start | bytes 983044
  68.2 3.6 %collective-permute-start.16 = (f32[8,1,16]{2,0,1:T(8,128)S(1)}, f32[8,1,16]{2,0,1:T(8,128)S(1)}, u32[]{:S(2)}, u32[]{:S(2)}) collective-permute-start(f32[8,1,16]{2,0,1:T(8,128)S(1)} %add.89), channel_id=1, source_target_pairs={{0,16},{8,24},{16,0},{24,8},{1,17},{9,25},{17,1},{25,9},{2,18},{10... | collective-permute-start | bytes 1544 | tf_op jit(solution)/shard_map/ppermute | solution.py:53
  73.7 2.4 %collective-permute-start.17 = (bf16[2,128,96]{1,2,0:T(8,128)(2,1)S(1)}, bf16[2,128,96]{1,2,0:T(8,128)(2,1)S(1)}, u32[]{:S(2)}, u32[]{:S(2)}) collective-permute-start(bf16[2,128,96]{1,2,0:T(8,128)(2,1)S(1)} %convolution_convert_fusion.5), channel_id=1, source_target_pairs={{0,8},{8,0},{16,24},{24,16},{1,9},{9,1},{17,25},{25,17},{2,10},{10... | collective-permute-start | bytes 147464 | tf_op jit(solution)/shard_map/ppermute | solution.py:67
  74.2 5.8 %collective-permute-start.9 = (bf16[2,128,96]{1,2,0:T(8,128)(2,1)S(1)}, bf16[2,128,96]{1,2,0:T(8,128)(2,1)S(1)}, u32[]{:S(2)}, u32[]{:S(2)}) collective-permute-start(bf16[2,128,96]{1,2,0:T(8,128)(2,1)S(1)} %convolution_convert_fusion.8), channel_id=1, source_target_pairs={{0,8},{8,0},{16,24},{24,16},{1,9},{9,1},{17,25},{25,17},{2,10},{10... | collective-permute-start | bytes 147464 | tf_op jit(solution)/shard_map/ppermute | solution.py:67
  75.5 2.3 %collective-permute-start.11 = (bf16[2,128,96]{1,2,0:T(8,128)(2,1)S(1)}, bf16[2,128,96]{1,2,0:T(8,128)(2,1)S(1)}, u32[]{:S(2)}, u32[]{:S(2)}) collective-permute-start(bf16[2,128,96]{1,2,0:T(8,128)(2,1)S(1)} %convolution_convert_fusion.7), channel_id=1, source_target_pairs={{0,8},{8,0},{16,24},{24,16},{1,9},{9,1},{17,25},{25,17},{2,10},{10... | collective-permute-start | bytes 147464 | tf_op jit(solution)/shard_map/ppermute | solution.py:67
  75.6 2.9 %collective-permute-start.13 = (bf16[2,128,96]{1,2,0:T(8,128)(2,1)S(1)}, bf16[2,128,96]{1,2,0:T(8,128)(2,1)S(1)}, u32[]{:S(2)}, u32[]{:S(2)}) collective-permute-start(bf16[2,128,96]{1,2,0:T(8,128)(2,1)S(1)} %convolution_convert_fusion.6), channel_id=1, source_target_pairs={{0,8},{8,0},{16,24},{24,16},{1,9},{9,1},{17,25},{25,17},{2,10},{10... | collective-permute-start | bytes 147464 | tf_op jit(solution)/shard_map/ppermute | solution.py:67
  76.1 4.6 %collective-permute-start.18 = (bf16[2,128,96]{1,2,0:T(8,128)(2,1)S(1)}, bf16[2,128,96]{1,2,0:T(8,128)(2,1)S(1)}, u32[]{:S(2)}, u32[]{:S(2)}) collective-permute-start(bf16[2,128,96]{1,2,0:T(8,128)(2,1)S(1)} %add_convert_fusion.6), channel_id=1, source_target_pairs={{0,16},{8,24},{16,0},{24,8},{1,17},{9,25},{17,1},{25,9},{2,18},{10... | collective-permute-start | bytes 147464 | tf_op jit(solution)/shard_map/ppermute | solution.py:67
  77.8 4.5 %collective-permute-start.12 = (bf16[2,128,96]{1,2,0:T(8,128)(2,1)S(1)}, bf16[2,128,96]{1,2,0:T(8,128)(2,1)S(1)}, u32[]{:S(2)}, u32[]{:S(2)}) collective-permute-start(bf16[2,128,96]{1,2,0:T(8,128)(2,1)S(1)} %add_convert_fusion.8), channel_id=1, source_target_pairs={{0,16},{8,24},{16,0},{24,8},{1,17},{9,25},{17,1},{25,9},{2,18},{10... | collective-permute-start | bytes 147464 | tf_op jit(solution)/shard_map/ppermute | solution.py:67
  78.5 4.6 %collective-permute-start.14 = (bf16[2,128,96]{1,2,0:T(8,128)(2,1)S(1)}, bf16[2,128,96]{1,2,0:T(8,128)(2,1)S(1)}, u32[]{:S(2)}, u32[]{:S(2)}) collective-permute-start(bf16[2,128,96]{1,2,0:T(8,128)(2,1)S(1)} %add_convert_fusion.7), channel_id=1, source_target_pairs={{0,16},{8,24},{16,0},{24,8},{1,17},{9,25},{17,1},{25,9},{2,18},{10... | collective-permute-start | bytes 147464 | tf_op jit(solution)/shard_map/ppermute | solution.py:67
  80.0 9.1 %collective-permute-start.10 = (bf16[2,128,96]{1,2,0:T(8,128)(2,1)S(1)}, bf16[2,128,96]{1,2,0:T(8,128)(2,1)}, u32[]{:S(2)}, u32[]{:S(2)}) collective-permute-start(bf16[2,128,96]{1,2,0:T(8,128)(2,1)S(1)} %add_convert_fusion.9), channel_id=1, source_target_pairs={{0,16},{8,24},{16,0},{24,8},{1,17},{9,25},{17,1},{25,9},{2,18},{10... | collective-permute-start | bytes 147464 | tf_op jit(solution)/shard_map/ppermute | solution.py:67
  84.6 8.7 %copy-start.14 = (f32[2,128]{1,0:T(2,128)S(1)}, f32[2,128]{1,0:T(2,128)}, u32[]{:S(2)}) copy-start(f32[2,128]{1,0:T(2,128)} %copy-done.13) | copy-start | bytes 3076
  85.2 10.5 %all-to-all-start.1 = ((f32[8,3,16]{2,1,0:T(4,128)}), f32[8,3,16]{2,1,0:T(4,128)}, u32[]{:S(2)}, u32[]{:S(2)}) async-start(f32[8,3,16]{2,1,0:T(4,128)} %copy.58), calls=%async_computation.1 | async-start | bytes 32768 | tf_op jit(solution)/shard_map/all_to_all | solution.py:236
  91.2 6.1 %copy-start.10 = (s32[256,6]{0,1:T(8,128)S(1)}, s32[256,6]{0,1:T(8,128)}, u32[]{:S(2)}) copy-start(s32[256,6]{0,1:T(8,128)} %param.14) | copy-start | bytes 18436
  91.2 6.1 %copy-start.12 = (s32[10]{0:T(128)S(1)}, s32[10]{0:T(128)}, u32[]{:S(2)}) copy-start(s32[10]{0:T(128)} %copy-done.11) | copy-start | bytes 124
  (6 other events, 8.3 us)
Sparse Core Ops, SparseCore 0:
  26.2 45.5 all-gather.2
